TPU v7x, 32 devices: a whole 2x2x4 slice. The times are simulated.
32 devices in a mesh: fsdp: 8 (over z, y), rows: 4 (over x, core).
Axes of the slice: x: 2, y: 2, z: 4, core: 2. Of those that a mesh axis runs over, the one named last changes fastest.
Arguments:
- frames: bfloat16 [8, 12, 16, 1536], P('fsdp', 'rows'), may hold values from -6 to 6
- kernel: float32 [7, 7, 1536], replicated, may hold values from -0.875 to 0.875
- kernel_bias: float32 [1536], replicated, may hold values from -3 to 3
- layer_norm_weight: float32 [1536], replicated, may hold values from 0.25 to 1.75
- layer_norm_bias: float32 [1536], replicated, may hold values from -3 to 3
- up_weight: bfloat16 [1536, 6144], P('fsdp', 'rows'), may hold values from -1 to 1, as said below
- up_bias: float32 [6144], P('rows'), may hold values from -3 to 3
- grn_gamma: float32 [6144], P('rows'), may hold values from 0.2 to 1
- grn_beta: float32 [6144], P('rows'), may hold values from -3 to 3
- grad_out: bfloat16 [8, 12, 16, 6144], P('fsdp', None, None, 'rows'), may hold values from -8 to 8, as said below
Outputs:
- activation: bfloat16 [8, 12, 16, 6144], P('fsdp', None, None, 'rows')
- frames_grad: bfloat16 [8, 12, 16, 1536], P('fsdp', 'rows')
- up_weight_grad: float32 [1536, 6144], P('fsdp', 'rows')
- kernel_grad: float32 [7, 7, 1536], replicated
Inputs may be any that keep to these rules, and one draw needn't show every extreme that they name: `up_weight`: entries lie within the bounds. `grad_out`: entries lie within the bounds.
All inputs are finite; a program needn't handle non-finite values.
Results may differ from a plain program's by a relative error of at most 0.014.
Values may be sent and summed in bfloat16 or wider, within the bound.
No kernel may reach another device: no remote copies, remote signals or barrier semaphores. Data moves between devices by JAX's collectives and lax.ppermute only.
A program may use at most 64 MiB of HBM per device.

v0:
```python
import jax
import jax.numpy as jnp
from jax import lax
from jax.sharding import PartitionSpec as P

FF = 6144


def extended(block, sides, width):
    for axis, dim in sides:
        count = lax.axis_size(axis)
        forward = [(i, i + 1) for i in range(count - 1)]
        backward = [(target, source) for source, target in forward]
        low = lax.ppermute(
            lax.slice_in_dim(block, block.shape[dim] - width, None, axis=dim), axis, forward
        )
        high = lax.ppermute(lax.slice_in_dim(block, 0, width, axis=dim), axis, backward)
        block = jnp.concatenate([low, block, high], axis=dim)
    return block


def conv_rows(framed, kern, kbias):
    rows = framed.shape[0] - 6
    cols = framed.shape[1]
    wide = jnp.pad(framed, ((0, 0), (3, 3), (0, 0)))
    total = jnp.zeros((rows, cols, framed.shape[2]), jnp.float32) + kbias
    for i in range(kern.shape[0]):
        for j in range(kern.shape[1]):
            total = total + wide[i : i + rows, j : j + cols].astype(jnp.float32) * kern[i, j]
    return total


def back_conv(grad_pad, kern):
    rows = grad_pad.shape[0] - 6
    cols = grad_pad.shape[1]
    wide = jnp.pad(grad_pad, ((0, 0), (3, 3), (0, 0)))
    total = jnp.zeros((rows, cols, grad_pad.shape[2]), jnp.float32)
    for i in range(kern.shape[0]):
        for j in range(kern.shape[1]):
            total = (
                total
                + wide[6 - i : 6 - i + rows, 6 - j : 6 - j + cols].astype(jnp.float32) * kern[i, j]
            )
    return total


def kern_grad(framed, grad_rows):
    rows = grad_rows.shape[0]
    cols = grad_rows.shape[1]
    wide = jnp.pad(framed, ((0, 0), (3, 3), (0, 0)))
    grad_f = grad_rows.astype(jnp.float32)
    parts = []
    for i in range(7):
        for j in range(7):
            parts.append(
                jnp.sum(wide[i : i + rows, j : j + cols].astype(jnp.float32) * grad_f, axis=(0, 1))
            )
    return jnp.stack(parts).reshape(7, 7, grad_rows.shape[2])


def apply_layer_norm(activation_rows, scale_factor, offset_bias):
    centered_input = activation_rows - jnp.mean(activation_rows, axis=-1, keepdims=True)
    inverse_deviation = lax.rsqrt(
        jnp.mean(centered_input * centered_input, axis=-1, keepdims=True) + 1e-06
    )
    standardized_input = centered_input * inverse_deviation
    return (
        (standardized_input * scale_factor + offset_bias).astype(jnp.bfloat16),
        standardized_input,
        inverse_deviation,
    )


def gelu_grad(value):
    return (
        0.5 * (1.0 + jax.scipy.special.erf(value * 0.7071067811865476))
        + value * jnp.exp(-0.5 * value * value) * 0.3989422804014327
    )


def layer_norm_backward(normed_input_gradient, scale_factor, standardized_input, inverse_deviation):
    scaled_output = normed_input_gradient * scale_factor
    return (
        inverse_deviation
        * (
            scaled_output
            - jnp.mean(scaled_output, axis=-1, keepdims=True)
            - standardized_input
            * jnp.mean(scaled_output * standardized_input, axis=-1, keepdims=True)
        )
    ).astype(jnp.bfloat16)


def body(
    frames,
    kernel,
    kernel_bias,
    layer_norm_weight,
    layer_norm_bias,
    up_weight,
    up_bias,
    grn_gamma,
    grn_beta,
    grad_out,
):
    slab = frames[0]
    chans = slab.shape[2]
    columns = lax.all_gather(up_weight, "fsdp", axis=0, tiled=True)
    padded = extended(slab, (("rows", 0),), 3)
    activation_rows = conv_rows(padded, kernel, kernel_bias)
    normed_output, standardized_input, inverse_deviation = apply_layer_norm(
        activation_rows, layer_norm_weight, layer_norm_bias
    )
    whole = lax.all_gather(normed_output, "rows", axis=0, tiled=True)
    height = whole.shape[0]
    cols = whole.shape[1]
    flat = whole.reshape(-1, chans)
    pre = jnp.dot(flat, columns, preferred_element_type=jnp.float32) + up_bias
    post = jax.nn.gelu(pre, approximate=False)
    norms = jnp.sqrt(jnp.sum(post * post, axis=0) + 1e-06)
    cot_f = grad_out[0].reshape(flat.shape[0], -1).astype(jnp.float32)
    dnorm = grn_gamma * jnp.sum(cot_f * post, axis=0)
    norm_total = lax.psum(jnp.sum(norms), "rows")
    denom = norm_total / FF + 1e-06
    ratio = norms / denom
    output = (grn_gamma * (post * ratio) + grn_beta + post).astype(jnp.bfloat16)
    cross = lax.psum(jnp.sum(dnorm * norms), "rows")
    dnorms = dnorm / denom - cross / (denom * denom) / FF
    dpost = cot_f * (1.0 + grn_gamma * ratio) + post * (dnorms / norms)
    dpre = (dpost * gelu_grad(pre)).astype(jnp.bfloat16)
    w_term = lax.dot_general(
        flat, dpre, (((0,), (0,)), ((), ())), preferred_element_type=jnp.float32
    )
    up_grad = lax.psum_scatter(
        w_term.astype(jnp.bfloat16), "fsdp", scatter_dimension=0, tiled=True
    ).astype(jnp.float32)
    dpre_rows = dpre.reshape(height, cols, -1)
    normed_input_gradient = lax.psum_scatter(
        jnp.einsum("hwf,cf->hwc", dpre_rows, columns, preferred_element_type=jnp.float32).astype(
            jnp.bfloat16
        ),
        "rows",
        scatter_dimension=0,
        tiled=True,
    ).astype(jnp.float32)
    activation_gradient = layer_norm_backward(
        normed_input_gradient, layer_norm_weight, standardized_input, inverse_deviation
    )
    grad_pad = extended(activation_gradient, (("rows", 0),), 3)
    dframe = back_conv(grad_pad, kernel).astype(jnp.bfloat16)
    kernel_local = kern_grad(padded, activation_gradient)
    kernel_total = lax.psum(kernel_local, ("fsdp", "rows"))
    activation = output.reshape(1, height, cols, -1)
    return (activation, dframe.reshape((1,) + dframe.shape), up_grad, kernel_total)


def solution(mesh):
    placed = (
        P("fsdp", "rows", None, None),
        P(),
        P(),
        P(),
        P(),
        P("fsdp", "rows"),
        P("rows"),
        P("rows"),
        P("rows"),
        P("fsdp", None, None, "rows"),
    )
    return jax.shard_map(
        body,
        mesh=mesh,
        in_specs=placed,
        out_specs=(
            P("fsdp", None, None, "rows"),
            P("fsdp", "rows", None, None),
            P("fsdp", "rows"),
            P(),
        ),
        check_vma=False,
    )
```

profile of v0, /device:TPU:0, one launch (start us, length us, event | category | flops | bytes accessed | tf_op | source)
XLA Modules:
  0.0 376.1 jit_solution(9324311914852352310)
XLA Ops:
  7.2 0.0 all-gather.2.cloned.1.call-start
  7.2 0.7 all-gather.2.cloned.1.call-update
  7.9 0.0 reduce-scatter.3.cloned.1.call-start
  8.0 1.3 collective-permute-start.1
  9.3 3.0 collective-permute-start
  12.3 2.0 slice_reduce_fusion.48
  14.3 1.3 slice_reduce_fusion.46
  15.6 0.0 copy-start.4
  15.6 1.8 slice_reduce_fusion.47
  17.6 0.2 select_maximum_fusion.2
  17.9 0.0 copy-start.3
  17.9 0.0 copy-start.50
  17.9 3.4 fusion.158
  21.5 0.0 copy-start.1
  21.5 0.0 copy-start.53
  21.5 0.2 multiply_reduce_fusion.2
  21.7 0.4 copy-done.46
  22.1 0.6 copy-done.48
  22.7 0.1 add_convert_fusion.1
  22.8 9.2 %all_gather.6 = bf16[12,16,1536]{2,1,0:T(8,128)(2,1)S(1)} all-gather(bf16[3,16,1536]{2,1,0:T(8,128)(2,1)S(1)} %add_convert_fusion.1), channel_id=1, replica_groups=mesh['fsdp'=8,'rows'=4] {'rows'}, dimensions={0}, use_global_device_ids=true | all-gather | bytes 737280 | tf_op jit(solution)/shard_map/all_gather | solution.py:114
  32.1 60.8 %all-gather.2.cloned.1.call-done = bf16[1536,1536]{1,0:T(8,128)(2,1)} async-done(((bf16[192,1536]{1,0:T(8,128)(2,1)}), bf16[1536,1536]{1,0:T(8,128)(2,1)}) %all-gather.2.cloned.1.call-update) | async-done | bytes 4718608 | tf_op jit(solution)/shard_map/all_gather | solution.py:108
  92.8 7.3 %fusion.9 = (f32[1536]{0:T(1024)S(1)}, f32[1536]{0:T(1024)S(1)}, f32[192,1536]{1,0:T(8,128)}, f32[192,1536]{1,0:T(8,128)}) fusion(bf16[1,12,16,1536]{3,2,1,0:T(8,128)(2,1)S(1)} %copy-done.1, f32[1536]{0:T(1024)S(1)} %copy-done.53, bf16[192,1536]{1,0:T(8,128)(2,1)S(1)} %bitcast.21, bf16[1536,1536]{1,0:T(8,128)(2,1)} %all-gather.2.cloned.1.call-done), kind=kOutput, calls=%fused_computation.65 | convolution fusion | flops 926610432 | bytes 8275968 | tf_op jit(solution)/shard_map/dot_general | solution.py:118
  100.2 0.7 multiply_reduce_fusion.3
  100.9 6.3 %all-reduce.2 = (f32[]{:T(128)}, f32[]{:T(128)}) all-reduce(f32[]{:T(128)} %get-tuple-element.115, f32[]{:T(128)} %get-tuple-element.114), channel_id=1, replica_groups=mesh['fsdp'=8,'rows'=4] {'rows'}, use_global_device_ids=true, to_apply=%region_4.5 | all-reduce | flops 2 | bytes 16 | tf_op jit(solution)/shard_map/psum | solution.py:123
  108.5 3.2 fusion.8
  111.7 4.8 %fusion.2 = bf16[12,16,1536]{2,1,0:T(8,128)(2,1)} fusion(bf16[12,16,1536]{2,1,0:T(8,128)(2,1)S(1)} %bitcast.23, bf16[1536,1536]{1,0:T(8,128)(2,1)} %all-gather.2.cloned.1.call-done), kind=kOutput, calls=%fused_computation.54 | convolution fusion | flops 906264576 | bytes 5898240 | tf_op jit(solution)/shard_map/hwf,cf->hwc/dot_general | solution.py:139
  116.6 0.0 reduce-scatter.3.cloned.1.call-update
  116.6 0.0 reduce-scatter.5.cloned.1.call-start
  116.6 3.6 convolution_convert_fusion
  120.2 0.0 reduce-scatter.5.cloned.1.call-update
  120.2 0.0 all-reduce.5.cloned.1.call-start
  120.3 17.0 %reduce-scatter.3.cloned.1.call-done = bf16[3,16,1536]{2,1,0:T(8,128)(2,1)} async-done(((bf16[12,16,1536]{2,1,0:T(8,128)(2,1)}), bf16[3,16,1536]{2,1,0:T(8,128)(2,1)}) %reduce-scatter.3.cloned.1.call-update) | async-done | bytes 147472 | tf_op jit(solution)/shard_map/reduce_scatter | solution.py:138
  137.2 1.1 fusion.147
  138.3 1.9 fusion.145
  140.2 1.5 collective-permute-start.3
  141.7 3.0 collective-permute-start.2
  144.7 0.8 fusion.146
  145.5 0.6 fusion.136
  146.7 0.5 stack.199
  147.3 0.0 copy-start.5
  147.5 0.8 reshape.62
  148.2 0.0 all-reduce.5.cloned.1.call-update
  148.3 0.2 select_maximum_fusion
  148.7 2.8 fusion.153
  151.5 85.0 %reduce-scatter.5.cloned.1.call-done = bf16[192,1536]{1,0:T(8,128)(2,1)} async-done(((bf16[1536,1536]{1,0:T(8,128)(2,1)}), bf16[192,1536]{1,0:T(8,128)(2,1)}) %reduce-scatter.5.cloned.1.call-update) | async-done | bytes 589840 | tf_op jit(solution)/shard_map/reduce_scatter | solution.py:134
  236.6 2.2 convert_element_type.489
  238.8 129.1 %all-reduce.5.cloned.1.call-done = f32[7,7,1536]{2,1,0:T(8,128)} async-done(((f32[7,7,1536]{2,1,0:T(8,128)}), f32[7,7,1536]{2,1,0:T(8,128)}) %all-reduce.5.cloned.1.call-update) | async-done | bytes 301072 | tf_op jit(solution)/shard_map/psum | solution.py:152
  367.8 1.7 copy.15
  (157 shorter events, 0.6 us)
Async XLA Ops:
  7.2 10.5 %copy-start = (bf16[1,3,16,1536]{3,2,1,0:T(8,128)(2,1)S(1)}, bf16[1,3,16,1536]{3,2,1,0:T(8,128)(2,1)}, u32[]{:S(2)}) copy-start(bf16[1,3,16,1536]{3,2,1,0:T(8,128)(2,1)} %param.10) | copy-start | bytes 442372
  7.2 10.7 %copy-start.52 = (f32[1536]{0:T(1024)S(1)}, f32[1536]{0:T(1024)}, u32[]{:S(2)}) copy-start(f32[1536]{0:T(1024)} %param.12) | copy-start | bytes 18436
  7.2 85.6 %all-gather.2.cloned.1.call-start = ((), (), s32[]{:S(2)}) async-start(), calls=%async_computation.2 | async-start | bytes 5308416 | tf_op jit(solution)/shard_map/all_gather | solution.py:108
  7.9 129.3 %reduce-scatter.3.cloned.1.call-start = ((), (), s32[]{:S(2)}) async-start(), calls=%async_computation.3 | async-start | bytes 737280 | tf_op jit(solution)/shard_map/reduce_scatter | solution.py:138
  8.0 9.6 %collective-permute-start.1 = (bf16[3,16,1536]{2,1,0:T(8,128)(2,1)}, bf16[3,16,1536]{2,1,0:T(8,128)(2,1)S(1)}, u32[]{:S(2)}, u32[]{:S(2)}) collective-permute-start(bf16[3,16,1536]{2,1,0:T(8,128)(2,1)} %bitcast.24), channel_id=1, source_target_pairs={{1,0},{2,1},{3,2},{5,4},{6,5},{7,6},{9,8},{10,9},{11,10},{13,12},{... | collective-permute-start | bytes 442376 | tf_op jit(solution)/shard_map/ppermute | solution.py:17
  9.3 8.3 %collective-permute-start = (bf16[3,16,1536]{2,1,0:T(8,128)(2,1)}, bf16[3,16,1536]{2,1,0:T(8,128)(2,1)S(1)}, u32[]{:S(2)}, u32[]{:S(2)}) collective-permute-start(bf16[3,16,1536]{2,1,0:T(8,128)(2,1)} %bitcast.25), channel_id=1, source_target_pairs={{0,1},{1,2},{2,3},{4,5},{5,6},{6,7},{8,9},{9,10},{10,11},{12,13},{... | collective-permute-start | bytes 442376 | tf_op jit(solution)/shard_map/ppermute | solution.py:14
  15.6 5.7 %copy-start.4 = (f32[1536]{0:T(1024)}, f32[1536]{0:T(1024)S(1)}, u32[]{:S(2)}) copy-start(f32[1536]{0:T(1024)S(1)} %get-tuple-element.99) | copy-start | bytes 18436
  15.6 5.7 %copy-start.6 = (f32[1536]{0:T(1024)}, f32[1536]{0:T(1024)S(1)}, u32[]{:S(2)}) copy-start(f32[1536]{0:T(1024)S(1)} %get-tuple-element.100) | copy-start | bytes 18436
  17.4 3.9 %copy-start.8 = (f32[1536]{0:T(1024)}, f32[1536]{0:T(1024)S(1)}, u32[]{:S(2)}) copy-start(f32[1536]{0:T(1024)S(1)} %get-tuple-element.71) | copy-start | bytes 18436
  17.4 3.9 %copy-start.10 = (f32[1536]{0:T(1024)}, f32[1536]{0:T(1024)S(1)}, u32[]{:S(2)}) copy-start(f32[1536]{0:T(1024)S(1)} %get-tuple-element.72) | copy-start | bytes 18436
  17.4 3.9 %copy-start.12 = (f32[1536]{0:T(1024)}, f32[1536]{0:T(1024)S(1)}, u32[]{:S(2)}) copy-start(f32[1536]{0:T(1024)S(1)} %get-tuple-element.73) | copy-start | bytes 18436
  17.4 3.9 %copy-start.14 = (f32[1536]{0:T(1024)}, f32[1536]{0:T(1024)S(1)}, u32[]{:S(2)}) copy-start(f32[1536]{0:T(1024)S(1)} %get-tuple-element.74) | copy-start | bytes 18436
  17.4 3.9 %copy-start.16 = (f32[1536]{0:T(1024)}, f32[1536]{0:T(1024)S(1)}, u32[]{:S(2)}) copy-start(f32[1536]{0:T(1024)S(1)} %get-tuple-element.75) | copy-start | bytes 18436
  17.5 3.9 %copy-start.18 = (f32[1536]{0:T(1024)}, f32[1536]{0:T(1024)S(1)}, u32[]{:S(2)}) copy-start(f32[1536]{0:T(1024)S(1)} %get-tuple-element.76) | copy-start | bytes 18436
  17.5 3.9 %copy-start.20 = (f32[1536]{0:T(1024)}, f32[1536]{0:T(1024)S(1)}, u32[]{:S(2)}) copy-start(f32[1536]{0:T(1024)S(1)} %get-tuple-element.77) | copy-start | bytes 18436
  17.5 3.9 %copy-start.22 = (f32[1536]{0:T(1024)}, f32[1536]{0:T(1024)S(1)}, u32[]{:S(2)}) copy-start(f32[1536]{0:T(1024)S(1)} %get-tuple-element.78) | copy-start | bytes 18436
  17.5 3.9 %copy-start.24 = (f32[1536]{0:T(1024)}, f32[1536]{0:T(1024)S(1)}, u32[]{:S(2)}) copy-start(f32[1536]{0:T(1024)S(1)} %get-tuple-element.79) | copy-start | bytes 18436
  17.5 3.9 %copy-start.26 = (f32[1536]{0:T(1024)}, f32[1536]{0:T(1024)S(1)}, u32[]{:S(2)}) copy-start(f32[1536]{0:T(1024)S(1)} %get-tuple-element.80) | copy-start | bytes 18436
  17.5 3.9 %copy-start.28 = (f32[1536]{0:T(1024)}, f32[1536]{0:T(1024)S(1)}, u32[]{:S(2)}) copy-start(f32[1536]{0:T(1024)S(1)} %get-tuple-element.81) | copy-start | bytes 18436
  17.5 3.9 %copy-start.30 = (f32[1536]{0:T(1024)}, f32[1536]{0:T(1024)S(1)}, u32[]{:S(2)}) copy-start(f32[1536]{0:T(1024)S(1)} %get-tuple-element.82) | copy-start | bytes 18436
  17.5 3.9 %copy-start.32 = (f32[1536]{0:T(1024)}, f32[1536]{0:T(1024)S(1)}, u32[]{:S(2)}) copy-start(f32[1536]{0:T(1024)S(1)} %get-tuple-element.83) | copy-start | bytes 18436
  17.5 3.9 %copy-start.34 = (f32[1536]{0:T(1024)}, f32[1536]{0:T(1024)S(1)}, u32[]{:S(2)}) copy-start(f32[1536]{0:T(1024)S(1)} %get-tuple-element.84) | copy-start | bytes 18436
  17.5 3.9 %copy-start.36 = (f32[1536]{0:T(1024)}, f32[1536]{0:T(1024)S(1)}, u32[]{:S(2)}) copy-start(f32[1536]{0:T(1024)S(1)} %get-tuple-element.85) | copy-start | bytes 18436
  17.6 3.9 %copy-start.38 = (f32[1536]{0:T(1024)}, f32[1536]{0:T(1024)S(1)}, u32[]{:S(2)}) copy-start(f32[1536]{0:T(1024)S(1)} %get-tuple-element.86) | copy-start | bytes 18436
  17.6 3.9 %copy-start.40 = (f32[1536]{0:T(1024)}, f32[1536]{0:T(1024)S(1)}, u32[]{:S(2)}) copy-start(f32[1536]{0:T(1024)S(1)} %get-tuple-element.87) | copy-start | bytes 18436
  17.6 3.9 %copy-start.42 = (f32[1536]{0:T(1024)}, f32[1536]{0:T(1024)S(1)}, u32[]{:S(2)}) copy-start(f32[1536]{0:T(1024)S(1)} %get-tuple-element.88) | copy-start | bytes 18436
  17.6 3.9 %copy-start.44 = (f32[1536]{0:T(1024)}, f32[1536]{0:T(1024)S(1)}, u32[]{:S(2)}) copy-start(f32[1536]{0:T(1024)S(1)} %get-tuple-element.89) | copy-start | bytes 18436
  17.9 4.8 %copy-start.3 = (f32[1536]{0:T(1024)S(1)}, f32[1536]{0:T(1024)}, u32[]{:S(2)}) copy-start(f32[1536]{0:T(1024)} %param.13) | copy-start | bytes 18436
  17.9 4.8 %copy-start.50 = (f32[1536]{0:T(1024)S(1)}, f32[1536]{0:T(1024)}, u32[]{:S(2)}) copy-start(f32[1536]{0:T(1024)} %param.14) | copy-start | bytes 18436
  21.5 71.3 %copy-start.1 = (bf16[1,12,16,1536]{3,2,1,0:T(8,128)(2,1)S(1)}, bf16[1,12,16,1536]{3,2,1,0:T(8,128)(2,1)}, u32[]{:S(2)}) copy-start(bf16[1,12,16,1536]{3,2,1,0:T(8,128)(2,1)} %param.19) | copy-start | bytes 1769476
  21.5 71.3 %copy-start.53 = (f32[1536]{0:T(1024)S(1)}, f32[1536]{0:T(1024)}, u32[]{:S(2)}) copy-start(f32[1536]{0:T(1024)} %param.16) | copy-start | bytes 18436
  92.8 7.4 %copy-start.2 = (f32[1536]{0:T(1024)S(1)}, f32[1536]{0:T(1024)}, u32[]{:S(2)}) copy-start(f32[1536]{0:T(1024)} %param.17) | copy-start | bytes 18436
  92.8 15.6 %copy-start.51 = (f32[1536]{0:T(1024)S(1)}, f32[1536]{0:T(1024)}, u32[]{:S(2)}) copy-start(f32[1536]{0:T(1024)} %param.18) | copy-start | bytes 18436
  116.6 120.0 %reduce-scatter.5.cloned.1.call-start = ((), (), s32[]{:S(2)}) async-start(), calls=%async_computation.4 | async-start | bytes 5308416 | tf_op jit(solution)/shard_map/reduce_scatter | solution.py:134
  120.2 17.0 %copy-start.47 = (f32[3,16]{1,0:T(4,128)S(1)}, f32[3,16]{1,0:T(4,128)}, u32[]{:S(2)}) copy-start(f32[3,16]{1,0:T(4,128)} %copy-done.46) | copy-start | bytes 580
  120.2 17.0 %copy-start.49 = (f32[3,16]{1,0:T(4,128)S(1)}, f32[3,16]{1,0:T(4,128)}, u32[]{:S(2)}) copy-start(f32[3,16]{1,0:T(4,128)} %copy-done.48) | copy-start | bytes 580
  120.2 247.6 %all-reduce.5.cloned.1.call-start = ((), (), s32[]{:S(2)}) async-start(), calls=%async_computation.5 | async-start | bytes 688128 | tf_op jit(solution)/shard_map/psum | solution.py:152
  140.2 8.1 %collective-permute-start.3 = (bf16[3,16,1536]{2,1,0:T(8,128)(2,1)S(1)}, bf16[3,16,1536]{2,1,0:T(8,128)(2,1)S(1)}, u32[]{:S(2)}, u32[]{:S(2)}) collective-permute-start(bf16[3,16,1536]{2,1,0:T(8,128)(2,1)S(1)} %get-tuple-element.118), channel_id=1, source_target_pairs={{1,0},{2,1},{3,2},{5,4},{6,5},{7,6},{9,8},{10,9},{11,10},{13,12},{... | collective-permute-start | bytes 442376 | tf_op jit(solution)/shard_map/ppermute | solution.py:17
  141.7 6.6 %collective-permute-start.2 = (bf16[3,16,1536]{2,1,0:T(8,128)(2,1)S(1)}, bf16[3,16,1536]{2,1,0:T(8,128)(2,1)S(1)}, u32[]{:S(2)}, u32[]{:S(2)}) collective-permute-start(bf16[3,16,1536]{2,1,0:T(8,128)(2,1)S(1)} %get-tuple-element.118), channel_id=1, source_target_pairs={{0,1},{1,2},{2,3},{4,5},{5,6},{6,7},{8,9},{9,10},{10,11},{12,13},{... | collective-permute-start | bytes 442376 | tf_op jit(solution)/shard_map/ppermute | solution.py:14
  147.3 1.3 copy-start.5
  147.3 1.3 copy-start.7
  147.3 1.3 copy-start.9
  147.3 1.3 copy-start.11
  147.3 1.3 copy-start.13
  147.3 1.3 copy-start.15
  147.3 1.3 copy-start.17
  147.3 1.3 copy-start.19
  147.3 1.3 copy-start.21
  (14 other events, 16.2 us)
Sparse Core Ops, SparseCore 0:
  10.2 82.5 all-gather.1
  116.7 20.4 reduce-scatter.2
  140.9 95.6 reduce-scatter.4
  242.3 125.4 all-reduce.4
where the time goes:
time: 377 us; the launch traced here: 376 us
  waiting for transfers between devices  293 us (78%)
  other arithmetic  17.4 us (5%)
  between operations  16.3 us (4%)
  matrix products  15.7 us (4%)
  blocking collectives  15.5 us (4%)
  local copies, waits for them, and re-layouts  9.57 us (3%)
  starting transfers between devices  9 us (2%)
    psum x1, waiting for transfers between devices, body(): kernel_total = lax.psum(kernel_local, ('fsdp', 'rows'))  129 us
    reduce_scatter x1, waiting for transfers between devices, body(): lax.psum_scatter(w_term.astype(jnp.bfloat16), 'fsdp', scatter_dimension=0...  85 us
    all_gather x1, waiting for transfers between devices, body(): columns = lax.all_gather(up_weight, 'fsdp', axis=0, tiled=True)  60.8 us
    reduce_scatter x1, waiting for transfers between devices, body(): lax.psum_scatter(jnp.einsum('hwf,cf->hwc', dpre_rows, columns, preferred_...  17 us
    all_gather x1, blocking collectives, body(): whole = lax.all_gather(normed_output, 'rows', axis=0, tiled=True)  9.25 us
  transfers between devices with their start and end apart: 8, of which 4 were waited for; matrix products, arithmetic and copies ran while one was open for 6% of the time, Pallas kernels for 0%

commit v1 on v0

--- a/solution.py
+++ b/solution.py
@@ -17,6 +17,39 @@
         high = lax.ppermute(lax.slice_in_dim(block, 0, width, axis=dim), axis, backward)
         block = jnp.concatenate([low, block, high], axis=dim)
     return block
+
+
+def _bit_steps(axes):
+    steps = []
+    for axis in axes:
+        size = lax.axis_size(axis)
+        assert size & (size - 1) == 0
+        mask = 1
+        while mask < size:
+            steps.append((axis, mask, size))
+            mask *= 2
+    return steps
+
+
+def tree_allreduce(value, axes):
+    shape = value.shape
+    flat = value.reshape(-1)
+    steps = _bit_steps(axes)
+    assert flat.shape[0] % (1 << len(steps)) == 0
+    bits = []
+    for axis, mask, size in steps:
+        bit = (lax.axis_index(axis) // mask) % 2
+        bits.append(bit)
+        halves = flat.reshape(2, -1)
+        keep = lax.dynamic_index_in_dim(halves, bit, keepdims=False)
+        give = lax.dynamic_index_in_dim(halves, 1 - bit, keepdims=False)
+        perm = [(j, j ^ mask) for j in range(size)]
+        flat = keep + lax.ppermute(give, axis, perm)
+    for (axis, mask, size), bit in reversed(list(zip(steps, bits))):
+        perm = [(j, j ^ mask) for j in range(size)]
+        other = lax.ppermute(flat, axis, perm)
+        flat = jnp.where(bit == 0, jnp.concatenate([flat, other]), jnp.concatenate([other, flat]))
+    return flat.reshape(shape)
 
 
 def conv_rows(framed, kern, kbias):
@@ -149,7 +182,7 @@
     grad_pad = extended(activation_gradient, (("rows", 0),), 3)
     dframe = back_conv(grad_pad, kernel).astype(jnp.bfloat16)
     kernel_local = kern_grad(padded, activation_gradient)
-    kernel_total = lax.psum(kernel_local, ("fsdp", "rows"))
+    kernel_total = tree_allreduce(kernel_local, ("rows", "fsdp"))
     activation = output.reshape(1, height, cols, -1)
     return (activation, dframe.reshape((1,) + dframe.shape), up_grad, kernel_total)
 

time: 377 us -> 247 us (0.66)
  waiting for transfers between devices: 293 us -> 151 us
  starting transfers between devices: 9 us -> 18.3 us
    psum x1 -> x0, waiting for transfers between devices: 129 us -> none  [body(): kernel_total = lax.psum(kernel_local, ('fsdp', 'rows'))]
    reduce_scatter x1, waiting for transfers between devices: 85 us -> 44.6 us  [body(): lax.psum_scatter(w_term.astype(jnp.bfloat16), 'fsdp', scatter_dimension=0...]
    ppermute x0 -> x10, waiting for transfers between devices: none -> 29 us  [the longest x5 17.1 us: tree_allreduce(): flat = keep + lax.ppermute(give, axis, perm)]
    ppermute x0 -> x10, starting transfers between devices: none -> 11.8 us  [the longest x5 6.79 us: tree_allreduce(): other = lax.ppermute(flat, axis, perm)]
  transfers between devices with their start and end apart: 8 -> 17, of which waited for: 4 -> 11; matrix products, arithmetic and copies ran while one was open for 6% -> 10% of each run, Pallas kernels for 0% -> 0%
where the time goes in v1:
time: 247 us; the launch traced here: 246 us
  waiting for transfers between devices  151 us (61%)
  starting transfers between devices  18.3 us (7%)
  other arithmetic  17.7 us (7%)
  blocking collectives  17.2 us (7%)
  between operations  16.5 us (7%)
  matrix products  15.7 us (6%)
  local copies, waits for them, and re-layouts  10.2 us (4%)
    all_gather x1, waiting for transfers between devices, body(): columns = lax.all_gather(up_weight, 'fsdp', axis=0, tiled=True)  59.8 us
    reduce_scatter x1, waiting for transfers between devices, body(): lax.psum_scatter(w_term.astype(jnp.bfloat16), 'fsdp', scatter_dimension=0...  44.6 us
    ppermute x5, waiting for transfers between devices, tree_allreduce(): flat = keep + lax.ppermute(give, axis, perm)  17.1 us
    reduce_scatter x1, waiting for transfers between devices, body(): lax.psum_scatter(jnp.einsum('hwf,cf->hwc', dpre_rows, columns, preferred_...  16.8 us
    ppermute x5, waiting for transfers between devices, tree_allreduce(): other = lax.ppermute(flat, axis, perm)  11.9 us
    all_gather x1, blocking collectives, body(): whole = lax.all_gather(normed_output, 'rows', axis=0, tiled=True)  10.9 us
    dot_general x1, matrix products, body(): pre = jnp.dot(flat, columns, preferred_element_type=jnp.float32) + up_bias  7.34 us
    ppermute x5, starting transfers between devices, tree_allreduce(): other = lax.ppermute(flat, axis, perm)  6.79 us
  transfers between devices with their start and end apart: 17, of which 11 were waited for; matrix products, arithmetic and copies ran while one was open for 10% of the time, Pallas kernels for 0%

profile of v1, /device:TPU:0, one launch (start us, length us, event | category | flops | bytes accessed | tf_op | source)
XLA Modules:
  0.0 246.5 jit_solution(1913901209624429076)
XLA Ops:
  7.2 0.7 all-gather.2.cloned.1.call-update
  8.0 2.4 collective-permute-start
  10.3 1.3 collective-permute-start.1
  11.6 2.0 slice_reduce_fusion.48
  13.6 1.3 slice_reduce_fusion.46
  14.9 1.8 slice_reduce_fusion.47
  17.2 3.4 %fusion.158 = (f32[3,16]{1,0:T(4,128)S(1)}, f32[3,16,1536]{2,1,0:T(8,128)S(1)}) fusion(f32[1536]{0:T(1024)S(1)} %get-tuple-element.99, bf16[9,22,1536]{2,1,0:T(8,128)(2,1)S(1)} %select_maximum_fusion.2, f32[1536]{0:T(1024)S(1)} %get-tuple-element.100, f32[1536]{0:T(1024)S(1)} %get-tuple-element.53, f32[1536]{0:T(1024)S(1)} %get-tuple-element.54, ...), kind=kLoop, calls=%fused_computation.365 | loop fusion | flops 11206608 | bytes 7237824 | tf_op jit(solution)/shard_map/reduce_sum | solution.py:95
  21.1 0.4 copy-done.46
  21.4 0.6 copy-done.48
  22.1 10.9 %all_gather.6 = bf16[12,16,1536]{2,1,0:T(8,128)(2,1)S(1)} all-gather(bf16[3,16,1536]{2,1,0:T(8,128)(2,1)S(1)} %add_convert_fusion.1), channel_id=1, replica_groups=mesh['fsdp'=8,'rows'=4] {'rows'}, dimensions={0}, use_global_device_ids=true | all-gather | bytes 737280 | tf_op jit(solution)/shard_map/all_gather | solution.py:147
  33.0 59.8 %all-gather.2.cloned.1.call-done = bf16[1536,1536]{1,0:T(8,128)(2,1)} async-done(((bf16[192,1536]{1,0:T(8,128)(2,1)}), bf16[1536,1536]{1,0:T(8,128)(2,1)}) %all-gather.2.cloned.1.call-update) | async-done | bytes 4718608 | tf_op jit(solution)/shard_map/all_gather | solution.py:141
  92.8 7.3 %fusion.9 = (f32[1536]{0:T(1024)S(1)}, f32[1536]{0:T(1024)S(1)}, f32[192,1536]{1,0:T(8,128)}, f32[192,1536]{1,0:T(8,128)}) fusion(bf16[1,12,16,1536]{3,2,1,0:T(8,128)(2,1)S(1)} %copy-done.1, f32[1536]{0:T(1024)S(1)} %copy-done.53, bf16[192,1536]{1,0:T(8,128)(2,1)S(1)} %bitcast.21, bf16[1536,1536]{1,0:T(8,128)(2,1)} %all-gather.2.cloned.1.call-done), kind=kOutput, calls=%fused_computation.65 | convolution fusion | flops 926610432 | bytes 8275968 | tf_op jit(solution)/shard_map/dot_general | solution.py:151
  100.2 0.7 multiply_reduce_fusion.3
  100.9 6.3 %all-reduce.2 = (f32[]{:T(128)}, f32[]{:T(128)}) all-reduce(f32[]{:T(128)} %get-tuple-element.125, f32[]{:T(128)} %get-tuple-element.124), channel_id=1, replica_groups=mesh['fsdp'=8,'rows'=4] {'rows'}, use_global_device_ids=true, to_apply=%region_4.5 | all-reduce | flops 2 | bytes 16 | tf_op jit(solution)/shard_map/psum | solution.py:156
  108.5 3.2 %fusion.8 = (bf16[192,1536]{1,0:T(8,128)(2,1)S(1)}, bf16[192,1536]{1,0:T(8,128)(2,1)}) fusion(f32[192,1536]{1,0:T(8,128)} %get-tuple-element.137, f32[192,1536]{1,0:T(8,128)} %get-tuple-element.131, bf16[1,12,16,1536]{3,2,1,0:T(8,128)(2,1)S(1)} %copy-done.1, f32[1536]{0:T(1024)S(1)} %get-tuple-element.136, f32[1536]{0:T(1024)S(1)} %get-tuple-element.129, ...), kind=kLoop, calls=%fused_computation.64 | loop fusion | flops 5603328 | bytes 4159488 | tf_op jit(solution)/shard_map/convert_element_type | solution.py:163
  111.7 4.8 %fusion.2 = bf16[12,16,1536]{2,1,0:T(8,128)(2,1)} fusion(bf16[12,16,1536]{2,1,0:T(8,128)(2,1)S(1)} %bitcast.23, bf16[1536,1536]{1,0:T(8,128)(2,1)} %all-gather.2.cloned.1.call-done), kind=kOutput, calls=%fused_computation.54 | convolution fusion | flops 906264576 | bytes 5898240 | tf_op jit(solution)/shard_map/hwf,cf->hwc/dot_general | solution.py:172
  116.8 3.6 %convolution_convert_fusion = bf16[1536,1536]{1,0:T(8,128)(2,1)} fusion(bf16[192,1536]{1,0:T(8,128)(2,1)S(1)} %bitcast.22, bf16[192,1536]{1,0:T(8,128)(2,1)S(1)} %get-tuple-element.134), kind=kOutput, calls=%fused_computation | convolution fusion | flops 908328960 | bytes 5898240 | tf_op jit(solution)/shard_map/dot_general | solution.py:164
  120.4 16.8 %reduce-scatter.3.cloned.1.call-done = bf16[3,16,1536]{2,1,0:T(8,128)(2,1)} async-done(((bf16[12,16,1536]{2,1,0:T(8,128)(2,1)}), bf16[3,16,1536]{2,1,0:T(8,128)(2,1)}) %reduce-scatter.3.cloned.1.call-update) | async-done | bytes 147472 | tf_op jit(solution)/shard_map/reduce_scatter | solution.py:171
  137.2 1.1 fusion.147
  138.3 1.9 fusion.145
  140.2 0.6 fusion.136
  140.9 0.8 fusion.146
  142.2 0.5 stack.199
  142.7 0.3 reshape_reshape_reshape.3
  143.0 0.9 dynamic-slice_reduce_fusion
  143.9 1.3 collective-permute-done.4
  145.4 0.4 dynamic-slice_reduce_fusion.2
  145.8 0.4 collective-permute-start.5
  146.2 4.1 %collective-permute-done.5 = f32[18816]{0:T(1024)S(1)} collective-permute-done((f32[18816]{0:T(1024)S(1)}, f32[18816]{0:T(1024)S(1)}, u32[]{:S(2)}, u32[]{:S(2)}) %collective-permute-start.5) | collective-permute-done | bytes 75296 | tf_op jit(solution)/shard_map/ppermute | solution.py:47
  150.9 1.5 collective-permute-start.6
  152.4 3.4 %collective-permute-done.6 = f32[9408]{0:T(1024)S(1)} collective-permute-done((f32[9408]{0:T(1024)S(1)}, f32[9408]{0:T(1024)S(1)}, u32[]{:S(2)}, u32[]{:S(2)}) %collective-permute-start.6) | collective-permute-done | bytes 37664 | tf_op jit(solution)/shard_map/ppermute | solution.py:47
  156.0 1.6 collective-permute-start.7
  157.6 4.0 %collective-permute-done.7 = f32[4704]{0:T(1024)S(1)} collective-permute-done((f32[4704]{0:T(1024)S(1)}, f32[4704]{0:T(1024)S(1)}, u32[]{:S(2)}, u32[]{:S(2)}) %collective-permute-start.7) | collective-permute-done | bytes 18848 | tf_op jit(solution)/shard_map/ppermute | solution.py:47
  161.7 1.4 collective-permute-start.8
  163.1 4.4 %collective-permute-done.8 = f32[2352]{0:T(1024)S(1)} collective-permute-done((f32[2352]{0:T(1024)S(1)}, f32[2352]{0:T(1024)S(1)}, u32[]{:S(2)}, u32[]{:S(2)}) %collective-permute-start.8) | collective-permute-done | bytes 9440 | tf_op jit(solution)/shard_map/ppermute | solution.py:47
  167.5 0.7 collective-permute-start.9
  168.2 4.6 %collective-permute-done.9 = f32[2352]{0:T(1024)S(1)} collective-permute-done((f32[2352]{0:T(1024)S(1)}, f32[2352]{0:T(1024)S(1)}, u32[]{:S(2)}, u32[]{:S(2)}) %collective-permute-start.9) | collective-permute-done | bytes 9440 | tf_op jit(solution)/shard_map/ppermute | solution.py:50
  172.9 1.4 collective-permute-start.10
  174.4 3.2 %collective-permute-done.10 = f32[4704]{0:T(1024)S(1)} collective-permute-done((f32[4704]{0:T(1024)S(1)}, f32[4704]{0:T(1024)S(1)}, u32[]{:S(2)}, u32[]{:S(2)}) %collective-permute-start.10) | collective-permute-done | bytes 18848 | tf_op jit(solution)/shard_map/ppermute | solution.py:50
  177.6 1.9 collective-permute-start.11
  179.5 1.3 collective-permute-start.2
  180.8 1.3 collective-permute-start.3
  182.2 2.7 %collective-permute-start.12 = (f32[18816]{0:T(1024)S(1)}, f32[18816]{0:T(1024)S(1)}, u32[]{:S(2)}, u32[]{:S(2)}) collective-permute-start(f32[18816]{0:T(1024)S(1)} %maximum_select_fusion.2), channel_id=1, source_target_pairs={{0,2},{1,3},{2,0},{3,1},{4,6},{5,7},{6,4},{7,5},{8,10},{9,11},{10,... | collective-permute-start | bytes 225800 | tf_op jit(solution)/shard_map/ppermute | solution.py:50
  185.1 4.1 %collective-permute-done.12 = f32[18816]{0:T(1024)S(1)} collective-permute-done((f32[18816]{0:T(1024)S(1)}, f32[18816]{0:T(1024)S(1)}, u32[]{:S(2)}, u32[]{:S(2)}) %collective-permute-start.12) | collective-permute-done | bytes 75296 | tf_op jit(solution)/shard_map/ppermute | solution.py:50
  189.5 2.8 %fusion.153 = bf16[1,3,16,1536]{3,2,1,0:T(8,128)(2,1)} fusion(f32[1536]{0:T(1024)S(1)} %copy-done.5, bf16[9,22,1536]{2,1,0:T(8,128)(2,1)S(1)} %select_maximum_fusion, f32[1536]{0:T(1024)S(1)} %copy-done.7, f32[1536]{0:T(1024)S(1)} %get-tuple-element.53, f32[1536]{0:T(1024)S(1)} %get-tuple-element.54, bf16[3,16,1536]{2,1,0:T(8,128)(2,1)S(1)} %collective-permute-done.2, ...), kind=kLoop, calls=%fused_computation.294 | loop fusion | flops 11132928 | bytes 7084032 | tf_op jit(solution)/shard_map/reshape | solution.py:187
  192.4 0.8 select_n.142
  193.1 44.6 %reduce-scatter.5.cloned.1.call-done = bf16[192,1536]{1,0:T(8,128)(2,1)} async-done(((bf16[1536,1536]{1,0:T(8,128)(2,1)}), bf16[192,1536]{1,0:T(8,128)(2,1)}) %reduce-scatter.5.cloned.1.call-update) | async-done | bytes 589840 | tf_op jit(solution)/shard_map/reduce_scatter | solution.py:167
  237.7 2.2 convert_element_type.489
  (193 shorter events, 2.9 us)
Async XLA Ops:
  7.2 9.8 %copy-start = (bf16[1,3,16,1536]{3,2,1,0:T(8,128)(2,1)S(1)}, bf16[1,3,16,1536]{3,2,1,0:T(8,128)(2,1)}, u32[]{:S(2)}) copy-start(bf16[1,3,16,1536]{3,2,1,0:T(8,128)(2,1)} %param.10) | copy-start | bytes 442372
  7.2 10.0 %copy-start.52 = (f32[1536]{0:T(1024)S(1)}, f32[1536]{0:T(1024)}, u32[]{:S(2)}) copy-start(f32[1536]{0:T(1024)} %param.12) | copy-start | bytes 18436
  7.2 85.6 %all-gather.2.cloned.1.call-start = ((), (), s32[]{:S(2)}) async-start(), calls=%async_computation.2 | async-start | bytes 5308416 | tf_op jit(solution)/shard_map/all_gather | solution.py:141
  7.9 129.3 %reduce-scatter.3.cloned.1.call-start = ((), (), s32[]{:S(2)}) async-start(), calls=%async_computation.3 | async-start | bytes 737280 | tf_op jit(solution)/shard_map/reduce_scatter | solution.py:171
  8.0 9.0 %collective-permute-start = (bf16[3,16,1536]{2,1,0:T(8,128)(2,1)}, bf16[3,16,1536]{2,1,0:T(8,128)(2,1)S(1)}, u32[]{:S(2)}, u32[]{:S(2)}) collective-permute-start(bf16[3,16,1536]{2,1,0:T(8,128)(2,1)} %bitcast.24), channel_id=1, source_target_pairs={{0,1},{1,2},{2,3},{4,5},{5,6},{6,7},{8,9},{9,10},{10,11},{12,13},{... | collective-permute-start | bytes 442376 | tf_op jit(solution)/shard_map/ppermute | solution.py:14
  10.3 6.6 %collective-permute-start.1 = (bf16[3,16,1536]{2,1,0:T(8,128)(2,1)}, bf16[3,16,1536]{2,1,0:T(8,128)(2,1)S(1)}, u32[]{:S(2)}, u32[]{:S(2)}) collective-permute-start(bf16[3,16,1536]{2,1,0:T(8,128)(2,1)} %bitcast.25), channel_id=1, source_target_pairs={{1,0},{2,1},{3,2},{5,4},{6,5},{7,6},{9,8},{10,9},{11,10},{13,12},{... | collective-permute-start | bytes 442376 | tf_op jit(solution)/shard_map/ppermute | solution.py:17
  14.9 5.7 %copy-start.4 = (f32[1536]{0:T(1024)}, f32[1536]{0:T(1024)S(1)}, u32[]{:S(2)}) copy-start(f32[1536]{0:T(1024)S(1)} %get-tuple-element.99) | copy-start | bytes 18436
  14.9 5.7 %copy-start.6 = (f32[1536]{0:T(1024)}, f32[1536]{0:T(1024)S(1)}, u32[]{:S(2)}) copy-start(f32[1536]{0:T(1024)S(1)} %get-tuple-element.100) | copy-start | bytes 18436
  20.8 72.0 %copy-start.1 = (bf16[1,12,16,1536]{3,2,1,0:T(8,128)(2,1)S(1)}, bf16[1,12,16,1536]{3,2,1,0:T(8,128)(2,1)}, u32[]{:S(2)}) copy-start(bf16[1,12,16,1536]{3,2,1,0:T(8,128)(2,1)} %param.19) | copy-start | bytes 1769476
  20.8 72.0 %copy-start.53 = (f32[1536]{0:T(1024)S(1)}, f32[1536]{0:T(1024)}, u32[]{:S(2)}) copy-start(f32[1536]{0:T(1024)} %param.16) | copy-start | bytes 18436
  92.8 7.4 %copy-start.2 = (f32[1536]{0:T(1024)S(1)}, f32[1536]{0:T(1024)}, u32[]{:S(2)}) copy-start(f32[1536]{0:T(1024)} %param.17) | copy-start | bytes 18436
  92.8 15.6 %copy-start.51 = (f32[1536]{0:T(1024)S(1)}, f32[1536]{0:T(1024)}, u32[]{:S(2)}) copy-start(f32[1536]{0:T(1024)} %param.18) | copy-start | bytes 18436
  116.6 121.2 %reduce-scatter.5.cloned.1.call-start = ((), (), s32[]{:S(2)}) async-start(), calls=%async_computation.4 | async-start | bytes 5308416 | tf_op jit(solution)/shard_map/reduce_scatter | solution.py:167
  120.4 16.8 %copy-start.47 = (f32[3,16]{1,0:T(4,128)S(1)}, f32[3,16]{1,0:T(4,128)}, u32[]{:S(2)}) copy-start(f32[3,16]{1,0:T(4,128)} %copy-done.46) | copy-start | bytes 580
  120.4 16.8 %copy-start.49 = (f32[3,16]{1,0:T(4,128)S(1)}, f32[3,16]{1,0:T(4,128)}, u32[]{:S(2)}) copy-start(f32[3,16]{1,0:T(4,128)} %copy-done.48) | copy-start | bytes 580
  143.8 1.4 collective-permute-start.4
  145.8 4.5 %collective-permute-start.5 = (f32[18816]{0:T(1024)S(1)}, f32[18816]{0:T(1024)S(1)}, u32[]{:S(2)}, u32[]{:S(2)}) collective-permute-start(f32[18816]{0:T(1024)S(1)} %get-tuple-element.109), channel_id=1, source_target_pairs={{0,2},{1,3},{2,0},{3,1},{4,6},{5,7},{6,4},{7,5},{8,10},{9,11},{10,... | collective-permute-start | bytes 225800 | tf_op jit(solution)/shard_map/ppermute | solution.py:47
  150.6 38.7 %copy-start.5 = (f32[1536]{0:T(1024)S(1)}, f32[1536]{0:T(1024)}, u32[]{:S(2)}) copy-start(f32[1536]{0:T(1024)} %copy-done.4) | copy-start | bytes 18436
  150.7 38.7 %copy-start.7 = (f32[1536]{0:T(1024)S(1)}, f32[1536]{0:T(1024)}, u32[]{:S(2)}) copy-start(f32[1536]{0:T(1024)} %copy-done.6) | copy-start | bytes 18436
  150.7 38.7 %copy-start.9 = (f32[1536]{0:T(1024)S(1)}, f32[1536]{0:T(1024)}, u32[]{:S(2)}) copy-start(f32[1536]{0:T(1024)} %copy-done.8) | copy-start | bytes 18436
  150.7 38.7 %copy-start.11 = (f32[1536]{0:T(1024)S(1)}, f32[1536]{0:T(1024)}, u32[]{:S(2)}) copy-start(f32[1536]{0:T(1024)} %copy-done.10) | copy-start | bytes 18436
  150.7 38.7 %copy-start.13 = (f32[1536]{0:T(1024)S(1)}, f32[1536]{0:T(1024)}, u32[]{:S(2)}) copy-start(f32[1536]{0:T(1024)} %copy-done.12) | copy-start | bytes 18436
  150.7 38.7 %copy-start.15 = (f32[1536]{0:T(1024)S(1)}, f32[1536]{0:T(1024)}, u32[]{:S(2)}) copy-start(f32[1536]{0:T(1024)} %copy-done.14) | copy-start | bytes 18436
  150.7 38.7 %copy-start.17 = (f32[1536]{0:T(1024)S(1)}, f32[1536]{0:T(1024)}, u32[]{:S(2)}) copy-start(f32[1536]{0:T(1024)} %copy-done.16) | copy-start | bytes 18436
  150.7 38.7 %copy-start.19 = (f32[1536]{0:T(1024)S(1)}, f32[1536]{0:T(1024)}, u32[]{:S(2)}) copy-start(f32[1536]{0:T(1024)} %copy-done.18) | copy-start | bytes 18436
  150.7 38.7 %copy-start.21 = (f32[1536]{0:T(1024)S(1)}, f32[1536]{0:T(1024)}, u32[]{:S(2)}) copy-start(f32[1536]{0:T(1024)} %copy-done.20) | copy-start | bytes 18436
  150.7 38.7 %copy-start.23 = (f32[1536]{0:T(1024)S(1)}, f32[1536]{0:T(1024)}, u32[]{:S(2)}) copy-start(f32[1536]{0:T(1024)} %copy-done.22) | copy-start | bytes 18436
  150.8 38.7 %copy-start.25 = (f32[1536]{0:T(1024)S(1)}, f32[1536]{0:T(1024)}, u32[]{:S(2)}) copy-start(f32[1536]{0:T(1024)} %copy-done.24) | copy-start | bytes 18436
  150.8 38.7 %copy-start.27 = (f32[1536]{0:T(1024)S(1)}, f32[1536]{0:T(1024)}, u32[]{:S(2)}) copy-start(f32[1536]{0:T(1024)} %copy-done.26) | copy-start | bytes 18436
  150.8 38.7 %copy-start.29 = (f32[1536]{0:T(1024)S(1)}, f32[1536]{0:T(1024)}, u32[]{:S(2)}) copy-start(f32[1536]{0:T(1024)} %copy-done.28) | copy-start | bytes 18436
  150.8 38.7 %copy-start.31 = (f32[1536]{0:T(1024)S(1)}, f32[1536]{0:T(1024)}, u32[]{:S(2)}) copy-start(f32[1536]{0:T(1024)} %copy-done.30) | copy-start | bytes 18436
  150.8 38.7 %copy-start.33 = (f32[1536]{0:T(1024)S(1)}, f32[1536]{0:T(1024)}, u32[]{:S(2)}) copy-start(f32[1536]{0:T(1024)} %copy-done.32) | copy-start | bytes 18436
  150.8 38.7 %copy-start.35 = (f32[1536]{0:T(1024)S(1)}, f32[1536]{0:T(1024)}, u32[]{:S(2)}) copy-start(f32[1536]{0:T(1024)} %copy-done.34) | copy-start | bytes 18436
  150.8 38.7 %copy-start.37 = (f32[1536]{0:T(1024)S(1)}, f32[1536]{0:T(1024)}, u32[]{:S(2)}) copy-start(f32[1536]{0:T(1024)} %copy-done.36) | copy-start | bytes 18436
  150.8 38.7 %copy-start.39 = (f32[1536]{0:T(1024)S(1)}, f32[1536]{0:T(1024)}, u32[]{:S(2)}) copy-start(f32[1536]{0:T(1024)} %copy-done.38) | copy-start | bytes 18436
  150.8 38.7 %copy-start.41 = (f32[1536]{0:T(1024)S(1)}, f32[1536]{0:T(1024)}, u32[]{:S(2)}) copy-start(f32[1536]{0:T(1024)} %copy-done.40) | copy-start | bytes 18436
  150.8 38.7 %copy-start.43 = (f32[1536]{0:T(1024)S(1)}, f32[1536]{0:T(1024)}, u32[]{:S(2)}) copy-start(f32[1536]{0:T(1024)} %copy-done.42) | copy-start | bytes 18436
  150.8 38.7 %copy-start.45 = (f32[1536]{0:T(1024)S(1)}, f32[1536]{0:T(1024)}, u32[]{:S(2)}) copy-start(f32[1536]{0:T(1024)} %copy-done.44) | copy-start | bytes 18436
  150.9 4.9 %collective-permute-start.6 = (f32[9408]{0:T(1024)S(1)}, f32[9408]{0:T(1024)S(1)}, u32[]{:S(2)}, u32[]{:S(2)}) collective-permute-start(f32[9408]{0:T(1024)S(1)} %get-tuple-element.118), channel_id=1, source_target_pairs={{0,4},{4,0},{8,12},{12,8},{16,20},{20,16},{24,28},{28,24},{1,5},{5... | collective-permute-start | bytes 112904 | tf_op jit(solution)/shard_map/ppermute | solution.py:47
  156.0 5.5 %collective-permute-start.7 = (f32[4704]{0:T(1024)S(1)}, f32[4704]{0:T(1024)S(1)}, u32[]{:S(2)}, u32[]{:S(2)}) collective-permute-start(f32[4704]{0:T(1024)S(1)} %get-tuple-element.120), channel_id=1, source_target_pairs={{0,8},{4,12},{8,0},{12,4},{16,24},{20,28},{24,16},{28,20},{1,9},{5... | collective-permute-start | bytes 56456 | tf_op jit(solution)/shard_map/ppermute | solution.py:47
  161.7 5.8 %collective-permute-start.8 = (f32[2352]{0:T(1024)S(1)}, f32[2352]{0:T(1024)S(1)}, u32[]{:S(2)}, u32[]{:S(2)}) collective-permute-start(f32[2352]{0:T(1024)S(1)} %get-tuple-element.122), channel_id=1, source_target_pairs={{0,16},{4,20},{8,24},{12,28},{16,0},{20,4},{24,8},{28,12},{1,17},{... | collective-permute-start | bytes 28232 | tf_op jit(solution)/shard_map/ppermute | solution.py:47
  167.5 5.4 %collective-permute-start.9 = (f32[2352]{0:T(1024)S(1)}, f32[2352]{0:T(1024)S(1)}, u32[]{:S(2)}, u32[]{:S(2)}) collective-permute-start(f32[2352]{0:T(1024)S(1)} %add.584), channel_id=1, source_target_pairs={{0,16},{4,20},{8,24},{12,28},{16,0},{20,4},{24,8},{28,12},{1,17},{... | collective-permute-start | bytes 28232 | tf_op jit(solution)/shard_map/ppermute | solution.py:50
  172.9 4.6 %collective-permute-start.10 = (f32[4704]{0:T(1024)S(1)}, f32[4704]{0:T(1024)S(1)}, u32[]{:S(2)}, u32[]{:S(2)}) collective-permute-start(f32[4704]{0:T(1024)S(1)} %maximum_select_fusion.4), channel_id=1, source_target_pairs={{0,8},{4,12},{8,0},{12,4},{16,24},{20,28},{24,16},{28,20},{1,9},{5... | collective-permute-start | bytes 56456 | tf_op jit(solution)/shard_map/ppermute | solution.py:50
  177.6 4.5 %collective-permute-start.11 = (f32[9408]{0:T(1024)S(1)}, f32[9408]{0:T(1024)S(1)}, u32[]{:S(2)}, u32[]{:S(2)}) collective-permute-start(f32[9408]{0:T(1024)S(1)} %maximum_select_fusion.3), channel_id=1, source_target_pairs={{0,4},{4,0},{8,12},{12,8},{16,20},{20,16},{24,28},{28,24},{1,5},{5... | collective-permute-start | bytes 112904 | tf_op jit(solution)/shard_map/ppermute | solution.py:50
  179.5 5.4 %collective-permute-start.2 = (bf16[3,16,1536]{2,1,0:T(8,128)(2,1)S(1)}, bf16[3,16,1536]{2,1,0:T(8,128)(2,1)S(1)}, u32[]{:S(2)}, u32[]{:S(2)}) collective-permute-start(bf16[3,16,1536]{2,1,0:T(8,128)(2,1)S(1)} %get-tuple-element.128), channel_id=1, source_target_pairs={{0,1},{1,2},{2,3},{4,5},{5,6},{6,7},{8,9},{9,10},{10,11},{12,13},{... | collective-permute-start | bytes 442376 | tf_op jit(solution)/shard_map/ppermute | solution.py:14
  180.8 4.1 %collective-permute-start.3 = (bf16[3,16,1536]{2,1,0:T(8,128)(2,1)S(1)}, bf16[3,16,1536]{2,1,0:T(8,128)(2,1)S(1)}, u32[]{:S(2)}, u32[]{:S(2)}) collective-permute-start(bf16[3,16,1536]{2,1,0:T(8,128)(2,1)S(1)} %get-tuple-element.128), channel_id=1, source_target_pairs={{1,0},{2,1},{3,2},{5,4},{6,5},{7,6},{9,8},{10,9},{11,10},{13,12},{... | collective-permute-start | bytes 442376 | tf_op jit(solution)/shard_map/ppermute | solution.py:17
  182.2 7.0 %collective-permute-start.12 = (f32[18816]{0:T(1024)S(1)}, f32[18816]{0:T(1024)S(1)}, u32[]{:S(2)}, u32[]{:S(2)}) collective-permute-start(f32[18816]{0:T(1024)S(1)} %maximum_select_fusion.2), channel_id=1, source_target_pairs={{0,2},{1,3},{2,0},{3,1},{4,6},{5,7},{6,4},{7,5},{8,10},{9,11},{10,... | collective-permute-start | bytes 225800 | tf_op jit(solution)/shard_map/ppermute | solution.py:50
  189.2 3.1 %collective-permute-start.13 = (f32[37632]{0:T(1024)S(1)}, f32[37632]{0:T(1024)S(1)}, u32[]{:S(2)}, u32[]{:S(2)}) collective-permute-start(f32[37632]{0:T(1024)S(1)} %maximum_select_fusion.1), channel_id=1, source_target_pairs={{0,1},{1,0},{2,3},{3,2},{4,5},{5,4},{6,7},{7,6},{8,9},{9,8},{10,11... | collective-permute-start | bytes 451592 | tf_op jit(solution)/shard_map/ppermute | solution.py:50
  (23 other events, 84.9 us)
Sparse Core Ops, SparseCore 0:
  10.2 82.5 all-gather.1
  116.7 20.4 reduce-scatter.2
  140.8 96.8 reduce-scatter.4

commit v2 on v1

--- a/solution.py
+++ b/solution.py
@@ -52,6 +52,23 @@
     return flat.reshape(shape)
 
 
+def tree_reduce_scatter(chunks, axis):
+    size = lax.axis_size(axis)
+    assert chunks.shape[0] == size and size & (size - 1) == 0
+    me = lax.axis_index(axis)
+    data = chunks
+    mask = 1
+    while mask < size:
+        bit = (me // mask) % 2
+        pairs = data.reshape((data.shape[0] // 2, 2) + data.shape[1:])
+        keep = lax.dynamic_index_in_dim(pairs, bit, axis=1, keepdims=False)
+        give = lax.dynamic_index_in_dim(pairs, 1 - bit, axis=1, keepdims=False)
+        perm = [(j, j ^ mask) for j in range(size)]
+        data = keep.astype(jnp.float32) + lax.ppermute(give, axis, perm).astype(jnp.float32)
+        mask *= 2
+    return data[0]
+
+
 def conv_rows(framed, kern, kbias):
     rows = framed.shape[0] - 6
     cols = framed.shape[1]
@@ -168,14 +185,13 @@
         w_term.astype(jnp.bfloat16), "fsdp", scatter_dimension=0, tiled=True
     ).astype(jnp.float32)
     dpre_rows = dpre.reshape(height, cols, -1)
-    normed_input_gradient = lax.psum_scatter(
-        jnp.einsum("hwf,cf->hwc", dpre_rows, columns, preferred_element_type=jnp.float32).astype(
-            jnp.bfloat16
-        ),
-        "rows",
-        scatter_dimension=0,
-        tiled=True,
-    ).astype(jnp.float32)
+    group_terms = jnp.einsum(
+        "hwf,cf->hwc", dpre_rows, columns, preferred_element_type=jnp.float32
+    ).astype(jnp.bfloat16)
+    n_rows = lax.axis_size("rows")
+    normed_input_gradient = tree_reduce_scatter(
+        group_terms.reshape((n_rows, height // n_rows) + group_terms.shape[1:]), "rows"
+    )
     activation_gradient = layer_norm_backward(
         normed_input_gradient, layer_norm_weight, standardized_input, inverse_deviation
     )

time: 247 us -> 221 us (0.89)
  waiting for transfers between devices: 151 us -> 127 us
    reduce_scatter x1, waiting for transfers between devices: 44.6 us -> 26.6 us  [body(): lax.psum_scatter(w_term.astype(jnp.bfloat16), 'fsdp', scatter_dimension=0...]
    reduce_scatter x1 -> x0, waiting for transfers between devices: 16.8 us -> none  [body(): lax.psum_scatter(jnp.einsum('hwf,cf->hwc', dpre_rows, columns, preferred_...]
    ppermute x0 -> x2, waiting for transfers between devices: none -> 8.83 us  [tree_reduce_scatter(): lax.ppermute(give, axis, perm).astype(jnp.float32)]
  transfers between devices with their start and end apart: 17 -> 18, of which waited for: 11 -> 13; matrix products, arithmetic and copies ran while one was open for 10% -> 10% of each run, Pallas kernels for 0% -> 0%
where the time goes in v2:
time: 221 us; the launch traced here: 220 us
  waiting for transfers between devices  127 us (57%)
  starting transfers between devices  19.1 us (9%)
  blocking collectives  17.3 us (8%)
  between operations  16.7 us (8%)
  other arithmetic  16 us (7%)
  matrix products  15 us (7%)
  local copies, waits for them, and re-layouts  8.88 us (4%)
    all_gather x1, waiting for transfers between devices, body(): columns = lax.all_gather(up_weight, 'fsdp', axis=0, tiled=True)  61.2 us
    reduce_scatter x1, waiting for transfers between devices, body(): lax.psum_scatter(w_term.astype(jnp.bfloat16), 'fsdp', scatter_dimension=0...  26.6 us
    ppermute x5, waiting for transfers between devices, tree_allreduce(): flat = keep + lax.ppermute(give, axis, perm)  17.8 us
    ppermute x5, waiting for transfers between devices, tree_allreduce(): other = lax.ppermute(flat, axis, perm)  11.8 us
    all_gather x1, blocking collectives, body(): whole = lax.all_gather(normed_output, 'rows', axis=0, tiled=True)  10.9 us
    ppermute x2, waiting for transfers between devices, tree_reduce_scatter(): lax.ppermute(give, axis, perm).astype(jnp.float32)  8.83 us
    dot_general x1, matrix products, body(): pre = jnp.dot(flat, columns, preferred_element_type=jnp.float32) + up_bias  7.34 us
    ppermute x5, starting transfers between devices, tree_allreduce(): other = lax.ppermute(flat, axis, perm)  6.82 us
  transfers between devices with their start and end apart: 18, of which 13 were waited for; matrix products, arithmetic and copies ran while one was open for 10% of the time, Pallas kernels for 0%

profile of v2, /device:TPU:0, one launch (start us, length us, event | category | flops | bytes accessed | tf_op | source)
XLA Modules:
  0.0 219.9 jit_solution(8541893716866066103)
XLA Ops:
  7.2 0.7 all-gather.2.cloned.1.call-update
  8.0 2.4 %collective-permute-start = (bf16[3,16,1536]{2,1,0:T(8,128)(2,1)}, bf16[3,16,1536]{2,1,0:T(8,128)(2,1)S(1)}, u32[]{:S(2)}, u32[]{:S(2)}) collective-permute-start(bf16[3,16,1536]{2,1,0:T(8,128)(2,1)} %bitcast.35), channel_id=1, source_target_pairs={{0,1},{1,2},{2,3},{4,5},{5,6},{6,7},{8,9},{9,10},{10,11},{12,13},{... | collective-permute-start | bytes 442376 | tf_op jit(solution)/shard_map/ppermute | solution.py:14
  10.3 1.3 collective-permute-start.1
  11.6 1.8 slice_reduce_fusion.48
  13.4 1.3 slice_reduce_fusion.46
  14.7 1.6 slice_reduce_fusion.47
  16.8 3.4 %fusion.158 = (f32[3,16]{1,0:T(4,128)S(1)}, f32[3,16,1536]{2,1,0:T(8,128)S(1)}) fusion(f32[1536]{0:T(1024)S(1)} %get-tuple-element.99, bf16[9,22,1536]{2,1,0:T(8,128)(2,1)S(1)} %select_maximum_fusion.2, f32[1536]{0:T(1024)S(1)} %get-tuple-element.100, f32[1536]{0:T(1024)S(1)} %get-tuple-element.53, f32[1536]{0:T(1024)S(1)} %get-tuple-element.54, ...), kind=kLoop, calls=%fused_computation.368 | loop fusion | flops 11206608 | bytes 7237824 | tf_op jit(solution)/shard_map/reduce_sum | solution.py:112
  20.8 10.9 %all_gather.6 = bf16[12,16,1536]{2,1,0:T(8,128)(2,1)S(1)} all-gather(bf16[3,16,1536]{2,1,0:T(8,128)(2,1)S(1)} %add_convert_fusion.1), channel_id=1, replica_groups=mesh['fsdp'=8,'rows'=4] {'rows'}, dimensions={0}, use_global_device_ids=true | all-gather | bytes 737280 | tf_op jit(solution)/shard_map/all_gather | solution.py:164
  31.7 61.2 %all-gather.2.cloned.1.call-done = bf16[1536,1536]{1,0:T(8,128)(2,1)} async-done(((bf16[192,1536]{1,0:T(8,128)(2,1)}), bf16[1536,1536]{1,0:T(8,128)(2,1)}) %all-gather.2.cloned.1.call-update) | async-done | bytes 4718608 | tf_op jit(solution)/shard_map/all_gather | solution.py:158
  92.8 7.3 %fusion.9 = (f32[1536]{0:T(1024)S(1)}, f32[1536]{0:T(1024)S(1)}, f32[192,1536]{1,0:T(8,128)}, f32[192,1536]{1,0:T(8,128)}) fusion(bf16[1,12,16,1536]{3,2,1,0:T(8,128)(2,1)S(1)} %copy-done.1, f32[1536]{0:T(1024)S(1)} %copy-done.52, bf16[192,1536]{1,0:T(8,128)(2,1)S(1)} %bitcast.32, bf16[1536,1536]{1,0:T(8,128)(2,1)} %all-gather.2.cloned.1.call-done), kind=kOutput, calls=%fused_computation.65 | convolution fusion | flops 926610432 | bytes 8275968 | tf_op jit(solution)/shard_map/dot_general | solution.py:168
  100.2 0.7 multiply_reduce_fusion.3
  100.9 6.5 %all-reduce.2 = (f32[]{:T(128)}, f32[]{:T(128)}) all-reduce(f32[]{:T(128)} %get-tuple-element.125, f32[]{:T(128)} %get-tuple-element.124), channel_id=1, replica_groups=mesh['fsdp'=8,'rows'=4] {'rows'}, use_global_device_ids=true, to_apply=%region_4.5 | all-reduce | flops 2 | bytes 16 | tf_op jit(solution)/shard_map/psum | solution.py:173
  108.6 3.2 %fusion.8 = (bf16[192,1536]{1,0:T(8,128)(2,1)S(1)}, bf16[192,1536]{1,0:T(8,128)(2,1)}) fusion(f32[192,1536]{1,0:T(8,128)} %get-tuple-element.138, f32[192,1536]{1,0:T(8,128)} %get-tuple-element.132, bf16[1,12,16,1536]{3,2,1,0:T(8,128)(2,1)S(1)} %copy-done.1, f32[1536]{0:T(1024)S(1)} %get-tuple-element.137, f32[1536]{0:T(1024)S(1)} %get-tuple-element.130, ...), kind=kLoop, calls=%fused_computation.64 | loop fusion | flops 5603328 | bytes 4159488 | tf_op jit(solution)/shard_map/convert_element_type | solution.py:180
  111.8 3.6 %convolution_convert_fusion = bf16[1536,1536]{1,0:T(8,128)(2,1)} fusion(bf16[192,1536]{1,0:T(8,128)(2,1)S(1)} %bitcast.33, bf16[192,1536]{1,0:T(8,128)(2,1)S(1)} %get-tuple-element.135), kind=kOutput, calls=%fused_computation | convolution fusion | flops 908328960 | bytes 5898240 | tf_op jit(solution)/shard_map/dot_general | solution.py:181
  115.5 4.0 %fusion.2 = bf16[12,16,1536]{2,1,0:T(8,128)(2,1)S(1)} fusion(bf16[12,16,1536]{2,1,0:T(8,128)(2,1)S(1)} %bitcast.34, bf16[1536,1536]{1,0:T(8,128)(2,1)} %all-gather.2.cloned.1.call-done), kind=kOutput, calls=%fused_computation.54 | convolution fusion | flops 906264576 | bytes 5898240 | tf_op jit(solution)/shard_map/hwf,cf->hwc/dot_general | solution.py:188
  119.7 1.5 collective-permute-done.2
  121.3 1.8 collective-permute-start.3
  123.2 7.3 %collective-permute-done.3 = f32[1,3,16,1536]{3,2,1,0:T(8,128)S(1)} collective-permute-done((f32[1,3,16,1536]{3,2,1,0:T(8,128)S(1)}, f32[1,3,16,1536]{3,2,1,0:T(8,128)S(1)}, u32[]{:S(2)}, u32[]{:S(2)}) %collective-permute-start.3) | collective-permute-done | bytes 294944 | tf_op jit(solution)/shard_map/ppermute | solution.py:67
  130.7 0.9 fusion.145
  131.6 0.6 fusion.136
  132.4 0.8 fusion.146
  133.6 0.5 stack.199
  134.2 0.3 reshape_reshape_reshape.3
  134.4 0.9 dynamic-slice_reduce_fusion
  135.4 1.4 collective-permute-done.6
  136.8 0.4 dynamic-slice_reduce_fusion.2
  137.3 1.8 collective-permute-start.7
  139.1 2.7 %collective-permute-done.7 = f32[18816]{0:T(1024)S(1)} collective-permute-done((f32[18816]{0:T(1024)S(1)}, f32[18816]{0:T(1024)S(1)}, u32[]{:S(2)}, u32[]{:S(2)}) %collective-permute-start.7) | collective-permute-done | bytes 75296 | tf_op jit(solution)/shard_map/ppermute | solution.py:47
  142.3 0.6 collective-permute-start.8
  142.9 4.3 %collective-permute-done.8 = f32[9408]{0:T(1024)S(1)} collective-permute-done((f32[9408]{0:T(1024)S(1)}, f32[9408]{0:T(1024)S(1)}, u32[]{:S(2)}, u32[]{:S(2)}) %collective-permute-start.8) | collective-permute-done | bytes 37664 | tf_op jit(solution)/shard_map/ppermute | solution.py:47
  147.4 0.5 collective-permute-start.9
  148.0 4.7 %collective-permute-done.9 = f32[4704]{0:T(1024)S(1)} collective-permute-done((f32[4704]{0:T(1024)S(1)}, f32[4704]{0:T(1024)S(1)}, u32[]{:S(2)}, u32[]{:S(2)}) %collective-permute-start.9) | collective-permute-done | bytes 18848 | tf_op jit(solution)/shard_map/ppermute | solution.py:47
  152.8 1.1 collective-permute-start.10
  153.9 4.8 %collective-permute-done.10 = f32[2352]{0:T(1024)S(1)} collective-permute-done((f32[2352]{0:T(1024)S(1)}, f32[2352]{0:T(1024)S(1)}, u32[]{:S(2)}, u32[]{:S(2)}) %collective-permute-start.10) | collective-permute-done | bytes 9440 | tf_op jit(solution)/shard_map/ppermute | solution.py:47
  158.7 0.3 collective-permute-start.11
  159.0 4.3 %collective-permute-done.11 = f32[2352]{0:T(1024)S(1)} collective-permute-done((f32[2352]{0:T(1024)S(1)}, f32[2352]{0:T(1024)S(1)}, u32[]{:S(2)}, u32[]{:S(2)}) %collective-permute-start.11) | collective-permute-done | bytes 9440 | tf_op jit(solution)/shard_map/ppermute | solution.py:50
  163.4 1.3 collective-permute-start.12
  164.7 2.5 %collective-permute-done.12 = f32[4704]{0:T(1024)S(1)} collective-permute-done((f32[4704]{0:T(1024)S(1)}, f32[4704]{0:T(1024)S(1)}, u32[]{:S(2)}, u32[]{:S(2)}) %collective-permute-start.12) | collective-permute-done | bytes 18848 | tf_op jit(solution)/shard_map/ppermute | solution.py:50
  167.3 0.6 collective-permute-start.13
  167.9 1.3 collective-permute-start.4
  169.2 1.3 collective-permute-start.5
  170.5 0.9 collective-permute-done.13
  171.5 4.6 %collective-permute-start.14 = (f32[18816]{0:T(1024)S(1)}, f32[18816]{0:T(1024)S(1)}, u32[]{:S(2)}, u32[]{:S(2)}) collective-permute-start(f32[18816]{0:T(1024)S(1)} %maximum_select_fusion.2), channel_id=1, source_target_pairs={{0,2},{1,3},{2,0},{3,1},{4,6},{5,7},{6,4},{7,5},{8,10},{9,11},{10,... | collective-permute-start | bytes 225800 | tf_op jit(solution)/shard_map/ppermute | solution.py:50
  176.3 4.0 %collective-permute-done.14 = f32[18816]{0:T(1024)S(1)} collective-permute-done((f32[18816]{0:T(1024)S(1)}, f32[18816]{0:T(1024)S(1)}, u32[]{:S(2)}, u32[]{:S(2)}) %collective-permute-start.14) | collective-permute-done | bytes 75296 | tf_op jit(solution)/shard_map/ppermute | solution.py:50
  180.6 2.8 %fusion.152 = bf16[1,3,16,1536]{3,2,1,0:T(8,128)(2,1)} fusion(f32[1536]{0:T(1024)S(1)} %get-tuple-element.99, bf16[9,22,1536]{2,1,0:T(8,128)(2,1)S(1)} %select_maximum_fusion, f32[1536]{0:T(1024)S(1)} %copy-done.4, f32[1536]{0:T(1024)S(1)} %get-tuple-element.53, f32[1536]{0:T(1024)S(1)} %get-tuple-element.54, ...), kind=kLoop, calls=%fused_computation.295 | loop fusion | flops 11132928 | bytes 7084032 | tf_op jit(solution)/shard_map/reshape | solution.py:203
  183.5 0.8 select_n.154
  184.3 26.6 %reduce-scatter.2.cloned.1.call-done = bf16[192,1536]{1,0:T(8,128)(2,1)} async-done(((bf16[1536,1536]{1,0:T(8,128)(2,1)}), bf16[192,1536]{1,0:T(8,128)(2,1)}) %reduce-scatter.2.cloned.1.call-update) | async-done | bytes 589840 | tf_op jit(solution)/shard_map/reduce_scatter | solution.py:184
  210.9 2.2 %convert_element_type.497 = f32[192,1536]{1,0:T(8,128)} convert(bf16[192,1536]{1,0:T(8,128)(2,1)} %reduce-scatter.2.cloned.1.call-done) | non-fusion elementwise | flops 294912 | bytes 1769472 | tf_op jit(solution)/shard_map/convert_element_type | solution.py:186
  (195 shorter events, 3.1 us)
Async XLA Ops:
  7.2 9.4 %copy-start = (bf16[1,3,16,1536]{3,2,1,0:T(8,128)(2,1)S(1)}, bf16[1,3,16,1536]{3,2,1,0:T(8,128)(2,1)}, u32[]{:S(2)}) copy-start(bf16[1,3,16,1536]{3,2,1,0:T(8,128)(2,1)} %param.10) | copy-start | bytes 442372
  7.2 9.6 %copy-start.51 = (f32[1536]{0:T(1024)S(1)}, f32[1536]{0:T(1024)}, u32[]{:S(2)}) copy-start(f32[1536]{0:T(1024)} %param.12) | copy-start | bytes 18436
  7.2 85.6 %all-gather.2.cloned.1.call-start = ((), (), s32[]{:S(2)}) async-start(), calls=%async_computation.1 | async-start | bytes 5308416 | tf_op jit(solution)/shard_map/all_gather | solution.py:158
  7.9 202.9 %reduce-scatter.2.cloned.1.call-start = ((), (), s32[]{:S(2)}) async-start(), calls=%async_computation.2 | async-start | bytes 5308416 | tf_op jit(solution)/shard_map/reduce_scatter | solution.py:184
  8.0 8.6 %collective-permute-start = (bf16[3,16,1536]{2,1,0:T(8,128)(2,1)}, bf16[3,16,1536]{2,1,0:T(8,128)(2,1)S(1)}, u32[]{:S(2)}, u32[]{:S(2)}) collective-permute-start(bf16[3,16,1536]{2,1,0:T(8,128)(2,1)} %bitcast.35), channel_id=1, source_target_pairs={{0,1},{1,2},{2,3},{4,5},{5,6},{6,7},{8,9},{9,10},{10,11},{12,13},{... | collective-permute-start | bytes 442376 | tf_op jit(solution)/shard_map/ppermute | solution.py:14
  10.3 6.2 %collective-permute-start.1 = (bf16[3,16,1536]{2,1,0:T(8,128)(2,1)}, bf16[3,16,1536]{2,1,0:T(8,128)(2,1)S(1)}, u32[]{:S(2)}, u32[]{:S(2)}) collective-permute-start(bf16[3,16,1536]{2,1,0:T(8,128)(2,1)} %bitcast.36), channel_id=1, source_target_pairs={{1,0},{2,1},{3,2},{5,4},{6,5},{7,6},{9,8},{10,9},{11,10},{13,12},{... | collective-permute-start | bytes 442376 | tf_op jit(solution)/shard_map/ppermute | solution.py:17
  20.4 72.4 %copy-start.1 = (bf16[1,12,16,1536]{3,2,1,0:T(8,128)(2,1)S(1)}, bf16[1,12,16,1536]{3,2,1,0:T(8,128)(2,1)}, u32[]{:S(2)}) copy-start(bf16[1,12,16,1536]{3,2,1,0:T(8,128)(2,1)} %param.19) | copy-start | bytes 1769476
  20.4 72.4 %copy-start.52 = (f32[1536]{0:T(1024)S(1)}, f32[1536]{0:T(1024)}, u32[]{:S(2)}) copy-start(f32[1536]{0:T(1024)} %param.16) | copy-start | bytes 18436
  20.4 79.7 %copy-start.43 = (f32[3,16]{1,0:T(4,128)}, f32[3,16]{1,0:T(4,128)S(1)}, u32[]{:S(2)}) copy-start(f32[3,16]{1,0:T(4,128)S(1)} %broadcast_multiply_fusion.2) | copy-start | bytes 580
  20.7 79.5 %copy-start.45 = (f32[3,16]{1,0:T(4,128)}, f32[3,16]{1,0:T(4,128)S(1)}, u32[]{:S(2)}) copy-start(f32[3,16]{1,0:T(4,128)S(1)} %add_rsqrt_fusion) | copy-start | bytes 580
  92.8 15.8 %copy-start.50 = (f32[1536]{0:T(1024)S(1)}, f32[1536]{0:T(1024)}, u32[]{:S(2)}) copy-start(f32[1536]{0:T(1024)} %param.18) | copy-start | bytes 18436
  119.5 11.0 %copy-start.44 = (f32[3,16]{1,0:T(4,128)S(1)}, f32[3,16]{1,0:T(4,128)}, u32[]{:S(2)}) copy-start(f32[3,16]{1,0:T(4,128)} %copy-done.43) | copy-start | bytes 580
  119.5 10.9 %copy-start.46 = (f32[3,16]{1,0:T(4,128)S(1)}, f32[3,16]{1,0:T(4,128)}, u32[]{:S(2)}) copy-start(f32[3,16]{1,0:T(4,128)} %copy-done.45) | copy-start | bytes 580
  119.5 10.9 %copy-start.48 = (f32[1536]{0:T(1024)S(1)}, f32[1536]{0:T(1024)}, u32[]{:S(2)}) copy-start(f32[1536]{0:T(1024)} %param.13) | copy-start | bytes 18436
  119.6 1.6 collective-permute-start.2
  121.3 9.1 %collective-permute-start.3 = (f32[1,3,16,1536]{3,2,1,0:T(8,128)S(1)}, f32[1,3,16,1536]{3,2,1,0:T(8,128)S(1)}, u32[]{:S(2)}, u32[]{:S(2)}) collective-permute-start(f32[1,3,16,1536]{3,2,1,0:T(8,128)S(1)} %constant_dynamic-slice_fusion), channel_id=1, source_target_pairs={{0,2},{1,3},{2,0},{3,1},{4,6},{5,7},{6,4},{7,5},{8,10},{9,11},{10,... | collective-permute-start | bytes 884744 | tf_op jit(solution)/shard_map/ppermute | solution.py:67
  135.3 1.4 collective-permute-start.6
  137.3 4.5 %collective-permute-start.7 = (f32[18816]{0:T(1024)S(1)}, f32[18816]{0:T(1024)S(1)}, u32[]{:S(2)}, u32[]{:S(2)}) collective-permute-start(f32[18816]{0:T(1024)S(1)} %get-tuple-element.109), channel_id=1, source_target_pairs={{0,2},{1,3},{2,0},{3,1},{4,6},{5,7},{6,4},{7,5},{8,10},{9,11},{10,... | collective-permute-start | bytes 225800 | tf_op jit(solution)/shard_map/ppermute | solution.py:47
  142.1 38.3 %copy-start.4 = (f32[1536]{0:T(1024)S(1)}, f32[1536]{0:T(1024)}, u32[]{:S(2)}) copy-start(f32[1536]{0:T(1024)} %copy-done.3) | copy-start | bytes 18436
  142.1 38.3 %copy-start.6 = (f32[1536]{0:T(1024)S(1)}, f32[1536]{0:T(1024)}, u32[]{:S(2)}) copy-start(f32[1536]{0:T(1024)} %copy-done.5) | copy-start | bytes 18436
  142.1 38.3 %copy-start.8 = (f32[1536]{0:T(1024)S(1)}, f32[1536]{0:T(1024)}, u32[]{:S(2)}) copy-start(f32[1536]{0:T(1024)} %copy-done.7) | copy-start | bytes 18436
  142.1 38.3 %copy-start.10 = (f32[1536]{0:T(1024)S(1)}, f32[1536]{0:T(1024)}, u32[]{:S(2)}) copy-start(f32[1536]{0:T(1024)} %copy-done.9) | copy-start | bytes 18436
  142.1 38.3 %copy-start.12 = (f32[1536]{0:T(1024)S(1)}, f32[1536]{0:T(1024)}, u32[]{:S(2)}) copy-start(f32[1536]{0:T(1024)} %copy-done.11) | copy-start | bytes 18436
  142.2 38.3 %copy-start.14 = (f32[1536]{0:T(1024)S(1)}, f32[1536]{0:T(1024)}, u32[]{:S(2)}) copy-start(f32[1536]{0:T(1024)} %copy-done.13) | copy-start | bytes 18436
  142.2 38.3 %copy-start.16 = (f32[1536]{0:T(1024)S(1)}, f32[1536]{0:T(1024)}, u32[]{:S(2)}) copy-start(f32[1536]{0:T(1024)} %copy-done.15) | copy-start | bytes 18436
  142.2 38.3 %copy-start.18 = (f32[1536]{0:T(1024)S(1)}, f32[1536]{0:T(1024)}, u32[]{:S(2)}) copy-start(f32[1536]{0:T(1024)} %copy-done.17) | copy-start | bytes 18436
  142.2 38.3 %copy-start.20 = (f32[1536]{0:T(1024)S(1)}, f32[1536]{0:T(1024)}, u32[]{:S(2)}) copy-start(f32[1536]{0:T(1024)} %copy-done.19) | copy-start | bytes 18436
  142.2 38.3 %copy-start.22 = (f32[1536]{0:T(1024)S(1)}, f32[1536]{0:T(1024)}, u32[]{:S(2)}) copy-start(f32[1536]{0:T(1024)} %copy-done.21) | copy-start | bytes 18436
  142.2 38.3 %copy-start.24 = (f32[1536]{0:T(1024)S(1)}, f32[1536]{0:T(1024)}, u32[]{:S(2)}) copy-start(f32[1536]{0:T(1024)} %copy-done.23) | copy-start | bytes 18436
  142.2 38.3 %copy-start.26 = (f32[1536]{0:T(1024)S(1)}, f32[1536]{0:T(1024)}, u32[]{:S(2)}) copy-start(f32[1536]{0:T(1024)} %copy-done.25) | copy-start | bytes 18436
  142.2 38.3 %copy-start.28 = (f32[1536]{0:T(1024)S(1)}, f32[1536]{0:T(1024)}, u32[]{:S(2)}) copy-start(f32[1536]{0:T(1024)} %copy-done.27) | copy-start | bytes 18436
  142.2 38.3 %copy-start.30 = (f32[1536]{0:T(1024)S(1)}, f32[1536]{0:T(1024)}, u32[]{:S(2)}) copy-start(f32[1536]{0:T(1024)} %copy-done.29) | copy-start | bytes 18436
  142.2 38.3 %copy-start.32 = (f32[1536]{0:T(1024)S(1)}, f32[1536]{0:T(1024)}, u32[]{:S(2)}) copy-start(f32[1536]{0:T(1024)} %copy-done.31) | copy-start | bytes 18436
  142.3 38.3 %copy-start.34 = (f32[1536]{0:T(1024)S(1)}, f32[1536]{0:T(1024)}, u32[]{:S(2)}) copy-start(f32[1536]{0:T(1024)} %copy-done.33) | copy-start | bytes 18436
  142.3 38.3 %copy-start.36 = (f32[1536]{0:T(1024)S(1)}, f32[1536]{0:T(1024)}, u32[]{:S(2)}) copy-start(f32[1536]{0:T(1024)} %copy-done.35) | copy-start | bytes 18436
  142.3 38.3 %copy-start.38 = (f32[1536]{0:T(1024)S(1)}, f32[1536]{0:T(1024)}, u32[]{:S(2)}) copy-start(f32[1536]{0:T(1024)} %copy-done.37) | copy-start | bytes 18436
  142.3 38.3 %copy-start.40 = (f32[1536]{0:T(1024)S(1)}, f32[1536]{0:T(1024)}, u32[]{:S(2)}) copy-start(f32[1536]{0:T(1024)} %copy-done.39) | copy-start | bytes 18436
  142.3 38.3 %copy-start.42 = (f32[1536]{0:T(1024)S(1)}, f32[1536]{0:T(1024)}, u32[]{:S(2)}) copy-start(f32[1536]{0:T(1024)} %copy-done.41) | copy-start | bytes 18436
  142.3 4.9 %collective-permute-start.8 = (f32[9408]{0:T(1024)S(1)}, f32[9408]{0:T(1024)S(1)}, u32[]{:S(2)}, u32[]{:S(2)}) collective-permute-start(f32[9408]{0:T(1024)S(1)} %get-tuple-element.118), channel_id=1, source_target_pairs={{0,4},{4,0},{8,12},{12,8},{16,20},{20,16},{24,28},{28,24},{1,5},{5... | collective-permute-start | bytes 112904 | tf_op jit(solution)/shard_map/ppermute | solution.py:47
  147.4 5.2 %collective-permute-start.9 = (f32[4704]{0:T(1024)S(1)}, f32[4704]{0:T(1024)S(1)}, u32[]{:S(2)}, u32[]{:S(2)}) collective-permute-start(f32[4704]{0:T(1024)S(1)} %get-tuple-element.120), channel_id=1, source_target_pairs={{0,8},{4,12},{8,0},{12,4},{16,24},{20,28},{24,16},{28,20},{1,9},{5... | collective-permute-start | bytes 56456 | tf_op jit(solution)/shard_map/ppermute | solution.py:47
  152.8 5.9 %collective-permute-start.10 = (f32[2352]{0:T(1024)S(1)}, f32[2352]{0:T(1024)S(1)}, u32[]{:S(2)}, u32[]{:S(2)}) collective-permute-start(f32[2352]{0:T(1024)S(1)} %get-tuple-element.122), channel_id=1, source_target_pairs={{0,16},{4,20},{8,24},{12,28},{16,0},{20,4},{24,8},{28,12},{1,17},{... | collective-permute-start | bytes 28232 | tf_op jit(solution)/shard_map/ppermute | solution.py:47
  158.7 4.6 %collective-permute-start.11 = (f32[2352]{0:T(1024)S(1)}, f32[2352]{0:T(1024)S(1)}, u32[]{:S(2)}, u32[]{:S(2)}) collective-permute-start(f32[2352]{0:T(1024)S(1)} %add.598), channel_id=1, source_target_pairs={{0,16},{4,20},{8,24},{12,28},{16,0},{20,4},{24,8},{28,12},{1,17},{... | collective-permute-start | bytes 28232 | tf_op jit(solution)/shard_map/ppermute | solution.py:50
  163.4 3.8 %collective-permute-start.12 = (f32[4704]{0:T(1024)S(1)}, f32[4704]{0:T(1024)S(1)}, u32[]{:S(2)}, u32[]{:S(2)}) collective-permute-start(f32[4704]{0:T(1024)S(1)} %maximum_select_fusion.4), channel_id=1, source_target_pairs={{0,8},{4,12},{8,0},{12,4},{16,24},{20,28},{24,16},{28,20},{1,9},{5... | collective-permute-start | bytes 56456 | tf_op jit(solution)/shard_map/ppermute | solution.py:50
  167.3 4.1 %collective-permute-start.13 = (f32[9408]{0:T(1024)S(1)}, f32[9408]{0:T(1024)S(1)}, u32[]{:S(2)}, u32[]{:S(2)}) collective-permute-start(f32[9408]{0:T(1024)S(1)} %maximum_select_fusion.3), channel_id=1, source_target_pairs={{0,4},{4,0},{8,12},{12,8},{16,20},{20,16},{24,28},{28,24},{1,5},{5... | collective-permute-start | bytes 112904 | tf_op jit(solution)/shard_map/ppermute | solution.py:50
  167.9 8.2 %collective-permute-start.4 = (bf16[3,16,1536]{2,1,0:T(8,128)(2,1)S(1)}, bf16[3,16,1536]{2,1,0:T(8,128)(2,1)S(1)}, u32[]{:S(2)}, u32[]{:S(2)}) collective-permute-start(bf16[3,16,1536]{2,1,0:T(8,128)(2,1)S(1)} %get-tuple-element.128), channel_id=1, source_target_pairs={{0,1},{1,2},{2,3},{4,5},{5,6},{6,7},{8,9},{9,10},{10,11},{12,13},{... | collective-permute-start | bytes 442376 | tf_op jit(solution)/shard_map/ppermute | solution.py:14
  169.2 7.0 %collective-permute-start.5 = (bf16[3,16,1536]{2,1,0:T(8,128)(2,1)S(1)}, bf16[3,16,1536]{2,1,0:T(8,128)(2,1)S(1)}, u32[]{:S(2)}, u32[]{:S(2)}) collective-permute-start(bf16[3,16,1536]{2,1,0:T(8,128)(2,1)S(1)} %get-tuple-element.128), channel_id=1, source_target_pairs={{1,0},{2,1},{3,2},{5,4},{6,5},{7,6},{9,8},{10,9},{11,10},{13,12},{... | collective-permute-start | bytes 442376 | tf_op jit(solution)/shard_map/ppermute | solution.py:17
  171.5 8.9 %collective-permute-start.14 = (f32[18816]{0:T(1024)S(1)}, f32[18816]{0:T(1024)S(1)}, u32[]{:S(2)}, u32[]{:S(2)}) collective-permute-start(f32[18816]{0:T(1024)S(1)} %maximum_select_fusion.2), channel_id=1, source_target_pairs={{0,2},{1,3},{2,0},{3,1},{4,6},{5,7},{6,4},{7,5},{8,10},{9,11},{10,... | collective-permute-start | bytes 225800 | tf_op jit(solution)/shard_map/ppermute | solution.py:50
  180.4 3.1 %collective-permute-start.15 = (f32[37632]{0:T(1024)S(1)}, f32[37632]{0:T(1024)S(1)}, u32[]{:S(2)}, u32[]{:S(2)}) collective-permute-start(f32[37632]{0:T(1024)S(1)} %maximum_select_fusion.1), channel_id=1, source_target_pairs={{0,1},{1,0},{2,3},{3,2},{4,5},{5,4},{6,7},{7,6},{8,9},{9,8},{10,11... | collective-permute-start | bytes 451592 | tf_op jit(solution)/shard_map/ppermute | solution.py:50
  (23 other events, 94.6 us)
Sparse Core Ops, SparseCore 0:
  10.2 82.5 all-gather.1
  115.6 95.2 reduce-scatter.1

commit v3 on v2

--- a/solution.py
+++ b/solution.py
@@ -1,3 +1,5 @@
+import functools
+
 import jax
 import jax.numpy as jnp
 from jax import lax
@@ -69,6 +71,55 @@
     return data[0]
 
 
+def fsdp_ring(mesh):
+    count = mesh.shape["fsdp"]
+    try:
+        members = [mesh.devices[j, 0] for j in range(count)]
+        spots = [(d.coords[2], d.coords[1]) for d in members]
+        zs = sorted({z for z, _ in spots})
+        ys = sorted({y for _, y in spots})
+        rows_a, cols_b = len(zs), len(ys)
+        where = {(zs.index(z), ys.index(y)): j for j, (z, y) in enumerate(spots)}
+        assert len(where) == count == rows_a * cols_b and rows_a % 2 == 0 and cols_b >= 2
+        cells = [(a, 0) for a in range(rows_a)]
+        for k, a in enumerate(range(rows_a - 1, -1, -1)):
+            span = range(1, cols_b) if k % 2 == 0 else range(cols_b - 1, 0, -1)
+            cells += [(a, b) for b in span]
+        ring = [where[c] for c in cells]
+        assert sorted(ring) == list(range(count))
+    except Exception:
+        ring = list(range(count))
+    return ring
+
+
+def ring_all_gather(block, axis, ring):
+    count = len(ring)
+    place = [0] * count
+    for k, j in enumerate(ring):
+        place[j] = k
+    ring_arr = jnp.array(ring, jnp.int32)
+    me = lax.axis_index(axis)
+    spot = jnp.array(place, jnp.int32)[me]
+    forward = [(ring[k], ring[(k + 1) % count]) for k in range(count)]
+    backward = [(ring[k], ring[(k - 1) % count]) for k in range(count)]
+    ahead = count // 2
+    behind = count - 1 - ahead
+    gathered = jnp.zeros((count,) + block.shape, block.dtype)
+    gathered = lax.dynamic_update_index_in_dim(gathered, block, me, 0)
+    cw = block
+    ccw = block
+    for s in range(1, ahead + 1):
+        cw = lax.ppermute(cw, axis, forward)
+        if s <= behind:
+            ccw = lax.ppermute(ccw, axis, backward)
+        gathered = lax.dynamic_update_index_in_dim(gathered, cw, ring_arr[(spot - s) % count], 0)
+        if s <= behind:
+            gathered = lax.dynamic_update_index_in_dim(
+                gathered, ccw, ring_arr[(spot + s) % count], 0
+            )
+    return gathered.reshape((count * block.shape[0],) + block.shape[1:])
+
+
 def conv_rows(framed, kern, kbias):
     rows = framed.shape[0] - 6
     cols = framed.shape[1]
@@ -142,6 +193,7 @@
 
 
 def body(
+    ring,
     frames,
     kernel,
     kernel_bias,
@@ -155,7 +207,7 @@
 ):
     slab = frames[0]
     chans = slab.shape[2]
-    columns = lax.all_gather(up_weight, "fsdp", axis=0, tiled=True)
+    columns = ring_all_gather(up_weight, "fsdp", ring)
     padded = extended(slab, (("rows", 0),), 3)
     activation_rows = conv_rows(padded, kernel, kernel_bias)
     normed_output, standardized_input, inverse_deviation = apply_layer_norm(
@@ -217,7 +269,7 @@
         P("fsdp", None, None, "rows"),
     )
     return jax.shard_map(
-        body,
+        functools.partial(body, fsdp_ring(mesh)),
         mesh=mesh,
         in_specs=placed,
         out_specs=(

time: 221 us -> 233 us (1.054)
  waiting for transfers between devices: 127 us -> 96 us
  between operations: 16.7 us -> 34.8 us
  local copies, waits for them, and re-layouts: 8.88 us -> 22.4 us
  starting transfers between devices: 19.1 us -> 30.7 us
    all_gather x1 -> x0, waiting for transfers between devices: 61.2 us -> none  [body(): columns = lax.all_gather(up_weight, 'fsdp', axis=0, tiled=True)]
    ppermute x0 -> x7, waiting for transfers between devices: none -> 32.6 us  [the longest x4 32.6 us: ring_all_gather(): cw = lax.ppermute(cw, axis, forward)]
    ppermute x0 -> x7, starting transfers between devices: none -> 8.69 us  [the longest x4 7.72 us: ring_all_gather(): cw = lax.ppermute(cw, axis, forward)]
    dynamic_update_slice x0 -> x8, local copies, waits for them, and re-layouts: none -> 8.09 us  [the longest x4 4.6 us: ring_all_gather(): lax.dynamic_update_index_in_dim(gathered, cw, ring_arr[(spot - s) % count...]
    ppermute x5, starting transfers between devices: 6.82 us -> 9.94 us  [tree_allreduce(): other = lax.ppermute(flat, axis, perm)]
    reduce_scatter x1, waiting for transfers between devices: 26.6 us -> 29.6 us  [body(): lax.psum_scatter(w_term.astype(jnp.bfloat16), 'fsdp', scatter_dimension=0...]
    ppermute x5, waiting for transfers between devices: 17.8 us -> 14.9 us  [tree_allreduce(): flat = keep + lax.ppermute(give, axis, perm)]
    ppermute x5, waiting for transfers between devices: 11.8 us -> 9.05 us  [tree_allreduce(): other = lax.ppermute(flat, axis, perm)]
  transfers between devices with their start and end apart: 18 -> 24, of which waited for: 13 -> 14; matrix products, arithmetic and copies ran while one was open for 10% -> 15% of each run, Pallas kernels for 0% -> 0%
where the time goes in v3:
time: 233 us; the launch traced here: 232 us
  waiting for transfers between devices  96 us (41%)
  between operations  34.8 us (15%)
  starting transfers between devices  30.7 us (13%)
  local copies, waits for them, and re-layouts  22.4 us (10%)
  blocking collectives  17.3 us (7%)
  other arithmetic  16 us (7%)
  matrix products  14.9 us (6%)
    ppermute x4, waiting for transfers between devices, ring_all_gather(): cw = lax.ppermute(cw, axis, forward)  32.6 us
    reduce_scatter x1, waiting for transfers between devices, body(): lax.psum_scatter(w_term.astype(jnp.bfloat16), 'fsdp', scatter_dimension=0...  29.6 us
    ppermute x5, waiting for transfers between devices, tree_allreduce(): flat = keep + lax.ppermute(give, axis, perm)  14.9 us
    all_gather x1, blocking collectives, body(): whole = lax.all_gather(normed_output, 'rows', axis=0, tiled=True)  10.8 us
    ppermute x5, starting transfers between devices, tree_allreduce(): other = lax.ppermute(flat, axis, perm)  9.94 us
    ppermute x2, waiting for transfers between devices, tree_reduce_scatter(): lax.ppermute(give, axis, perm).astype(jnp.float32)  9.91 us
    ppermute x5, waiting for transfers between devices, tree_allreduce(): other = lax.ppermute(flat, axis, perm)  9.05 us
    ppermute x4, starting transfers between devices, ring_all_gather(): cw = lax.ppermute(cw, axis, forward)  7.72 us
  transfers between devices with their start and end apart: 24, of which 14 were waited for; matrix products, arithmetic and copies ran while one was open for 15% of the time, Pallas kernels for 0%

profile of v3, /device:TPU:0, one launch (start us, length us, event | category | flops | bytes accessed | tf_op | source)
XLA Modules:
  0.0 232.0 jit_solution(1035656213600915281)
XLA Ops:
  7.2 3.1 %collective-permute-start.2 = (bf16[192,1536]{1,0:T(8,128)(2,1)}, bf16[192,1536]{1,0:T(8,128)(2,1)}, u32[]{:S(2)}, u32[]{:S(2)}) collective-permute-start(bf16[192,1536]{1,0:T(8,128)(2,1)} %param.17), channel_id=1, source_target_pairs={{0,8},{8,16},{16,24},{24,28},{28,20},{20,12},{12,4},{4,0},{1,9},{9... | collective-permute-start | bytes 1769480 | tf_op jit(solution)/shard_map/ppermute | solution.py:112
  10.3 1.5 collective-permute-start
  11.8 1.3 collective-permute-start.1
  13.1 1.2 dynamic_slice.69
  16.3 1.8 slice_reduce_fusion.48
  18.1 1.3 slice_reduce_fusion.46
  19.4 2.6 %broadcast_in_dim.42 = bf16[8,192,1536]{2,1,0:T(8,128)(2,1)} broadcast(bf16[]{:T(256)} %constant.243.clone.1), dimensions={} | broadcast | bytes 4718594 | tf_op jit(solution)/shard_map/broadcast_in_dim | solution.py:107
  22.0 0.9 bitcast_dynamic-update-slice_fusion.7
  39.5 1.6 slice_reduce_fusion.47
  41.6 3.4 %fusion.153 = (f32[3,16]{1,0:T(4,128)S(1)}, f32[3,16,1536]{2,1,0:T(8,128)S(1)}) fusion(f32[1536]{0:T(1024)S(1)} %get-tuple-element.99, bf16[9,22,1536]{2,1,0:T(8,128)(2,1)S(1)} %select_maximum_fusion.2, f32[1536]{0:T(1024)S(1)} %get-tuple-element.100, f32[1536]{0:T(1024)S(1)} %get-tuple-element.53, f32[1536]{0:T(1024)S(1)} %get-tuple-element.54, ...), kind=kLoop, calls=%fused_computation.374 | loop fusion | flops 11206608 | bytes 7237824 | tf_op jit(solution)/shard_map/reduce_sum | solution.py:163
  46.4 10.8 %all_gather.3 = bf16[12,16,1536]{2,1,0:T(8,128)(2,1)S(1)} all-gather(bf16[3,16,1536]{2,1,0:T(8,128)(2,1)S(1)} %add_convert_fusion.1), channel_id=1, replica_groups=mesh['fsdp'=8,'rows'=4] {'rows'}, dimensions={0}, use_global_device_ids=true | all-gather | bytes 737280 | tf_op jit(solution)/shard_map/all_gather | solution.py:216
  57.2 1.5 collective-permute-start.4
  59.3 1.9 bitcast_dynamic-update-slice_fusion.6
  62.0 11.0 %collective-permute-done.4 = bf16[192,1536]{1,0:T(8,128)(2,1)S(1)} collective-permute-done((bf16[192,1536]{1,0:T(8,128)(2,1)}, bf16[192,1536]{1,0:T(8,128)(2,1)S(1)}, u32[]{:S(2)}, u32[]{:S(2)}) %collective-permute-start.4) | collective-permute-done | bytes 589856 | tf_op jit(solution)/shard_map/ppermute | solution.py:112
  73.0 1.5 collective-permute-start.6
  76.8 11.0 %collective-permute-done.6 = bf16[192,1536]{1,0:T(8,128)(2,1)S(1)} collective-permute-done((bf16[192,1536]{1,0:T(8,128)(2,1)S(1)}, bf16[192,1536]{1,0:T(8,128)(2,1)S(1)}, u32[]{:S(2)}, u32[]{:S(2)}) %collective-permute-start.6) | collective-permute-done | bytes 589856 | tf_op jit(solution)/shard_map/ppermute | solution.py:112
  87.8 1.5 collective-permute-start.8
  90.2 0.9 bitcast_dynamic-update-slice_fusion.1
  91.1 10.5 %collective-permute-done.8 = bf16[192,1536]{1,0:T(8,128)(2,1)S(1)} collective-permute-done((bf16[192,1536]{1,0:T(8,128)(2,1)S(1)}, bf16[192,1536]{1,0:T(8,128)(2,1)S(1)}, u32[]{:S(2)}, u32[]{:S(2)}) %collective-permute-start.8) | collective-permute-done | bytes 589856 | tf_op jit(solution)/shard_map/ppermute | solution.py:112
  101.7 0.9 bitcast_dynamic-update-slice_fusion
  102.6 7.3 %fusion.4 = (f32[1536]{0:T(1024)S(1)}, f32[1536]{0:T(1024)S(1)}, f32[192,1536]{1,0:T(8,128)}, f32[192,1536]{1,0:T(8,128)}) fusion(bf16[1,12,16,1536]{3,2,1,0:T(8,128)(2,1)S(1)} %copy-done.2, f32[1536]{0:T(1024)S(1)} %copy-done.56, bf16[192,1536]{1,0:T(8,128)(2,1)S(1)} %bitcast.61, bf16[1536,1536]{1,0:T(8,128)(2,1)} %bitcast.24), kind=kOutput, calls=%fused_computation.63 | convolution fusion | flops 926610432 | bytes 8275968 | tf_op jit(solution)/shard_map/dot_general | solution.py:220
  110.6 6.5 %all-reduce.2 = (f32[]{:T(128)}, f32[]{:T(128)}) all-reduce(f32[]{:T(128)} %get-tuple-element.125, f32[]{:T(128)} %get-tuple-element.124), channel_id=1, replica_groups=mesh['fsdp'=8,'rows'=4] {'rows'}, use_global_device_ids=true, to_apply=%region_4.5 | all-reduce | flops 2 | bytes 16 | tf_op jit(solution)/shard_map/psum | solution.py:225
  118.5 3.2 %fusion.3 = (bf16[192,1536]{1,0:T(8,128)(2,1)S(1)}, bf16[192,1536]{1,0:T(8,128)(2,1)}) fusion(f32[192,1536]{1,0:T(8,128)} %get-tuple-element.145, f32[192,1536]{1,0:T(8,128)} %get-tuple-element.132, bf16[1,12,16,1536]{3,2,1,0:T(8,128)(2,1)S(1)} %copy-done.2, f32[1536]{0:T(1024)S(1)} %get-tuple-element.137, f32[1536]{0:T(1024)S(1)} %get-tuple-element.130, ...), kind=kLoop, calls=%fused_computation.62 | loop fusion | flops 5603328 | bytes 4159488 | tf_op jit(solution)/shard_map/convert_element_type | solution.py:232
  121.8 3.6 %convolution_convert_fusion = bf16[1536,1536]{1,0:T(8,128)(2,1)} fusion(bf16[192,1536]{1,0:T(8,128)(2,1)S(1)} %bitcast.62, bf16[192,1536]{1,0:T(8,128)(2,1)S(1)} %get-tuple-element.135), kind=kOutput, calls=%fused_computation | convolution fusion | flops 908328960 | bytes 5898240 | tf_op jit(solution)/shard_map/dot_general | solution.py:233
  125.4 4.0 %convolution_convert_fusion.1 = bf16[12,16,1536]{2,1,0:T(8,128)(2,1)S(1)} fusion(bf16[12,16,1536]{2,1,0:T(8,128)(2,1)S(1)} %bitcast.63, bf16[1536,1536,1]{1,0,2:T(8,128)(2,1)} %bitcast.29), kind=kOutput, calls=%fused_computation.52 | convolution fusion | flops 906264576 | bytes 5898240 | tf_op jit(solution)/shard_map/hwf,cf->hwc/dot_general | solution.py:240
  129.6 1.5 collective-permute-done.9
  132.0 8.4 %collective-permute-done.10 = f32[1,3,16,1536]{3,2,1,0:T(8,128)S(1)} collective-permute-done((f32[1,3,16,1536]{3,2,1,0:T(8,128)S(1)}, f32[1,3,16,1536]{3,2,1,0:T(8,128)S(1)}, u32[]{:S(2)}, u32[]{:S(2)}) %collective-permute-start.10) | collective-permute-done | bytes 294944 | tf_op jit(solution)/shard_map/ppermute | solution.py:69
  140.6 0.9 fusion.140
  145.3 1.4 collective-permute-done.13
  147.9 3.7 %collective-permute-done.14 = f32[18816]{0:T(1024)S(1)} collective-permute-done((f32[18816]{0:T(1024)S(1)}, f32[18816]{0:T(1024)S(1)}, u32[]{:S(2)}, u32[]{:S(2)}) %collective-permute-start.14) | collective-permute-done | bytes 75296 | tf_op jit(solution)/shard_map/ppermute | solution.py:49
  152.2 1.6 collective-permute-start.15
  153.8 3.4 %collective-permute-done.15 = f32[9408]{0:T(1024)S(1)} collective-permute-done((f32[9408]{0:T(1024)S(1)}, f32[9408]{0:T(1024)S(1)}, u32[]{:S(2)}, u32[]{:S(2)}) %collective-permute-start.15) | collective-permute-done | bytes 37664 | tf_op jit(solution)/shard_map/ppermute | solution.py:49
  157.4 1.3 collective-permute-start.16
  158.7 3.3 %collective-permute-done.16 = f32[4704]{0:T(1024)S(1)} collective-permute-done((f32[4704]{0:T(1024)S(1)}, f32[4704]{0:T(1024)S(1)}, u32[]{:S(2)}, u32[]{:S(2)}) %collective-permute-start.16) | collective-permute-done | bytes 18848 | tf_op jit(solution)/shard_map/ppermute | solution.py:49
  162.2 2.2 collective-permute-start.17
  164.4 3.1 %collective-permute-done.17 = f32[2352]{0:T(1024)S(1)} collective-permute-done((f32[2352]{0:T(1024)S(1)}, f32[2352]{0:T(1024)S(1)}, u32[]{:S(2)}, u32[]{:S(2)}) %collective-permute-start.17) | collective-permute-done | bytes 9440 | tf_op jit(solution)/shard_map/ppermute | solution.py:49
  167.5 2.0 collective-permute-start.18
  169.4 3.3 %collective-permute-done.18 = f32[2352]{0:T(1024)S(1)} collective-permute-done((f32[2352]{0:T(1024)S(1)}, f32[2352]{0:T(1024)S(1)}, u32[]{:S(2)}, u32[]{:S(2)}) %collective-permute-start.18) | collective-permute-done | bytes 9440 | tf_op jit(solution)/shard_map/ppermute | solution.py:52
  172.8 2.4 %collective-permute-start.19 = (f32[4704]{0:T(1024)S(1)}, f32[4704]{0:T(1024)S(1)}, u32[]{:S(2)}, u32[]{:S(2)}) collective-permute-start(f32[4704]{0:T(1024)S(1)} %maximum_select_fusion.4), channel_id=1, source_target_pairs={{0,8},{4,12},{8,0},{12,4},{16,24},{20,28},{24,16},{28,20},{1,9},{5... | collective-permute-start | bytes 56456 | tf_op jit(solution)/shard_map/ppermute | solution.py:52
  175.2 1.8 collective-permute-done.19
  177.1 2.3 collective-permute-start.20
  179.4 1.3 collective-permute-start.11
  180.7 1.3 collective-permute-start.12
  182.1 3.2 %collective-permute-start.21 = (f32[18816]{0:T(1024)S(1)}, f32[18816]{0:T(1024)S(1)}, u32[]{:S(2)}, u32[]{:S(2)}) collective-permute-start(f32[18816]{0:T(1024)S(1)} %maximum_select_fusion.2), channel_id=1, source_target_pairs={{0,2},{1,3},{2,0},{3,1},{4,6},{5,7},{6,4},{7,5},{8,10},{9,11},{10,... | collective-permute-start | bytes 225800 | tf_op jit(solution)/shard_map/ppermute | solution.py:52
  185.5 4.0 %collective-permute-done.21 = f32[18816]{0:T(1024)S(1)} collective-permute-done((f32[18816]{0:T(1024)S(1)}, f32[18816]{0:T(1024)S(1)}, u32[]{:S(2)}, u32[]{:S(2)}) %collective-permute-start.21) | collective-permute-done | bytes 75296 | tf_op jit(solution)/shard_map/ppermute | solution.py:52
  189.8 2.8 %fusion.147 = bf16[1,3,16,1536]{3,2,1,0:T(8,128)(2,1)} fusion(f32[1536]{0:T(1024)S(1)} %get-tuple-element.99, bf16[9,22,1536]{2,1,0:T(8,128)(2,1)S(1)} %select_maximum_fusion, f32[1536]{0:T(1024)S(1)} %copy-done.5, f32[1536]{0:T(1024)S(1)} %get-tuple-element.53, f32[1536]{0:T(1024)S(1)} %get-tuple-element.54, ...), kind=kLoop, calls=%fused_computation.301 | loop fusion | flops 11132928 | bytes 7084032 | tf_op jit(solution)/shard_map/reshape | solution.py:255
  193.4 29.6 %reduce-scatter.2.cloned.1.call-done = bf16[192,1536]{1,0:T(8,128)(2,1)} async-done(((bf16[1536,1536]{1,0:T(8,128)(2,1)}), bf16[192,1536]{1,0:T(8,128)(2,1)}) %reduce-scatter.2.cloned.1.call-update) | async-done | bytes 589840 | tf_op jit(solution)/shard_map/reduce_scatter | solution.py:236
  223.0 2.2 convert_element_type.497
  (225 shorter events, 15.3 us)
Async XLA Ops:
  7.2 215.8 %reduce-scatter.2.cloned.1.call-start = ((), (), s32[]{:S(2)}) async-start(), calls=%async_computation.1 | async-start | bytes 5308416 | tf_op jit(solution)/shard_map/reduce_scatter | solution.py:236
  7.2 50.0 %collective-permute-start.2 = (bf16[192,1536]{1,0:T(8,128)(2,1)}, bf16[192,1536]{1,0:T(8,128)(2,1)}, u32[]{:S(2)}, u32[]{:S(2)}) collective-permute-start(bf16[192,1536]{1,0:T(8,128)(2,1)} %param.17), channel_id=1, source_target_pairs={{0,8},{8,16},{16,24},{24,28},{28,20},{20,12},{12,4},{4,0},{1,9},{9... | collective-permute-start | bytes 1769480 | tf_op jit(solution)/shard_map/ppermute | solution.py:112
  10.3 48.5 %collective-permute-start.3 = (bf16[192,1536]{1,0:T(8,128)(2,1)}, bf16[192,1536]{1,0:T(8,128)(2,1)S(1)}, u32[]{:S(2)}, u32[]{:S(2)}) collective-permute-start(bf16[192,1536]{1,0:T(8,128)(2,1)} %param.17), channel_id=1, source_target_pairs={{0,4},{8,0},{16,8},{24,16},{28,24},{20,28},{12,20},{4,12},{1,5},{9... | collective-permute-start | bytes 1769480 | tf_op jit(solution)/shard_map/ppermute | solution.py:114
  10.3 31.0 %collective-permute-start = (bf16[3,16,1536]{2,1,0:T(8,128)(2,1)}, bf16[3,16,1536]{2,1,0:T(8,128)(2,1)S(1)}, u32[]{:S(2)}, u32[]{:S(2)}) collective-permute-start(bf16[3,16,1536]{2,1,0:T(8,128)(2,1)} %bitcast.64), channel_id=1, source_target_pairs={{0,1},{1,2},{2,3},{4,5},{5,6},{6,7},{8,9},{9,10},{10,11},{12,13},{... | collective-permute-start | bytes 442376 | tf_op jit(solution)/shard_map/ppermute | solution.py:16
  11.8 29.5 %collective-permute-start.1 = (bf16[3,16,1536]{2,1,0:T(8,128)(2,1)}, bf16[3,16,1536]{2,1,0:T(8,128)(2,1)S(1)}, u32[]{:S(2)}, u32[]{:S(2)}) collective-permute-start(bf16[3,16,1536]{2,1,0:T(8,128)(2,1)} %bitcast.65), channel_id=1, source_target_pairs={{1,0},{2,1},{3,2},{5,4},{6,5},{7,6},{9,8},{10,9},{11,10},{13,12},{... | collective-permute-start | bytes 442376 | tf_op jit(solution)/shard_map/ppermute | solution.py:19
  19.3 22.2 %copy-start.4 = (f32[1536]{0:T(1024)}, f32[1536]{0:T(1024)S(1)}, u32[]{:S(2)}) copy-start(f32[1536]{0:T(1024)S(1)} %get-tuple-element.100) | copy-start | bytes 18436
  21.9 19.4 %copy-start = (bf16[1,3,16,1536]{3,2,1,0:T(8,128)(2,1)S(1)}, bf16[1,3,16,1536]{3,2,1,0:T(8,128)(2,1)}, u32[]{:S(2)}) copy-start(bf16[1,3,16,1536]{3,2,1,0:T(8,128)(2,1)} %param.12) | copy-start | bytes 442372
  22.0 19.6 %copy-start.55 = (f32[1536]{0:T(1024)S(1)}, f32[1536]{0:T(1024)}, u32[]{:S(2)}) copy-start(f32[1536]{0:T(1024)} %param.14) | copy-start | bytes 18436
  57.2 15.8 %collective-permute-start.4 = (bf16[192,1536]{1,0:T(8,128)(2,1)}, bf16[192,1536]{1,0:T(8,128)(2,1)S(1)}, u32[]{:S(2)}, u32[]{:S(2)}) collective-permute-start(bf16[192,1536]{1,0:T(8,128)(2,1)} %collective-permute-done.2), channel_id=1, source_target_pairs={{0,8},{8,16},{16,24},{24,28},{28,20},{20,12},{12,4},{4,0},{1,9},{9... | collective-permute-start | bytes 1769480 | tf_op jit(solution)/shard_map/ppermute | solution.py:112
  58.8 15.8 %collective-permute-start.5 = (bf16[192,1536]{1,0:T(8,128)(2,1)S(1)}, bf16[192,1536]{1,0:T(8,128)(2,1)S(1)}, u32[]{:S(2)}, u32[]{:S(2)}) collective-permute-start(bf16[192,1536]{1,0:T(8,128)(2,1)S(1)} %collective-permute-done.3), channel_id=1, source_target_pairs={{0,4},{8,0},{16,8},{24,16},{28,24},{20,28},{12,20},{4,12},{1,5},{9... | collective-permute-start | bytes 1769480 | tf_op jit(solution)/shard_map/ppermute | solution.py:114
  73.0 14.8 %collective-permute-start.6 = (bf16[192,1536]{1,0:T(8,128)(2,1)S(1)}, bf16[192,1536]{1,0:T(8,128)(2,1)S(1)}, u32[]{:S(2)}, u32[]{:S(2)}) collective-permute-start(bf16[192,1536]{1,0:T(8,128)(2,1)S(1)} %collective-permute-done.4), channel_id=1, source_target_pairs={{0,8},{8,16},{16,24},{24,28},{28,20},{20,12},{12,4},{4,0},{1,9},{9... | collective-permute-start | bytes 1769480 | tf_op jit(solution)/shard_map/ppermute | solution.py:112
  74.6 15.6 %collective-permute-start.7 = (bf16[192,1536]{1,0:T(8,128)(2,1)S(1)}, bf16[192,1536]{1,0:T(8,128)(2,1)S(1)}, u32[]{:S(2)}, u32[]{:S(2)}) collective-permute-start(bf16[192,1536]{1,0:T(8,128)(2,1)S(1)} %collective-permute-done.5), channel_id=1, source_target_pairs={{0,4},{8,0},{16,8},{24,16},{28,24},{20,28},{12,20},{4,12},{1,5},{9... | collective-permute-start | bytes 1769480 | tf_op jit(solution)/shard_map/ppermute | solution.py:114
  87.8 13.9 %collective-permute-start.8 = (bf16[192,1536]{1,0:T(8,128)(2,1)S(1)}, bf16[192,1536]{1,0:T(8,128)(2,1)S(1)}, u32[]{:S(2)}, u32[]{:S(2)}) collective-permute-start(bf16[192,1536]{1,0:T(8,128)(2,1)S(1)} %collective-permute-done.6), channel_id=1, source_target_pairs={{0,8},{8,16},{16,24},{24,28},{28,20},{20,12},{12,4},{4,0},{1,9},{9... | collective-permute-start | bytes 1769480 | tf_op jit(solution)/shard_map/ppermute | solution.py:112
  102.6 15.9 %copy-start.54 = (f32[1536]{0:T(1024)S(1)}, f32[1536]{0:T(1024)}, u32[]{:S(2)}) copy-start(f32[1536]{0:T(1024)} %param.20) | copy-start | bytes 18436
  129.5 1.6 collective-permute-start.9
  131.2 9.1 %collective-permute-start.10 = (f32[1,3,16,1536]{3,2,1,0:T(8,128)S(1)}, f32[1,3,16,1536]{3,2,1,0:T(8,128)S(1)}, u32[]{:S(2)}, u32[]{:S(2)}) collective-permute-start(f32[1,3,16,1536]{3,2,1,0:T(8,128)S(1)} %constant_dynamic-slice_fusion), channel_id=1, source_target_pairs={{0,2},{1,3},{2,0},{3,1},{4,6},{5,7},{6,4},{7,5},{8,10},{9,11},{10,... | collective-permute-start | bytes 884744 | tf_op jit(solution)/shard_map/ppermute | solution.py:69
  145.2 1.4 collective-permute-start.13
  147.2 4.5 %collective-permute-start.14 = (f32[18816]{0:T(1024)S(1)}, f32[18816]{0:T(1024)S(1)}, u32[]{:S(2)}, u32[]{:S(2)}) collective-permute-start(f32[18816]{0:T(1024)S(1)} %get-tuple-element.109), channel_id=1, source_target_pairs={{0,2},{1,3},{2,0},{3,1},{4,6},{5,7},{6,4},{7,5},{8,10},{9,11},{10,... | collective-permute-start | bytes 225800 | tf_op jit(solution)/shard_map/ppermute | solution.py:49
  152.0 37.6 %copy-start.5 = (f32[1536]{0:T(1024)S(1)}, f32[1536]{0:T(1024)}, u32[]{:S(2)}) copy-start(f32[1536]{0:T(1024)} %copy-done.4) | copy-start | bytes 18436
  152.0 37.6 %copy-start.7 = (f32[1536]{0:T(1024)S(1)}, f32[1536]{0:T(1024)}, u32[]{:S(2)}) copy-start(f32[1536]{0:T(1024)} %copy-done.6) | copy-start | bytes 18436
  152.0 37.6 %copy-start.9 = (f32[1536]{0:T(1024)S(1)}, f32[1536]{0:T(1024)}, u32[]{:S(2)}) copy-start(f32[1536]{0:T(1024)} %copy-done.8) | copy-start | bytes 18436
  152.0 37.6 %copy-start.11 = (f32[1536]{0:T(1024)S(1)}, f32[1536]{0:T(1024)}, u32[]{:S(2)}) copy-start(f32[1536]{0:T(1024)} %copy-done.10) | copy-start | bytes 18436
  152.1 37.6 %copy-start.13 = (f32[1536]{0:T(1024)S(1)}, f32[1536]{0:T(1024)}, u32[]{:S(2)}) copy-start(f32[1536]{0:T(1024)} %copy-done.12) | copy-start | bytes 18436
  152.1 37.6 %copy-start.15 = (f32[1536]{0:T(1024)S(1)}, f32[1536]{0:T(1024)}, u32[]{:S(2)}) copy-start(f32[1536]{0:T(1024)} %copy-done.14) | copy-start | bytes 18436
  152.1 37.6 %copy-start.17 = (f32[1536]{0:T(1024)S(1)}, f32[1536]{0:T(1024)}, u32[]{:S(2)}) copy-start(f32[1536]{0:T(1024)} %copy-done.16) | copy-start | bytes 18436
  152.1 37.6 %copy-start.19 = (f32[1536]{0:T(1024)S(1)}, f32[1536]{0:T(1024)}, u32[]{:S(2)}) copy-start(f32[1536]{0:T(1024)} %copy-done.18) | copy-start | bytes 18436
  152.1 37.6 %copy-start.21 = (f32[1536]{0:T(1024)S(1)}, f32[1536]{0:T(1024)}, u32[]{:S(2)}) copy-start(f32[1536]{0:T(1024)} %copy-done.20) | copy-start | bytes 18436
  152.1 37.6 %copy-start.23 = (f32[1536]{0:T(1024)S(1)}, f32[1536]{0:T(1024)}, u32[]{:S(2)}) copy-start(f32[1536]{0:T(1024)} %copy-done.22) | copy-start | bytes 18436
  152.1 37.6 %copy-start.25 = (f32[1536]{0:T(1024)S(1)}, f32[1536]{0:T(1024)}, u32[]{:S(2)}) copy-start(f32[1536]{0:T(1024)} %copy-done.24) | copy-start | bytes 18436
  152.1 37.6 %copy-start.27 = (f32[1536]{0:T(1024)S(1)}, f32[1536]{0:T(1024)}, u32[]{:S(2)}) copy-start(f32[1536]{0:T(1024)} %copy-done.26) | copy-start | bytes 18436
  152.1 37.6 %copy-start.29 = (f32[1536]{0:T(1024)S(1)}, f32[1536]{0:T(1024)}, u32[]{:S(2)}) copy-start(f32[1536]{0:T(1024)} %copy-done.28) | copy-start | bytes 18436
  152.1 37.6 %copy-start.31 = (f32[1536]{0:T(1024)S(1)}, f32[1536]{0:T(1024)}, u32[]{:S(2)}) copy-start(f32[1536]{0:T(1024)} %copy-done.30) | copy-start | bytes 18436
  152.2 37.6 %copy-start.33 = (f32[1536]{0:T(1024)S(1)}, f32[1536]{0:T(1024)}, u32[]{:S(2)}) copy-start(f32[1536]{0:T(1024)} %copy-done.32) | copy-start | bytes 18436
  152.2 37.6 %copy-start.35 = (f32[1536]{0:T(1024)S(1)}, f32[1536]{0:T(1024)}, u32[]{:S(2)}) copy-start(f32[1536]{0:T(1024)} %copy-done.34) | copy-start | bytes 18436
  152.2 37.6 %copy-start.37 = (f32[1536]{0:T(1024)S(1)}, f32[1536]{0:T(1024)}, u32[]{:S(2)}) copy-start(f32[1536]{0:T(1024)} %copy-done.36) | copy-start | bytes 18436
  152.2 37.6 %copy-start.39 = (f32[1536]{0:T(1024)S(1)}, f32[1536]{0:T(1024)}, u32[]{:S(2)}) copy-start(f32[1536]{0:T(1024)} %copy-done.38) | copy-start | bytes 18436
  152.2 37.6 %copy-start.41 = (f32[1536]{0:T(1024)S(1)}, f32[1536]{0:T(1024)}, u32[]{:S(2)}) copy-start(f32[1536]{0:T(1024)} %copy-done.40) | copy-start | bytes 18436
  152.2 37.6 %copy-start.43 = (f32[1536]{0:T(1024)S(1)}, f32[1536]{0:T(1024)}, u32[]{:S(2)}) copy-start(f32[1536]{0:T(1024)} %copy-done.42) | copy-start | bytes 18436
  152.2 4.9 %collective-permute-start.15 = (f32[9408]{0:T(1024)S(1)}, f32[9408]{0:T(1024)S(1)}, u32[]{:S(2)}, u32[]{:S(2)}) collective-permute-start(f32[9408]{0:T(1024)S(1)} %get-tuple-element.118), channel_id=1, source_target_pairs={{0,4},{4,0},{8,12},{12,8},{16,20},{20,16},{24,28},{28,24},{1,5},{5... | collective-permute-start | bytes 112904 | tf_op jit(solution)/shard_map/ppermute | solution.py:49
  157.4 4.7 %collective-permute-start.16 = (f32[4704]{0:T(1024)S(1)}, f32[4704]{0:T(1024)S(1)}, u32[]{:S(2)}, u32[]{:S(2)}) collective-permute-start(f32[4704]{0:T(1024)S(1)} %get-tuple-element.120), channel_id=1, source_target_pairs={{0,8},{4,12},{8,0},{12,4},{16,24},{20,28},{24,16},{28,20},{1,9},{5... | collective-permute-start | bytes 56456 | tf_op jit(solution)/shard_map/ppermute | solution.py:49
  162.2 5.3 %collective-permute-start.17 = (f32[2352]{0:T(1024)S(1)}, f32[2352]{0:T(1024)S(1)}, u32[]{:S(2)}, u32[]{:S(2)}) collective-permute-start(f32[2352]{0:T(1024)S(1)} %get-tuple-element.122), channel_id=1, source_target_pairs={{0,16},{4,20},{8,24},{12,28},{16,0},{20,4},{24,8},{28,12},{1,17},{... | collective-permute-start | bytes 28232 | tf_op jit(solution)/shard_map/ppermute | solution.py:49
  167.5 5.2 %collective-permute-start.18 = (f32[2352]{0:T(1024)S(1)}, f32[2352]{0:T(1024)S(1)}, u32[]{:S(2)}, u32[]{:S(2)}) collective-permute-start(f32[2352]{0:T(1024)S(1)} %add.720), channel_id=1, source_target_pairs={{0,16},{4,20},{8,24},{12,28},{16,0},{20,4},{24,8},{28,12},{1,17},{... | collective-permute-start | bytes 28232 | tf_op jit(solution)/shard_map/ppermute | solution.py:52
  172.8 4.2 %collective-permute-start.19 = (f32[4704]{0:T(1024)S(1)}, f32[4704]{0:T(1024)S(1)}, u32[]{:S(2)}, u32[]{:S(2)}) collective-permute-start(f32[4704]{0:T(1024)S(1)} %maximum_select_fusion.4), channel_id=1, source_target_pairs={{0,8},{4,12},{8,0},{12,4},{16,24},{20,28},{24,16},{28,20},{1,9},{5... | collective-permute-start | bytes 56456 | tf_op jit(solution)/shard_map/ppermute | solution.py:52
  177.1 4.9 %collective-permute-start.20 = (f32[9408]{0:T(1024)S(1)}, f32[9408]{0:T(1024)S(1)}, u32[]{:S(2)}, u32[]{:S(2)}) collective-permute-start(f32[9408]{0:T(1024)S(1)} %maximum_select_fusion.3), channel_id=1, source_target_pairs={{0,4},{4,0},{8,12},{12,8},{16,20},{20,16},{24,28},{28,24},{1,5},{5... | collective-permute-start | bytes 112904 | tf_op jit(solution)/shard_map/ppermute | solution.py:52
  179.4 5.9 %collective-permute-start.11 = (bf16[3,16,1536]{2,1,0:T(8,128)(2,1)S(1)}, bf16[3,16,1536]{2,1,0:T(8,128)(2,1)S(1)}, u32[]{:S(2)}, u32[]{:S(2)}) collective-permute-start(bf16[3,16,1536]{2,1,0:T(8,128)(2,1)S(1)} %get-tuple-element.128), channel_id=1, source_target_pairs={{0,1},{1,2},{2,3},{4,5},{5,6},{6,7},{8,9},{9,10},{10,11},{12,13},{... | collective-permute-start | bytes 442376 | tf_op jit(solution)/shard_map/ppermute | solution.py:16
  180.7 4.6 %collective-permute-start.12 = (bf16[3,16,1536]{2,1,0:T(8,128)(2,1)S(1)}, bf16[3,16,1536]{2,1,0:T(8,128)(2,1)S(1)}, u32[]{:S(2)}, u32[]{:S(2)}) collective-permute-start(bf16[3,16,1536]{2,1,0:T(8,128)(2,1)S(1)} %get-tuple-element.128), channel_id=1, source_target_pairs={{1,0},{2,1},{3,2},{5,4},{6,5},{7,6},{9,8},{10,9},{11,10},{13,12},{... | collective-permute-start | bytes 442376 | tf_op jit(solution)/shard_map/ppermute | solution.py:19
  182.1 7.4 %collective-permute-start.21 = (f32[18816]{0:T(1024)S(1)}, f32[18816]{0:T(1024)S(1)}, u32[]{:S(2)}, u32[]{:S(2)}) collective-permute-start(f32[18816]{0:T(1024)S(1)} %maximum_select_fusion.2), channel_id=1, source_target_pairs={{0,2},{1,3},{2,0},{3,1},{4,6},{5,7},{6,4},{7,5},{8,10},{9,11},{10,... | collective-permute-start | bytes 225800 | tf_op jit(solution)/shard_map/ppermute | solution.py:52
  189.5 3.1 %collective-permute-start.22 = (f32[37632]{0:T(1024)S(1)}, f32[37632]{0:T(1024)S(1)}, u32[]{:S(2)}, u32[]{:S(2)}) collective-permute-start(f32[37632]{0:T(1024)S(1)} %maximum_select_fusion.1), channel_id=1, source_target_pairs={{0,1},{1,0},{2,3},{3,2},{4,5},{5,4},{6,7},{7,6},{8,9},{9,8},{10,11... | collective-permute-start | bytes 451592 | tf_op jit(solution)/shard_map/ppermute | solution.py:52
  (33 other events, 174.7 us)
Sparse Core Ops, SparseCore 0:
  125.5 97.4 reduce-scatter.1

commit v4 on v3

--- a/solution.py
+++ b/solution.py
@@ -120,6 +120,40 @@
     return gathered.reshape((count * block.shape[0],) + block.shape[1:])
 
 
+def ring_reduce_scatter(terms, axis, ring):
+    count = len(ring)
+    place = [0] * count
+    for k, j in enumerate(ring):
+        place[j] = k
+    ring_arr = jnp.array(ring, jnp.int32)
+    me = lax.axis_index(axis)
+    spot = jnp.array(place, jnp.int32)[me]
+    forward = [(ring[k], ring[(k + 1) % count]) for k in range(count)]
+    backward = [(ring[k], ring[(k - 1) % count]) for k in range(count)]
+    ahead = count // 2
+    behind = count - 1 - ahead
+
+    def term(offset):
+        return lax.dynamic_index_in_dim(terms, ring_arr[(spot + offset) % count], 0, keepdims=False)
+
+    total = term(0).astype(jnp.float32)
+    cw = term(ahead)
+    ccw = term(-behind) if behind else None
+    for s in range(1, ahead + 1):
+        cw = lax.ppermute(cw, axis, forward)
+        if s <= behind:
+            ccw = lax.ppermute(ccw, axis, backward)
+        if s < ahead:
+            cw = (cw.astype(jnp.float32) + term(ahead - s).astype(jnp.float32)).astype(terms.dtype)
+        else:
+            total = total + cw.astype(jnp.float32)
+        if s < behind:
+            ccw = (ccw.astype(jnp.float32) + term(s - behind).astype(jnp.float32)).astype(terms.dtype)
+        elif s == behind:
+            total = total + ccw.astype(jnp.float32)
+    return total
+
+
 def conv_rows(framed, kern, kbias):
     rows = framed.shape[0] - 6
     cols = framed.shape[1]
@@ -207,7 +241,7 @@
 ):
     slab = frames[0]
     chans = slab.shape[2]
-    columns = ring_all_gather(up_weight, "fsdp", ring)
+    columns = lax.all_gather(up_weight, "fsdp", axis=0, tiled=True)
     padded = extended(slab, (("rows", 0),), 3)
     activation_rows = conv_rows(padded, kernel, kernel_bias)
     normed_output, standardized_input, inverse_deviation = apply_layer_norm(
@@ -233,9 +267,10 @@
     w_term = lax.dot_general(
         flat, dpre, (((0,), (0,)), ((), ())), preferred_element_type=jnp.float32
     )
-    up_grad = lax.psum_scatter(
-        w_term.astype(jnp.bfloat16), "fsdp", scatter_dimension=0, tiled=True
-    ).astype(jnp.float32)
+    n_fsdp = lax.axis_size("fsdp")
+    up_grad = ring_reduce_scatter(
+        w_term.astype(jnp.bfloat16).reshape((n_fsdp, chans // n_fsdp, -1)), "fsdp", ring
+    )
     dpre_rows = dpre.reshape(height, cols, -1)
     group_terms = jnp.einsum(
         "hwf,cf->hwc", dpre_rows, columns, preferred_element_type=jnp.float32

time: 233 us -> 242 us (1.039)
  waiting for transfers between devices: 96 us -> 113 us
  local copies, waits for them, and re-layouts: 22.4 us -> 12.2 us
  other arithmetic: 16 us -> 21.3 us
  starting transfers between devices: 30.7 us -> 26.3 us
  between operations: 34.8 us -> 38.3 us
    all_gather x0 -> x1, waiting for transfers between devices: none -> 60 us  [body(): columns = lax.all_gather(up_weight, 'fsdp', axis=0, tiled=True)]
    reduce_scatter x1 -> x0, waiting for transfers between devices: 29.6 us -> none  [body(): lax.psum_scatter(w_term.astype(jnp.bfloat16), 'fsdp', scatter_dimension=0...]
    ppermute x7, waiting for transfers between devices: 32.6 us -> 18.9 us  [the longest x4 17.6 us: ring_reduce_scatter(): cw = lax.ppermute(cw, axis, forward)]
    dynamic_update_slice x8 -> x0, local copies, waits for them, and re-layouts: 8.09 us -> none  [the longest x4 4.6 us: ring_all_gather(): lax.dynamic_update_index_in_dim(gathered, cw, ring_arr[(spot - s) % count...]
    ppermute x5, waiting for transfers between devices: 9.05 us -> 14.6 us  [tree_allreduce(): other = lax.ppermute(flat, axis, perm)]
    ppermute x2, waiting for transfers between devices: 9.91 us -> 5.34 us  [tree_reduce_scatter(): lax.ppermute(give, axis, perm).astype(jnp.float32)]
    ppermute x5, starting transfers between devices: 9.94 us -> 6.97 us  [tree_allreduce(): other = lax.ppermute(flat, axis, perm)]
    ppermute x7, starting transfers between devices: 8.69 us -> 6.11 us  [the longest x3 4.41 us: ring_reduce_scatter(): ccw = lax.ppermute(ccw, axis, backward)]
  transfers between devices with their start and end apart: 24 -> 24, of which waited for: 14 -> 13; matrix products, arithmetic and copies ran while one was open for 15% -> 11% of each run, Pallas kernels for 0% -> 0%
where the time goes in v4:
time: 242 us; the launch traced here: 241 us
  waiting for transfers between devices  113 us (47%)
  between operations  38.3 us (16%)
  starting transfers between devices  26.3 us (11%)
  other arithmetic  21.3 us (9%)
  blocking collectives  17.1 us (7%)
  matrix products  12.8 us (5%)
  local copies, waits for them, and re-layouts  12.2 us (5%)
    all_gather x1, waiting for transfers between devices, body(): columns = lax.all_gather(up_weight, 'fsdp', axis=0, tiled=True)  60 us
    ppermute x4, waiting for transfers between devices, ring_reduce_scatter(): cw = lax.ppermute(cw, axis, forward)  17.6 us
    ppermute x5, waiting for transfers between devices, tree_allreduce(): other = lax.ppermute(flat, axis, perm)  14.6 us
    ppermute x5, waiting for transfers between devices, tree_allreduce(): flat = keep + lax.ppermute(give, axis, perm)  13.5 us
    all_gather x1, blocking collectives, body(): whole = lax.all_gather(normed_output, 'rows', axis=0, tiled=True)  10.9 us
    dot_general x1, matrix products, body(): pre = jnp.dot(flat, columns, preferred_element_type=jnp.float32) + up_bias  7.34 us
    ppermute x5, starting transfers between devices, tree_allreduce(): other = lax.ppermute(flat, axis, perm)  6.97 us
    psum x1, blocking collectives, body(): norm_total = lax.psum(jnp.sum(norms), 'rows')  6.27 us
  transfers between devices with their start and end apart: 24, of which 13 were waited for; matrix products, arithmetic and copies ran while one was open for 11% of the time, Pallas kernels for 0%

profile of v4, /device:TPU:0, one launch (start us, length us, event | category | flops | bytes accessed | tf_op | source)
XLA Modules:
  0.0 241.0 jit_solution(11757666092016051045)
XLA Ops:
  7.2 0.7 all-gather.2.cloned.1.call-update
  7.9 2.4 collective-permute-start
  10.3 1.3 collective-permute-start.1
  11.6 1.7 slice_reduce_fusion.48
  13.3 1.4 slice_reduce_fusion.46
  14.8 1.8 slice_reduce_fusion.47
  17.0 3.4 %fusion.164 = (f32[3,16]{1,0:T(4,128)S(1)}, f32[3,16,1536]{2,1,0:T(8,128)S(1)}) fusion(f32[1536]{0:T(1024)S(1)} %get-tuple-element.99, bf16[9,22,1536]{2,1,0:T(8,128)(2,1)S(1)} %select_maximum_fusion.2, f32[1536]{0:T(1024)S(1)} %get-tuple-element.100, f32[1536]{0:T(1024)S(1)} %get-tuple-element.53, f32[1536]{0:T(1024)S(1)} %get-tuple-element.54, ...), kind=kLoop, calls=%fused_computation.382 | loop fusion | flops 11206608 | bytes 7237824 | tf_op jit(solution)/shard_map/reduce_sum | solution.py:197
  21.9 10.9 %all_gather.6 = bf16[12,16,1536]{2,1,0:T(8,128)(2,1)S(1)} all-gather(bf16[3,16,1536]{2,1,0:T(8,128)(2,1)S(1)} %add_convert_fusion.1), channel_id=1, replica_groups=mesh['fsdp'=8,'rows'=4] {'rows'}, dimensions={0}, use_global_device_ids=true | all-gather | bytes 737280 | tf_op jit(solution)/shard_map/all_gather | solution.py:250
  32.8 60.0 %all-gather.2.cloned.1.call-done = bf16[1536,1536]{1,0:T(8,128)(2,1)} async-done(((bf16[192,1536]{1,0:T(8,128)(2,1)}), bf16[1536,1536]{1,0:T(8,128)(2,1)}) %all-gather.2.cloned.1.call-update) | async-done | bytes 4718608 | tf_op jit(solution)/shard_map/all_gather | solution.py:244
  92.9 7.3 %fusion.9 = (f32[1536]{0:T(1024)S(1)}, f32[1536]{0:T(1024)S(1)}, f32[192,1536]{1,0:T(8,128)}, f32[192,1536]{1,0:T(8,128)}) fusion(bf16[1,12,16,1536]{3,2,1,0:T(8,128)(2,1)S(1)} %copy-done.2, f32[1536]{0:T(1024)S(1)} %copy-done.54, bf16[192,1536]{1,0:T(8,128)(2,1)S(1)} %bitcast.69, bf16[1536,1536]{1,0:T(8,128)(2,1)} %all-gather.2.cloned.1.call-done), kind=kOutput, calls=%fused_computation.65 | convolution fusion | flops 926610432 | bytes 8275968 | tf_op jit(solution)/shard_map/dot_general | solution.py:254
  100.8 6.3 %all-reduce.2 = (f32[]{:T(128)}, f32[]{:T(128)}) all-reduce(f32[]{:T(128)} %get-tuple-element.125, f32[]{:T(128)} %get-tuple-element.124), channel_id=1, replica_groups=mesh['fsdp'=8,'rows'=4] {'rows'}, use_global_device_ids=true, to_apply=%region_4.5 | all-reduce | flops 2 | bytes 16 | tf_op jit(solution)/shard_map/psum | solution.py:259
  108.4 3.2 %fusion.8 = (bf16[192,1536]{1,0:T(8,128)(2,1)S(1)}, bf16[192,1536]{1,0:T(8,128)(2,1)}) fusion(f32[192,1536]{1,0:T(8,128)} %get-tuple-element.152, f32[192,1536]{1,0:T(8,128)} %get-tuple-element.132, bf16[1,12,16,1536]{3,2,1,0:T(8,128)(2,1)S(1)} %copy-done.2, f32[1536]{0:T(1024)S(1)} %get-tuple-element.143, f32[1536]{0:T(1024)S(1)} %get-tuple-element.130, ...), kind=kLoop, calls=%fused_computation.64 | loop fusion | flops 5603328 | bytes 4159488 | tf_op jit(solution)/shard_map/convert_element_type | solution.py:266
  111.7 4.0 %fusion.2 = bf16[12,16,1536]{2,1,0:T(8,128)(2,1)S(1)} fusion(bf16[12,16,1536]{2,1,0:T(8,128)(2,1)S(1)} %bitcast.71, bf16[1536,1536]{1,0:T(8,128)(2,1)} %all-gather.2.cloned.1.call-done), kind=kOutput, calls=%fused_computation.54 | convolution fusion | flops 906264576 | bytes 5898240 | tf_op jit(solution)/shard_map/hwf,cf->hwc/dot_general | solution.py:275
  115.7 0.7 dynamic-slice_bitcast_fusion.2
  123.7 0.7 fusion.166
  128.2 1.0 convert_add_fusion.6
  129.2 1.8 collective-permute-start.3
  131.0 1.4 convolution_convert_fusion
  132.6 0.8 collective-permute-start.9
  133.4 5.3 %collective-permute-done.3 = f32[1,3,16,1536]{3,2,1,0:T(8,128)S(1)} collective-permute-done((f32[1,3,16,1536]{3,2,1,0:T(8,128)S(1)}, f32[1,3,16,1536]{3,2,1,0:T(8,128)S(1)}, u32[]{:S(2)}, u32[]{:S(2)}) %collective-permute-start.3) | collective-permute-done | bytes 294944 | tf_op jit(solution)/shard_map/ppermute | solution.py:69
  138.9 0.9 fusion.151
  139.9 0.8 fusion.152
  142.7 0.9 dynamic-slice_reduce_fusion
  143.7 1.4 collective-permute-done.13
  145.6 1.8 collective-permute-start.14
  147.4 2.7 %collective-permute-done.14 = f32[18816]{0:T(1024)S(1)} collective-permute-done((f32[18816]{0:T(1024)S(1)}, f32[18816]{0:T(1024)S(1)}, u32[]{:S(2)}, u32[]{:S(2)}) %collective-permute-start.14) | collective-permute-done | bytes 75296 | tf_op jit(solution)/shard_map/ppermute | solution.py:49
  151.0 3.4 %collective-permute-done.15 = f32[9408]{0:T(1024)S(1)} collective-permute-done((f32[9408]{0:T(1024)S(1)}, f32[9408]{0:T(1024)S(1)}, u32[]{:S(2)}, u32[]{:S(2)}) %collective-permute-start.15) | collective-permute-done | bytes 37664 | tf_op jit(solution)/shard_map/ppermute | solution.py:49
  155.3 3.2 %collective-permute-done.16 = f32[4704]{0:T(1024)S(1)} collective-permute-done((f32[4704]{0:T(1024)S(1)}, f32[4704]{0:T(1024)S(1)}, u32[]{:S(2)}, u32[]{:S(2)}) %collective-permute-start.16) | collective-permute-done | bytes 18848 | tf_op jit(solution)/shard_map/ppermute | solution.py:49
  158.7 2.0 collective-permute-start.17
  160.7 2.7 %collective-permute-done.17 = f32[2352]{0:T(1024)S(1)} collective-permute-done((f32[2352]{0:T(1024)S(1)}, f32[2352]{0:T(1024)S(1)}, u32[]{:S(2)}, u32[]{:S(2)}) %collective-permute-start.17) | collective-permute-done | bytes 9440 | tf_op jit(solution)/shard_map/ppermute | solution.py:49
  163.5 1.9 collective-permute-start.18
  177.0 1.3 collective-permute-start.4
  178.3 1.3 collective-permute-start.5
  179.7 1.5 collective-permute-start.19
  181.2 1.3 fusion.18
  183.0 4.7 %collective-permute-done.19 = f32[4704]{0:T(1024)S(1)} collective-permute-done((f32[4704]{0:T(1024)S(1)}, f32[4704]{0:T(1024)S(1)}, u32[]{:S(2)}, u32[]{:S(2)}) %collective-permute-start.19) | collective-permute-done | bytes 18848 | tf_op jit(solution)/shard_map/ppermute | solution.py:52
  188.1 9.9 %collective-permute-done.20 = f32[9408]{0:T(1024)S(1)} collective-permute-done((f32[9408]{0:T(1024)S(1)}, f32[9408]{0:T(1024)S(1)}, u32[]{:S(2)}, u32[]{:S(2)}) %collective-permute-start.20) | collective-permute-done | bytes 37664 | tf_op jit(solution)/shard_map/ppermute | solution.py:52
  198.3 3.5 %collective-permute-start.21 = (f32[18816]{0:T(1024)S(1)}, f32[18816]{0:T(1024)S(1)}, u32[]{:S(2)}, u32[]{:S(2)}) collective-permute-start(f32[18816]{0:T(1024)S(1)} %maximum_select_fusion.2), channel_id=1, source_target_pairs={{0,2},{1,3},{2,0},{3,1},{4,6},{5,7},{6,4},{7,5},{8,10},{9,11},{10,... | collective-permute-start | bytes 225800 | tf_op jit(solution)/shard_map/ppermute | solution.py:52
  201.8 1.5 fusion.20
  203.4 2.0 collective-permute-start.7
  205.6 2.8 %fusion.158 = bf16[1,3,16,1536]{3,2,1,0:T(8,128)(2,1)} fusion(f32[1536]{0:T(1024)S(1)} %get-tuple-element.99, bf16[9,22,1536]{2,1,0:T(8,128)(2,1)S(1)} %select_maximum_fusion, f32[1536]{0:T(1024)S(1)} %copy-done.5, f32[1536]{0:T(1024)S(1)} %get-tuple-element.53, f32[1536]{0:T(1024)S(1)} %get-tuple-element.54, ...), kind=kLoop, calls=%fused_computation.309 | loop fusion | flops 11132928 | bytes 7084032 | tf_op jit(solution)/shard_map/reshape | solution.py:290
  208.5 8.1 %collective-permute-done.11 = bf16[192,1536]{1,0:T(8,128)(2,1)S(1)} collective-permute-done((bf16[192,1536]{1,0:T(8,128)(2,1)S(1)}, bf16[192,1536]{1,0:T(8,128)(2,1)S(1)}, u32[]{:S(2)}, u32[]{:S(2)}) %collective-permute-start.11) | collective-permute-done | bytes 589856 | tf_op jit(solution)/shard_map/ppermute | solution.py:143
  216.7 1.5 fusion.19
  218.5 1.8 collective-permute-start.8
  220.3 0.8 select_n.263
  221.1 9.4 %collective-permute-done.12 = bf16[192,1536]{1,0:T(8,128)(2,1)S(1)} collective-permute-done((bf16[192,1536]{1,0:T(8,128)(2,1)S(1)}, bf16[192,1536]{1,0:T(8,128)(2,1)S(1)}, u32[]{:S(2)}, u32[]{:S(2)}) %collective-permute-start.12) | collective-permute-done | bytes 589856 | tf_op jit(solution)/shard_map/ppermute | solution.py:143
  230.6 1.3 collective-permute-done.8
  231.9 2.3 fusion.21
  (218 shorter events, 9.8 us)
Async XLA Ops:
  7.2 9.6 %copy-start.1 = (bf16[1,3,16,1536]{3,2,1,0:T(8,128)(2,1)S(1)}, bf16[1,3,16,1536]{3,2,1,0:T(8,128)(2,1)}, u32[]{:S(2)}) copy-start(bf16[1,3,16,1536]{3,2,1,0:T(8,128)(2,1)} %param.12) | copy-start | bytes 442372
  7.2 9.8 %copy-start.53 = (f32[1536]{0:T(1024)S(1)}, f32[1536]{0:T(1024)}, u32[]{:S(2)}) copy-start(f32[1536]{0:T(1024)} %param.14) | copy-start | bytes 18436
  7.2 85.7 %all-gather.2.cloned.1.call-start = ((), (), s32[]{:S(2)}) async-start(), calls=%async_computation | async-start | bytes 5308416 | tf_op jit(solution)/shard_map/all_gather | solution.py:244
  7.9 8.8 %collective-permute-start = (bf16[3,16,1536]{2,1,0:T(8,128)(2,1)}, bf16[3,16,1536]{2,1,0:T(8,128)(2,1)S(1)}, u32[]{:S(2)}, u32[]{:S(2)}) collective-permute-start(bf16[3,16,1536]{2,1,0:T(8,128)(2,1)} %bitcast.72), channel_id=1, source_target_pairs={{0,1},{1,2},{2,3},{4,5},{5,6},{6,7},{8,9},{9,10},{10,11},{12,13},{... | collective-permute-start | bytes 442376 | tf_op jit(solution)/shard_map/ppermute | solution.py:16
  10.3 6.5 %collective-permute-start.1 = (bf16[3,16,1536]{2,1,0:T(8,128)(2,1)}, bf16[3,16,1536]{2,1,0:T(8,128)(2,1)S(1)}, u32[]{:S(2)}, u32[]{:S(2)}) collective-permute-start(bf16[3,16,1536]{2,1,0:T(8,128)(2,1)} %bitcast.73), channel_id=1, source_target_pairs={{1,0},{2,1},{3,2},{5,4},{6,5},{7,6},{9,8},{10,9},{11,10},{13,12},{... | collective-permute-start | bytes 442376 | tf_op jit(solution)/shard_map/ppermute | solution.py:19
  20.6 72.2 %copy-start.2 = (bf16[1,12,16,1536]{3,2,1,0:T(8,128)(2,1)S(1)}, bf16[1,12,16,1536]{3,2,1,0:T(8,128)(2,1)}, u32[]{:S(2)}) copy-start(bf16[1,12,16,1536]{3,2,1,0:T(8,128)(2,1)} %param.21) | copy-start | bytes 1769476
  20.6 72.2 %copy-start.54 = (f32[1536]{0:T(1024)S(1)}, f32[1536]{0:T(1024)}, u32[]{:S(2)}) copy-start(f32[1536]{0:T(1024)} %param.18) | copy-start | bytes 18436
  92.8 7.3 %copy-start.3 = (f32[1536]{0:T(1024)S(1)}, f32[1536]{0:T(1024)}, u32[]{:S(2)}) copy-start(f32[1536]{0:T(1024)} %param.19) | copy-start | bytes 18436
  92.8 15.6 %copy-start.52 = (f32[1536]{0:T(1024)S(1)}, f32[1536]{0:T(1024)}, u32[]{:S(2)}) copy-start(f32[1536]{0:T(1024)} %param.20) | copy-start | bytes 18436
  111.7 12.0 %copy-start.50 = (s32[8]{0:T(128)S(1)}, s32[8]{0:T(128)}, u32[]{:S(2)}) copy-start(s32[8]{0:T(128)} %constant.287.clone) | copy-start | bytes 100
  116.5 11.7 %collective-permute-start.2 = (bf16[2,3,16,1536]{3,2,1,0:T(8,128)(2,1)}, bf16[2,3,16,1536]{3,2,1,0:T(8,128)(2,1)}, u32[]{:S(2)}, u32[]{:S(2)}) collective-permute-start(bf16[2,3,16,1536]{3,2,1,0:T(8,128)(2,1)} %dynamic-slice_bitcast_fusion.2), channel_id=1, source_target_pairs={{0,1},{1,0},{2,3},{3,2},{4,5},{5,4},{6,7},{7,6},{8,9},{9,8},{10,11... | collective-permute-start | bytes 884744 | tf_op jit(solution)/shard_map/ppermute | solution.py:69
  129.2 9.5 %collective-permute-start.3 = (f32[1,3,16,1536]{3,2,1,0:T(8,128)S(1)}, f32[1,3,16,1536]{3,2,1,0:T(8,128)S(1)}, u32[]{:S(2)}, u32[]{:S(2)}) collective-permute-start(f32[1,3,16,1536]{3,2,1,0:T(8,128)S(1)} %constant_dynamic-slice_fusion), channel_id=1, source_target_pairs={{0,2},{1,3},{2,0},{3,1},{4,6},{5,7},{6,4},{7,5},{8,10},{9,11},{10,... | collective-permute-start | bytes 884744 | tf_op jit(solution)/shard_map/ppermute | solution.py:69
  132.5 7.4 %copy-start = (bf16[1536,1536]{1,0:T(8,128)(2,1)}, bf16[1536,1536]{1,0:T(8,128)(2,1)S(1)}, u32[]{:S(2)}) copy-start(bf16[1536,1536]{1,0:T(8,128)(2,1)S(1)} %convolution_convert_fusion) | copy-start | bytes 14155780
  132.6 48.6 %collective-permute-start.9 = (bf16[192,1536]{1,0:T(8,128)(2,1)S(1)}, bf16[192,1536]{1,0:T(8,128)(2,1)S(1)}, u32[]{:S(2)}, u32[]{:S(2)}) collective-permute-start(bf16[192,1536]{1,0:T(8,128)(2,1)S(1)} %get-tuple-element.140), channel_id=1, source_target_pairs={{0,8},{8,16},{16,24},{24,28},{28,20},{20,12},{12,4},{4,0},{1,9},{9... | collective-permute-start | bytes 1769480 | tf_op jit(solution)/shard_map/ppermute | solution.py:143
  143.6 1.4 collective-permute-start.13
  145.6 4.5 %collective-permute-start.14 = (f32[18816]{0:T(1024)S(1)}, f32[18816]{0:T(1024)S(1)}, u32[]{:S(2)}, u32[]{:S(2)}) collective-permute-start(f32[18816]{0:T(1024)S(1)} %get-tuple-element.109), channel_id=1, source_target_pairs={{0,2},{1,3},{2,0},{3,1},{4,6},{5,7},{6,4},{7,5},{8,10},{9,11},{10,... | collective-permute-start | bytes 225800 | tf_op jit(solution)/shard_map/ppermute | solution.py:49
  150.4 4.1 %collective-permute-start.15 = (f32[9408]{0:T(1024)S(1)}, f32[9408]{0:T(1024)S(1)}, u32[]{:S(2)}, u32[]{:S(2)}) collective-permute-start(f32[9408]{0:T(1024)S(1)} %get-tuple-element.118), channel_id=1, source_target_pairs={{0,4},{4,0},{8,12},{12,8},{16,20},{20,16},{24,28},{28,24},{1,5},{5... | collective-permute-start | bytes 112904 | tf_op jit(solution)/shard_map/ppermute | solution.py:49
  154.7 3.8 %collective-permute-start.16 = (f32[4704]{0:T(1024)S(1)}, f32[4704]{0:T(1024)S(1)}, u32[]{:S(2)}, u32[]{:S(2)}) collective-permute-start(f32[4704]{0:T(1024)S(1)} %get-tuple-element.120), channel_id=1, source_target_pairs={{0,8},{4,12},{8,0},{12,4},{16,24},{20,28},{24,16},{28,20},{1,9},{5... | collective-permute-start | bytes 56456 | tf_op jit(solution)/shard_map/ppermute | solution.py:49
  158.7 4.8 %collective-permute-start.17 = (f32[2352]{0:T(1024)S(1)}, f32[2352]{0:T(1024)S(1)}, u32[]{:S(2)}, u32[]{:S(2)}) collective-permute-start(f32[2352]{0:T(1024)S(1)} %get-tuple-element.122), channel_id=1, source_target_pairs={{0,16},{4,20},{8,24},{12,28},{16,0},{20,4},{24,8},{28,12},{1,17},{... | collective-permute-start | bytes 28232 | tf_op jit(solution)/shard_map/ppermute | solution.py:49
  163.5 16.1 %collective-permute-start.18 = (f32[2352]{0:T(1024)S(1)}, f32[2352]{0:T(1024)S(1)}, u32[]{:S(2)}, u32[]{:S(2)}) collective-permute-start(f32[2352]{0:T(1024)S(1)} %add.753), channel_id=1, source_target_pairs={{0,16},{4,20},{8,24},{12,28},{16,0},{20,4},{24,8},{28,12},{1,17},{... | collective-permute-start | bytes 28232 | tf_op jit(solution)/shard_map/ppermute | solution.py:52
  176.4 25.4 %collective-permute-start.6 = (bf16[192,1536]{1,0:T(8,128)(2,1)S(1)}, bf16[192,1536]{1,0:T(8,128)(2,1)S(1)}, u32[]{:S(2)}, u32[]{:S(2)}) collective-permute-start(bf16[192,1536]{1,0:T(8,128)(2,1)S(1)} %get-tuple-element.139), channel_id=1, source_target_pairs={{0,4},{8,0},{16,8},{24,16},{28,24},{20,28},{12,20},{4,12},{1,5},{9... | collective-permute-start | bytes 1769480 | tf_op jit(solution)/shard_map/ppermute | solution.py:145
  177.0 10.9 %collective-permute-start.4 = (bf16[3,16,1536]{2,1,0:T(8,128)(2,1)S(1)}, bf16[3,16,1536]{2,1,0:T(8,128)(2,1)S(1)}, u32[]{:S(2)}, u32[]{:S(2)}) collective-permute-start(bf16[3,16,1536]{2,1,0:T(8,128)(2,1)S(1)} %get-tuple-element.128), channel_id=1, source_target_pairs={{0,1},{1,2},{2,3},{4,5},{5,6},{6,7},{8,9},{9,10},{10,11},{12,13},{... | collective-permute-start | bytes 442376 | tf_op jit(solution)/shard_map/ppermute | solution.py:16
  178.3 9.6 %collective-permute-start.5 = (bf16[3,16,1536]{2,1,0:T(8,128)(2,1)S(1)}, bf16[3,16,1536]{2,1,0:T(8,128)(2,1)S(1)}, u32[]{:S(2)}, u32[]{:S(2)}) collective-permute-start(bf16[3,16,1536]{2,1,0:T(8,128)(2,1)S(1)} %get-tuple-element.128), channel_id=1, source_target_pairs={{1,0},{2,1},{3,2},{5,4},{6,5},{7,6},{9,8},{10,9},{11,10},{13,12},{... | collective-permute-start | bytes 442376 | tf_op jit(solution)/shard_map/ppermute | solution.py:19
  179.7 8.0 %collective-permute-start.19 = (f32[4704]{0:T(1024)S(1)}, f32[4704]{0:T(1024)S(1)}, u32[]{:S(2)}, u32[]{:S(2)}) collective-permute-start(f32[4704]{0:T(1024)S(1)} %maximum_select_fusion.4), channel_id=1, source_target_pairs={{0,8},{4,12},{8,0},{12,4},{16,24},{20,28},{24,16},{28,20},{1,9},{5... | collective-permute-start | bytes 56456 | tf_op jit(solution)/shard_map/ppermute | solution.py:52
  182.4 19.4 %collective-permute-start.10 = (bf16[192,1536]{1,0:T(8,128)(2,1)S(1)}, bf16[192,1536]{1,0:T(8,128)(2,1)S(1)}, u32[]{:S(2)}, u32[]{:S(2)}) collective-permute-start(bf16[192,1536]{1,0:T(8,128)(2,1)S(1)} %fusion.18), channel_id=1, source_target_pairs={{0,8},{8,16},{16,24},{24,28},{28,20},{20,12},{12,4},{4,0},{1,9},{9... | collective-permute-start | bytes 1769480 | tf_op jit(solution)/shard_map/ppermute | solution.py:143
  187.8 10.2 %collective-permute-start.20 = (f32[9408]{0:T(1024)S(1)}, f32[9408]{0:T(1024)S(1)}, u32[]{:S(2)}, u32[]{:S(2)}) collective-permute-start(f32[9408]{0:T(1024)S(1)} %maximum_select_fusion.3), channel_id=1, source_target_pairs={{0,4},{4,0},{8,12},{12,8},{16,20},{20,16},{24,28},{28,24},{1,5},{5... | collective-permute-start | bytes 112904 | tf_op jit(solution)/shard_map/ppermute | solution.py:52
  198.1 7.3 %copy-start.5 = (f32[1536]{0:T(1024)S(1)}, f32[1536]{0:T(1024)}, u32[]{:S(2)}) copy-start(f32[1536]{0:T(1024)} %copy-done.4) | copy-start | bytes 18436
  198.1 7.3 %copy-start.7 = (f32[1536]{0:T(1024)S(1)}, f32[1536]{0:T(1024)}, u32[]{:S(2)}) copy-start(f32[1536]{0:T(1024)} %copy-done.6) | copy-start | bytes 18436
  198.1 7.3 %copy-start.9 = (f32[1536]{0:T(1024)S(1)}, f32[1536]{0:T(1024)}, u32[]{:S(2)}) copy-start(f32[1536]{0:T(1024)} %copy-done.8) | copy-start | bytes 18436
  198.1 7.3 %copy-start.11 = (f32[1536]{0:T(1024)S(1)}, f32[1536]{0:T(1024)}, u32[]{:S(2)}) copy-start(f32[1536]{0:T(1024)} %copy-done.10) | copy-start | bytes 18436
  198.2 7.3 %copy-start.13 = (f32[1536]{0:T(1024)S(1)}, f32[1536]{0:T(1024)}, u32[]{:S(2)}) copy-start(f32[1536]{0:T(1024)} %copy-done.12) | copy-start | bytes 18436
  198.2 7.3 %copy-start.15 = (f32[1536]{0:T(1024)S(1)}, f32[1536]{0:T(1024)}, u32[]{:S(2)}) copy-start(f32[1536]{0:T(1024)} %copy-done.14) | copy-start | bytes 18436
  198.2 7.3 %copy-start.17 = (f32[1536]{0:T(1024)S(1)}, f32[1536]{0:T(1024)}, u32[]{:S(2)}) copy-start(f32[1536]{0:T(1024)} %copy-done.16) | copy-start | bytes 18436
  198.2 7.3 %copy-start.19 = (f32[1536]{0:T(1024)S(1)}, f32[1536]{0:T(1024)}, u32[]{:S(2)}) copy-start(f32[1536]{0:T(1024)} %copy-done.18) | copy-start | bytes 18436
  198.2 7.3 %copy-start.21 = (f32[1536]{0:T(1024)S(1)}, f32[1536]{0:T(1024)}, u32[]{:S(2)}) copy-start(f32[1536]{0:T(1024)} %copy-done.20) | copy-start | bytes 18436
  198.2 7.3 %copy-start.23 = (f32[1536]{0:T(1024)S(1)}, f32[1536]{0:T(1024)}, u32[]{:S(2)}) copy-start(f32[1536]{0:T(1024)} %copy-done.22) | copy-start | bytes 18436
  198.2 7.3 %copy-start.25 = (f32[1536]{0:T(1024)S(1)}, f32[1536]{0:T(1024)}, u32[]{:S(2)}) copy-start(f32[1536]{0:T(1024)} %copy-done.24) | copy-start | bytes 18436
  198.2 7.3 %copy-start.27 = (f32[1536]{0:T(1024)S(1)}, f32[1536]{0:T(1024)}, u32[]{:S(2)}) copy-start(f32[1536]{0:T(1024)} %copy-done.26) | copy-start | bytes 18436
  198.2 7.3 %copy-start.29 = (f32[1536]{0:T(1024)S(1)}, f32[1536]{0:T(1024)}, u32[]{:S(2)}) copy-start(f32[1536]{0:T(1024)} %copy-done.28) | copy-start | bytes 18436
  198.2 7.3 %copy-start.31 = (f32[1536]{0:T(1024)S(1)}, f32[1536]{0:T(1024)}, u32[]{:S(2)}) copy-start(f32[1536]{0:T(1024)} %copy-done.30) | copy-start | bytes 18436
  198.3 7.3 %copy-start.33 = (f32[1536]{0:T(1024)S(1)}, f32[1536]{0:T(1024)}, u32[]{:S(2)}) copy-start(f32[1536]{0:T(1024)} %copy-done.32) | copy-start | bytes 18436
  198.3 7.3 %copy-start.35 = (f32[1536]{0:T(1024)S(1)}, f32[1536]{0:T(1024)}, u32[]{:S(2)}) copy-start(f32[1536]{0:T(1024)} %copy-done.34) | copy-start | bytes 18436
  198.3 10.1 %collective-permute-start.21 = (f32[18816]{0:T(1024)S(1)}, f32[18816]{0:T(1024)S(1)}, u32[]{:S(2)}, u32[]{:S(2)}) collective-permute-start(f32[18816]{0:T(1024)S(1)} %maximum_select_fusion.2), channel_id=1, source_target_pairs={{0,2},{1,3},{2,0},{3,1},{4,6},{5,7},{6,4},{7,5},{8,10},{9,11},{10,... | collective-permute-start | bytes 225800 | tf_op jit(solution)/shard_map/ppermute | solution.py:52
  203.3 13.3 %collective-permute-start.11 = (bf16[192,1536]{1,0:T(8,128)(2,1)S(1)}, bf16[192,1536]{1,0:T(8,128)(2,1)S(1)}, u32[]{:S(2)}, u32[]{:S(2)}) collective-permute-start(bf16[192,1536]{1,0:T(8,128)(2,1)S(1)} %get-tuple-element.138), channel_id=1, source_target_pairs={{0,8},{8,16},{16,24},{24,28},{28,20},{20,12},{12,4},{4,0},{1,9},{9... | collective-permute-start | bytes 1769480 | tf_op jit(solution)/shard_map/ppermute | solution.py:143
  203.4 13.3 %collective-permute-start.7 = (bf16[192,1536]{1,0:T(8,128)(2,1)S(1)}, bf16[192,1536]{1,0:T(8,128)(2,1)S(1)}, u32[]{:S(2)}, u32[]{:S(2)}) collective-permute-start(bf16[192,1536]{1,0:T(8,128)(2,1)S(1)} %get-tuple-element.137), channel_id=1, source_target_pairs={{0,4},{8,0},{16,8},{24,16},{28,24},{20,28},{12,20},{4,12},{1,5},{9... | collective-permute-start | bytes 1769480 | tf_op jit(solution)/shard_map/ppermute | solution.py:145
  208.4 11.9 %collective-permute-start.22 = (f32[37632]{0:T(1024)S(1)}, f32[37632]{0:T(1024)S(1)}, u32[]{:S(2)}, u32[]{:S(2)}) collective-permute-start(f32[37632]{0:T(1024)S(1)} %maximum_select_fusion.1), channel_id=1, source_target_pairs={{0,1},{1,0},{2,3},{3,2},{4,5},{5,4},{6,7},{7,6},{8,9},{9,8},{10,11... | collective-permute-start | bytes 451592 | tf_op jit(solution)/shard_map/ppermute | solution.py:52
  218.2 12.4 %collective-permute-start.12 = (bf16[192,1536]{1,0:T(8,128)(2,1)S(1)}, bf16[192,1536]{1,0:T(8,128)(2,1)S(1)}, u32[]{:S(2)}, u32[]{:S(2)}) collective-permute-start(bf16[192,1536]{1,0:T(8,128)(2,1)S(1)} %get-tuple-element.136), channel_id=1, source_target_pairs={{0,8},{8,16},{16,24},{24,28},{28,20},{20,12},{12,4},{4,0},{1,9},{9... | collective-permute-start | bytes 1769480 | tf_op jit(solution)/shard_map/ppermute | solution.py:143
  218.5 13.4 %collective-permute-start.8 = (bf16[192,1536]{1,0:T(8,128)(2,1)S(1)}, bf16[192,1536]{1,0:T(8,128)(2,1)S(1)}, u32[]{:S(2)}, u32[]{:S(2)}) collective-permute-start(bf16[192,1536]{1,0:T(8,128)(2,1)S(1)} %get-tuple-element.135), channel_id=1, source_target_pairs={{0,4},{8,0},{16,8},{24,16},{28,24},{20,28},{12,20},{4,12},{1,5},{9... | collective-permute-start | bytes 1769480 | tf_op jit(solution)/shard_map/ppermute | solution.py:145
  (32 other events, 143.3 us)
Sparse Core Ops, SparseCore 0:
  10.2 82.5 all-gather.1

commit v5 on v4

--- a/solution.py
+++ b/solution.py
@@ -241,7 +241,14 @@
 ):
     slab = frames[0]
     chans = slab.shape[2]
-    columns = lax.all_gather(up_weight, "fsdp", axis=0, tiled=True)
+    split = up_weight.shape[1] // 2
+    columns = jnp.concatenate(
+        [
+            lax.all_gather(up_weight[:, :split], "fsdp", axis=0, tiled=True),
+            ring_all_gather(up_weight[:, split:], "fsdp", ring),
+        ],
+        axis=1,
+    )
     padded = extended(slab, (("rows", 0),), 3)
     activation_rows = conv_rows(padded, kernel, kernel_bias)
     normed_output, standardized_input, inverse_deviation = apply_layer_norm(
@@ -267,10 +274,9 @@
     w_term = lax.dot_general(
         flat, dpre, (((0,), (0,)), ((), ())), preferred_element_type=jnp.float32
     )
-    n_fsdp = lax.axis_size("fsdp")
-    up_grad = ring_reduce_scatter(
-        w_term.astype(jnp.bfloat16).reshape((n_fsdp, chans // n_fsdp, -1)), "fsdp", ring
-    )
+    up_grad = lax.psum_scatter(
+        w_term.astype(jnp.bfloat16), "fsdp", scatter_dimension=0, tiled=True
+    ).astype(jnp.float32)
     dpre_rows = dpre.reshape(height, cols, -1)
     group_terms = jnp.einsum(
         "hwf,cf->hwc", dpre_rows, columns, preferred_element_type=jnp.float32

time: 242 us -> 221 us (0.913)
  waiting for transfers between devices: 113 us -> 94.9 us
  other arithmetic: 21.3 us -> 15.9 us
  local copies, waits for them, and re-layouts: 12.2 us -> 15.8 us
  between operations: 38.3 us -> 34.8 us
    all_gather x1, waiting for transfers between devices: 60 us -> 0.01 us  [body(): lax.all_gather(up_weight[:, :split], 'fsdp', axis=0, tiled=True)]
    reduce_scatter x0 -> x1, waiting for transfers between devices: none -> 26.9 us  [body(): lax.psum_scatter(w_term.astype(jnp.bfloat16), 'fsdp', scatter_dimension=0...]
    ppermute x7, waiting for transfers between devices: 18.9 us -> 28.5 us  [the longest x4 24.4 us: ring_all_gather(): cw = lax.ppermute(cw, axis, forward)]
    dynamic_update_slice x0 -> x8, local copies, waits for them, and re-layouts: none -> 6 us  [the longest x4 2.99 us: ring_all_gather(): lax.dynamic_update_index_in_dim(gathered, cw, ring_arr[(spot - s) % count...]
    ppermute x5, waiting for transfers between devices: 13.5 us -> 18 us  [tree_allreduce(): flat = keep + lax.ppermute(give, axis, perm)]
    slice x3, local copies, waits for them, and re-layouts: 4.91 us -> 0.82 us  [conv_rows(): kern[i, j]]
    ppermute x2, waiting for transfers between devices: 5.34 us -> 8.86 us  [tree_reduce_scatter(): lax.ppermute(give, axis, perm).astype(jnp.float32)]
    ppermute x7, starting transfers between devices: 6.11 us -> 8.79 us  [the longest x4 6.82 us: ring_all_gather(): cw = lax.ppermute(cw, axis, forward)]
  transfers between devices with their start and end apart: 24 -> 25, of which waited for: 13 -> 15; matrix products, arithmetic and copies ran while one was open for 11% -> 13% of each run, Pallas kernels for 0% -> 0%
where the time goes in v5:
time: 221 us; the launch traced here: 220 us
  waiting for transfers between devices  94.9 us (43%)
  between operations  34.8 us (16%)
  starting transfers between devices  26.5 us (12%)
  blocking collectives  17.2 us (8%)
  other arithmetic  15.9 us (7%)
  local copies, waits for them, and re-layouts  15.8 us (7%)
  matrix products  15 us (7%)
    reduce_scatter x1, waiting for transfers between devices, body(): lax.psum_scatter(w_term.astype(jnp.bfloat16), 'fsdp', scatter_dimension=0...  26.9 us
    ppermute x4, waiting for transfers between devices, ring_all_gather(): cw = lax.ppermute(cw, axis, forward)  24.4 us
    ppermute x5, waiting for transfers between devices, tree_allreduce(): flat = keep + lax.ppermute(give, axis, perm)  18 us
    ppermute x5, waiting for transfers between devices, tree_allreduce(): other = lax.ppermute(flat, axis, perm)  12.6 us
    all_gather x1, blocking collectives, body(): whole = lax.all_gather(normed_output, 'rows', axis=0, tiled=True)  10.8 us
    ppermute x2, waiting for transfers between devices, tree_reduce_scatter(): lax.ppermute(give, axis, perm).astype(jnp.float32)  8.86 us
    dot_general x1, matrix products, body(): pre = jnp.dot(flat, columns, preferred_element_type=jnp.float32) + up_bias  7.37 us
    ppermute x4, starting transfers between devices, ring_all_gather(): cw = lax.ppermute(cw, axis, forward)  6.82 us
  transfers between devices with their start and end apart: 25, of which 15 were waited for; matrix products, arithmetic and copies ran while one was open for 13% of the time, Pallas kernels for 0%

profile of v5, /device:TPU:0, one launch (start us, length us, event | category | flops | bytes accessed | tf_op | source)
XLA Modules:
  0.0 220.2 jit_solution(12617456404670016398)
XLA Ops:
  7.2 1.8 fusion.164
  9.1 3.0 %collective-permute-start.2 = (bf16[192,768]{1,0:T(8,128)(2,1)S(1)}, bf16[192,768]{1,0:T(8,128)(2,1)S(1)}, u32[]{:S(2)}, u32[]{:S(2)}) collective-permute-start(bf16[192,768]{1,0:T(8,128)(2,1)S(1)} %get-tuple-element.138), channel_id=1, source_target_pairs={{0,8},{8,16},{16,24},{24,28},{28,20},{20,12},{12,4},{4,0},{1,9},{9... | collective-permute-start | bytes 884744 | tf_op jit(solution)/shard_map/ppermute | solution.py:112
  12.1 1.5 collective-permute-start
  13.5 1.3 collective-permute-start.1
  15.0 1.6 broadcast_in_dim.42
  16.6 0.8 bitcast_dynamic-update-slice_fusion.7
  37.9 3.4 %fusion.162 = (f32[3,16]{1,0:T(4,128)S(1)}, f32[3,16,1536]{2,1,0:T(8,128)S(1)}) fusion(f32[1536]{0:T(1024)S(1)} %get-tuple-element.99, bf16[9,22,1536]{2,1,0:T(8,128)(2,1)S(1)} %select_maximum_fusion.2, f32[1536]{0:T(1024)S(1)} %get-tuple-element.100, f32[1536]{0:T(1024)S(1)} %get-tuple-element.53, f32[1536]{0:T(1024)S(1)} %get-tuple-element.54, ...), kind=kLoop, calls=%fused_computation.380 | loop fusion | flops 11206608 | bytes 7237824 | tf_op jit(solution)/shard_map/reduce_sum | solution.py:197
  41.9 10.8 %all_gather.6 = bf16[12,16,1536]{2,1,0:T(8,128)(2,1)S(1)} all-gather(bf16[3,16,1536]{2,1,0:T(8,128)(2,1)S(1)} %add_convert_fusion.1), channel_id=1, replica_groups=mesh['fsdp'=8,'rows'=4] {'rows'}, dimensions={0}, use_global_device_ids=true | all-gather | bytes 737280 | tf_op jit(solution)/shard_map/all_gather | solution.py:257
  52.6 1.5 collective-permute-start.4
  56.1 11.8 %collective-permute-done.4 = bf16[192,768]{1,0:T(8,128)(2,1)S(1)} collective-permute-done((bf16[192,768]{1,0:T(8,128)(2,1)S(1)}, bf16[192,768]{1,0:T(8,128)(2,1)S(1)}, u32[]{:S(2)}, u32[]{:S(2)}) %collective-permute-start.4) | collective-permute-done | bytes 294944 | tf_op jit(solution)/shard_map/ppermute | solution.py:112
  67.9 2.2 collective-permute-start.6
  70.1 4.1 %collective-permute-done.5 = bf16[192,768]{1,0:T(8,128)(2,1)S(1)} collective-permute-done((bf16[192,768]{1,0:T(8,128)(2,1)S(1)}, bf16[192,768]{1,0:T(8,128)(2,1)S(1)}, u32[]{:S(2)}, u32[]{:S(2)}) %collective-permute-start.5) | collective-permute-done | bytes 294944 | tf_op jit(solution)/shard_map/ppermute | solution.py:114
  74.3 1.5 collective-permute-start.7
  76.5 0.8 bitcast_dynamic-update-slice_fusion.3
  77.3 5.7 %collective-permute-done.6 = bf16[192,768]{1,0:T(8,128)(2,1)S(1)} collective-permute-done((bf16[192,768]{1,0:T(8,128)(2,1)S(1)}, bf16[192,768]{1,0:T(8,128)(2,1)S(1)}, u32[]{:S(2)}, u32[]{:S(2)}) %collective-permute-start.6) | collective-permute-done | bytes 294944 | tf_op jit(solution)/shard_map/ppermute | solution.py:112
  83.0 0.8 bitcast_dynamic-update-slice_fusion.2
  83.8 0.8 bitcast_dynamic-update-slice_fusion.1
  84.6 6.8 %collective-permute-done.8 = bf16[192,768]{1,0:T(8,128)(2,1)S(1)} collective-permute-done((bf16[192,768]{1,0:T(8,128)(2,1)S(1)}, bf16[192,768]{1,0:T(8,128)(2,1)S(1)}, u32[]{:S(2)}, u32[]{:S(2)}) %collective-permute-start.8) | collective-permute-done | bytes 294944 | tf_op jit(solution)/shard_map/ppermute | solution.py:112
  91.4 0.8 bitcast_dynamic-update-slice_fusion
  92.2 7.4 %fusion.11 = (f32[1536]{0:T(1024)S(1)}, f32[1536]{0:T(1024)S(1)}, f32[192,1536]{1,0:T(8,128)}, f32[192,1536]{1,0:T(8,128)}) fusion(bf16[1,12,16,1536]{3,2,1,0:T(8,128)(2,1)S(1)} %copy-done.2, f32[1536]{0:T(1024)S(1)} %copy-done.57, bf16[192,1536]{1,0:T(8,128)(2,1)S(1)} %bitcast.62, bf16[1536,768]{1,0:T(8,128)(2,1)} %bitcast.24, ...), kind=kOutput, calls=%fused_computation.67 | convolution fusion | flops 936047616 | bytes 8275968 | tf_op jit(solution)/shard_map/dot_general | solution.py:261
  100.2 6.5 %all-reduce.2 = (f32[]{:T(128)}, f32[]{:T(128)}) all-reduce(f32[]{:T(128)} %get-tuple-element.125, f32[]{:T(128)} %get-tuple-element.124), channel_id=1, replica_groups=mesh['fsdp'=8,'rows'=4] {'rows'}, use_global_device_ids=true, to_apply=%region_4.5 | all-reduce | flops 2 | bytes 16 | tf_op jit(solution)/shard_map/psum | solution.py:266
  108.0 3.2 %fusion.10 = (bf16[192,1536]{1,0:T(8,128)(2,1)S(1)}, bf16[192,1536]{1,0:T(8,128)(2,1)}) fusion(f32[192,1536]{1,0:T(8,128)} %get-tuple-element.147, f32[192,1536]{1,0:T(8,128)} %get-tuple-element.132, bf16[1,12,16,1536]{3,2,1,0:T(8,128)(2,1)S(1)} %copy-done.2, f32[1536]{0:T(1024)S(1)} %get-tuple-element.139, f32[1536]{0:T(1024)S(1)} %get-tuple-element.130, ...), kind=kLoop, calls=%fused_computation.66 | loop fusion | flops 5603328 | bytes 4159488 | tf_op jit(solution)/shard_map/convert_element_type | solution.py:273
  111.2 3.6 %convolution_convert_fusion = bf16[1536,1536]{1,0:T(8,128)(2,1)} fusion(bf16[192,1536]{1,0:T(8,128)(2,1)S(1)} %bitcast.63, bf16[192,1536]{1,0:T(8,128)(2,1)S(1)} %get-tuple-element.135), kind=kOutput, calls=%fused_computation | convolution fusion | flops 908328960 | bytes 5898240 | tf_op jit(solution)/shard_map/dot_general | solution.py:274
  114.8 4.1 %fusion.4 = bf16[12,16,1536]{2,1,0:T(8,128)(2,1)S(1)} fusion(bf16[12,16,1536]{2,1,0:T(8,128)(2,1)S(1)} %bitcast.64, bf16[1536,768]{1,0:T(8,128)(2,1)} %bitcast.24, bf16[1536,768]{1,0:T(8,128)(2,1)} %all-gather.2.cloned.1.call-done), kind=kOutput, calls=%fused_computation.56 | convolution fusion | flops 915701760 | bytes 5898240 | tf_op jit(solution)/shard_map/hwf,cf->hwc/dot_general | solution.py:281
  119.1 1.5 collective-permute-done.9
  120.8 1.8 collective-permute-start.10
  122.5 7.3 %collective-permute-done.10 = f32[1,3,16,1536]{3,2,1,0:T(8,128)S(1)} collective-permute-done((f32[1,3,16,1536]{3,2,1,0:T(8,128)S(1)}, f32[1,3,16,1536]{3,2,1,0:T(8,128)S(1)}, u32[]{:S(2)}, u32[]{:S(2)}) %collective-permute-start.10) | collective-permute-done | bytes 294944 | tf_op jit(solution)/shard_map/ppermute | solution.py:69
  130.1 0.9 fusion.147
  131.8 0.8 fusion.148
  133.8 0.9 dynamic-slice_reduce_fusion
  134.8 1.4 collective-permute-done.13
  136.7 1.8 collective-permute-start.14
  138.5 2.7 %collective-permute-done.14 = f32[18816]{0:T(1024)S(1)} collective-permute-done((f32[18816]{0:T(1024)S(1)}, f32[18816]{0:T(1024)S(1)}, u32[]{:S(2)}, u32[]{:S(2)}) %collective-permute-start.14) | collective-permute-done | bytes 75296 | tf_op jit(solution)/shard_map/ppermute | solution.py:49
  141.7 1.5 collective-permute-start.15
  143.2 3.4 %collective-permute-done.15 = f32[9408]{0:T(1024)S(1)} collective-permute-done((f32[9408]{0:T(1024)S(1)}, f32[9408]{0:T(1024)S(1)}, u32[]{:S(2)}, u32[]{:S(2)}) %collective-permute-start.15) | collective-permute-done | bytes 37664 | tf_op jit(solution)/shard_map/ppermute | solution.py:49
  147.6 4.7 %collective-permute-done.16 = f32[4704]{0:T(1024)S(1)} collective-permute-done((f32[4704]{0:T(1024)S(1)}, f32[4704]{0:T(1024)S(1)}, u32[]{:S(2)}, u32[]{:S(2)}) %collective-permute-start.16) | collective-permute-done | bytes 18848 | tf_op jit(solution)/shard_map/ppermute | solution.py:49
  152.8 5.8 %collective-permute-done.17 = f32[2352]{0:T(1024)S(1)} collective-permute-done((f32[2352]{0:T(1024)S(1)}, f32[2352]{0:T(1024)S(1)}, u32[]{:S(2)}, u32[]{:S(2)}) %collective-permute-start.17) | collective-permute-done | bytes 9440 | tf_op jit(solution)/shard_map/ppermute | solution.py:49
  158.5 4.9 %collective-permute-done.18 = f32[2352]{0:T(1024)S(1)} collective-permute-done((f32[2352]{0:T(1024)S(1)}, f32[2352]{0:T(1024)S(1)}, u32[]{:S(2)}, u32[]{:S(2)}) %collective-permute-start.18) | collective-permute-done | bytes 9440 | tf_op jit(solution)/shard_map/ppermute | solution.py:52
  163.5 3.8 %collective-permute-done.19 = f32[4704]{0:T(1024)S(1)} collective-permute-done((f32[4704]{0:T(1024)S(1)}, f32[4704]{0:T(1024)S(1)}, u32[]{:S(2)}, u32[]{:S(2)}) %collective-permute-start.19) | collective-permute-done | bytes 18848 | tf_op jit(solution)/shard_map/ppermute | solution.py:52
  167.3 1.5 collective-permute-start.20
  168.9 1.3 collective-permute-start.11
  170.2 1.3 collective-permute-start.12
  171.6 4.5 %collective-permute-start.21 = (f32[18816]{0:T(1024)S(1)}, f32[18816]{0:T(1024)S(1)}, u32[]{:S(2)}, u32[]{:S(2)}) collective-permute-start(f32[18816]{0:T(1024)S(1)} %maximum_select_fusion.2), channel_id=1, source_target_pairs={{0,2},{1,3},{2,0},{3,1},{4,6},{5,7},{6,4},{7,5},{8,10},{9,11},{10,... | collective-permute-start | bytes 225800 | tf_op jit(solution)/shard_map/ppermute | solution.py:52
  176.3 4.0 %collective-permute-done.21 = f32[18816]{0:T(1024)S(1)} collective-permute-done((f32[18816]{0:T(1024)S(1)}, f32[18816]{0:T(1024)S(1)}, u32[]{:S(2)}, u32[]{:S(2)}) %collective-permute-start.21) | collective-permute-done | bytes 75296 | tf_op jit(solution)/shard_map/ppermute | solution.py:52
  180.6 2.8 %fusion.154 = bf16[1,3,16,1536]{3,2,1,0:T(8,128)(2,1)} fusion(f32[1536]{0:T(1024)S(1)} %get-tuple-element.99, bf16[9,22,1536]{2,1,0:T(8,128)(2,1)S(1)} %select_maximum_fusion, f32[1536]{0:T(1024)S(1)} %get-tuple-element.100, f32[1536]{0:T(1024)S(1)} %get-tuple-element.53, f32[1536]{0:T(1024)S(1)} %get-tuple-element.54, ...), kind=kLoop, calls=%fused_computation.305 | loop fusion | flops 11132928 | bytes 7084032 | tf_op jit(solution)/shard_map/reshape | solution.py:296
  183.5 0.8 select_n.251
  184.2 26.9 %reduce-scatter.2.cloned.1.call-done = bf16[192,1536]{1,0:T(8,128)(2,1)} async-done(((bf16[1536,1536]{1,0:T(8,128)(2,1)}), bf16[192,1536]{1,0:T(8,128)(2,1)}) %reduce-scatter.2.cloned.1.call-update) | async-done | bytes 589840 | tf_op jit(solution)/shard_map/reduce_scatter | solution.py:277
  211.2 2.2 %convert_element_type.497 = f32[192,1536]{1,0:T(8,128)} convert(bf16[192,1536]{1,0:T(8,128)(2,1)} %reduce-scatter.2.cloned.1.call-done) | non-fusion elementwise | flops 294912 | bytes 1769472 | tf_op jit(solution)/shard_map/convert_element_type | solution.py:279
  (233 shorter events, 11.4 us)
Async XLA Ops:
  7.2 85.0 %all-gather.2.cloned.1.call-start = ((), (), s32[]{:S(2)}) async-start(), calls=%async_computation.1 | async-start | bytes 2654208 | tf_op jit(solution)/shard_map/all_gather | solution.py:247
  9.1 43.6 %collective-permute-start.2 = (bf16[192,768]{1,0:T(8,128)(2,1)S(1)}, bf16[192,768]{1,0:T(8,128)(2,1)S(1)}, u32[]{:S(2)}, u32[]{:S(2)}) collective-permute-start(bf16[192,768]{1,0:T(8,128)(2,1)S(1)} %get-tuple-element.138), channel_id=1, source_target_pairs={{0,8},{8,16},{16,24},{24,28},{28,20},{20,12},{12,4},{4,0},{1,9},{9... | collective-permute-start | bytes 884744 | tf_op jit(solution)/shard_map/ppermute | solution.py:112
  12.1 42.1 %collective-permute-start.3 = (bf16[192,768]{1,0:T(8,128)(2,1)S(1)}, bf16[192,768]{1,0:T(8,128)(2,1)S(1)}, u32[]{:S(2)}, u32[]{:S(2)}) collective-permute-start(bf16[192,768]{1,0:T(8,128)(2,1)S(1)} %get-tuple-element.138), channel_id=1, source_target_pairs={{0,4},{8,0},{16,8},{24,16},{28,24},{20,28},{12,20},{4,12},{1,5},{9... | collective-permute-start | bytes 884744 | tf_op jit(solution)/shard_map/ppermute | solution.py:114
  12.1 25.5 %collective-permute-start = (bf16[3,16,1536]{2,1,0:T(8,128)(2,1)S(1)}, bf16[3,16,1536]{2,1,0:T(8,128)(2,1)S(1)}, u32[]{:S(2)}, u32[]{:S(2)}) collective-permute-start(bf16[3,16,1536]{2,1,0:T(8,128)(2,1)S(1)} %bitcast.65), channel_id=1, source_target_pairs={{0,1},{1,2},{2,3},{4,5},{5,6},{6,7},{8,9},{9,10},{10,11},{12,13},{... | collective-permute-start | bytes 442376 | tf_op jit(solution)/shard_map/ppermute | solution.py:16
  13.5 24.1 %collective-permute-start.1 = (bf16[3,16,1536]{2,1,0:T(8,128)(2,1)S(1)}, bf16[3,16,1536]{2,1,0:T(8,128)(2,1)S(1)}, u32[]{:S(2)}, u32[]{:S(2)}) collective-permute-start(bf16[3,16,1536]{2,1,0:T(8,128)(2,1)S(1)} %bitcast.66), channel_id=1, source_target_pairs={{1,0},{2,1},{3,2},{5,4},{6,5},{7,6},{9,8},{10,9},{11,10},{13,12},{... | collective-permute-start | bytes 442376 | tf_op jit(solution)/shard_map/ppermute | solution.py:19
  14.9 196.3 %reduce-scatter.2.cloned.1.call-start = ((), (), s32[]{:S(2)}) async-start(), calls=%async_computation.2 | async-start | bytes 5308416 | tf_op jit(solution)/shard_map/reduce_scatter | solution.py:277
  17.4 20.5 %copy-start.56 = (f32[1536]{0:T(1024)S(1)}, f32[1536]{0:T(1024)}, u32[]{:S(2)}) copy-start(f32[1536]{0:T(1024)} %param.14) | copy-start | bytes 18436
  20.5 20.9 %copy-start.5 = (f32[1536]{0:T(1024)}, f32[1536]{0:T(1024)S(1)}, u32[]{:S(2)}) copy-start(f32[1536]{0:T(1024)S(1)} %get-tuple-element.70) | copy-start | bytes 18436
  52.6 15.3 %collective-permute-start.4 = (bf16[192,768]{1,0:T(8,128)(2,1)S(1)}, bf16[192,768]{1,0:T(8,128)(2,1)S(1)}, u32[]{:S(2)}, u32[]{:S(2)}) collective-permute-start(bf16[192,768]{1,0:T(8,128)(2,1)S(1)} %collective-permute-done.2), channel_id=1, source_target_pairs={{0,8},{8,16},{16,24},{24,28},{28,20},{20,12},{12,4},{4,0},{1,9},{9... | collective-permute-start | bytes 884744 | tf_op jit(solution)/shard_map/ppermute | solution.py:112
  54.2 20.1 %collective-permute-start.5 = (bf16[192,768]{1,0:T(8,128)(2,1)S(1)}, bf16[192,768]{1,0:T(8,128)(2,1)S(1)}, u32[]{:S(2)}, u32[]{:S(2)}) collective-permute-start(bf16[192,768]{1,0:T(8,128)(2,1)S(1)} %collective-permute-done.3), channel_id=1, source_target_pairs={{0,4},{8,0},{16,8},{24,16},{28,24},{20,28},{12,20},{4,12},{1,5},{9... | collective-permute-start | bytes 884744 | tf_op jit(solution)/shard_map/ppermute | solution.py:114
  67.9 15.0 %collective-permute-start.6 = (bf16[192,768]{1,0:T(8,128)(2,1)S(1)}, bf16[192,768]{1,0:T(8,128)(2,1)S(1)}, u32[]{:S(2)}, u32[]{:S(2)}) collective-permute-start(bf16[192,768]{1,0:T(8,128)(2,1)S(1)} %collective-permute-done.4), channel_id=1, source_target_pairs={{0,8},{8,16},{16,24},{24,28},{28,20},{20,12},{12,4},{4,0},{1,9},{9... | collective-permute-start | bytes 884744 | tf_op jit(solution)/shard_map/ppermute | solution.py:112
  74.3 9.6 %collective-permute-start.7 = (bf16[192,768]{1,0:T(8,128)(2,1)S(1)}, bf16[192,768]{1,0:T(8,128)(2,1)S(1)}, u32[]{:S(2)}, u32[]{:S(2)}) collective-permute-start(bf16[192,768]{1,0:T(8,128)(2,1)S(1)} %collective-permute-done.5), channel_id=1, source_target_pairs={{0,4},{8,0},{16,8},{24,16},{28,24},{20,28},{12,20},{4,12},{1,5},{9... | collective-permute-start | bytes 884744 | tf_op jit(solution)/shard_map/ppermute | solution.py:114
  83.0 8.5 %collective-permute-start.8 = (bf16[192,768]{1,0:T(8,128)(2,1)S(1)}, bf16[192,768]{1,0:T(8,128)(2,1)S(1)}, u32[]{:S(2)}, u32[]{:S(2)}) collective-permute-start(bf16[192,768]{1,0:T(8,128)(2,1)S(1)} %collective-permute-done.6), channel_id=1, source_target_pairs={{0,8},{8,16},{16,24},{24,28},{28,20},{20,12},{12,4},{4,0},{1,9},{9... | collective-permute-start | bytes 884744 | tf_op jit(solution)/shard_map/ppermute | solution.py:112
  92.2 15.8 %copy-start.55 = (f32[1536]{0:T(1024)S(1)}, f32[1536]{0:T(1024)}, u32[]{:S(2)}) copy-start(f32[1536]{0:T(1024)} %param.20) | copy-start | bytes 18436
  119.0 1.6 collective-permute-start.9
  120.8 9.1 %collective-permute-start.10 = (f32[1,3,16,1536]{3,2,1,0:T(8,128)S(1)}, f32[1,3,16,1536]{3,2,1,0:T(8,128)S(1)}, u32[]{:S(2)}, u32[]{:S(2)}) collective-permute-start(f32[1,3,16,1536]{3,2,1,0:T(8,128)S(1)} %constant_dynamic-slice_fusion), channel_id=1, source_target_pairs={{0,2},{1,3},{2,0},{3,1},{4,6},{5,7},{6,4},{7,5},{8,10},{9,11},{10,... | collective-permute-start | bytes 884744 | tf_op jit(solution)/shard_map/ppermute | solution.py:69
  134.7 1.4 collective-permute-start.13
  136.7 4.5 %collective-permute-start.14 = (f32[18816]{0:T(1024)S(1)}, f32[18816]{0:T(1024)S(1)}, u32[]{:S(2)}, u32[]{:S(2)}) collective-permute-start(f32[18816]{0:T(1024)S(1)} %get-tuple-element.109), channel_id=1, source_target_pairs={{0,2},{1,3},{2,0},{3,1},{4,6},{5,7},{6,4},{7,5},{8,10},{9,11},{10,... | collective-permute-start | bytes 225800 | tf_op jit(solution)/shard_map/ppermute | solution.py:49
  141.5 38.9 %copy-start.6 = (f32[1536]{0:T(1024)S(1)}, f32[1536]{0:T(1024)}, u32[]{:S(2)}) copy-start(f32[1536]{0:T(1024)} %copy-done.5) | copy-start | bytes 18436
  141.5 38.9 %copy-start.8 = (f32[1536]{0:T(1024)S(1)}, f32[1536]{0:T(1024)}, u32[]{:S(2)}) copy-start(f32[1536]{0:T(1024)} %copy-done.7) | copy-start | bytes 18436
  141.5 38.9 %copy-start.10 = (f32[1536]{0:T(1024)S(1)}, f32[1536]{0:T(1024)}, u32[]{:S(2)}) copy-start(f32[1536]{0:T(1024)} %copy-done.9) | copy-start | bytes 18436
  141.6 38.9 %copy-start.12 = (f32[1536]{0:T(1024)S(1)}, f32[1536]{0:T(1024)}, u32[]{:S(2)}) copy-start(f32[1536]{0:T(1024)} %copy-done.11) | copy-start | bytes 18436
  141.6 38.9 %copy-start.14 = (f32[1536]{0:T(1024)S(1)}, f32[1536]{0:T(1024)}, u32[]{:S(2)}) copy-start(f32[1536]{0:T(1024)} %copy-done.13) | copy-start | bytes 18436
  141.6 38.9 %copy-start.16 = (f32[1536]{0:T(1024)S(1)}, f32[1536]{0:T(1024)}, u32[]{:S(2)}) copy-start(f32[1536]{0:T(1024)} %copy-done.15) | copy-start | bytes 18436
  141.6 38.9 %copy-start.18 = (f32[1536]{0:T(1024)S(1)}, f32[1536]{0:T(1024)}, u32[]{:S(2)}) copy-start(f32[1536]{0:T(1024)} %copy-done.17) | copy-start | bytes 18436
  141.6 38.9 %copy-start.20 = (f32[1536]{0:T(1024)S(1)}, f32[1536]{0:T(1024)}, u32[]{:S(2)}) copy-start(f32[1536]{0:T(1024)} %copy-done.19) | copy-start | bytes 18436
  141.6 38.9 %copy-start.22 = (f32[1536]{0:T(1024)S(1)}, f32[1536]{0:T(1024)}, u32[]{:S(2)}) copy-start(f32[1536]{0:T(1024)} %copy-done.21) | copy-start | bytes 18436
  141.6 38.9 %copy-start.24 = (f32[1536]{0:T(1024)S(1)}, f32[1536]{0:T(1024)}, u32[]{:S(2)}) copy-start(f32[1536]{0:T(1024)} %copy-done.23) | copy-start | bytes 18436
  141.6 38.9 %copy-start.26 = (f32[1536]{0:T(1024)S(1)}, f32[1536]{0:T(1024)}, u32[]{:S(2)}) copy-start(f32[1536]{0:T(1024)} %copy-done.25) | copy-start | bytes 18436
  141.6 38.9 %copy-start.28 = (f32[1536]{0:T(1024)S(1)}, f32[1536]{0:T(1024)}, u32[]{:S(2)}) copy-start(f32[1536]{0:T(1024)} %copy-done.27) | copy-start | bytes 18436
  141.6 38.9 %copy-start.30 = (f32[1536]{0:T(1024)S(1)}, f32[1536]{0:T(1024)}, u32[]{:S(2)}) copy-start(f32[1536]{0:T(1024)} %copy-done.29) | copy-start | bytes 18436
  141.7 38.9 %copy-start.32 = (f32[1536]{0:T(1024)S(1)}, f32[1536]{0:T(1024)}, u32[]{:S(2)}) copy-start(f32[1536]{0:T(1024)} %copy-done.31) | copy-start | bytes 18436
  141.7 38.9 %copy-start.34 = (f32[1536]{0:T(1024)S(1)}, f32[1536]{0:T(1024)}, u32[]{:S(2)}) copy-start(f32[1536]{0:T(1024)} %copy-done.33) | copy-start | bytes 18436
  141.7 38.9 %copy-start.36 = (f32[1536]{0:T(1024)S(1)}, f32[1536]{0:T(1024)}, u32[]{:S(2)}) copy-start(f32[1536]{0:T(1024)} %copy-done.35) | copy-start | bytes 18436
  141.7 38.9 %copy-start.38 = (f32[1536]{0:T(1024)S(1)}, f32[1536]{0:T(1024)}, u32[]{:S(2)}) copy-start(f32[1536]{0:T(1024)} %copy-done.37) | copy-start | bytes 18436
  141.7 38.9 %copy-start.40 = (f32[1536]{0:T(1024)S(1)}, f32[1536]{0:T(1024)}, u32[]{:S(2)}) copy-start(f32[1536]{0:T(1024)} %copy-done.39) | copy-start | bytes 18436
  141.7 38.9 %copy-start.42 = (f32[1536]{0:T(1024)S(1)}, f32[1536]{0:T(1024)}, u32[]{:S(2)}) copy-start(f32[1536]{0:T(1024)} %copy-done.41) | copy-start | bytes 18436
  141.7 38.9 %copy-start.44 = (f32[1536]{0:T(1024)S(1)}, f32[1536]{0:T(1024)}, u32[]{:S(2)}) copy-start(f32[1536]{0:T(1024)} %copy-done.43) | copy-start | bytes 18436
  141.7 4.9 %collective-permute-start.15 = (f32[9408]{0:T(1024)S(1)}, f32[9408]{0:T(1024)S(1)}, u32[]{:S(2)}, u32[]{:S(2)}) collective-permute-start(f32[9408]{0:T(1024)S(1)} %get-tuple-element.118), channel_id=1, source_target_pairs={{0,4},{4,0},{8,12},{12,8},{16,20},{20,16},{24,28},{28,24},{1,5},{5... | collective-permute-start | bytes 112904 | tf_op jit(solution)/shard_map/ppermute | solution.py:49
  146.9 5.5 %collective-permute-start.16 = (f32[4704]{0:T(1024)S(1)}, f32[4704]{0:T(1024)S(1)}, u32[]{:S(2)}, u32[]{:S(2)}) collective-permute-start(f32[4704]{0:T(1024)S(1)} %get-tuple-element.120), channel_id=1, source_target_pairs={{0,8},{4,12},{8,0},{12,4},{16,24},{20,28},{24,16},{28,20},{1,9},{5... | collective-permute-start | bytes 56456 | tf_op jit(solution)/shard_map/ppermute | solution.py:49
  152.5 6.0 %collective-permute-start.17 = (f32[2352]{0:T(1024)S(1)}, f32[2352]{0:T(1024)S(1)}, u32[]{:S(2)}, u32[]{:S(2)}) collective-permute-start(f32[2352]{0:T(1024)S(1)} %get-tuple-element.122), channel_id=1, source_target_pairs={{0,16},{4,20},{8,24},{12,28},{16,0},{20,4},{24,8},{28,12},{1,17},{... | collective-permute-start | bytes 28232 | tf_op jit(solution)/shard_map/ppermute | solution.py:49
  158.5 4.9 %collective-permute-start.18 = (f32[2352]{0:T(1024)S(1)}, f32[2352]{0:T(1024)S(1)}, u32[]{:S(2)}, u32[]{:S(2)}) collective-permute-start(f32[2352]{0:T(1024)S(1)} %add.720), channel_id=1, source_target_pairs={{0,16},{4,20},{8,24},{12,28},{16,0},{20,4},{24,8},{28,12},{1,17},{... | collective-permute-start | bytes 28232 | tf_op jit(solution)/shard_map/ppermute | solution.py:52
  163.5 3.8 %collective-permute-start.19 = (f32[4704]{0:T(1024)S(1)}, f32[4704]{0:T(1024)S(1)}, u32[]{:S(2)}, u32[]{:S(2)}) collective-permute-start(f32[4704]{0:T(1024)S(1)} %maximum_select_fusion.4), channel_id=1, source_target_pairs={{0,8},{4,12},{8,0},{12,4},{16,24},{20,28},{24,16},{28,20},{1,9},{5... | collective-permute-start | bytes 56456 | tf_op jit(solution)/shard_map/ppermute | solution.py:52
  167.3 4.1 %collective-permute-start.20 = (f32[9408]{0:T(1024)S(1)}, f32[9408]{0:T(1024)S(1)}, u32[]{:S(2)}, u32[]{:S(2)}) collective-permute-start(f32[9408]{0:T(1024)S(1)} %maximum_select_fusion.3), channel_id=1, source_target_pairs={{0,4},{4,0},{8,12},{12,8},{16,20},{20,16},{24,28},{28,24},{1,5},{5... | collective-permute-start | bytes 112904 | tf_op jit(solution)/shard_map/ppermute | solution.py:52
  168.9 7.2 %collective-permute-start.11 = (bf16[3,16,1536]{2,1,0:T(8,128)(2,1)S(1)}, bf16[3,16,1536]{2,1,0:T(8,128)(2,1)S(1)}, u32[]{:S(2)}, u32[]{:S(2)}) collective-permute-start(bf16[3,16,1536]{2,1,0:T(8,128)(2,1)S(1)} %get-tuple-element.128), channel_id=1, source_target_pairs={{0,1},{1,2},{2,3},{4,5},{5,6},{6,7},{8,9},{9,10},{10,11},{12,13},{... | collective-permute-start | bytes 442376 | tf_op jit(solution)/shard_map/ppermute | solution.py:16
  170.2 5.9 %collective-permute-start.12 = (bf16[3,16,1536]{2,1,0:T(8,128)(2,1)S(1)}, bf16[3,16,1536]{2,1,0:T(8,128)(2,1)S(1)}, u32[]{:S(2)}, u32[]{:S(2)}) collective-permute-start(bf16[3,16,1536]{2,1,0:T(8,128)(2,1)S(1)} %get-tuple-element.128), channel_id=1, source_target_pairs={{1,0},{2,1},{3,2},{5,4},{6,5},{7,6},{9,8},{10,9},{11,10},{13,12},{... | collective-permute-start | bytes 442376 | tf_op jit(solution)/shard_map/ppermute | solution.py:19
  171.6 8.7 %collective-permute-start.21 = (f32[18816]{0:T(1024)S(1)}, f32[18816]{0:T(1024)S(1)}, u32[]{:S(2)}, u32[]{:S(2)}) collective-permute-start(f32[18816]{0:T(1024)S(1)} %maximum_select_fusion.2), channel_id=1, source_target_pairs={{0,2},{1,3},{2,0},{3,1},{4,6},{5,7},{6,4},{7,5},{8,10},{9,11},{10,... | collective-permute-start | bytes 225800 | tf_op jit(solution)/shard_map/ppermute | solution.py:52
  180.3 3.1 %collective-permute-start.22 = (f32[37632]{0:T(1024)S(1)}, f32[37632]{0:T(1024)S(1)}, u32[]{:S(2)}, u32[]{:S(2)}) collective-permute-start(f32[37632]{0:T(1024)S(1)} %maximum_select_fusion.1), channel_id=1, source_target_pairs={{0,1},{1,0},{2,3},{3,2},{4,5},{5,4},{6,7},{7,6},{8,9},{9,8},{10,11... | collective-permute-start | bytes 451592 | tf_op jit(solution)/shard_map/ppermute | solution.py:52
  (36 other events, 219.1 us)
Sparse Core Ops, SparseCore 0:
  15.0 64.6 all-gather.1
  114.9 96.1 reduce-scatter.1

commit v6 on v5

--- a/solution.py
+++ b/solution.py
@@ -154,6 +154,21 @@
     return total
 
 
+def tree_all_gather(block, axis):
+    size = lax.axis_size(axis)
+    assert size & (size - 1) == 0
+    me = lax.axis_index(axis)
+    data = block[None]
+    mask = 1
+    while mask < size:
+        bit = (me // mask) % 2
+        perm = [(j, j ^ mask) for j in range(size)]
+        other = lax.ppermute(data, axis, perm)
+        data = jnp.where(bit == 0, jnp.concatenate([data, other]), jnp.concatenate([other, data]))
+        mask *= 2
+    return data.reshape((size * block.shape[0],) + block.shape[1:])
+
+
 def conv_rows(framed, kern, kbias):
     rows = framed.shape[0] - 6
     cols = framed.shape[1]
@@ -241,20 +256,14 @@
 ):
     slab = frames[0]
     chans = slab.shape[2]
-    split = up_weight.shape[1] // 2
-    columns = jnp.concatenate(
-        [
-            lax.all_gather(up_weight[:, :split], "fsdp", axis=0, tiled=True),
-            ring_all_gather(up_weight[:, split:], "fsdp", ring),
-        ],
-        axis=1,
-    )
     padded = extended(slab, (("rows", 0),), 3)
+    own_block, padded = lax.optimization_barrier((up_weight, padded))
+    columns = ring_all_gather(own_block, "fsdp", ring)
     activation_rows = conv_rows(padded, kernel, kernel_bias)
     normed_output, standardized_input, inverse_deviation = apply_layer_norm(
         activation_rows, layer_norm_weight, layer_norm_bias
     )
-    whole = lax.all_gather(normed_output, "rows", axis=0, tiled=True)
+    whole = tree_all_gather(normed_output, "rows")
     height = whole.shape[0]
     cols = whole.shape[1]
     flat = whole.reshape(-1, chans)

time: 221 us -> 229 us (1.036)
  waiting for transfers between devices: 94.9 us -> 110 us
  starting transfers between devices: 26.5 us -> 36.2 us
  blocking collectives: 17.2 us -> 7.97 us
  local copies, waits for them, and re-layouts: 15.8 us -> 11.1 us
  matrix products: 15 us -> 12.2 us
    ppermute x4, waiting for transfers between devices: 24.4 us -> 38.9 us  [ring_all_gather(): cw = lax.ppermute(cw, axis, forward)]
    all_gather x1 -> x0, blocking collectives: 10.8 us -> none  [body(): whole = lax.all_gather(normed_output, 'rows', axis=0, tiled=True)]
    ppermute x0 -> x2, waiting for transfers between devices: none -> 6.64 us  [tree_all_gather(): other = lax.ppermute(data, axis, perm)]
    ppermute x0 -> x2, starting transfers between devices: none -> 5.01 us  [tree_all_gather(): other = lax.ppermute(data, axis, perm)]
    slice x3, local copies, waits for them, and re-layouts: 0.82 us -> 5 us  [conv_rows(): kern[i, j]]
    ppermute x3, waiting for transfers between devices: 4.15 us -> 0.01 us  [ring_all_gather(): ccw = lax.ppermute(ccw, axis, backward)]
    ppermute x5, waiting for transfers between devices: 18 us -> 14.3 us  [tree_allreduce(): flat = keep + lax.ppermute(give, axis, perm)]
    dynamic_update_slice x4, local copies, waits for them, and re-layouts: 2.99 us -> 0.17 us  [ring_all_gather(): lax.dynamic_update_index_in_dim(gathered, cw, ring_arr[(spot - s) % count...]
  transfers between devices with their start and end apart: 25 -> 26, of which waited for: 15 -> 16; matrix products, arithmetic and copies ran while one was open for 13% -> 9% of each run, Pallas kernels for 0% -> 0%
where the time goes in v6:
time: 229 us
  waiting for transfers between devices  110 us (48%)
  starting transfers between devices  36.2 us (16%)
  between operations  34.3 us (15%)
  other arithmetic  16.7 us (7%)
  matrix products  12.2 us (5%)
  local copies, waits for them, and re-layouts  11.1 us (5%)
  blocking collectives  7.97 us (3%)
    ppermute x4, waiting for transfers between devices, ring_all_gather(): cw = lax.ppermute(cw, axis, forward)  38.9 us
    reduce_scatter x1, waiting for transfers between devices, body(): lax.psum_scatter(w_term.astype(jnp.bfloat16), 'fsdp', scatter_dimension=0...  29.3 us
    ppermute x5, waiting for transfers between devices, tree_allreduce(): flat = keep + lax.ppermute(give, axis, perm)  14.3 us
    ppermute x5, waiting for transfers between devices, tree_allreduce(): other = lax.ppermute(flat, axis, perm)  12.3 us
    ppermute x2, waiting for transfers between devices, tree_reduce_scatter(): lax.ppermute(give, axis, perm).astype(jnp.float32)  8.53 us
    psum x1, blocking collectives, body(): norm_total = lax.psum(jnp.sum(norms), 'rows')  7.97 us
    ppermute x5, starting transfers between devices, tree_allreduce(): other = lax.ppermute(flat, axis, perm)  7.43 us
    ppermute x5, starting transfers between devices, tree_allreduce(): flat = keep + lax.ppermute(give, axis, perm)  7.11 us
  transfers between devices with their start and end apart: 26, of which 16 were waited for; matrix products, arithmetic and copies ran while one was open for 9% of the time, Pallas kernels for 0%

profile of v6, /device:TPU:0, one launch (start us, length us, event | category | flops | bytes accessed | tf_op | source)
XLA Modules:
  0.0 228.6 jit_solution(5478035637281769312)
XLA Ops:
  7.2 2.4 %collective-permute-start = (bf16[3,16,1536]{2,1,0:T(8,128)(2,1)}, bf16[3,16,1536]{2,1,0:T(8,128)(2,1)S(1)}, u32[]{:S(2)}, u32[]{:S(2)}) collective-permute-start(bf16[3,16,1536]{2,1,0:T(8,128)(2,1)} %bitcast.70), channel_id=1, source_target_pairs={{0,1},{1,2},{2,3},{4,5},{5,6},{6,7},{8,9},{9,10},{10,11},{12,13},{... | collective-permute-start | bytes 442376 | tf_op jit(solution)/shard_map/ppermute | solution.py:16
  9.6 1.3 collective-permute-start.1
  10.9 1.8 slice_reduce_fusion.48
  12.7 1.3 slice_reduce_fusion.46
  14.1 1.8 slice_reduce_fusion.47
  15.9 1.0 pad_maximum_fusion
  17.0 3.5 %fusion.156 = (f32[3,16]{1,0:T(4,128)S(1)}, f32[3,16,1536]{2,1,0:T(8,128)S(1)}) fusion(f32[1536]{0:T(1024)S(1)} %get-tuple-element.106, f32[1536]{0:T(1024)S(1)} %get-tuple-element.107, f32[1536]{0:T(1024)S(1)} %get-tuple-element.60, f32[1536]{0:T(1024)S(1)} %get-tuple-element.61, bf16[9,16,1536]{2,1,0:T(8,128)(2,1)S(1)} %pad_maximum_fusion, ...), kind=kLoop, calls=%fused_computation.412 | loop fusion | flops 10911696 | bytes 2179264 | tf_op jit(solution)/shard_map/reduce_sum | solution.py:212
  20.8 3.3 %collective-permute-start.2 = (bf16[1,3,16,1536]{3,2,1,0:T(8,128)(2,1)S(1)}, bf16[1,3,16,1536]{3,2,1,0:T(8,128)(2,1)S(1)}, u32[]{:S(2)}, u32[]{:S(2)}) collective-permute-start(bf16[1,3,16,1536]{3,2,1,0:T(8,128)(2,1)S(1)} %fusion.147), channel_id=1, source_target_pairs={{0,1},{1,0},{2,3},{3,2},{4,5},{5,4},{6,7},{7,6},{8,9},{9,8},{10,11... | collective-permute-start | bytes 442376 | tf_op jit(solution)/shard_map/ppermute | solution.py:166
  43.5 1.6 collective-permute-start.4
  45.6 1.7 collective-permute-start.3
  47.8 6.6 %collective-permute-done.3 = bf16[2,3,16,1536]{3,2,1,0:T(8,128)(2,1)S(1)} collective-permute-done((bf16[2,3,16,1536]{3,2,1,0:T(8,128)(2,1)S(1)}, bf16[2,3,16,1536]{3,2,1,0:T(8,128)(2,1)S(1)}, u32[]{:S(2)}, u32[]{:S(2)}) %collective-permute-start.3) | collective-permute-done | bytes 294944 | tf_op jit(solution)/shard_map/ppermute | solution.py:166
  54.5 4.3 %collective-permute-done.4 = bf16[192,1536]{1,0:T(8,128)(2,1)S(1)} collective-permute-done((bf16[192,1536]{1,0:T(8,128)(2,1)S(1)}, bf16[192,1536]{1,0:T(8,128)(2,1)S(1)}, u32[]{:S(2)}, u32[]{:S(2)}) %collective-permute-start.4) | collective-permute-done | bytes 589856 | tf_op jit(solution)/shard_map/ppermute | solution.py:112
  58.8 1.6 collective-permute-start.6
  61.0 12.3 %collective-permute-done.6 = bf16[192,1536]{1,0:T(8,128)(2,1)S(1)} collective-permute-done((bf16[192,1536]{1,0:T(8,128)(2,1)S(1)}, bf16[192,1536]{1,0:T(8,128)(2,1)S(1)}, u32[]{:S(2)}, u32[]{:S(2)}) %collective-permute-start.6) | collective-permute-done | bytes 589856 | tf_op jit(solution)/shard_map/ppermute | solution.py:112
  73.3 1.6 collective-permute-start.8
  75.4 11.4 %collective-permute-done.8 = bf16[192,1536]{1,0:T(8,128)(2,1)S(1)} collective-permute-done((bf16[192,1536]{1,0:T(8,128)(2,1)S(1)}, bf16[192,1536]{1,0:T(8,128)(2,1)S(1)}, u32[]{:S(2)}, u32[]{:S(2)}) %collective-permute-start.8) | collective-permute-done | bytes 589856 | tf_op jit(solution)/shard_map/ppermute | solution.py:112
  86.7 1.6 collective-permute-start.10
  88.5 10.9 %collective-permute-done.10 = bf16[192,1536]{1,0:T(8,128)(2,1)S(1)} collective-permute-done((bf16[192,1536]{1,0:T(8,128)(2,1)S(1)}, bf16[192,1536]{1,0:T(8,128)(2,1)S(1)}, u32[]{:S(2)}, u32[]{:S(2)}) %collective-permute-start.10) | collective-permute-done | bytes 589856 | tf_op jit(solution)/shard_map/ppermute | solution.py:112
  99.5 4.6 %fusion.4 = (f32[1536]{0:T(1024)S(1)}, f32[1536]{0:T(1024)S(1)}, f32[192,1536]{1,0:T(8,128)S(1)}, f32[192,1536]{1,0:T(8,128)}) fusion(bf16[1,12,16,1536]{3,2,1,0:T(8,128)(2,1)S(1)} %copy-done.2, f32[1536]{0:T(1024)S(1)} %copy-done.9, bf16[192,1536]{1,0:T(8,128)(2,1)S(1)} %bitcast.64, bf16[1536,1536]{1,0:T(8,128)(2,1)S(1)} %bitcast.62), kind=kOutput, calls=%fused_computation.105 | convolution fusion | flops 926610432 | bytes 8275968 | tf_op jit(solution)/shard_map/dot_general | solution.py:270
  104.7 8.0 %all-reduce.2 = (f32[]{:T(128)}, f32[]{:T(128)}) all-reduce(f32[]{:T(128)} %get-tuple-element.121, f32[]{:T(128)} %get-tuple-element.120), channel_id=1, replica_groups=mesh['fsdp'=8,'rows'=4] {'rows'}, use_global_device_ids=true, to_apply=%region_4.5 | all-reduce | flops 2 | bytes 16 | tf_op jit(solution)/shard_map/psum | solution.py:275
  114.1 3.0 %fusion.3 = (bf16[192,1536]{1,0:T(8,128)(2,1)S(1)}, bf16[192,1536]{1,0:T(8,128)(2,1)}) fusion(f32[192,1536]{1,0:T(8,128)} %get-tuple-element.141, f32[192,1536]{1,0:T(8,128)S(1)} %get-tuple-element.128, bf16[1,12,16,1536]{3,2,1,0:T(8,128)(2,1)} %param.21, f32[1536]{0:T(1024)S(1)} %get-tuple-element.133, f32[1536]{0:T(1024)S(1)} %get-tuple-element.126, ...), kind=kLoop, calls=%fused_computation.104 | loop fusion | flops 5603328 | bytes 4159488 | tf_op jit(solution)/shard_map/convert_element_type | solution.py:282
  117.1 3.6 %convolution_convert_fusion = bf16[1536,1536]{1,0:T(8,128)(2,1)} fusion(bf16[192,1536]{1,0:T(8,128)(2,1)S(1)} %bitcast.65, bf16[192,1536]{1,0:T(8,128)(2,1)S(1)} %get-tuple-element.131), kind=kOutput, calls=%fused_computation | convolution fusion | flops 908328960 | bytes 5898240 | tf_op jit(solution)/shard_map/dot_general | solution.py:283
  120.7 4.0 %convolution_convert_fusion.1 = bf16[12,16,1536]{2,1,0:T(8,128)(2,1)S(1)} fusion(bf16[12,16,1536]{2,1,0:T(8,128)(2,1)S(1)} %bitcast.66, bf16[1536,1536,1]{1,0,2:T(8,128)(2,1)} %bitcast.63), kind=kOutput, calls=%fused_computation.52 | convolution fusion | flops 906264576 | bytes 5898240 | tf_op jit(solution)/shard_map/hwf,cf->hwc/dot_general | solution.py:290
  125.2 1.2 collective-permute-done.11
  126.5 2.3 collective-permute-start.12
  128.8 7.3 %collective-permute-done.12 = f32[1,3,16,1536]{3,2,1,0:T(8,128)S(1)} collective-permute-done((f32[1,3,16,1536]{3,2,1,0:T(8,128)S(1)}, f32[1,3,16,1536]{3,2,1,0:T(8,128)S(1)}, u32[]{:S(2)}, u32[]{:S(2)}) %collective-permute-start.12) | collective-permute-done | bytes 294944 | tf_op jit(solution)/shard_map/ppermute | solution.py:69
  136.3 0.9 fusion.144
  140.1 0.9 dynamic-slice_reduce_fusion
  141.0 1.4 collective-permute-done.15
  143.0 1.8 collective-permute-start.16
  144.8 2.7 %collective-permute-done.16 = f32[18816]{0:T(1024)S(1)} collective-permute-done((f32[18816]{0:T(1024)S(1)}, f32[18816]{0:T(1024)S(1)}, u32[]{:S(2)}, u32[]{:S(2)}) %collective-permute-start.16) | collective-permute-done | bytes 75296 | tf_op jit(solution)/shard_map/ppermute | solution.py:49
  147.8 1.6 collective-permute-start.17
  149.4 3.0 %collective-permute-done.17 = f32[9408]{0:T(1024)S(1)} collective-permute-done((f32[9408]{0:T(1024)S(1)}, f32[9408]{0:T(1024)S(1)}, u32[]{:S(2)}, u32[]{:S(2)}) %collective-permute-start.17) | collective-permute-done | bytes 37664 | tf_op jit(solution)/shard_map/ppermute | solution.py:49
  152.6 1.7 collective-permute-start.18
  154.3 3.4 %collective-permute-done.18 = f32[4704]{0:T(1024)S(1)} collective-permute-done((f32[4704]{0:T(1024)S(1)}, f32[4704]{0:T(1024)S(1)}, u32[]{:S(2)}, u32[]{:S(2)}) %collective-permute-start.18) | collective-permute-done | bytes 18848 | tf_op jit(solution)/shard_map/ppermute | solution.py:49
  157.8 2.0 collective-permute-start.19
  159.8 3.9 %collective-permute-done.19 = f32[2352]{0:T(1024)S(1)} collective-permute-done((f32[2352]{0:T(1024)S(1)}, f32[2352]{0:T(1024)S(1)}, u32[]{:S(2)}, u32[]{:S(2)}) %collective-permute-start.19) | collective-permute-done | bytes 9440 | tf_op jit(solution)/shard_map/ppermute | solution.py:49
  163.7 1.1 collective-permute-start.20
  164.8 4.5 %collective-permute-done.20 = f32[2352]{0:T(1024)S(1)} collective-permute-done((f32[2352]{0:T(1024)S(1)}, f32[2352]{0:T(1024)S(1)}, u32[]{:S(2)}, u32[]{:S(2)}) %collective-permute-start.20) | collective-permute-done | bytes 9440 | tf_op jit(solution)/shard_map/ppermute | solution.py:52
  169.5 3.8 %collective-permute-done.21 = f32[4704]{0:T(1024)S(1)} collective-permute-done((f32[4704]{0:T(1024)S(1)}, f32[4704]{0:T(1024)S(1)}, u32[]{:S(2)}, u32[]{:S(2)}) %collective-permute-start.21) | collective-permute-done | bytes 18848 | tf_op jit(solution)/shard_map/ppermute | solution.py:52
  173.3 1.7 collective-permute-start.22
  175.0 1.3 collective-permute-start.13
  176.3 1.3 collective-permute-start.14
  177.7 4.5 %collective-permute-start.23 = (f32[18816]{0:T(1024)S(1)}, f32[18816]{0:T(1024)S(1)}, u32[]{:S(2)}, u32[]{:S(2)}) collective-permute-start(f32[18816]{0:T(1024)S(1)} %maximum_select_fusion.4), channel_id=1, source_target_pairs={{0,2},{1,3},{2,0},{3,1},{4,6},{5,7},{6,4},{7,5},{8,10},{9,11},{10,... | collective-permute-start | bytes 225800 | tf_op jit(solution)/shard_map/ppermute | solution.py:52
  182.5 4.0 %collective-permute-done.23 = f32[18816]{0:T(1024)S(1)} collective-permute-done((f32[18816]{0:T(1024)S(1)}, f32[18816]{0:T(1024)S(1)}, u32[]{:S(2)}, u32[]{:S(2)}) %collective-permute-start.23) | collective-permute-done | bytes 75296 | tf_op jit(solution)/shard_map/ppermute | solution.py:52
  186.6 2.8 %fusion.150 = bf16[1,3,16,1536]{3,2,1,0:T(8,128)(2,1)} fusion(f32[1536]{0:T(1024)S(1)} %get-tuple-element.106, bf16[9,22,1536]{2,1,0:T(8,128)(2,1)S(1)} %fusion.22, f32[1536]{0:T(1024)S(1)} %get-tuple-element.107, f32[1536]{0:T(1024)S(1)} %get-tuple-element.60, f32[1536]{0:T(1024)S(1)} %get-tuple-element.61, ...), kind=kLoop, calls=%fused_computation.339 | loop fusion | flops 11132928 | bytes 7084032 | tf_op jit(solution)/shard_map/reshape | solution.py:305
  190.2 29.3 %reduce-scatter.2.cloned.1.call-done = bf16[192,1536]{1,0:T(8,128)(2,1)} async-done(((bf16[1536,1536]{1,0:T(8,128)(2,1)}), bf16[192,1536]{1,0:T(8,128)(2,1)}) %reduce-scatter.2.cloned.1.call-update) | async-done | bytes 589840 | tf_op jit(solution)/shard_map/reduce_scatter | solution.py:286
  219.5 2.2 convert_element_type.497
  (138 shorter events, 10.5 us)
Async XLA Ops:
  7.2 9.7 %copy-start.6 = (f32[1536]{0:T(1024)S(1)}, f32[1536]{0:T(1024)}, u32[]{:S(2)}) copy-start(f32[1536]{0:T(1024)} %param.14) | copy-start | bytes 18436
  7.2 212.3 %reduce-scatter.2.cloned.1.call-start = ((), (), s32[]{:S(2)}) async-start(), calls=%async_computation.1 | async-start | bytes 5308416 | tf_op jit(solution)/shard_map/reduce_scatter | solution.py:286
  7.2 8.7 %collective-permute-start = (bf16[3,16,1536]{2,1,0:T(8,128)(2,1)}, bf16[3,16,1536]{2,1,0:T(8,128)(2,1)S(1)}, u32[]{:S(2)}, u32[]{:S(2)}) collective-permute-start(bf16[3,16,1536]{2,1,0:T(8,128)(2,1)} %bitcast.70), channel_id=1, source_target_pairs={{0,1},{1,2},{2,3},{4,5},{5,6},{6,7},{8,9},{9,10},{10,11},{12,13},{... | collective-permute-start | bytes 442376 | tf_op jit(solution)/shard_map/ppermute | solution.py:16
  9.6 6.3 %collective-permute-start.1 = (bf16[3,16,1536]{2,1,0:T(8,128)(2,1)}, bf16[3,16,1536]{2,1,0:T(8,128)(2,1)S(1)}, u32[]{:S(2)}, u32[]{:S(2)}) collective-permute-start(bf16[3,16,1536]{2,1,0:T(8,128)(2,1)} %bitcast.71), channel_id=1, source_target_pairs={{1,0},{2,1},{3,2},{5,4},{6,5},{7,6},{9,8},{10,9},{11,10},{13,12},{... | collective-permute-start | bytes 442376 | tf_op jit(solution)/shard_map/ppermute | solution.py:19
  16.9 3.8 %copy-start.4 = (f32[1536]{0:T(1024)S(1)}, f32[1536]{0:T(1024)}, u32[]{:S(2)}) copy-start(f32[1536]{0:T(1024)} %param.15) | copy-start | bytes 18436
  16.9 3.8 %copy-start.7 = (f32[1536]{0:T(1024)S(1)}, f32[1536]{0:T(1024)}, u32[]{:S(2)}) copy-start(f32[1536]{0:T(1024)} %param.16) | copy-start | bytes 18436
  16.9 7.2 %copy-start.10 = (s32[8]{0:T(128)S(1)}, s32[8]{0:T(128)}, u32[]{:S(2)}) copy-start(s32[8]{0:T(128)} %constant.305.clone) | copy-start | bytes 100
  16.9 12.4 %copy-start.5 = (s32[8]{0:T(128)S(1)}, s32[8]{0:T(128)}, u32[]{:S(2)}) copy-start(s32[8]{0:T(128)} %constant.304.clone) | copy-start | bytes 100
  16.9 26.6 %copy-start.1 = (bf16[192,1536]{1,0:T(8,128)(2,1)S(1)}, bf16[192,1536]{1,0:T(8,128)(2,1)}, u32[]{:S(2)}) copy-start(bf16[192,1536]{1,0:T(8,128)(2,1)} %param.17) | copy-start | bytes 1769476
  20.8 24.8 %collective-permute-start.2 = (bf16[1,3,16,1536]{3,2,1,0:T(8,128)(2,1)S(1)}, bf16[1,3,16,1536]{3,2,1,0:T(8,128)(2,1)S(1)}, u32[]{:S(2)}, u32[]{:S(2)}) collective-permute-start(bf16[1,3,16,1536]{3,2,1,0:T(8,128)(2,1)S(1)} %fusion.147), channel_id=1, source_target_pairs={{0,1},{1,0},{2,3},{3,2},{4,5},{5,4},{6,7},{7,6},{8,9},{9,8},{10,11... | collective-permute-start | bytes 442376 | tf_op jit(solution)/shard_map/ppermute | solution.py:166
  43.5 15.3 %collective-permute-start.4 = (bf16[192,1536]{1,0:T(8,128)(2,1)S(1)}, bf16[192,1536]{1,0:T(8,128)(2,1)S(1)}, u32[]{:S(2)}, u32[]{:S(2)}) collective-permute-start(bf16[192,1536]{1,0:T(8,128)(2,1)S(1)} %copy-done.1), channel_id=1, source_target_pairs={{0,8},{8,16},{16,24},{24,28},{28,20},{20,12},{12,4},{4,0},{1,9},{9... | collective-permute-start | bytes 1769480 | tf_op jit(solution)/shard_map/ppermute | solution.py:112
  45.1 15.3 %collective-permute-start.5 = (bf16[192,1536]{1,0:T(8,128)(2,1)S(1)}, bf16[192,1536]{1,0:T(8,128)(2,1)S(1)}, u32[]{:S(2)}, u32[]{:S(2)}) collective-permute-start(bf16[192,1536]{1,0:T(8,128)(2,1)S(1)} %copy-done.1), channel_id=1, source_target_pairs={{0,4},{8,0},{16,8},{24,16},{28,24},{20,28},{12,20},{4,12},{1,5},{9... | collective-permute-start | bytes 1769480 | tf_op jit(solution)/shard_map/ppermute | solution.py:114
  45.6 8.8 %collective-permute-start.3 = (bf16[2,3,16,1536]{3,2,1,0:T(8,128)(2,1)S(1)}, bf16[2,3,16,1536]{3,2,1,0:T(8,128)(2,1)S(1)}, u32[]{:S(2)}, u32[]{:S(2)}) collective-permute-start(bf16[2,3,16,1536]{3,2,1,0:T(8,128)(2,1)S(1)} %maximum_select_fusion.2), channel_id=1, source_target_pairs={{0,2},{1,3},{2,0},{3,1},{4,6},{5,7},{6,4},{7,5},{8,10},{9,11},{10,... | collective-permute-start | bytes 884744 | tf_op jit(solution)/shard_map/ppermute | solution.py:166
  58.8 14.4 %collective-permute-start.6 = (bf16[192,1536]{1,0:T(8,128)(2,1)S(1)}, bf16[192,1536]{1,0:T(8,128)(2,1)S(1)}, u32[]{:S(2)}, u32[]{:S(2)}) collective-permute-start(bf16[192,1536]{1,0:T(8,128)(2,1)S(1)} %collective-permute-done.4), channel_id=1, source_target_pairs={{0,8},{8,16},{16,24},{24,28},{28,20},{20,12},{12,4},{4,0},{1,9},{9... | collective-permute-start | bytes 1769480 | tf_op jit(solution)/shard_map/ppermute | solution.py:112
  60.4 14.4 %collective-permute-start.7 = (bf16[192,1536]{1,0:T(8,128)(2,1)S(1)}, bf16[192,1536]{1,0:T(8,128)(2,1)S(1)}, u32[]{:S(2)}, u32[]{:S(2)}) collective-permute-start(bf16[192,1536]{1,0:T(8,128)(2,1)S(1)} %collective-permute-done.5), channel_id=1, source_target_pairs={{0,4},{8,0},{16,8},{24,16},{28,24},{20,28},{12,20},{4,12},{1,5},{9... | collective-permute-start | bytes 1769480 | tf_op jit(solution)/shard_map/ppermute | solution.py:114
  73.3 13.5 %collective-permute-start.8 = (bf16[192,1536]{1,0:T(8,128)(2,1)S(1)}, bf16[192,1536]{1,0:T(8,128)(2,1)S(1)}, u32[]{:S(2)}, u32[]{:S(2)}) collective-permute-start(bf16[192,1536]{1,0:T(8,128)(2,1)S(1)} %collective-permute-done.6), channel_id=1, source_target_pairs={{0,8},{8,16},{16,24},{24,28},{28,20},{20,12},{12,4},{4,0},{1,9},{9... | collective-permute-start | bytes 1769480 | tf_op jit(solution)/shard_map/ppermute | solution.py:112
  74.8 13.6 %collective-permute-start.9 = (bf16[192,1536]{1,0:T(8,128)(2,1)S(1)}, bf16[192,1536]{1,0:T(8,128)(2,1)S(1)}, u32[]{:S(2)}, u32[]{:S(2)}) collective-permute-start(bf16[192,1536]{1,0:T(8,128)(2,1)S(1)} %collective-permute-done.7), channel_id=1, source_target_pairs={{0,4},{8,0},{16,8},{24,16},{28,24},{20,28},{12,20},{4,12},{1,5},{9... | collective-permute-start | bytes 1769480 | tf_op jit(solution)/shard_map/ppermute | solution.py:114
  86.7 12.6 %collective-permute-start.10 = (bf16[192,1536]{1,0:T(8,128)(2,1)S(1)}, bf16[192,1536]{1,0:T(8,128)(2,1)S(1)}, u32[]{:S(2)}, u32[]{:S(2)}) collective-permute-start(bf16[192,1536]{1,0:T(8,128)(2,1)S(1)} %collective-permute-done.8), channel_id=1, source_target_pairs={{0,8},{8,16},{16,24},{24,28},{28,20},{20,12},{12,4},{4,0},{1,9},{9... | collective-permute-start | bytes 1769480 | tf_op jit(solution)/shard_map/ppermute | solution.py:112
  88.4 11.1 %copy-start.2 = (bf16[1,12,16,1536]{3,2,1,0:T(8,128)(2,1)S(1)}, bf16[1,12,16,1536]{3,2,1,0:T(8,128)(2,1)}, u32[]{:S(2)}) copy-start(bf16[1,12,16,1536]{3,2,1,0:T(8,128)(2,1)} %param.21) | copy-start | bytes 1769476
  88.4 11.1 %copy-start.9 = (f32[1536]{0:T(1024)S(1)}, f32[1536]{0:T(1024)}, u32[]{:S(2)}) copy-start(f32[1536]{0:T(1024)} %param.18) | copy-start | bytes 18436
  99.4 4.7 %copy-start = (bf16[8,192,1536]{2,1,0:T(8,128)(2,1)}, bf16[8,192,1536]{2,1,0:T(8,128)(2,1)S(1)}, u32[]{:S(2)}) copy-start(bf16[8,192,1536]{2,1,0:T(8,128)(2,1)S(1)} %bitcast_dynamic-update-slice_fusion) | copy-start | bytes 14155780
  99.5 4.7 %copy-start.3 = (f32[1536]{0:T(1024)S(1)}, f32[1536]{0:T(1024)}, u32[]{:S(2)}) copy-start(f32[1536]{0:T(1024)} %param.19) | copy-start | bytes 18436
  99.5 14.6 %copy-start.8 = (f32[1536]{0:T(1024)S(1)}, f32[1536]{0:T(1024)}, u32[]{:S(2)}) copy-start(f32[1536]{0:T(1024)} %param.20) | copy-start | bytes 18436
  124.8 1.6 collective-permute-start.11
  126.5 9.6 %collective-permute-start.12 = (f32[1,3,16,1536]{3,2,1,0:T(8,128)S(1)}, f32[1,3,16,1536]{3,2,1,0:T(8,128)S(1)}, u32[]{:S(2)}, u32[]{:S(2)}) collective-permute-start(f32[1,3,16,1536]{3,2,1,0:T(8,128)S(1)} %constant_dynamic-slice_fusion), channel_id=1, source_target_pairs={{0,2},{1,3},{2,0},{3,1},{4,6},{5,7},{6,4},{7,5},{8,10},{9,11},{10,... | collective-permute-start | bytes 884744 | tf_op jit(solution)/shard_map/ppermute | solution.py:69
  141.0 1.4 collective-permute-start.15
  143.0 4.5 %collective-permute-start.16 = (f32[18816]{0:T(1024)S(1)}, f32[18816]{0:T(1024)S(1)}, u32[]{:S(2)}, u32[]{:S(2)}) collective-permute-start(f32[18816]{0:T(1024)S(1)} %get-tuple-element.112), channel_id=1, source_target_pairs={{0,2},{1,3},{2,0},{3,1},{4,6},{5,7},{6,4},{7,5},{8,10},{9,11},{10,... | collective-permute-start | bytes 225800 | tf_op jit(solution)/shard_map/ppermute | solution.py:49
  147.8 4.6 %collective-permute-start.17 = (f32[9408]{0:T(1024)S(1)}, f32[9408]{0:T(1024)S(1)}, u32[]{:S(2)}, u32[]{:S(2)}) collective-permute-start(f32[9408]{0:T(1024)S(1)} %get-tuple-element.114), channel_id=1, source_target_pairs={{0,4},{4,0},{8,12},{12,8},{16,20},{20,16},{24,28},{28,24},{1,5},{5... | collective-permute-start | bytes 112904 | tf_op jit(solution)/shard_map/ppermute | solution.py:49
  152.6 5.0 %collective-permute-start.18 = (f32[4704]{0:T(1024)S(1)}, f32[4704]{0:T(1024)S(1)}, u32[]{:S(2)}, u32[]{:S(2)}) collective-permute-start(f32[4704]{0:T(1024)S(1)} %get-tuple-element.116), channel_id=1, source_target_pairs={{0,8},{4,12},{8,0},{12,4},{16,24},{20,28},{24,16},{28,20},{1,9},{5... | collective-permute-start | bytes 56456 | tf_op jit(solution)/shard_map/ppermute | solution.py:49
  157.8 5.8 %collective-permute-start.19 = (f32[2352]{0:T(1024)S(1)}, f32[2352]{0:T(1024)S(1)}, u32[]{:S(2)}, u32[]{:S(2)}) collective-permute-start(f32[2352]{0:T(1024)S(1)} %get-tuple-element.118), channel_id=1, source_target_pairs={{0,16},{4,20},{8,24},{12,28},{16,0},{20,4},{24,8},{28,12},{1,17},{... | collective-permute-start | bytes 28232 | tf_op jit(solution)/shard_map/ppermute | solution.py:49
  163.7 5.7 %collective-permute-start.20 = (f32[2352]{0:T(1024)S(1)}, f32[2352]{0:T(1024)S(1)}, u32[]{:S(2)}, u32[]{:S(2)}) collective-permute-start(f32[2352]{0:T(1024)S(1)} %add.722), channel_id=1, source_target_pairs={{0,16},{4,20},{8,24},{12,28},{16,0},{20,4},{24,8},{28,12},{1,17},{... | collective-permute-start | bytes 28232 | tf_op jit(solution)/shard_map/ppermute | solution.py:52
  169.5 3.8 %collective-permute-start.21 = (f32[4704]{0:T(1024)S(1)}, f32[4704]{0:T(1024)S(1)}, u32[]{:S(2)}, u32[]{:S(2)}) collective-permute-start(f32[4704]{0:T(1024)S(1)} %maximum_select_fusion.6), channel_id=1, source_target_pairs={{0,8},{4,12},{8,0},{12,4},{16,24},{20,28},{24,16},{28,20},{1,9},{5... | collective-permute-start | bytes 56456 | tf_op jit(solution)/shard_map/ppermute | solution.py:52
  173.3 4.3 %collective-permute-start.22 = (f32[9408]{0:T(1024)S(1)}, f32[9408]{0:T(1024)S(1)}, u32[]{:S(2)}, u32[]{:S(2)}) collective-permute-start(f32[9408]{0:T(1024)S(1)} %maximum_select_fusion.5), channel_id=1, source_target_pairs={{0,4},{4,0},{8,12},{12,8},{16,20},{20,16},{24,28},{28,24},{1,5},{5... | collective-permute-start | bytes 112904 | tf_op jit(solution)/shard_map/ppermute | solution.py:52
  175.0 7.2 %collective-permute-start.13 = (bf16[3,16,1536]{2,1,0:T(8,128)(2,1)S(1)}, bf16[3,16,1536]{2,1,0:T(8,128)(2,1)S(1)}, u32[]{:S(2)}, u32[]{:S(2)}) collective-permute-start(bf16[3,16,1536]{2,1,0:T(8,128)(2,1)S(1)} %get-tuple-element.124), channel_id=1, source_target_pairs={{0,1},{1,2},{2,3},{4,5},{5,6},{6,7},{8,9},{9,10},{10,11},{12,13},{... | collective-permute-start | bytes 442376 | tf_op jit(solution)/shard_map/ppermute | solution.py:16
  176.3 5.9 %collective-permute-start.14 = (bf16[3,16,1536]{2,1,0:T(8,128)(2,1)S(1)}, bf16[3,16,1536]{2,1,0:T(8,128)(2,1)S(1)}, u32[]{:S(2)}, u32[]{:S(2)}) collective-permute-start(bf16[3,16,1536]{2,1,0:T(8,128)(2,1)S(1)} %get-tuple-element.124), channel_id=1, source_target_pairs={{1,0},{2,1},{3,2},{5,4},{6,5},{7,6},{9,8},{10,9},{11,10},{13,12},{... | collective-permute-start | bytes 442376 | tf_op jit(solution)/shard_map/ppermute | solution.py:19
  177.7 8.7 %collective-permute-start.23 = (f32[18816]{0:T(1024)S(1)}, f32[18816]{0:T(1024)S(1)}, u32[]{:S(2)}, u32[]{:S(2)}) collective-permute-start(f32[18816]{0:T(1024)S(1)} %maximum_select_fusion.4), channel_id=1, source_target_pairs={{0,2},{1,3},{2,0},{3,1},{4,6},{5,7},{6,4},{7,5},{8,10},{9,11},{10,... | collective-permute-start | bytes 225800 | tf_op jit(solution)/shard_map/ppermute | solution.py:52
  186.5 2.9 %collective-permute-start.24 = (f32[37632]{0:T(1024)S(1)}, f32[37632]{0:T(1024)S(1)}, u32[]{:S(2)}, u32[]{:S(2)}) collective-permute-start(f32[37632]{0:T(1024)S(1)} %maximum_select_fusion.3), channel_id=1, source_target_pairs={{0,1},{1,0},{2,3},{3,2},{4,5},{5,4},{6,7},{7,6},{8,9},{9,8},{10,11... | collective-permute-start | bytes 451592 | tf_op jit(solution)/shard_map/ppermute | solution.py:52
Sparse Core Ops, SparseCore 0:
  120.8 98.6 reduce-scatter.1

commit v7 on v6

--- a/solution.py
+++ b/solution.py
@@ -92,7 +92,7 @@
     return ring
 
 
-def ring_all_gather(block, axis, ring):
+def ring_all_gather(block, axis, ring, held=None):
     count = len(ring)
     place = [0] * count
     for k, j in enumerate(ring):
@@ -112,12 +112,14 @@
         cw = lax.ppermute(cw, axis, forward)
         if s <= behind:
             ccw = lax.ppermute(ccw, axis, backward)
+        if s == 1 and held is not None:
+            cw, ccw, held = lax.optimization_barrier((cw, ccw, held))
         gathered = lax.dynamic_update_index_in_dim(gathered, cw, ring_arr[(spot - s) % count], 0)
         if s <= behind:
             gathered = lax.dynamic_update_index_in_dim(
                 gathered, ccw, ring_arr[(spot + s) % count], 0
             )
-    return gathered.reshape((count * block.shape[0],) + block.shape[1:])
+    return gathered.reshape((count * block.shape[0],) + block.shape[1:]), held
 
 
 def ring_reduce_scatter(terms, axis, ring):
@@ -256,9 +258,8 @@
 ):
     slab = frames[0]
     chans = slab.shape[2]
+    columns, slab = ring_all_gather(up_weight, "fsdp", ring, slab)
     padded = extended(slab, (("rows", 0),), 3)
-    own_block, padded = lax.optimization_barrier((up_weight, padded))
-    columns = ring_all_gather(own_block, "fsdp", ring)
     activation_rows = conv_rows(padded, kernel, kernel_bias)
     normed_output, standardized_input, inverse_deviation = apply_layer_norm(
         activation_rows, layer_norm_weight, layer_norm_bias

time: 229 us -> 216 us (0.943)
  waiting for transfers between devices: 110 us -> 91.7 us
  local copies, waits for them, and re-layouts: 11.1 us -> 14.7 us
    ppermute x4, waiting for transfers between devices: 38.9 us -> 20.6 us  [ring_all_gather(): cw = lax.ppermute(cw, axis, forward)]
    ppermute x4, starting transfers between devices: 6.36 us -> 9.53 us  [ring_all_gather(): cw = lax.ppermute(cw, axis, forward)]
    unnamed x22 -> x109, local copies, waits for them, and re-layouts: 0.07 us -> 2.41 us
  transfers between devices with their start and end apart: 26 -> 26, of which waited for: 16 -> 19; matrix products, arithmetic and copies ran while one was open for 9% -> 13% of each run, Pallas kernels for 0% -> 0%
where the time goes in v7:
time: 216 us; the launch traced here: 215 us
  waiting for transfers between devices  91.7 us (42%)
  starting transfers between devices  36.7 us (17%)
  between operations  35 us (16%)
  other arithmetic  17.9 us (8%)
  local copies, waits for them, and re-layouts  14.7 us (7%)
  matrix products  12.4 us (6%)
  blocking collectives  6.61 us (3%)
    reduce_scatter x1, waiting for transfers between devices, body(): lax.psum_scatter(w_term.astype(jnp.bfloat16), 'fsdp', scatter_dimension=0...  27.9 us
    ppermute x4, waiting for transfers between devices, ring_all_gather(): cw = lax.ppermute(cw, axis, forward)  20.6 us
    ppermute x5, waiting for transfers between devices, tree_allreduce(): flat = keep + lax.ppermute(give, axis, perm)  14.9 us
    ppermute x5, waiting for transfers between devices, tree_allreduce(): other = lax.ppermute(flat, axis, perm)  10.4 us
    ppermute x4, starting transfers between devices, ring_all_gather(): cw = lax.ppermute(cw, axis, forward)  9.53 us
    ppermute x5, starting transfers between devices, tree_allreduce(): other = lax.ppermute(flat, axis, perm)  8.5 us
    ppermute x2, waiting for transfers between devices, tree_reduce_scatter(): lax.ppermute(give, axis, perm).astype(jnp.float32)  8.31 us
    ppermute x5, starting transfers between devices, tree_allreduce(): flat = keep + lax.ppermute(give, axis, perm)  7.21 us
  transfers between devices with their start and end apart: 26, of which 19 were waited for; matrix products, arithmetic and copies ran while one was open for 13% of the time, Pallas kernels for 0%

profile of v7, /device:TPU:0, one launch (start us, length us, event | category | flops | bytes accessed | tf_op | source)
XLA Modules:
  0.0 215.1 jit_solution(13949378422551636450)
XLA Ops:
  7.2 3.1 %collective-permute-start = (bf16[192,1536]{1,0:T(8,128)(2,1)}, bf16[192,1536]{1,0:T(8,128)(2,1)S(1)}, u32[]{:S(2)}, u32[]{:S(2)}) collective-permute-start(bf16[192,1536]{1,0:T(8,128)(2,1)} %param.17), channel_id=1, source_target_pairs={{0,8},{8,16},{16,24},{24,28},{28,20},{20,12},{12,4},{4,0},{1,9},{9... | collective-permute-start | bytes 1769480 | tf_op jit(solution)/shard_map/ppermute | solution.py:112
  10.3 1.2 dynamic_slice.69
  16.2 1.6 fusion.154
  26.8 1.8 slice_reduce_fusion.48
  28.5 1.6 slice_reduce_fusion.47
  34.8 1.3 slice_reduce_fusion.46
  38.1 1.5 collective-permute-start.2
  39.6 1.3 collective-permute-start.3
  40.9 1.9 collective-permute-start.6
  43.1 1.8 collective-permute-done.3
  45.3 3.4 %fusion.152 = (f32[3,16]{1,0:T(4,128)S(1)}, f32[3,16,1536]{2,1,0:T(8,128)S(1)}) fusion(f32[1536]{0:T(1024)S(1)} %get-tuple-element.105, bf16[9,22,1536]{2,1,0:T(8,128)(2,1)S(1)} %select_maximum_fusion.2, f32[1536]{0:T(1024)S(1)} %get-tuple-element.106, f32[1536]{0:T(1024)S(1)} %get-tuple-element.59, f32[1536]{0:T(1024)S(1)} %get-tuple-element.60, ...), kind=kLoop, calls=%fused_computation.373 | loop fusion | flops 10911696 | bytes 7827648 | tf_op jit(solution)/shard_map/reduce_sum | solution.py:214
  49.1 4.1 %collective-permute-start.4 = (bf16[1,3,16,1536]{3,2,1,0:T(8,128)(2,1)S(1)}, bf16[1,3,16,1536]{3,2,1,0:T(8,128)(2,1)S(1)}, u32[]{:S(2)}, u32[]{:S(2)}) collective-permute-start(bf16[1,3,16,1536]{3,2,1,0:T(8,128)(2,1)S(1)} %fusion.143), channel_id=1, source_target_pairs={{0,1},{1,0},{2,3},{3,2},{4,5},{5,4},{6,7},{7,6},{8,9},{9,8},{10,11... | collective-permute-start | bytes 442376 | tf_op jit(solution)/shard_map/ppermute | solution.py:168
  53.2 1.0 collective-permute-done.4
  54.9 2.1 collective-permute-start.8
  57.4 6.1 %collective-permute-done.5 = bf16[2,3,16,1536]{3,2,1,0:T(8,128)(2,1)S(1)} collective-permute-done((bf16[2,3,16,1536]{3,2,1,0:T(8,128)(2,1)S(1)}, bf16[2,3,16,1536]{3,2,1,0:T(8,128)(2,1)S(1)}, u32[]{:S(2)}, u32[]{:S(2)}) %collective-permute-start.5) | collective-permute-done | bytes 294944 | tf_op jit(solution)/shard_map/ppermute | solution.py:168
  63.6 6.2 %collective-permute-done.8 = bf16[192,1536]{1,0:T(8,128)(2,1)S(1)} collective-permute-done((bf16[192,1536]{1,0:T(8,128)(2,1)S(1)}, bf16[192,1536]{1,0:T(8,128)(2,1)S(1)}, u32[]{:S(2)}, u32[]{:S(2)}) %collective-permute-start.8) | collective-permute-done | bytes 589856 | tf_op jit(solution)/shard_map/ppermute | solution.py:112
  69.8 2.4 %collective-permute-start.10 = (bf16[192,1536]{1,0:T(8,128)(2,1)S(1)}, bf16[192,1536]{1,0:T(8,128)(2,1)S(1)}, u32[]{:S(2)}, u32[]{:S(2)}) collective-permute-start(bf16[192,1536]{1,0:T(8,128)(2,1)S(1)} %collective-permute-done.8), channel_id=1, source_target_pairs={{0,8},{8,16},{16,24},{24,28},{28,20},{20,12},{12,4},{4,0},{1,9},{9... | collective-permute-start | bytes 1769480 | tf_op jit(solution)/shard_map/ppermute | solution.py:112
  72.8 13.7 %collective-permute-done.10 = bf16[192,1536]{1,0:T(8,128)(2,1)S(1)} collective-permute-done((bf16[192,1536]{1,0:T(8,128)(2,1)S(1)}, bf16[192,1536]{1,0:T(8,128)(2,1)S(1)}, u32[]{:S(2)}, u32[]{:S(2)}) %collective-permute-start.10) | collective-permute-done | bytes 589856 | tf_op jit(solution)/shard_map/ppermute | solution.py:112
  86.6 4.8 %fusion.4 = (f32[1536]{0:T(1024)S(1)}, f32[1536]{0:T(1024)S(1)}, f32[192,1536]{1,0:T(8,128)}, f32[192,1536]{1,0:T(8,128)}) fusion(bf16[1,12,16,1536]{3,2,1,0:T(8,128)(2,1)S(1)} %copy-done.3, f32[1536]{0:T(1024)S(1)} %copy-done.53, bf16[192,1536]{1,0:T(8,128)(2,1)S(1)} %bitcast.64, bf16[1536,1536]{1,0:T(8,128)(2,1)S(1)} %bitcast.62), kind=kOutput, calls=%fused_computation.63 | convolution fusion | flops 926610432 | bytes 8275968 | tf_op jit(solution)/shard_map/dot_general | solution.py:271
  92.1 6.6 %all-reduce.2 = (f32[]{:T(128)}, f32[]{:T(128)}) all-reduce(f32[]{:T(128)} %get-tuple-element.127, f32[]{:T(128)} %get-tuple-element.126), channel_id=1, replica_groups=mesh['fsdp'=8,'rows'=4] {'rows'}, use_global_device_ids=true, to_apply=%region_4.5 | all-reduce | flops 2 | bytes 16 | tf_op jit(solution)/shard_map/psum | solution.py:276
  100.1 3.4 %fusion.3 = (bf16[192,1536]{1,0:T(8,128)(2,1)S(1)}, bf16[192,1536]{1,0:T(8,128)(2,1)}) fusion(f32[192,1536]{1,0:T(8,128)} %get-tuple-element.149, f32[192,1536]{1,0:T(8,128)} %get-tuple-element.134, bf16[1,12,16,1536]{3,2,1,0:T(8,128)(2,1)} %param.21, f32[1536]{0:T(1024)S(1)} %get-tuple-element.141, f32[1536]{0:T(1024)S(1)} %get-tuple-element.132, ...), kind=kLoop, calls=%fused_computation.62 | loop fusion | flops 5603328 | bytes 4159488 | tf_op jit(solution)/shard_map/convert_element_type | solution.py:283
  103.5 3.6 %convolution_convert_fusion = bf16[1536,1536]{1,0:T(8,128)(2,1)} fusion(bf16[192,1536]{1,0:T(8,128)(2,1)S(1)} %bitcast.65, bf16[192,1536]{1,0:T(8,128)(2,1)S(1)} %get-tuple-element.137), kind=kOutput, calls=%fused_computation | convolution fusion | flops 908328960 | bytes 5898240 | tf_op jit(solution)/shard_map/dot_general | solution.py:284
  107.1 4.0 %convolution_convert_fusion.1 = bf16[12,16,1536]{2,1,0:T(8,128)(2,1)S(1)} fusion(bf16[12,16,1536]{2,1,0:T(8,128)(2,1)S(1)} %bitcast.66, bf16[1536,1536,1]{1,0,2:T(8,128)(2,1)} %bitcast.63), kind=kOutput, calls=%fused_computation.52 | convolution fusion | flops 906264576 | bytes 5898240 | tf_op jit(solution)/shard_map/hwf,cf->hwc/dot_general | solution.py:291
  112.8 1.0 convert_add_fusion
  113.9 1.7 collective-permute-start.12
  115.6 7.4 %collective-permute-done.12 = f32[1,3,16,1536]{3,2,1,0:T(8,128)S(1)} collective-permute-done((f32[1,3,16,1536]{3,2,1,0:T(8,128)S(1)}, f32[1,3,16,1536]{3,2,1,0:T(8,128)S(1)}, u32[]{:S(2)}, u32[]{:S(2)}) %collective-permute-start.12) | collective-permute-done | bytes 294944 | tf_op jit(solution)/shard_map/ppermute | solution.py:69
  123.2 1.6 fusion.140
  128.7 1.4 collective-permute-done.15
  130.6 1.7 collective-permute-start.16
  132.3 2.8 %collective-permute-done.16 = f32[18816]{0:T(1024)S(1)} collective-permute-done((f32[18816]{0:T(1024)S(1)}, f32[18816]{0:T(1024)S(1)}, u32[]{:S(2)}, u32[]{:S(2)}) %collective-permute-start.16) | collective-permute-done | bytes 75296 | tf_op jit(solution)/shard_map/ppermute | solution.py:49
  135.6 1.9 collective-permute-start.17
  137.5 3.0 %collective-permute-done.17 = f32[9408]{0:T(1024)S(1)} collective-permute-done((f32[9408]{0:T(1024)S(1)}, f32[9408]{0:T(1024)S(1)}, u32[]{:S(2)}, u32[]{:S(2)}) %collective-permute-start.17) | collective-permute-done | bytes 37664 | tf_op jit(solution)/shard_map/ppermute | solution.py:49
  140.7 1.6 collective-permute-start.18
  142.4 3.7 %collective-permute-done.18 = f32[4704]{0:T(1024)S(1)} collective-permute-done((f32[4704]{0:T(1024)S(1)}, f32[4704]{0:T(1024)S(1)}, u32[]{:S(2)}, u32[]{:S(2)}) %collective-permute-start.18) | collective-permute-done | bytes 18848 | tf_op jit(solution)/shard_map/ppermute | solution.py:49
  146.2 1.9 collective-permute-start.19
  148.2 4.0 %collective-permute-done.19 = f32[2352]{0:T(1024)S(1)} collective-permute-done((f32[2352]{0:T(1024)S(1)}, f32[2352]{0:T(1024)S(1)}, u32[]{:S(2)}, u32[]{:S(2)}) %collective-permute-start.19) | collective-permute-done | bytes 9440 | tf_op jit(solution)/shard_map/ppermute | solution.py:49
  152.2 1.1 collective-permute-start.20
  153.2 4.0 %collective-permute-done.20 = f32[2352]{0:T(1024)S(1)} collective-permute-done((f32[2352]{0:T(1024)S(1)}, f32[2352]{0:T(1024)S(1)}, u32[]{:S(2)}, u32[]{:S(2)}) %collective-permute-start.20) | collective-permute-done | bytes 9440 | tf_op jit(solution)/shard_map/ppermute | solution.py:52
  157.3 1.3 collective-permute-start.21
  158.6 2.5 %collective-permute-done.21 = f32[4704]{0:T(1024)S(1)} collective-permute-done((f32[4704]{0:T(1024)S(1)}, f32[4704]{0:T(1024)S(1)}, u32[]{:S(2)}, u32[]{:S(2)}) %collective-permute-start.21) | collective-permute-done | bytes 18848 | tf_op jit(solution)/shard_map/ppermute | solution.py:52
  161.2 1.6 collective-permute-start.22
  162.7 1.3 collective-permute-start.13
  164.0 1.3 collective-permute-start.14
  165.4 4.5 %collective-permute-start.23 = (f32[18816]{0:T(1024)S(1)}, f32[18816]{0:T(1024)S(1)}, u32[]{:S(2)}, u32[]{:S(2)}) collective-permute-start(f32[18816]{0:T(1024)S(1)} %maximum_select_fusion.4), channel_id=1, source_target_pairs={{0,2},{1,3},{2,0},{3,1},{4,6},{5,7},{6,4},{7,5},{8,10},{9,11},{10,... | collective-permute-start | bytes 225800 | tf_op jit(solution)/shard_map/ppermute | solution.py:52
  170.2 4.0 %collective-permute-done.23 = f32[18816]{0:T(1024)S(1)} collective-permute-done((f32[18816]{0:T(1024)S(1)}, f32[18816]{0:T(1024)S(1)}, u32[]{:S(2)}, u32[]{:S(2)}) %collective-permute-start.23) | collective-permute-done | bytes 75296 | tf_op jit(solution)/shard_map/ppermute | solution.py:52
  174.5 2.8 %fusion.146 = bf16[1,3,16,1536]{3,2,1,0:T(8,128)(2,1)} fusion(f32[1536]{0:T(1024)S(1)} %copy-done.43, bf16[9,22,1536]{2,1,0:T(8,128)(2,1)S(1)} %select_maximum_fusion, f32[1536]{0:T(1024)S(1)} %copy-done.45, f32[1536]{0:T(1024)S(1)} %get-tuple-element.59, f32[1536]{0:T(1024)S(1)} %get-tuple-element.60, bf16[3,16,1536]{2,1,0:T(8,128)(2,1)S(1)} %collective-permute-done.13, ...), kind=kLoop, calls=%fused_computation.296 | loop fusion | flops 11132928 | bytes 7084032 | tf_op jit(solution)/shard_map/reshape | solution.py:306
  178.1 27.9 %reduce-scatter.2.cloned.1.call-done = bf16[192,1536]{1,0:T(8,128)(2,1)} async-done(((bf16[1536,1536]{1,0:T(8,128)(2,1)}), bf16[192,1536]{1,0:T(8,128)(2,1)}) %reduce-scatter.2.cloned.1.call-update) | async-done | bytes 589840 | tf_op jit(solution)/shard_map/reduce_scatter | solution.py:287
  206.0 2.2 %convert_element_type.497 = f32[192,1536]{1,0:T(8,128)} convert(bf16[192,1536]{1,0:T(8,128)(2,1)} %reduce-scatter.2.cloned.1.call-done) | non-fusion elementwise | flops 294912 | bytes 1769472 | tf_op jit(solution)/shard_map/convert_element_type | solution.py:289
  (227 shorter events, 13.4 us)
Async XLA Ops:
  7.2 198.8 %reduce-scatter.2.cloned.1.call-start = ((), (), s32[]{:S(2)}) async-start(), calls=%async_computation.1 | async-start | bytes 5308416 | tf_op jit(solution)/shard_map/reduce_scatter | solution.py:287
  7.2 30.1 %collective-permute-start = (bf16[192,1536]{1,0:T(8,128)(2,1)}, bf16[192,1536]{1,0:T(8,128)(2,1)S(1)}, u32[]{:S(2)}, u32[]{:S(2)}) collective-permute-start(bf16[192,1536]{1,0:T(8,128)(2,1)} %param.17), channel_id=1, source_target_pairs={{0,8},{8,16},{16,24},{24,28},{28,20},{20,12},{12,4},{4,0},{1,9},{9... | collective-permute-start | bytes 1769480 | tf_op jit(solution)/shard_map/ppermute | solution.py:112
  10.3 27.0 %collective-permute-start.1 = (bf16[192,1536]{1,0:T(8,128)(2,1)}, bf16[192,1536]{1,0:T(8,128)(2,1)S(1)}, u32[]{:S(2)}, u32[]{:S(2)}) collective-permute-start(bf16[192,1536]{1,0:T(8,128)(2,1)} %param.17), channel_id=1, source_target_pairs={{0,4},{8,0},{16,8},{24,16},{28,24},{20,28},{12,20},{4,12},{1,5},{9... | collective-permute-start | bytes 1769480 | tf_op jit(solution)/shard_map/ppermute | solution.py:114
  38.1 4.9 %collective-permute-start.2 = (bf16[3,16,1536]{2,1,0:T(8,128)(2,1)S(1)}, bf16[3,16,1536]{2,1,0:T(8,128)(2,1)S(1)}, u32[]{:S(2)}, u32[]{:S(2)}) collective-permute-start(bf16[3,16,1536]{2,1,0:T(8,128)(2,1)S(1)} %bitcast.67), channel_id=1, source_target_pairs={{0,1},{1,2},{2,3},{4,5},{5,6},{6,7},{8,9},{9,10},{10,11},{12,13},{... | collective-permute-start | bytes 442376 | tf_op jit(solution)/shard_map/ppermute | solution.py:16
  39.6 5.3 %collective-permute-start.3 = (bf16[3,16,1536]{2,1,0:T(8,128)(2,1)S(1)}, bf16[3,16,1536]{2,1,0:T(8,128)(2,1)S(1)}, u32[]{:S(2)}, u32[]{:S(2)}) collective-permute-start(bf16[3,16,1536]{2,1,0:T(8,128)(2,1)S(1)} %bitcast.68), channel_id=1, source_target_pairs={{1,0},{2,1},{3,2},{5,4},{6,5},{7,6},{9,8},{10,9},{11,10},{13,12},{... | collective-permute-start | bytes 442376 | tf_op jit(solution)/shard_map/ppermute | solution.py:19
  40.9 14.0 %collective-permute-start.6 = (bf16[192,1536]{1,0:T(8,128)(2,1)S(1)}, bf16[192,1536]{1,0:T(8,128)(2,1)S(1)}, u32[]{:S(2)}, u32[]{:S(2)}) collective-permute-start(bf16[192,1536]{1,0:T(8,128)(2,1)S(1)} %collective-permute-done), channel_id=1, source_target_pairs={{0,8},{8,16},{16,24},{24,28},{28,20},{20,12},{12,4},{4,0},{1,9},{9... | collective-permute-start | bytes 1769480 | tf_op jit(solution)/shard_map/ppermute | solution.py:112
  42.8 14.5 %collective-permute-start.7 = (bf16[192,1536]{1,0:T(8,128)(2,1)S(1)}, bf16[192,1536]{1,0:T(8,128)(2,1)S(1)}, u32[]{:S(2)}, u32[]{:S(2)}) collective-permute-start(bf16[192,1536]{1,0:T(8,128)(2,1)S(1)} %collective-permute-done.1), channel_id=1, source_target_pairs={{0,4},{8,0},{16,8},{24,16},{28,24},{20,28},{12,20},{4,12},{1,5},{9... | collective-permute-start | bytes 1769480 | tf_op jit(solution)/shard_map/ppermute | solution.py:114
  48.8 74.3 %copy-start.46 = (f32[3,16]{1,0:T(4,128)}, f32[3,16]{1,0:T(4,128)S(1)}, u32[]{:S(2)}) copy-start(f32[3,16]{1,0:T(4,128)S(1)} %broadcast_multiply_fusion.2) | copy-start | bytes 580
  49.0 74.1 %copy-start.47 = (f32[3,16]{1,0:T(4,128)}, f32[3,16]{1,0:T(4,128)S(1)}, u32[]{:S(2)}) copy-start(f32[3,16]{1,0:T(4,128)S(1)} %add_rsqrt_fusion) | copy-start | bytes 580
  49.1 5.1 %collective-permute-start.4 = (bf16[1,3,16,1536]{3,2,1,0:T(8,128)(2,1)S(1)}, bf16[1,3,16,1536]{3,2,1,0:T(8,128)(2,1)S(1)}, u32[]{:S(2)}, u32[]{:S(2)}) collective-permute-start(bf16[1,3,16,1536]{3,2,1,0:T(8,128)(2,1)S(1)} %fusion.143), channel_id=1, source_target_pairs={{0,1},{1,0},{2,3},{3,2},{4,5},{5,4},{6,7},{7,6},{8,9},{9,8},{10,11... | collective-permute-start | bytes 442376 | tf_op jit(solution)/shard_map/ppermute | solution.py:168
  54.2 9.3 %collective-permute-start.5 = (bf16[2,3,16,1536]{3,2,1,0:T(8,128)(2,1)S(1)}, bf16[2,3,16,1536]{3,2,1,0:T(8,128)(2,1)S(1)}, u32[]{:S(2)}, u32[]{:S(2)}) collective-permute-start(bf16[2,3,16,1536]{3,2,1,0:T(8,128)(2,1)S(1)} %maximum_select_fusion.2), channel_id=1, source_target_pairs={{0,2},{1,3},{2,0},{3,1},{4,6},{5,7},{6,4},{7,5},{8,10},{9,11},{10,... | collective-permute-start | bytes 884744 | tf_op jit(solution)/shard_map/ppermute | solution.py:168
  54.9 14.9 %collective-permute-start.8 = (bf16[192,1536]{1,0:T(8,128)(2,1)S(1)}, bf16[192,1536]{1,0:T(8,128)(2,1)S(1)}, u32[]{:S(2)}, u32[]{:S(2)}) collective-permute-start(bf16[192,1536]{1,0:T(8,128)(2,1)S(1)} %collective-permute-done.6), channel_id=1, source_target_pairs={{0,8},{8,16},{16,24},{24,28},{28,20},{20,12},{12,4},{4,0},{1,9},{9... | collective-permute-start | bytes 1769480 | tf_op jit(solution)/shard_map/ppermute | solution.py:112
  57.3 15.4 %collective-permute-start.9 = (bf16[192,1536]{1,0:T(8,128)(2,1)S(1)}, bf16[192,1536]{1,0:T(8,128)(2,1)S(1)}, u32[]{:S(2)}, u32[]{:S(2)}) collective-permute-start(bf16[192,1536]{1,0:T(8,128)(2,1)S(1)} %collective-permute-done.7), channel_id=1, source_target_pairs={{0,4},{8,0},{16,8},{24,16},{28,24},{20,28},{12,20},{4,12},{1,5},{9... | collective-permute-start | bytes 1769480 | tf_op jit(solution)/shard_map/ppermute | solution.py:114
  69.8 16.7 %collective-permute-start.10 = (bf16[192,1536]{1,0:T(8,128)(2,1)S(1)}, bf16[192,1536]{1,0:T(8,128)(2,1)S(1)}, u32[]{:S(2)}, u32[]{:S(2)}) collective-permute-start(bf16[192,1536]{1,0:T(8,128)(2,1)S(1)} %collective-permute-done.8), channel_id=1, source_target_pairs={{0,8},{8,16},{16,24},{24,28},{28,20},{20,12},{12,4},{4,0},{1,9},{9... | collective-permute-start | bytes 1769480 | tf_op jit(solution)/shard_map/ppermute | solution.py:112
  111.2 1.6 collective-permute-start.11
  113.9 9.1 %collective-permute-start.12 = (f32[1,3,16,1536]{3,2,1,0:T(8,128)S(1)}, f32[1,3,16,1536]{3,2,1,0:T(8,128)S(1)}, u32[]{:S(2)}, u32[]{:S(2)}) collective-permute-start(f32[1,3,16,1536]{3,2,1,0:T(8,128)S(1)} %constant_dynamic-slice_fusion), channel_id=1, source_target_pairs={{0,2},{1,3},{2,0},{3,1},{4,6},{5,7},{6,4},{7,5},{8,10},{9,11},{10,... | collective-permute-start | bytes 884744 | tf_op jit(solution)/shard_map/ppermute | solution.py:69
  128.6 1.4 collective-permute-start.15
  130.6 4.5 %collective-permute-start.16 = (f32[18816]{0:T(1024)S(1)}, f32[18816]{0:T(1024)S(1)}, u32[]{:S(2)}, u32[]{:S(2)}) collective-permute-start(f32[18816]{0:T(1024)S(1)} %get-tuple-element.111), channel_id=1, source_target_pairs={{0,2},{1,3},{2,0},{3,1},{4,6},{5,7},{6,4},{7,5},{8,10},{9,11},{10,... | collective-permute-start | bytes 225800 | tf_op jit(solution)/shard_map/ppermute | solution.py:49
  135.4 38.9 %copy-start.7 = (f32[1536]{0:T(1024)S(1)}, f32[1536]{0:T(1024)}, u32[]{:S(2)}) copy-start(f32[1536]{0:T(1024)} %copy-done.6) | copy-start | bytes 18436
  135.4 38.9 %copy-start.9 = (f32[1536]{0:T(1024)S(1)}, f32[1536]{0:T(1024)}, u32[]{:S(2)}) copy-start(f32[1536]{0:T(1024)} %copy-done.8) | copy-start | bytes 18436
  135.4 38.9 %copy-start.11 = (f32[1536]{0:T(1024)S(1)}, f32[1536]{0:T(1024)}, u32[]{:S(2)}) copy-start(f32[1536]{0:T(1024)} %copy-done.10) | copy-start | bytes 18436
  135.4 38.9 %copy-start.13 = (f32[1536]{0:T(1024)S(1)}, f32[1536]{0:T(1024)}, u32[]{:S(2)}) copy-start(f32[1536]{0:T(1024)} %copy-done.12) | copy-start | bytes 18436
  135.4 38.9 %copy-start.15 = (f32[1536]{0:T(1024)S(1)}, f32[1536]{0:T(1024)}, u32[]{:S(2)}) copy-start(f32[1536]{0:T(1024)} %copy-done.14) | copy-start | bytes 18436
  135.4 38.9 %copy-start.17 = (f32[1536]{0:T(1024)S(1)}, f32[1536]{0:T(1024)}, u32[]{:S(2)}) copy-start(f32[1536]{0:T(1024)} %copy-done.16) | copy-start | bytes 18436
  135.4 38.9 %copy-start.19 = (f32[1536]{0:T(1024)S(1)}, f32[1536]{0:T(1024)}, u32[]{:S(2)}) copy-start(f32[1536]{0:T(1024)} %copy-done.18) | copy-start | bytes 18436
  135.5 38.9 %copy-start.21 = (f32[1536]{0:T(1024)S(1)}, f32[1536]{0:T(1024)}, u32[]{:S(2)}) copy-start(f32[1536]{0:T(1024)} %copy-done.20) | copy-start | bytes 18436
  135.5 38.9 %copy-start.23 = (f32[1536]{0:T(1024)S(1)}, f32[1536]{0:T(1024)}, u32[]{:S(2)}) copy-start(f32[1536]{0:T(1024)} %copy-done.22) | copy-start | bytes 18436
  135.5 38.9 %copy-start.25 = (f32[1536]{0:T(1024)S(1)}, f32[1536]{0:T(1024)}, u32[]{:S(2)}) copy-start(f32[1536]{0:T(1024)} %copy-done.24) | copy-start | bytes 18436
  135.5 38.9 %copy-start.27 = (f32[1536]{0:T(1024)S(1)}, f32[1536]{0:T(1024)}, u32[]{:S(2)}) copy-start(f32[1536]{0:T(1024)} %copy-done.26) | copy-start | bytes 18436
  135.5 38.9 %copy-start.29 = (f32[1536]{0:T(1024)S(1)}, f32[1536]{0:T(1024)}, u32[]{:S(2)}) copy-start(f32[1536]{0:T(1024)} %copy-done.28) | copy-start | bytes 18436
  135.5 38.9 %copy-start.31 = (f32[1536]{0:T(1024)S(1)}, f32[1536]{0:T(1024)}, u32[]{:S(2)}) copy-start(f32[1536]{0:T(1024)} %copy-done.30) | copy-start | bytes 18436
  135.5 38.9 %copy-start.33 = (f32[1536]{0:T(1024)S(1)}, f32[1536]{0:T(1024)}, u32[]{:S(2)}) copy-start(f32[1536]{0:T(1024)} %copy-done.32) | copy-start | bytes 18436
  135.5 38.9 %copy-start.35 = (f32[1536]{0:T(1024)S(1)}, f32[1536]{0:T(1024)}, u32[]{:S(2)}) copy-start(f32[1536]{0:T(1024)} %copy-done.34) | copy-start | bytes 18436
  135.5 38.9 %copy-start.37 = (f32[1536]{0:T(1024)S(1)}, f32[1536]{0:T(1024)}, u32[]{:S(2)}) copy-start(f32[1536]{0:T(1024)} %copy-done.36) | copy-start | bytes 18436
  135.5 38.9 %copy-start.39 = (f32[1536]{0:T(1024)S(1)}, f32[1536]{0:T(1024)}, u32[]{:S(2)}) copy-start(f32[1536]{0:T(1024)} %copy-done.38) | copy-start | bytes 18436
  135.6 38.9 %copy-start.41 = (f32[1536]{0:T(1024)S(1)}, f32[1536]{0:T(1024)}, u32[]{:S(2)}) copy-start(f32[1536]{0:T(1024)} %copy-done.40) | copy-start | bytes 18436
  135.6 38.9 %copy-start.43 = (f32[1536]{0:T(1024)S(1)}, f32[1536]{0:T(1024)}, u32[]{:S(2)}) copy-start(f32[1536]{0:T(1024)} %copy-done.42) | copy-start | bytes 18436
  135.6 38.9 %copy-start.45 = (f32[1536]{0:T(1024)S(1)}, f32[1536]{0:T(1024)}, u32[]{:S(2)}) copy-start(f32[1536]{0:T(1024)} %copy-done.44) | copy-start | bytes 18436
  135.6 4.9 %collective-permute-start.17 = (f32[9408]{0:T(1024)S(1)}, f32[9408]{0:T(1024)S(1)}, u32[]{:S(2)}, u32[]{:S(2)}) collective-permute-start(f32[9408]{0:T(1024)S(1)} %get-tuple-element.120), channel_id=1, source_target_pairs={{0,4},{4,0},{8,12},{12,8},{16,20},{20,16},{24,28},{28,24},{1,5},{5... | collective-permute-start | bytes 112904 | tf_op jit(solution)/shard_map/ppermute | solution.py:49
  140.7 5.3 %collective-permute-start.18 = (f32[4704]{0:T(1024)S(1)}, f32[4704]{0:T(1024)S(1)}, u32[]{:S(2)}, u32[]{:S(2)}) collective-permute-start(f32[4704]{0:T(1024)S(1)} %get-tuple-element.122), channel_id=1, source_target_pairs={{0,8},{4,12},{8,0},{12,4},{16,24},{20,28},{24,16},{28,20},{1,9},{5... | collective-permute-start | bytes 56456 | tf_op jit(solution)/shard_map/ppermute | solution.py:49
  146.2 6.0 %collective-permute-start.19 = (f32[2352]{0:T(1024)S(1)}, f32[2352]{0:T(1024)S(1)}, u32[]{:S(2)}, u32[]{:S(2)}) collective-permute-start(f32[2352]{0:T(1024)S(1)} %get-tuple-element.124), channel_id=1, source_target_pairs={{0,16},{4,20},{8,24},{12,28},{16,0},{20,4},{24,8},{28,12},{1,17},{... | collective-permute-start | bytes 28232 | tf_op jit(solution)/shard_map/ppermute | solution.py:49
  152.2 5.0 %collective-permute-start.20 = (f32[2352]{0:T(1024)S(1)}, f32[2352]{0:T(1024)S(1)}, u32[]{:S(2)}, u32[]{:S(2)}) collective-permute-start(f32[2352]{0:T(1024)S(1)} %add.722), channel_id=1, source_target_pairs={{0,16},{4,20},{8,24},{12,28},{16,0},{20,4},{24,8},{28,12},{1,17},{... | collective-permute-start | bytes 28232 | tf_op jit(solution)/shard_map/ppermute | solution.py:52
  157.3 3.8 %collective-permute-start.21 = (f32[4704]{0:T(1024)S(1)}, f32[4704]{0:T(1024)S(1)}, u32[]{:S(2)}, u32[]{:S(2)}) collective-permute-start(f32[4704]{0:T(1024)S(1)} %maximum_select_fusion.6), channel_id=1, source_target_pairs={{0,8},{4,12},{8,0},{12,4},{16,24},{20,28},{24,16},{28,20},{1,9},{5... | collective-permute-start | bytes 56456 | tf_op jit(solution)/shard_map/ppermute | solution.py:52
  161.2 4.2 %collective-permute-start.22 = (f32[9408]{0:T(1024)S(1)}, f32[9408]{0:T(1024)S(1)}, u32[]{:S(2)}, u32[]{:S(2)}) collective-permute-start(f32[9408]{0:T(1024)S(1)} %maximum_select_fusion.5), channel_id=1, source_target_pairs={{0,4},{4,0},{8,12},{12,8},{16,20},{20,16},{24,28},{28,24},{1,5},{5... | collective-permute-start | bytes 112904 | tf_op jit(solution)/shard_map/ppermute | solution.py:52
  162.7 7.2 %collective-permute-start.13 = (bf16[3,16,1536]{2,1,0:T(8,128)(2,1)S(1)}, bf16[3,16,1536]{2,1,0:T(8,128)(2,1)S(1)}, u32[]{:S(2)}, u32[]{:S(2)}) collective-permute-start(bf16[3,16,1536]{2,1,0:T(8,128)(2,1)S(1)} %get-tuple-element.130), channel_id=1, source_target_pairs={{0,1},{1,2},{2,3},{4,5},{5,6},{6,7},{8,9},{9,10},{10,11},{12,13},{... | collective-permute-start | bytes 442376 | tf_op jit(solution)/shard_map/ppermute | solution.py:16
  164.0 5.9 %collective-permute-start.14 = (bf16[3,16,1536]{2,1,0:T(8,128)(2,1)S(1)}, bf16[3,16,1536]{2,1,0:T(8,128)(2,1)S(1)}, u32[]{:S(2)}, u32[]{:S(2)}) collective-permute-start(bf16[3,16,1536]{2,1,0:T(8,128)(2,1)S(1)} %get-tuple-element.130), channel_id=1, source_target_pairs={{1,0},{2,1},{3,2},{5,4},{6,5},{7,6},{9,8},{10,9},{11,10},{13,12},{... | collective-permute-start | bytes 442376 | tf_op jit(solution)/shard_map/ppermute | solution.py:19
  165.4 8.7 %collective-permute-start.23 = (f32[18816]{0:T(1024)S(1)}, f32[18816]{0:T(1024)S(1)}, u32[]{:S(2)}, u32[]{:S(2)}) collective-permute-start(f32[18816]{0:T(1024)S(1)} %maximum_select_fusion.4), channel_id=1, source_target_pairs={{0,2},{1,3},{2,0},{3,1},{4,6},{5,7},{6,4},{7,5},{8,10},{9,11},{10,... | collective-permute-start | bytes 225800 | tf_op jit(solution)/shard_map/ppermute | solution.py:52
  174.2 3.1 %collective-permute-start.24 = (f32[37632]{0:T(1024)S(1)}, f32[37632]{0:T(1024)S(1)}, u32[]{:S(2)}, u32[]{:S(2)}) collective-permute-start(f32[37632]{0:T(1024)S(1)} %maximum_select_fusion.3), channel_id=1, source_target_pairs={{0,1},{1,0},{2,3},{3,2},{4,5},{5,4},{6,7},{7,6},{8,9},{9,8},{10,11... | collective-permute-start | bytes 451592 | tf_op jit(solution)/shard_map/ppermute | solution.py:52
  (32 other events, 311.1 us)
Sparse Core Ops, SparseCore 0:
  107.2 98.7 reduce-scatter.1

commit v8 on v7

--- a/solution.py
+++ b/solution.py
@@ -284,9 +284,20 @@
     w_term = lax.dot_general(
         flat, dpre, (((0,), (0,)), ((), ())), preferred_element_type=jnp.float32
     )
-    up_grad = lax.psum_scatter(
-        w_term.astype(jnp.bfloat16), "fsdp", scatter_dimension=0, tiled=True
-    ).astype(jnp.float32)
+    n_fsdp = lax.axis_size("fsdp")
+    w_bf = w_term.astype(jnp.bfloat16)
+    keep = w_bf.shape[1] - (w_bf.shape[1] // 3) // 128 * 128
+    up_grad = jnp.concatenate(
+        [
+            lax.psum_scatter(w_bf[:, :keep], "fsdp", scatter_dimension=0, tiled=True).astype(
+                jnp.float32
+            ),
+            ring_reduce_scatter(
+                w_bf[:, keep:].reshape((n_fsdp, chans // n_fsdp, -1)), "fsdp", ring
+            ),
+        ],
+        axis=1,
+    )
     dpre_rows = dpre.reshape(height, cols, -1)
     group_terms = jnp.einsum(
         "hwf,cf->hwc", dpre_rows, columns, preferred_element_type=jnp.float32

time: 216 us -> 220 us (1.019)
  waiting for transfers between devices: 91.7 us -> 62 us
  between operations: 35 us -> 56.9 us
  local copies, waits for them, and re-layouts: 14.7 us -> 20.5 us
  starting transfers between devices: 36.7 us -> 41.2 us
  other arithmetic: 17.9 us -> 21 us
    reduce_scatter x1, waiting for transfers between devices: 27.9 us -> 6.96 us  [body(): lax.psum_scatter(w_bf[:, :keep], 'fsdp', scatter_dimension=0, tiled=True)]
    ppermute x0 -> x7, starting transfers between devices: none -> 7.56 us  [the longest x4 5.43 us: ring_reduce_scatter(): cw = lax.ppermute(cw, axis, forward)]
    ppermute x2, waiting for transfers between devices: 8.31 us -> 1.96 us  [tree_reduce_scatter(): lax.ppermute(give, axis, perm).astype(jnp.float32)]
    ppermute x5, waiting for transfers between devices: 10.4 us -> 5.71 us  [tree_allreduce(): other = lax.ppermute(flat, axis, perm)]
    ppermute x5, starting transfers between devices: 7.21 us -> 4.75 us  [tree_allreduce(): flat = keep + lax.ppermute(give, axis, perm)]
    slice x0 -> x2, local copies, waits for them, and re-layouts: none -> 2.26 us  [the longest x1 2.16 us: body(): w_bf[:, :keep]]
  transfers between devices with their start and end apart: 26 -> 33, of which waited for: 19 -> 14; matrix products, arithmetic and copies ran while one was open for 13% -> 15% of each run, Pallas kernels for 0% -> 0%
where the time goes in v8:
time: 220 us; the launch traced here: 218 us
  waiting for transfers between devices  62 us (28%)
  between operations  56.9 us (26%)
  starting transfers between devices  41.2 us (19%)
  other arithmetic  21 us (10%)
  local copies, waits for them, and re-layouts  20.5 us (9%)
  matrix products  10.3 us (5%)
  blocking collectives  6.55 us (3%)
    ppermute x4, waiting for transfers between devices, ring_all_gather(): cw = lax.ppermute(cw, axis, forward)  20.2 us
    ppermute x5, waiting for transfers between devices, tree_allreduce(): flat = keep + lax.ppermute(give, axis, perm)  16.6 us
    ppermute x5, starting transfers between devices, tree_allreduce(): other = lax.ppermute(flat, axis, perm)  9.25 us
    ppermute x4, starting transfers between devices, ring_all_gather(): cw = lax.ppermute(cw, axis, forward)  8.13 us
    ppermute x2, waiting for transfers between devices, tree_all_gather(): other = lax.ppermute(data, axis, perm)  8.03 us
    reduce_scatter x1, waiting for transfers between devices, body(): lax.psum_scatter(w_bf[:, :keep], 'fsdp', scatter_dimension=0, tiled=True)  6.96 us
    psum x1, blocking collectives, body(): norm_total = lax.psum(jnp.sum(norms), 'rows')  6.55 us
    ppermute x5, waiting for transfers between devices, tree_allreduce(): other = lax.ppermute(flat, axis, perm)  5.71 us
  transfers between devices with their start and end apart: 33, of which 14 were waited for; matrix products, arithmetic and copies ran while one was open for 15% of the time, Pallas kernels for 0%

profile of v8, /device:TPU:0, one launch (start us, length us, event | category | flops | bytes accessed | tf_op | source)
XLA Modules:
  0.0 218.4 jit_solution(364080588233171420)
XLA Ops:
  7.2 3.1 %collective-permute-start = (bf16[192,1536]{1,0:T(8,128)(2,1)}, bf16[192,1536]{1,0:T(8,128)(2,1)S(1)}, u32[]{:S(2)}, u32[]{:S(2)}) collective-permute-start(bf16[192,1536]{1,0:T(8,128)(2,1)} %param.19), channel_id=1, source_target_pairs={{0,8},{8,16},{16,24},{24,28},{28,20},{20,12},{12,4},{4,0},{1,9},{9... | collective-permute-start | bytes 1769480 | tf_op jit(solution)/shard_map/ppermute | solution.py:112
  10.3 1.2 dynamic_slice.121
  22.8 1.9 fusion.160
  33.3 2.0 slice_reduce_fusion.48
  35.3 1.8 slice_reduce_fusion.47
  45.5 1.3 slice_reduce_fusion.46
  48.9 1.5 collective-permute-start.2
  50.3 1.3 collective-permute-start.3
  51.6 1.9 collective-permute-start.6
  53.9 1.7 collective-permute-done.3
  56.2 3.4 %fusion.158 = (f32[3,16]{1,0:T(4,128)S(1)}, f32[3,16,1536]{2,1,0:T(8,128)S(1)}) fusion(f32[1536]{0:T(1024)S(1)} %get-tuple-element.105, bf16[9,22,1536]{2,1,0:T(8,128)(2,1)S(1)} %select_maximum_fusion.2, f32[1536]{0:T(1024)S(1)} %get-tuple-element.106, f32[1536]{0:T(1024)S(1)} %get-tuple-element.59, f32[1536]{0:T(1024)S(1)} %get-tuple-element.60, ...), kind=kLoop, calls=%fused_computation.388 | loop fusion | flops 10911696 | bytes 7827648 | tf_op jit(solution)/shard_map/reduce_sum | solution.py:214
  60.9 4.1 %collective-permute-start.4 = (bf16[1,3,16,1536]{3,2,1,0:T(8,128)(2,1)S(1)}, bf16[1,3,16,1536]{3,2,1,0:T(8,128)(2,1)S(1)}, u32[]{:S(2)}, u32[]{:S(2)}) collective-permute-start(bf16[1,3,16,1536]{3,2,1,0:T(8,128)(2,1)S(1)} %fusion.149), channel_id=1, source_target_pairs={{0,1},{1,0},{2,3},{3,2},{4,5},{5,4},{6,7},{7,6},{8,9},{9,8},{10,11... | collective-permute-start | bytes 442376 | tf_op jit(solution)/shard_map/ppermute | solution.py:168
  66.1 1.7 collective-permute-start.8
  68.3 7.1 %collective-permute-done.5 = bf16[2,3,16,1536]{3,2,1,0:T(8,128)(2,1)S(1)} collective-permute-done((bf16[2,3,16,1536]{3,2,1,0:T(8,128)(2,1)S(1)}, bf16[2,3,16,1536]{3,2,1,0:T(8,128)(2,1)S(1)}, u32[]{:S(2)}, u32[]{:S(2)}) %collective-permute-start.5) | collective-permute-done | bytes 294944 | tf_op jit(solution)/shard_map/ppermute | solution.py:168
  75.5 6.1 %collective-permute-done.8 = bf16[192,1536]{1,0:T(8,128)(2,1)S(1)} collective-permute-done((bf16[192,1536]{1,0:T(8,128)(2,1)S(1)}, bf16[192,1536]{1,0:T(8,128)(2,1)S(1)}, u32[]{:S(2)}, u32[]{:S(2)}) %collective-permute-start.8) | collective-permute-done | bytes 589856 | tf_op jit(solution)/shard_map/ppermute | solution.py:112
  81.5 1.5 collective-permute-start.10
  83.6 14.2 %collective-permute-done.10 = bf16[192,1536]{1,0:T(8,128)(2,1)S(1)} collective-permute-done((bf16[192,1536]{1,0:T(8,128)(2,1)S(1)}, bf16[192,1536]{1,0:T(8,128)(2,1)S(1)}, u32[]{:S(2)}, u32[]{:S(2)}) %collective-permute-start.10) | collective-permute-done | bytes 589856 | tf_op jit(solution)/shard_map/ppermute | solution.py:112
  97.8 4.8 %fusion.4 = (f32[1536]{0:T(1024)S(1)}, f32[1536]{0:T(1024)S(1)}, f32[192,1536]{1,0:T(8,128)}, f32[192,1536]{1,0:T(8,128)}) fusion(bf16[1,12,16,1536]{3,2,1,0:T(8,128)(2,1)S(1)} %copy-done.9, f32[1536]{0:T(1024)S(1)} %copy-done.84, bf16[192,1536]{1,0:T(8,128)(2,1)S(1)} %bitcast.101, bf16[1536,1536]{1,0:T(8,128)(2,1)S(1)} %bitcast.99), kind=kOutput, calls=%fused_computation.63 | convolution fusion | flops 926610432 | bytes 8275968 | tf_op jit(solution)/shard_map/dot_general | solution.py:271
  103.3 6.5 %all-reduce.2 = (f32[]{:T(128)}, f32[]{:T(128)}) all-reduce(f32[]{:T(128)} %get-tuple-element.127, f32[]{:T(128)} %get-tuple-element.126), channel_id=1, replica_groups=mesh['fsdp'=8,'rows'=4] {'rows'}, use_global_device_ids=true, to_apply=%region_4.5 | all-reduce | flops 2 | bytes 16 | tf_op jit(solution)/shard_map/psum | solution.py:276
  111.2 3.2 %fusion.3 = (bf16[192,1536]{1,0:T(8,128)(2,1)S(1)}, bf16[192,1536]{1,0:T(8,128)(2,1)}) fusion(f32[192,1536]{1,0:T(8,128)} %get-tuple-element.163, f32[192,1536]{1,0:T(8,128)} %get-tuple-element.134, bf16[1,12,16,1536]{3,2,1,0:T(8,128)(2,1)S(1)} %copy-done.9, f32[1536]{0:T(1024)S(1)} %get-tuple-element.147, f32[1536]{0:T(1024)S(1)} %get-tuple-element.132, ...), kind=kLoop, calls=%fused_computation.62 | loop fusion | flops 5603328 | bytes 4159488 | tf_op jit(solution)/shard_map/convert_element_type | solution.py:283
  114.4 4.0 %convolution_convert_fusion.1 = bf16[12,16,1536]{2,1,0:T(8,128)(2,1)S(1)} fusion(bf16[12,16,1536]{2,1,0:T(8,128)(2,1)S(1)} %bitcast.103, bf16[1536,1536,1]{1,0,2:T(8,128)(2,1)} %bitcast.100), kind=kOutput, calls=%fused_computation.52 | convolution fusion | flops 906264576 | bytes 5898240 | tf_op jit(solution)/shard_map/hwf,cf->hwc/dot_general | solution.py:302
  119.3 1.4 convolution_convert_fusion
  120.8 2.2 slice.790
  123.7 1.3 collective-permute-start.18
  125.1 1.1 convert_add_fusion
  127.0 1.7 collective-permute-start.12
  131.5 1.7 fusion.21
  133.1 1.3 collective-permute-start.19
  134.5 2.0 collective-permute-done.12
  136.4 1.2 fusion.155
  146.7 1.7 collective-permute-start.23
  148.4 1.1 fusion.23
  149.5 1.2 collective-permute-start.16
  151.9 1.2 collective-permute-start.24
  153.1 8.4 %collective-permute-done.24 = f32[9408]{0:T(1024)S(1)} collective-permute-done((f32[9408]{0:T(1024)S(1)}, f32[9408]{0:T(1024)S(1)}, u32[]{:S(2)}, u32[]{:S(2)}) %collective-permute-start.24) | collective-permute-done | bytes 37664 | tf_op jit(solution)/shard_map/ppermute | solution.py:49
  161.9 5.1 %collective-permute-done.25 = f32[4704]{0:T(1024)S(1)} collective-permute-done((f32[4704]{0:T(1024)S(1)}, f32[4704]{0:T(1024)S(1)}, u32[]{:S(2)}, u32[]{:S(2)}) %collective-permute-start.25) | collective-permute-done | bytes 18848 | tf_op jit(solution)/shard_map/ppermute | solution.py:49
  167.2 1.7 collective-permute-start.26
  168.9 3.1 %collective-permute-done.26 = f32[2352]{0:T(1024)S(1)} collective-permute-done((f32[2352]{0:T(1024)S(1)}, f32[2352]{0:T(1024)S(1)}, u32[]{:S(2)}, u32[]{:S(2)}) %collective-permute-start.26) | collective-permute-done | bytes 9440 | tf_op jit(solution)/shard_map/ppermute | solution.py:49
  171.9 1.5 collective-permute-start.27
  179.3 1.3 collective-permute-start.13
  180.6 1.3 collective-permute-start.14
  182.3 3.0 %collective-permute-start.28 = (f32[4704]{0:T(1024)S(1)}, f32[4704]{0:T(1024)S(1)}, u32[]{:S(2)}, u32[]{:S(2)}) collective-permute-start(f32[4704]{0:T(1024)S(1)} %maximum_select_fusion.6), channel_id=1, source_target_pairs={{0,8},{4,12},{8,0},{12,4},{16,24},{20,28},{24,16},{28,20},{1,9},{5... | collective-permute-start | bytes 56456 | tf_op jit(solution)/shard_map/ppermute | solution.py:52
  185.6 1.9 collective-permute-start.21
  188.0 4.4 %collective-permute-done.29 = f32[9408]{0:T(1024)S(1)} collective-permute-done((f32[9408]{0:T(1024)S(1)}, f32[9408]{0:T(1024)S(1)}, u32[]{:S(2)}, u32[]{:S(2)}) %collective-permute-start.29) | collective-permute-done | bytes 37664 | tf_op jit(solution)/shard_map/ppermute | solution.py:52
  192.6 4.4 %collective-permute-start.30 = (f32[18816]{0:T(1024)S(1)}, f32[18816]{0:T(1024)S(1)}, u32[]{:S(2)}, u32[]{:S(2)}) collective-permute-start(f32[18816]{0:T(1024)S(1)} %maximum_select_fusion.4), channel_id=1, source_target_pairs={{0,2},{1,3},{2,0},{3,1},{4,6},{5,7},{6,4},{7,5},{8,10},{9,11},{10,... | collective-permute-start | bytes 225800 | tf_op jit(solution)/shard_map/ppermute | solution.py:52
  197.3 2.8 %fusion.152 = bf16[1,3,16,1536]{3,2,1,0:T(8,128)(2,1)} fusion(f32[1536]{0:T(1024)S(1)} %copy-done.73, bf16[9,22,1536]{2,1,0:T(8,128)(2,1)S(1)} %select_maximum_fusion, f32[1536]{0:T(1024)S(1)} %copy-done.75, f32[1536]{0:T(1024)S(1)} %get-tuple-element.59, f32[1536]{0:T(1024)S(1)} %get-tuple-element.60, bf16[3,16,1536]{2,1,0:T(8,128)(2,1)S(1)} %collective-permute-done.13, ...), kind=kLoop, calls=%fused_computation.311 | loop fusion | flops 11132928 | bytes 7084032 | tf_op jit(solution)/shard_map/reshape | solution.py:317
  200.3 1.3 collective-permute-done.31
  202.4 7.0 %reduce-scatter.2.cloned.1.call-done = bf16[192,1024]{1,0:T(8,128)(2,1)} async-done(((bf16[1536,1024]{1,0:T(8,128)(2,1)}), bf16[192,1024]{1,0:T(8,128)(2,1)}) %reduce-scatter.2.cloned.1.call-update) | async-done | bytes 393232 | tf_op jit(solution)/shard_map/reduce_scatter | solution.py:292
  (311 shorter events, 21.0 us)
Async XLA Ops:
  7.2 202.2 %reduce-scatter.2.cloned.1.call-start = ((), (), s32[]{:S(2)}) async-start(), calls=%async_computation.1 | async-start | bytes 3538944 | tf_op jit(solution)/shard_map/reduce_scatter | solution.py:292
  7.2 40.8 %collective-permute-start = (bf16[192,1536]{1,0:T(8,128)(2,1)}, bf16[192,1536]{1,0:T(8,128)(2,1)S(1)}, u32[]{:S(2)}, u32[]{:S(2)}) collective-permute-start(bf16[192,1536]{1,0:T(8,128)(2,1)} %param.19), channel_id=1, source_target_pairs={{0,8},{8,16},{16,24},{24,28},{28,20},{20,12},{12,4},{4,0},{1,9},{9... | collective-permute-start | bytes 1769480 | tf_op jit(solution)/shard_map/ppermute | solution.py:112
  10.3 37.7 %collective-permute-start.1 = (bf16[192,1536]{1,0:T(8,128)(2,1)}, bf16[192,1536]{1,0:T(8,128)(2,1)S(1)}, u32[]{:S(2)}, u32[]{:S(2)}) collective-permute-start(bf16[192,1536]{1,0:T(8,128)(2,1)} %param.19), channel_id=1, source_target_pairs={{0,4},{8,0},{16,8},{24,16},{28,24},{20,28},{12,20},{4,12},{1,5},{9... | collective-permute-start | bytes 1769480 | tf_op jit(solution)/shard_map/ppermute | solution.py:114
  35.3 20.6 %copy-start.12 = (f32[1536]{0:T(1024)}, f32[1536]{0:T(1024)S(1)}, u32[]{:S(2)}) copy-start(f32[1536]{0:T(1024)S(1)} %get-tuple-element.75) | copy-start | bytes 18436
  35.3 20.6 %copy-start.14 = (f32[1536]{0:T(1024)}, f32[1536]{0:T(1024)S(1)}, u32[]{:S(2)}) copy-start(f32[1536]{0:T(1024)S(1)} %get-tuple-element.76) | copy-start | bytes 18436
  37.1 18.7 %copy-start.16 = (f32[1536]{0:T(1024)}, f32[1536]{0:T(1024)S(1)}, u32[]{:S(2)}) copy-start(f32[1536]{0:T(1024)S(1)} %get-tuple-element.77) | copy-start | bytes 18436
  37.1 18.7 %copy-start.18 = (f32[1536]{0:T(1024)}, f32[1536]{0:T(1024)S(1)}, u32[]{:S(2)}) copy-start(f32[1536]{0:T(1024)S(1)} %get-tuple-element.78) | copy-start | bytes 18436
  37.2 18.7 %copy-start.20 = (f32[1536]{0:T(1024)}, f32[1536]{0:T(1024)S(1)}, u32[]{:S(2)}) copy-start(f32[1536]{0:T(1024)S(1)} %get-tuple-element.79) | copy-start | bytes 18436
  37.2 18.7 %copy-start.22 = (f32[1536]{0:T(1024)}, f32[1536]{0:T(1024)S(1)}, u32[]{:S(2)}) copy-start(f32[1536]{0:T(1024)S(1)} %get-tuple-element.80) | copy-start | bytes 18436
  37.2 18.7 %copy-start.24 = (f32[1536]{0:T(1024)}, f32[1536]{0:T(1024)S(1)}, u32[]{:S(2)}) copy-start(f32[1536]{0:T(1024)S(1)} %get-tuple-element.81) | copy-start | bytes 18436
  37.2 18.7 %copy-start.26 = (f32[1536]{0:T(1024)}, f32[1536]{0:T(1024)S(1)}, u32[]{:S(2)}) copy-start(f32[1536]{0:T(1024)S(1)} %get-tuple-element.82) | copy-start | bytes 18436
  37.2 18.7 %copy-start.28 = (f32[1536]{0:T(1024)}, f32[1536]{0:T(1024)S(1)}, u32[]{:S(2)}) copy-start(f32[1536]{0:T(1024)S(1)} %get-tuple-element.83) | copy-start | bytes 18436
  37.2 18.7 %copy-start.30 = (f32[1536]{0:T(1024)}, f32[1536]{0:T(1024)S(1)}, u32[]{:S(2)}) copy-start(f32[1536]{0:T(1024)S(1)} %get-tuple-element.84) | copy-start | bytes 18436
  37.2 18.7 %copy-start.32 = (f32[1536]{0:T(1024)}, f32[1536]{0:T(1024)S(1)}, u32[]{:S(2)}) copy-start(f32[1536]{0:T(1024)S(1)} %get-tuple-element.85) | copy-start | bytes 18436
  37.2 18.7 %copy-start.34 = (f32[1536]{0:T(1024)}, f32[1536]{0:T(1024)S(1)}, u32[]{:S(2)}) copy-start(f32[1536]{0:T(1024)S(1)} %get-tuple-element.86) | copy-start | bytes 18436
  37.2 18.7 %copy-start.36 = (f32[1536]{0:T(1024)}, f32[1536]{0:T(1024)S(1)}, u32[]{:S(2)}) copy-start(f32[1536]{0:T(1024)S(1)} %get-tuple-element.87) | copy-start | bytes 18436
  37.2 18.7 %copy-start.38 = (f32[1536]{0:T(1024)}, f32[1536]{0:T(1024)S(1)}, u32[]{:S(2)}) copy-start(f32[1536]{0:T(1024)S(1)} %get-tuple-element.88) | copy-start | bytes 18436
  37.3 18.7 %copy-start.40 = (f32[1536]{0:T(1024)}, f32[1536]{0:T(1024)S(1)}, u32[]{:S(2)}) copy-start(f32[1536]{0:T(1024)S(1)} %get-tuple-element.89) | copy-start | bytes 18436
  48.9 4.9 %collective-permute-start.2 = (bf16[3,16,1536]{2,1,0:T(8,128)(2,1)S(1)}, bf16[3,16,1536]{2,1,0:T(8,128)(2,1)S(1)}, u32[]{:S(2)}, u32[]{:S(2)}) collective-permute-start(bf16[3,16,1536]{2,1,0:T(8,128)(2,1)S(1)} %bitcast.104), channel_id=1, source_target_pairs={{0,1},{1,2},{2,3},{4,5},{5,6},{6,7},{8,9},{9,10},{10,11},{12,13},{... | collective-permute-start | bytes 442376 | tf_op jit(solution)/shard_map/ppermute | solution.py:16
  50.3 5.3 %collective-permute-start.3 = (bf16[3,16,1536]{2,1,0:T(8,128)(2,1)S(1)}, bf16[3,16,1536]{2,1,0:T(8,128)(2,1)S(1)}, u32[]{:S(2)}, u32[]{:S(2)}) collective-permute-start(bf16[3,16,1536]{2,1,0:T(8,128)(2,1)S(1)} %bitcast.105), channel_id=1, source_target_pairs={{1,0},{2,1},{3,2},{5,4},{6,5},{7,6},{9,8},{10,9},{11,10},{13,12},{... | collective-permute-start | bytes 442376 | tf_op jit(solution)/shard_map/ppermute | solution.py:19
  51.6 14.5 %collective-permute-start.6 = (bf16[192,1536]{1,0:T(8,128)(2,1)S(1)}, bf16[192,1536]{1,0:T(8,128)(2,1)S(1)}, u32[]{:S(2)}, u32[]{:S(2)}) collective-permute-start(bf16[192,1536]{1,0:T(8,128)(2,1)S(1)} %collective-permute-done), channel_id=1, source_target_pairs={{0,8},{8,16},{16,24},{24,28},{28,20},{20,12},{12,4},{4,0},{1,9},{9... | collective-permute-start | bytes 1769480 | tf_op jit(solution)/shard_map/ppermute | solution.py:112
  53.5 14.5 %collective-permute-start.7 = (bf16[192,1536]{1,0:T(8,128)(2,1)S(1)}, bf16[192,1536]{1,0:T(8,128)(2,1)S(1)}, u32[]{:S(2)}, u32[]{:S(2)}) collective-permute-start(bf16[192,1536]{1,0:T(8,128)(2,1)S(1)} %collective-permute-done.1), channel_id=1, source_target_pairs={{0,4},{8,0},{16,8},{24,16},{28,24},{20,28},{12,20},{4,12},{1,5},{9... | collective-permute-start | bytes 1769480 | tf_op jit(solution)/shard_map/ppermute | solution.py:114
  60.9 5.1 %collective-permute-start.4 = (bf16[1,3,16,1536]{3,2,1,0:T(8,128)(2,1)S(1)}, bf16[1,3,16,1536]{3,2,1,0:T(8,128)(2,1)S(1)}, u32[]{:S(2)}, u32[]{:S(2)}) collective-permute-start(bf16[1,3,16,1536]{3,2,1,0:T(8,128)(2,1)S(1)} %fusion.149), channel_id=1, source_target_pairs={{0,1},{1,0},{2,3},{3,2},{4,5},{5,4},{6,7},{7,6},{8,9},{9,8},{10,11... | collective-permute-start | bytes 442376 | tf_op jit(solution)/shard_map/ppermute | solution.py:168
  66.0 9.3 %collective-permute-start.5 = (bf16[2,3,16,1536]{3,2,1,0:T(8,128)(2,1)S(1)}, bf16[2,3,16,1536]{3,2,1,0:T(8,128)(2,1)S(1)}, u32[]{:S(2)}, u32[]{:S(2)}) collective-permute-start(bf16[2,3,16,1536]{3,2,1,0:T(8,128)(2,1)S(1)} %maximum_select_fusion.2), channel_id=1, source_target_pairs={{0,2},{1,3},{2,0},{3,1},{4,6},{5,7},{6,4},{7,5},{8,10},{9,11},{10,... | collective-permute-start | bytes 884744 | tf_op jit(solution)/shard_map/ppermute | solution.py:168
  66.1 15.4 %collective-permute-start.8 = (bf16[192,1536]{1,0:T(8,128)(2,1)S(1)}, bf16[192,1536]{1,0:T(8,128)(2,1)S(1)}, u32[]{:S(2)}, u32[]{:S(2)}) collective-permute-start(bf16[192,1536]{1,0:T(8,128)(2,1)S(1)} %collective-permute-done.6), channel_id=1, source_target_pairs={{0,8},{8,16},{16,24},{24,28},{28,20},{20,12},{12,4},{4,0},{1,9},{9... | collective-permute-start | bytes 1769480 | tf_op jit(solution)/shard_map/ppermute | solution.py:112
  68.1 15.4 %collective-permute-start.9 = (bf16[192,1536]{1,0:T(8,128)(2,1)S(1)}, bf16[192,1536]{1,0:T(8,128)(2,1)S(1)}, u32[]{:S(2)}, u32[]{:S(2)}) collective-permute-start(bf16[192,1536]{1,0:T(8,128)(2,1)S(1)} %collective-permute-done.7), channel_id=1, source_target_pairs={{0,4},{8,0},{16,8},{24,16},{28,24},{20,28},{12,20},{4,12},{1,5},{9... | collective-permute-start | bytes 1769480 | tf_op jit(solution)/shard_map/ppermute | solution.py:114
  81.5 16.2 %collective-permute-start.10 = (bf16[192,1536]{1,0:T(8,128)(2,1)S(1)}, bf16[192,1536]{1,0:T(8,128)(2,1)S(1)}, u32[]{:S(2)}, u32[]{:S(2)}) collective-permute-start(bf16[192,1536]{1,0:T(8,128)(2,1)S(1)} %collective-permute-done.8), channel_id=1, source_target_pairs={{0,8},{8,16},{16,24},{24,28},{28,20},{20,12},{12,4},{4,0},{1,9},{9... | collective-permute-start | bytes 1769480 | tf_op jit(solution)/shard_map/ppermute | solution.py:112
  119.3 5.8 %collective-permute-start.11 = (bf16[2,3,16,1536]{3,2,1,0:T(8,128)(2,1)}, bf16[2,3,16,1536]{3,2,1,0:T(8,128)(2,1)}, u32[]{:S(2)}, u32[]{:S(2)}) collective-permute-start(bf16[2,3,16,1536]{3,2,1,0:T(8,128)(2,1)} %dynamic-slice_bitcast_fusion), channel_id=1, source_target_pairs={{0,1},{1,0},{2,3},{3,2},{4,5},{5,4},{6,7},{7,6},{8,9},{9,8},{10,11... | collective-permute-start | bytes 884744 | tf_op jit(solution)/shard_map/ppermute | solution.py:69
  123.7 7.7 %collective-permute-start.18 = (bf16[192,512]{1,0:T(8,128)(2,1)}, bf16[192,512]{1,0:T(8,128)(2,1)}, u32[]{:S(2)}, u32[]{:S(2)}) collective-permute-start(bf16[192,512]{1,0:T(8,128)(2,1)} %get-tuple-element.142), channel_id=1, source_target_pairs={{0,8},{8,16},{16,24},{24,28},{28,20},{20,12},{12,4},{4,0},{1,9},{9... | collective-permute-start | bytes 589832 | tf_op jit(solution)/shard_map/ppermute | solution.py:145
  127.0 9.4 %collective-permute-start.12 = (f32[1,3,16,1536]{3,2,1,0:T(8,128)}, f32[1,3,16,1536]{3,2,1,0:T(8,128)}, u32[]{:S(2)}, u32[]{:S(2)}) collective-permute-start(f32[1,3,16,1536]{3,2,1,0:T(8,128)} %constant_dynamic-slice_fusion), channel_id=1, source_target_pairs={{0,2},{1,3},{2,0},{3,1},{4,6},{5,7},{6,4},{7,5},{8,10},{9,11},{10,... | collective-permute-start | bytes 884744 | tf_op jit(solution)/shard_map/ppermute | solution.py:69
  130.7 17.6 %collective-permute-start.15 = (bf16[192,512]{1,0:T(8,128)(2,1)}, bf16[192,512]{1,0:T(8,128)(2,1)}, u32[]{:S(2)}, u32[]{:S(2)}) collective-permute-start(bf16[192,512]{1,0:T(8,128)(2,1)} %get-tuple-element.141), channel_id=1, source_target_pairs={{0,4},{8,0},{16,8},{24,16},{28,24},{20,28},{12,20},{4,12},{1,5},{9... | collective-permute-start | bytes 589832 | tf_op jit(solution)/shard_map/ppermute | solution.py:147
  133.1 15.3 %collective-permute-start.19 = (bf16[192,512]{1,0:T(8,128)(2,1)}, bf16[192,512]{1,0:T(8,128)(2,1)}, u32[]{:S(2)}, u32[]{:S(2)}) collective-permute-start(bf16[192,512]{1,0:T(8,128)(2,1)} %fusion.21), channel_id=1, source_target_pairs={{0,8},{8,16},{16,24},{24,28},{28,20},{20,12},{12,4},{4,0},{1,9},{9... | collective-permute-start | bytes 589832 | tf_op jit(solution)/shard_map/ppermute | solution.py:145
  142.5 3.6 %collective-permute-start.22 = (f32[37632]{0:T(1024)S(1)}, f32[37632]{0:T(1024)S(1)}, u32[]{:S(2)}, u32[]{:S(2)}) collective-permute-start(f32[37632]{0:T(1024)S(1)} %get-tuple-element.107), channel_id=1, source_target_pairs={{0,1},{1,0},{2,3},{3,2},{4,5},{5,4},{6,7},{7,6},{8,9},{9,8},{10,11... | collective-permute-start | bytes 451592 | tf_op jit(solution)/shard_map/ppermute | solution.py:49
  146.7 4.9 %collective-permute-start.23 = (f32[18816]{0:T(1024)S(1)}, f32[18816]{0:T(1024)S(1)}, u32[]{:S(2)}, u32[]{:S(2)}) collective-permute-start(f32[18816]{0:T(1024)S(1)} %get-tuple-element.111), channel_id=1, source_target_pairs={{0,2},{1,3},{2,0},{3,1},{4,6},{5,7},{6,4},{7,5},{8,10},{9,11},{10,... | collective-permute-start | bytes 225800 | tf_op jit(solution)/shard_map/ppermute | solution.py:49
  149.5 35.8 %collective-permute-start.16 = (bf16[192,512]{1,0:T(8,128)(2,1)S(1)}, bf16[192,512]{1,0:T(8,128)(2,1)S(1)}, u32[]{:S(2)}, u32[]{:S(2)}) collective-permute-start(bf16[192,512]{1,0:T(8,128)(2,1)S(1)} %get-tuple-element.139), channel_id=1, source_target_pairs={{0,4},{8,0},{16,8},{24,16},{28,24},{20,28},{12,20},{4,12},{1,5},{9... | collective-permute-start | bytes 589832 | tf_op jit(solution)/shard_map/ppermute | solution.py:147
  150.7 34.6 %collective-permute-start.20 = (bf16[192,512]{1,0:T(8,128)(2,1)S(1)}, bf16[192,512]{1,0:T(8,128)(2,1)S(1)}, u32[]{:S(2)}, u32[]{:S(2)}) collective-permute-start(bf16[192,512]{1,0:T(8,128)(2,1)S(1)} %get-tuple-element.140), channel_id=1, source_target_pairs={{0,8},{8,16},{16,24},{24,28},{28,20},{20,12},{12,4},{4,0},{1,9},{9... | collective-permute-start | bytes 589832 | tf_op jit(solution)/shard_map/ppermute | solution.py:145
  151.9 9.6 %collective-permute-start.24 = (f32[9408]{0:T(1024)S(1)}, f32[9408]{0:T(1024)S(1)}, u32[]{:S(2)}, u32[]{:S(2)}) collective-permute-start(f32[9408]{0:T(1024)S(1)} %get-tuple-element.120), channel_id=1, source_target_pairs={{0,4},{4,0},{8,12},{12,8},{16,20},{20,16},{24,28},{28,24},{1,5},{5... | collective-permute-start | bytes 112904 | tf_op jit(solution)/shard_map/ppermute | solution.py:49
  161.8 5.2 %collective-permute-start.25 = (f32[4704]{0:T(1024)S(1)}, f32[4704]{0:T(1024)S(1)}, u32[]{:S(2)}, u32[]{:S(2)}) collective-permute-start(f32[4704]{0:T(1024)S(1)} %get-tuple-element.122), channel_id=1, source_target_pairs={{0,8},{4,12},{8,0},{12,4},{16,24},{20,28},{24,16},{28,20},{1,9},{5... | collective-permute-start | bytes 56456 | tf_op jit(solution)/shard_map/ppermute | solution.py:49
  167.2 4.8 %collective-permute-start.26 = (f32[2352]{0:T(1024)S(1)}, f32[2352]{0:T(1024)S(1)}, u32[]{:S(2)}, u32[]{:S(2)}) collective-permute-start(f32[2352]{0:T(1024)S(1)} %get-tuple-element.124), channel_id=1, source_target_pairs={{0,16},{4,20},{8,24},{12,28},{16,0},{20,4},{24,8},{28,12},{1,17},{... | collective-permute-start | bytes 28232 | tf_op jit(solution)/shard_map/ppermute | solution.py:49
  171.9 10.0 %collective-permute-start.27 = (f32[2352]{0:T(1024)S(1)}, f32[2352]{0:T(1024)S(1)}, u32[]{:S(2)}, u32[]{:S(2)}) collective-permute-start(f32[2352]{0:T(1024)S(1)} %add.876), channel_id=1, source_target_pairs={{0,16},{4,20},{8,24},{12,28},{16,0},{20,4},{24,8},{28,12},{1,17},{... | collective-permute-start | bytes 28232 | tf_op jit(solution)/shard_map/ppermute | solution.py:52
  179.3 8.5 %collective-permute-start.13 = (bf16[3,16,1536]{2,1,0:T(8,128)(2,1)S(1)}, bf16[3,16,1536]{2,1,0:T(8,128)(2,1)S(1)}, u32[]{:S(2)}, u32[]{:S(2)}) collective-permute-start(bf16[3,16,1536]{2,1,0:T(8,128)(2,1)S(1)} %get-tuple-element.130), channel_id=1, source_target_pairs={{0,1},{1,2},{2,3},{4,5},{5,6},{6,7},{8,9},{9,10},{10,11},{12,13},{... | collective-permute-start | bytes 442376 | tf_op jit(solution)/shard_map/ppermute | solution.py:16
  180.6 7.2 %collective-permute-start.14 = (bf16[3,16,1536]{2,1,0:T(8,128)(2,1)S(1)}, bf16[3,16,1536]{2,1,0:T(8,128)(2,1)S(1)}, u32[]{:S(2)}, u32[]{:S(2)}) collective-permute-start(bf16[3,16,1536]{2,1,0:T(8,128)(2,1)S(1)} %get-tuple-element.130), channel_id=1, source_target_pairs={{1,0},{2,1},{3,2},{5,4},{6,5},{7,6},{9,8},{10,9},{11,10},{13,12},{... | collective-permute-start | bytes 442376 | tf_op jit(solution)/shard_map/ppermute | solution.py:19
  182.3 5.2 %collective-permute-start.28 = (f32[4704]{0:T(1024)S(1)}, f32[4704]{0:T(1024)S(1)}, u32[]{:S(2)}, u32[]{:S(2)}) collective-permute-start(f32[4704]{0:T(1024)S(1)} %maximum_select_fusion.6), channel_id=1, source_target_pairs={{0,8},{4,12},{8,0},{12,4},{16,24},{20,28},{24,16},{28,20},{1,9},{5... | collective-permute-start | bytes 56456 | tf_op jit(solution)/shard_map/ppermute | solution.py:52
  185.4 14.8 %collective-permute-start.17 = (bf16[192,512]{1,0:T(8,128)(2,1)S(1)}, bf16[192,512]{1,0:T(8,128)(2,1)S(1)}, u32[]{:S(2)}, u32[]{:S(2)}) collective-permute-start(bf16[192,512]{1,0:T(8,128)(2,1)S(1)} %get-tuple-element.137), channel_id=1, source_target_pairs={{0,4},{8,0},{16,8},{24,16},{28,24},{20,28},{12,20},{4,12},{1,5},{9... | collective-permute-start | bytes 589832 | tf_op jit(solution)/shard_map/ppermute | solution.py:147
  185.6 14.6 %collective-permute-start.21 = (bf16[192,512]{1,0:T(8,128)(2,1)S(1)}, bf16[192,512]{1,0:T(8,128)(2,1)S(1)}, u32[]{:S(2)}, u32[]{:S(2)}) collective-permute-start(bf16[192,512]{1,0:T(8,128)(2,1)S(1)} %get-tuple-element.138), channel_id=1, source_target_pairs={{0,8},{8,16},{16,24},{24,28},{28,20},{20,12},{12,4},{4,0},{1,9},{9... | collective-permute-start | bytes 589832 | tf_op jit(solution)/shard_map/ppermute | solution.py:145
  187.6 4.9 %collective-permute-start.29 = (f32[9408]{0:T(1024)S(1)}, f32[9408]{0:T(1024)S(1)}, u32[]{:S(2)}, u32[]{:S(2)}) collective-permute-start(f32[9408]{0:T(1024)S(1)} %maximum_select_fusion.5), channel_id=1, source_target_pairs={{0,4},{4,0},{8,12},{12,8},{16,20},{20,16},{24,28},{28,24},{1,5},{5... | collective-permute-start | bytes 112904 | tf_op jit(solution)/shard_map/ppermute | solution.py:52
  192.6 7.5 %collective-permute-start.30 = (f32[18816]{0:T(1024)S(1)}, f32[18816]{0:T(1024)S(1)}, u32[]{:S(2)}, u32[]{:S(2)}) collective-permute-start(f32[18816]{0:T(1024)S(1)} %maximum_select_fusion.4), channel_id=1, source_target_pairs={{0,2},{1,3},{2,0},{3,1},{4,6},{5,7},{6,4},{7,5},{8,10},{9,11},{10,... | collective-permute-start | bytes 225800 | tf_op jit(solution)/shard_map/ppermute | solution.py:52
  200.1 1.4 collective-permute-start.31
  (70 other events, 794.6 us)
Sparse Core Ops, SparseCore 0:
  125.2 84.0 reduce-scatter.1

commit v9 on v7

--- a/solution.py
+++ b/solution.py
@@ -284,9 +284,10 @@
     w_term = lax.dot_general(
         flat, dpre, (((0,), (0,)), ((), ())), preferred_element_type=jnp.float32
     )
-    up_grad = lax.psum_scatter(
-        w_term.astype(jnp.bfloat16), "fsdp", scatter_dimension=0, tiled=True
-    ).astype(jnp.float32)
+    n_fsdp = lax.axis_size("fsdp")
+    up_grad = ring_reduce_scatter(
+        w_term.astype(jnp.bfloat16).reshape((n_fsdp, chans // n_fsdp, -1)), "fsdp", ring
+    )
     dpre_rows = dpre.reshape(height, cols, -1)
     group_terms = jnp.einsum(
         "hwf,cf->hwc", dpre_rows, columns, preferred_element_type=jnp.float32
@@ -301,7 +302,9 @@
     grad_pad = extended(activation_gradient, (("rows", 0),), 3)
     dframe = back_conv(grad_pad, kernel).astype(jnp.bfloat16)
     kernel_local = kern_grad(padded, activation_gradient)
-    kernel_total = tree_allreduce(kernel_local, ("rows", "fsdp"))
+    n_rows = lax.axis_size("rows")
+    kernel_part = tree_reduce_scatter(kernel_local.reshape(n_rows, -1), "rows")
+    kernel_total = tree_all_gather(lax.psum(kernel_part, "fsdp"), "rows").reshape(kernel_local.shape)
     activation = output.reshape(1, height, cols, -1)
     return (activation, dframe.reshape((1,) + dframe.shape), up_grad, kernel_total)
 

time: 216 us -> 277 us (1.28)
  waiting for transfers between devices: 91.7 us -> 128 us
  between operations: 35 us -> 56.1 us
  other arithmetic: 17.9 us -> 24.5 us
    psum x0 -> x1, waiting for transfers between devices: none -> 65.4 us  [body(): lax.psum(kernel_part, 'fsdp')]
    reduce_scatter x1 -> x0, waiting for transfers between devices: 27.9 us -> none  [body(): lax.psum_scatter(w_term.astype(jnp.bfloat16), 'fsdp', scatter_dimension=0...]
    ppermute x10 -> x7, starting transfers between devices: 15.7 us -> 7.94 us  [the longest x4 4.56 us: ring_reduce_scatter(): cw = lax.ppermute(cw, axis, forward)]
    ppermute x2 -> x4, starting transfers between devices: 1.77 us -> 5.55 us  [tree_reduce_scatter(): lax.ppermute(give, axis, perm).astype(jnp.float32)]
    convert_element_type x1 -> x3, other arithmetic: 2.21 us -> 5.29 us  [the longest x2 3.1 us: ring_reduce_scatter(): (ccw.astype(jnp.float32) + term(s - behind).astype(jnp.float32)).astype(t...]
    ppermute x2 -> x4, waiting for transfers between devices: 8.31 us -> 6.24 us  [tree_reduce_scatter(): lax.ppermute(give, axis, perm).astype(jnp.float32)]
    ppermute x2 -> x4, starting transfers between devices: 4.13 us -> 5.65 us  [tree_all_gather(): other = lax.ppermute(data, axis, perm)]
    ppermute x10 -> x7, waiting for transfers between devices: 25.3 us -> 26.4 us  [the longest x3 23.4 us: ring_reduce_scatter(): ccw = lax.ppermute(ccw, axis, backward)]
  transfers between devices with their start and end apart: 26 -> 27, of which waited for: 19 -> 16; matrix products, arithmetic and copies ran while one was open for 13% -> 11% of each run, Pallas kernels for 0% -> 0%
where the time goes in v9:
time: 277 us; the launch traced here: 276 us
  waiting for transfers between devices  128 us (46%)
  between operations  56.1 us (20%)
  starting transfers between devices  34.7 us (13%)
  other arithmetic  24.5 us (9%)
  local copies, waits for them, and re-layouts  15.5 us (6%)
  matrix products  10.3 us (4%)
  blocking collectives  6.37 us (2%)
    psum x1, waiting for transfers between devices, body(): lax.psum(kernel_part, 'fsdp')  65.4 us
    ppermute x3, waiting for transfers between devices, ring_reduce_scatter(): ccw = lax.ppermute(ccw, axis, backward)  23.4 us
    ppermute x4, waiting for transfers between devices, ring_all_gather(): cw = lax.ppermute(cw, axis, forward)  20.5 us
    ppermute x4, starting transfers between devices, ring_all_gather(): cw = lax.ppermute(cw, axis, forward)  9.53 us
    ppermute x4, waiting for transfers between devices, tree_all_gather(): other = lax.ppermute(data, axis, perm)  7.08 us
    psum x1, blocking collectives, body(): norm_total = lax.psum(jnp.sum(norms), 'rows')  6.37 us
    ppermute x4, waiting for transfers between devices, tree_reduce_scatter(): lax.ppermute(give, axis, perm).astype(jnp.float32)  6.24 us
    ppermute x4, starting transfers between devices, tree_all_gather(): other = lax.ppermute(data, axis, perm)  5.65 us
  transfers between devices with their start and end apart: 27, of which 16 were waited for; matrix products, arithmetic and copies ran while one was open for 11% of the time, Pallas kernels for 0%

profile of v9, /device:TPU:0, one launch (start us, length us, event | category | flops | bytes accessed | tf_op | source)
XLA Modules:
  0.0 275.6 jit_solution(5724363738028582769)
XLA Ops:
  7.2 3.1 %collective-permute-start = (bf16[192,1536]{1,0:T(8,128)(2,1)}, bf16[192,1536]{1,0:T(8,128)(2,1)S(1)}, u32[]{:S(2)}, u32[]{:S(2)}) collective-permute-start(bf16[192,1536]{1,0:T(8,128)(2,1)} %param.19), channel_id=1, source_target_pairs={{0,8},{8,16},{16,24},{24,28},{28,20},{20,12},{12,4},{4,0},{1,9},{9... | collective-permute-start | bytes 1769480 | tf_op jit(solution)/shard_map/ppermute | solution.py:112
  10.3 1.2 dynamic_slice.96
  22.8 2.0 fusion.160
  33.7 1.7 slice_reduce_fusion.48
  35.4 1.8 slice_reduce_fusion.47
  41.8 1.4 slice_reduce_fusion.46
  45.3 1.5 collective-permute-start.2
  46.8 1.3 collective-permute-start.3
  48.1 1.9 collective-permute-start.6
  50.2 1.8 collective-permute-done.3
  52.5 3.4 %fusion.158 = (f32[3,16]{1,0:T(4,128)S(1)}, f32[3,16,1536]{2,1,0:T(8,128)S(1)}) fusion(f32[1536]{0:T(1024)S(1)} %get-tuple-element.105, bf16[9,22,1536]{2,1,0:T(8,128)(2,1)S(1)} %select_maximum_fusion.2, f32[1536]{0:T(1024)S(1)} %get-tuple-element.106, f32[1536]{0:T(1024)S(1)} %get-tuple-element.59, f32[1536]{0:T(1024)S(1)} %get-tuple-element.60, ...), kind=kLoop, calls=%fused_computation.380 | loop fusion | flops 10911696 | bytes 7827648 | tf_op jit(solution)/shard_map/reduce_sum | solution.py:214
  56.3 4.1 %collective-permute-start.4 = (bf16[1,3,16,1536]{3,2,1,0:T(8,128)(2,1)S(1)}, bf16[1,3,16,1536]{3,2,1,0:T(8,128)(2,1)S(1)}, u32[]{:S(2)}, u32[]{:S(2)}) collective-permute-start(bf16[1,3,16,1536]{3,2,1,0:T(8,128)(2,1)S(1)} %fusion.149), channel_id=1, source_target_pairs={{0,1},{1,0},{2,3},{3,2},{4,5},{5,4},{6,7},{7,6},{8,9},{9,8},{10,11... | collective-permute-start | bytes 442376 | tf_op jit(solution)/shard_map/ppermute | solution.py:168
  60.4 1.0 collective-permute-done.4
  62.1 2.1 collective-permute-start.8
  64.6 6.1 %collective-permute-done.5 = bf16[2,3,16,1536]{3,2,1,0:T(8,128)(2,1)S(1)} collective-permute-done((bf16[2,3,16,1536]{3,2,1,0:T(8,128)(2,1)S(1)}, bf16[2,3,16,1536]{3,2,1,0:T(8,128)(2,1)S(1)}, u32[]{:S(2)}, u32[]{:S(2)}) %collective-permute-start.5) | collective-permute-done | bytes 294944 | tf_op jit(solution)/shard_map/ppermute | solution.py:168
  70.8 6.2 %collective-permute-done.8 = bf16[192,1536]{1,0:T(8,128)(2,1)S(1)} collective-permute-done((bf16[192,1536]{1,0:T(8,128)(2,1)S(1)}, bf16[192,1536]{1,0:T(8,128)(2,1)S(1)}, u32[]{:S(2)}, u32[]{:S(2)}) %collective-permute-start.8) | collective-permute-done | bytes 589856 | tf_op jit(solution)/shard_map/ppermute | solution.py:112
  77.0 2.4 collective-permute-start.10
  80.0 13.7 %collective-permute-done.10 = bf16[192,1536]{1,0:T(8,128)(2,1)S(1)} collective-permute-done((bf16[192,1536]{1,0:T(8,128)(2,1)S(1)}, bf16[192,1536]{1,0:T(8,128)(2,1)S(1)}, u32[]{:S(2)}, u32[]{:S(2)}) %collective-permute-start.10) | collective-permute-done | bytes 589856 | tf_op jit(solution)/shard_map/ppermute | solution.py:112
  93.8 4.8 %fusion.4 = (f32[1536]{0:T(1024)S(1)}, f32[1536]{0:T(1024)S(1)}, f32[192,1536]{1,0:T(8,128)}, f32[192,1536]{1,0:T(8,128)}) fusion(bf16[1,12,16,1536]{3,2,1,0:T(8,128)(2,1)S(1)} %copy-done.4, f32[1536]{0:T(1024)S(1)} %copy-done.44, bf16[192,1536]{1,0:T(8,128)(2,1)S(1)} %bitcast.106, bf16[1536,1536]{1,0:T(8,128)(2,1)S(1)} %bitcast.104), kind=kOutput, calls=%fused_computation.63 | convolution fusion | flops 926610432 | bytes 8275968 | tf_op jit(solution)/shard_map/dot_general | solution.py:271
  99.2 6.4 %all-reduce.2 = (f32[]{:T(128)}, f32[]{:T(128)}) all-reduce(f32[]{:T(128)} %get-tuple-element.117, f32[]{:T(128)} %get-tuple-element.116), channel_id=1, replica_groups=mesh['fsdp'=8,'rows'=4] {'rows'}, use_global_device_ids=true, to_apply=%region_4.5 | all-reduce | flops 2 | bytes 16 | tf_op jit(solution)/shard_map/psum | solution.py:276
  106.9 3.4 %fusion.3 = (bf16[192,1536]{1,0:T(8,128)(2,1)S(1)}, bf16[192,1536]{1,0:T(8,128)(2,1)}) fusion(f32[192,1536]{1,0:T(8,128)} %get-tuple-element.155, f32[192,1536]{1,0:T(8,128)} %get-tuple-element.124, bf16[1,12,16,1536]{3,2,1,0:T(8,128)(2,1)} %param.23, f32[1536]{0:T(1024)S(1)} %get-tuple-element.139, f32[1536]{0:T(1024)S(1)} %get-tuple-element.122, ...), kind=kLoop, calls=%fused_computation.62 | loop fusion | flops 5603328 | bytes 4159488 | tf_op jit(solution)/shard_map/convert_element_type | solution.py:283
  110.3 4.0 %convolution_convert_fusion.1 = bf16[12,16,1536]{2,1,0:T(8,128)(2,1)S(1)} fusion(bf16[12,16,1536]{2,1,0:T(8,128)(2,1)S(1)} %bitcast.108, bf16[1536,1536,1]{1,0,2:T(8,128)(2,1)} %bitcast.105), kind=kOutput, calls=%fused_computation.52 | convolution fusion | flops 906264576 | bytes 5898240 | tf_op jit(solution)/shard_map/hwf,cf->hwc/dot_general | solution.py:292
  130.7 1.1 convert_add_fusion.6
  131.9 1.7 collective-permute-start.12
  133.6 1.4 convolution_convert_fusion
  135.1 1.0 dynamic-slice_bitcast_fusion.1
  136.1 1.8 collective-permute-start.18
  138.1 3.3 %collective-permute-done.12 = f32[1,3,16,1536]{3,2,1,0:T(8,128)S(1)} collective-permute-done((f32[1,3,16,1536]{3,2,1,0:T(8,128)S(1)}, f32[1,3,16,1536]{3,2,1,0:T(8,128)S(1)}, u32[]{:S(2)}, u32[]{:S(2)}) %collective-permute-start.12) | collective-permute-done | bytes 294944 | tf_op jit(solution)/shard_map/ppermute | solution.py:69
  141.6 0.9 fusion.146
  143.3 1.7 collective-permute-start.13
  145.0 1.3 collective-permute-start.14
  148.8 2.6 collective-permute-start.22
  151.9 2.2 fusion.13
  154.2 1.8 collective-permute-start.19
  156.1 1.2 collective-permute-start.23
  157.6 3.0 %collective-permute-done.23 = f32[1,18816]{1,0:T(1,128)S(1)} collective-permute-done((f32[1,18816]{1,0:T(1,128)S(1)}, f32[1,18816]{1,0:T(1,128)S(1)}, u32[]{:S(2)}, u32[]{:S(2)}) %collective-permute-start.23) | collective-permute-done | bytes 75296 | tf_op jit(solution)/shard_map/ppermute | solution.py:69
  161.4 3.7 %fusion.152 = bf16[1,3,16,1536]{3,2,1,0:T(8,128)(2,1)} fusion(f32[1536]{0:T(1024)} %copy-done.33, bf16[9,22,1536]{2,1,0:T(8,128)(2,1)S(1)} %select_maximum_fusion, f32[1536]{0:T(1024)} %copy-done.34, f32[1536]{0:T(1024)S(1)} %get-tuple-element.59, f32[1536]{0:T(1024)S(1)} %get-tuple-element.60, bf16[3,16,1536]{2,1,0:T(8,128)(2,1)S(1)} %collective-permute-done.13, ...), kind=kLoop, calls=%fused_computation.310 | loop fusion | flops 11132928 | bytes 7084032 | tf_op jit(solution)/shard_map/reshape | solution.py:309
  165.1 65.4 %all-reduce.5.cloned.1.call-done = f32[1,18816]{1,0:T(1,128)} async-done(((f32[1,18816]{1,0:T(1,128)}), f32[1,18816]{1,0:T(1,128)}) %all-reduce.5.cloned.1.call-update) | async-done | bytes 75280 | tf_op jit(solution)/shard_map/psum | solution.py:307
  230.5 1.6 fusion.15
  232.0 1.4 collective-permute-start.16
  234.4 1.5 collective-permute-start.25
  235.9 11.9 %collective-permute-done.16 = bf16[192,1536]{1,0:T(8,128)(2,1)S(1)} collective-permute-done((bf16[192,1536]{1,0:T(8,128)(2,1)S(1)}, bf16[192,1536]{1,0:T(8,128)(2,1)S(1)}, u32[]{:S(2)}, u32[]{:S(2)}) %collective-permute-start.16) | collective-permute-done | bytes 589856 | tf_op jit(solution)/shard_map/ppermute | solution.py:147
  247.8 1.1 collective-permute-done.20
  248.9 1.5 fusion.14
  250.4 1.7 collective-permute-start.17
  253.6 11.5 %collective-permute-done.17 = bf16[192,1536]{1,0:T(8,128)(2,1)S(1)} collective-permute-done((bf16[192,1536]{1,0:T(8,128)(2,1)S(1)}, bf16[192,1536]{1,0:T(8,128)(2,1)S(1)}, u32[]{:S(2)}, u32[]{:S(2)}) %collective-permute-start.17) | collective-permute-done | bytes 589856 | tf_op jit(solution)/shard_map/ppermute | solution.py:147
  265.1 1.4 collective-permute-done.21
  266.4 2.3 fusion.16
  (203 shorter events, 14.3 us)
Async XLA Ops:
  7.2 223.3 %all-reduce.5.cloned.1.call-start = ((), (), s32[]{:S(2)}) async-start(), calls=%async_computation | async-start | bytes 150528 | tf_op jit(solution)/shard_map/psum | solution.py:307
  7.2 37.2 %collective-permute-start = (bf16[192,1536]{1,0:T(8,128)(2,1)}, bf16[192,1536]{1,0:T(8,128)(2,1)S(1)}, u32[]{:S(2)}, u32[]{:S(2)}) collective-permute-start(bf16[192,1536]{1,0:T(8,128)(2,1)} %param.19), channel_id=1, source_target_pairs={{0,8},{8,16},{16,24},{24,28},{28,20},{20,12},{12,4},{4,0},{1,9},{9... | collective-permute-start | bytes 1769480 | tf_op jit(solution)/shard_map/ppermute | solution.py:112
  10.3 34.2 %collective-permute-start.1 = (bf16[192,1536]{1,0:T(8,128)(2,1)}, bf16[192,1536]{1,0:T(8,128)(2,1)S(1)}, u32[]{:S(2)}, u32[]{:S(2)}) collective-permute-start(bf16[192,1536]{1,0:T(8,128)(2,1)} %param.19), channel_id=1, source_target_pairs={{0,4},{8,0},{16,8},{24,16},{28,24},{20,28},{12,20},{4,12},{1,5},{9... | collective-permute-start | bytes 1769480 | tf_op jit(solution)/shard_map/ppermute | solution.py:114
  37.2 15.0 %copy-start.8 = (f32[1536]{0:T(1024)}, f32[1536]{0:T(1024)S(1)}, u32[]{:S(2)}) copy-start(f32[1536]{0:T(1024)S(1)} %get-tuple-element.87) | copy-start | bytes 18436
  37.2 15.0 %copy-start.10 = (f32[1536]{0:T(1024)}, f32[1536]{0:T(1024)S(1)}, u32[]{:S(2)}) copy-start(f32[1536]{0:T(1024)S(1)} %get-tuple-element.88) | copy-start | bytes 18436
  37.3 15.0 %copy-start.12 = (f32[1536]{0:T(1024)}, f32[1536]{0:T(1024)S(1)}, u32[]{:S(2)}) copy-start(f32[1536]{0:T(1024)S(1)} %get-tuple-element.89) | copy-start | bytes 18436
  37.3 15.0 %copy-start.14 = (f32[1536]{0:T(1024)}, f32[1536]{0:T(1024)S(1)}, u32[]{:S(2)}) copy-start(f32[1536]{0:T(1024)S(1)} %get-tuple-element.90) | copy-start | bytes 18436
  37.3 15.0 %copy-start.16 = (f32[1536]{0:T(1024)}, f32[1536]{0:T(1024)S(1)}, u32[]{:S(2)}) copy-start(f32[1536]{0:T(1024)S(1)} %get-tuple-element.91) | copy-start | bytes 18436
  37.3 15.0 %copy-start.18 = (f32[1536]{0:T(1024)}, f32[1536]{0:T(1024)S(1)}, u32[]{:S(2)}) copy-start(f32[1536]{0:T(1024)S(1)} %get-tuple-element.92) | copy-start | bytes 18436
  37.3 15.0 %copy-start.20 = (f32[1536]{0:T(1024)}, f32[1536]{0:T(1024)S(1)}, u32[]{:S(2)}) copy-start(f32[1536]{0:T(1024)S(1)} %get-tuple-element.93) | copy-start | bytes 18436
  37.3 15.0 %copy-start.22 = (f32[1536]{0:T(1024)}, f32[1536]{0:T(1024)S(1)}, u32[]{:S(2)}) copy-start(f32[1536]{0:T(1024)S(1)} %get-tuple-element.94) | copy-start | bytes 18436
  37.3 15.0 %copy-start.23 = (f32[1536]{0:T(1024)}, f32[1536]{0:T(1024)S(1)}, u32[]{:S(2)}) copy-start(f32[1536]{0:T(1024)S(1)} %get-tuple-element.95) | copy-start | bytes 18436
  43.2 9.1 %copy-start.24 = (f32[1536]{0:T(1024)}, f32[1536]{0:T(1024)S(1)}, u32[]{:S(2)}) copy-start(f32[1536]{0:T(1024)S(1)} %get-tuple-element.96) | copy-start | bytes 18436
  43.2 9.1 %copy-start.25 = (f32[1536]{0:T(1024)}, f32[1536]{0:T(1024)S(1)}, u32[]{:S(2)}) copy-start(f32[1536]{0:T(1024)S(1)} %get-tuple-element.97) | copy-start | bytes 18436
  43.2 9.1 %copy-start.26 = (f32[1536]{0:T(1024)}, f32[1536]{0:T(1024)S(1)}, u32[]{:S(2)}) copy-start(f32[1536]{0:T(1024)S(1)} %get-tuple-element.98) | copy-start | bytes 18436
  43.2 9.1 %copy-start.27 = (f32[1536]{0:T(1024)}, f32[1536]{0:T(1024)S(1)}, u32[]{:S(2)}) copy-start(f32[1536]{0:T(1024)S(1)} %get-tuple-element.99) | copy-start | bytes 18436
  43.2 9.1 %copy-start.28 = (f32[1536]{0:T(1024)}, f32[1536]{0:T(1024)S(1)}, u32[]{:S(2)}) copy-start(f32[1536]{0:T(1024)S(1)} %get-tuple-element.100) | copy-start | bytes 18436
  43.2 9.1 %copy-start.29 = (f32[1536]{0:T(1024)}, f32[1536]{0:T(1024)S(1)}, u32[]{:S(2)}) copy-start(f32[1536]{0:T(1024)S(1)} %get-tuple-element.101) | copy-start | bytes 18436
  43.3 9.1 %copy-start.30 = (f32[1536]{0:T(1024)}, f32[1536]{0:T(1024)S(1)}, u32[]{:S(2)}) copy-start(f32[1536]{0:T(1024)S(1)} %get-tuple-element.102) | copy-start | bytes 18436
  43.3 9.1 %copy-start.31 = (f32[1536]{0:T(1024)}, f32[1536]{0:T(1024)S(1)}, u32[]{:S(2)}) copy-start(f32[1536]{0:T(1024)S(1)} %get-tuple-element.103) | copy-start | bytes 18436
  43.3 9.1 %copy-start.32 = (f32[1536]{0:T(1024)}, f32[1536]{0:T(1024)S(1)}, u32[]{:S(2)}) copy-start(f32[1536]{0:T(1024)S(1)} %get-tuple-element.104) | copy-start | bytes 18436
  45.3 4.9 %collective-permute-start.2 = (bf16[3,16,1536]{2,1,0:T(8,128)(2,1)S(1)}, bf16[3,16,1536]{2,1,0:T(8,128)(2,1)S(1)}, u32[]{:S(2)}, u32[]{:S(2)}) collective-permute-start(bf16[3,16,1536]{2,1,0:T(8,128)(2,1)S(1)} %bitcast.109), channel_id=1, source_target_pairs={{0,1},{1,2},{2,3},{4,5},{5,6},{6,7},{8,9},{9,10},{10,11},{12,13},{... | collective-permute-start | bytes 442376 | tf_op jit(solution)/shard_map/ppermute | solution.py:16
  46.8 5.3 %collective-permute-start.3 = (bf16[3,16,1536]{2,1,0:T(8,128)(2,1)S(1)}, bf16[3,16,1536]{2,1,0:T(8,128)(2,1)S(1)}, u32[]{:S(2)}, u32[]{:S(2)}) collective-permute-start(bf16[3,16,1536]{2,1,0:T(8,128)(2,1)S(1)} %bitcast.110), channel_id=1, source_target_pairs={{1,0},{2,1},{3,2},{5,4},{6,5},{7,6},{9,8},{10,9},{11,10},{13,12},{... | collective-permute-start | bytes 442376 | tf_op jit(solution)/shard_map/ppermute | solution.py:19
  48.1 14.0 %collective-permute-start.6 = (bf16[192,1536]{1,0:T(8,128)(2,1)S(1)}, bf16[192,1536]{1,0:T(8,128)(2,1)S(1)}, u32[]{:S(2)}, u32[]{:S(2)}) collective-permute-start(bf16[192,1536]{1,0:T(8,128)(2,1)S(1)} %collective-permute-done), channel_id=1, source_target_pairs={{0,8},{8,16},{16,24},{24,28},{28,20},{20,12},{12,4},{4,0},{1,9},{9... | collective-permute-start | bytes 1769480 | tf_op jit(solution)/shard_map/ppermute | solution.py:112
  49.9 14.5 %collective-permute-start.7 = (bf16[192,1536]{1,0:T(8,128)(2,1)S(1)}, bf16[192,1536]{1,0:T(8,128)(2,1)S(1)}, u32[]{:S(2)}, u32[]{:S(2)}) collective-permute-start(bf16[192,1536]{1,0:T(8,128)(2,1)S(1)} %collective-permute-done.1), channel_id=1, source_target_pairs={{0,4},{8,0},{16,8},{24,16},{28,24},{20,28},{12,20},{4,12},{1,5},{9... | collective-permute-start | bytes 1769480 | tf_op jit(solution)/shard_map/ppermute | solution.py:114
  56.3 5.1 %collective-permute-start.4 = (bf16[1,3,16,1536]{3,2,1,0:T(8,128)(2,1)S(1)}, bf16[1,3,16,1536]{3,2,1,0:T(8,128)(2,1)S(1)}, u32[]{:S(2)}, u32[]{:S(2)}) collective-permute-start(bf16[1,3,16,1536]{3,2,1,0:T(8,128)(2,1)S(1)} %fusion.149), channel_id=1, source_target_pairs={{0,1},{1,0},{2,3},{3,2},{4,5},{5,4},{6,7},{7,6},{8,9},{9,8},{10,11... | collective-permute-start | bytes 442376 | tf_op jit(solution)/shard_map/ppermute | solution.py:168
  61.4 9.3 %collective-permute-start.5 = (bf16[2,3,16,1536]{3,2,1,0:T(8,128)(2,1)S(1)}, bf16[2,3,16,1536]{3,2,1,0:T(8,128)(2,1)S(1)}, u32[]{:S(2)}, u32[]{:S(2)}) collective-permute-start(bf16[2,3,16,1536]{3,2,1,0:T(8,128)(2,1)S(1)} %maximum_select_fusion.2), channel_id=1, source_target_pairs={{0,2},{1,3},{2,0},{3,1},{4,6},{5,7},{6,4},{7,5},{8,10},{9,11},{10,... | collective-permute-start | bytes 884744 | tf_op jit(solution)/shard_map/ppermute | solution.py:168
  62.1 14.9 %collective-permute-start.8 = (bf16[192,1536]{1,0:T(8,128)(2,1)S(1)}, bf16[192,1536]{1,0:T(8,128)(2,1)S(1)}, u32[]{:S(2)}, u32[]{:S(2)}) collective-permute-start(bf16[192,1536]{1,0:T(8,128)(2,1)S(1)} %collective-permute-done.6), channel_id=1, source_target_pairs={{0,8},{8,16},{16,24},{24,28},{28,20},{20,12},{12,4},{4,0},{1,9},{9... | collective-permute-start | bytes 1769480 | tf_op jit(solution)/shard_map/ppermute | solution.py:112
  64.5 15.4 %collective-permute-start.9 = (bf16[192,1536]{1,0:T(8,128)(2,1)S(1)}, bf16[192,1536]{1,0:T(8,128)(2,1)S(1)}, u32[]{:S(2)}, u32[]{:S(2)}) collective-permute-start(bf16[192,1536]{1,0:T(8,128)(2,1)S(1)} %collective-permute-done.7), channel_id=1, source_target_pairs={{0,4},{8,0},{16,8},{24,16},{28,24},{20,28},{12,20},{4,12},{1,5},{9... | collective-permute-start | bytes 1769480 | tf_op jit(solution)/shard_map/ppermute | solution.py:114
  77.0 16.7 %collective-permute-start.10 = (bf16[192,1536]{1,0:T(8,128)(2,1)S(1)}, bf16[192,1536]{1,0:T(8,128)(2,1)S(1)}, u32[]{:S(2)}, u32[]{:S(2)}) collective-permute-start(bf16[192,1536]{1,0:T(8,128)(2,1)S(1)} %collective-permute-done.8), channel_id=1, source_target_pairs={{0,8},{8,16},{16,24},{24,28},{28,20},{20,12},{12,4},{4,0},{1,9},{9... | collective-permute-start | bytes 1769480 | tf_op jit(solution)/shard_map/ppermute | solution.py:112
  79.5 14.3 %copy-start.4 = (bf16[1,12,16,1536]{3,2,1,0:T(8,128)(2,1)S(1)}, bf16[1,12,16,1536]{3,2,1,0:T(8,128)(2,1)}, u32[]{:S(2)}) copy-start(bf16[1,12,16,1536]{3,2,1,0:T(8,128)(2,1)} %param.23) | copy-start | bytes 1769476
  79.5 14.3 %copy-start.44 = (f32[1536]{0:T(1024)S(1)}, f32[1536]{0:T(1024)}, u32[]{:S(2)}) copy-start(f32[1536]{0:T(1024)} %param.20) | copy-start | bytes 18436
  93.8 13.2 %copy-start.42 = (f32[1536]{0:T(1024)S(1)}, f32[1536]{0:T(1024)}, u32[]{:S(2)}) copy-start(f32[1536]{0:T(1024)} %param.22) | copy-start | bytes 18436
  115.9 14.8 %collective-permute-start.11 = (bf16[2,3,16,1536]{3,2,1,0:T(8,128)(2,1)}, bf16[2,3,16,1536]{3,2,1,0:T(8,128)(2,1)}, u32[]{:S(2)}, u32[]{:S(2)}) collective-permute-start(bf16[2,3,16,1536]{3,2,1,0:T(8,128)(2,1)} %dynamic-slice_bitcast_fusion.2), channel_id=1, source_target_pairs={{0,1},{1,0},{2,3},{3,2},{4,5},{5,4},{6,7},{7,6},{8,9},{9,8},{10,11... | collective-permute-start | bytes 884744 | tf_op jit(solution)/shard_map/ppermute | solution.py:69
  131.9 9.5 %collective-permute-start.12 = (f32[1,3,16,1536]{3,2,1,0:T(8,128)S(1)}, f32[1,3,16,1536]{3,2,1,0:T(8,128)S(1)}, u32[]{:S(2)}, u32[]{:S(2)}) collective-permute-start(f32[1,3,16,1536]{3,2,1,0:T(8,128)S(1)} %constant_dynamic-slice_fusion.3), channel_id=1, source_target_pairs={{0,2},{1,3},{2,0},{3,1},{4,6},{5,7},{6,4},{7,5},{8,10},{9,11},{10,... | collective-permute-start | bytes 884744 | tf_op jit(solution)/shard_map/ppermute | solution.py:69
  136.1 15.9 %collective-permute-start.18 = (bf16[192,1536]{1,0:T(8,128)(2,1)}, bf16[192,1536]{1,0:T(8,128)(2,1)}, u32[]{:S(2)}, u32[]{:S(2)}) collective-permute-start(bf16[192,1536]{1,0:T(8,128)(2,1)} %get-tuple-element.132), channel_id=1, source_target_pairs={{0,8},{8,16},{16,24},{24,28},{28,20},{20,12},{12,4},{4,0},{1,9},{9... | collective-permute-start | bytes 1769480 | tf_op jit(solution)/shard_map/ppermute | solution.py:145
  137.9 92.6 %collective-permute-start.15 = (bf16[192,1536]{1,0:T(8,128)(2,1)S(1)}, bf16[192,1536]{1,0:T(8,128)(2,1)S(1)}, u32[]{:S(2)}, u32[]{:S(2)}) collective-permute-start(bf16[192,1536]{1,0:T(8,128)(2,1)S(1)} %get-tuple-element.131), channel_id=1, source_target_pairs={{0,4},{8,0},{16,8},{24,16},{28,24},{20,28},{12,20},{4,12},{1,5},{9... | collective-permute-start | bytes 1769480 | tf_op jit(solution)/shard_map/ppermute | solution.py:147
  143.3 14.1 %collective-permute-start.13 = (bf16[3,16,1536]{2,1,0:T(8,128)(2,1)S(1)}, bf16[3,16,1536]{2,1,0:T(8,128)(2,1)S(1)}, u32[]{:S(2)}, u32[]{:S(2)}) collective-permute-start(bf16[3,16,1536]{2,1,0:T(8,128)(2,1)S(1)} %get-tuple-element.120), channel_id=1, source_target_pairs={{0,1},{1,2},{2,3},{4,5},{5,6},{6,7},{8,9},{9,10},{10,11},{12,13},{... | collective-permute-start | bytes 442376 | tf_op jit(solution)/shard_map/ppermute | solution.py:16
  145.0 12.3 %collective-permute-start.14 = (bf16[3,16,1536]{2,1,0:T(8,128)(2,1)S(1)}, bf16[3,16,1536]{2,1,0:T(8,128)(2,1)S(1)}, u32[]{:S(2)}, u32[]{:S(2)}) collective-permute-start(bf16[3,16,1536]{2,1,0:T(8,128)(2,1)S(1)} %get-tuple-element.120), channel_id=1, source_target_pairs={{1,0},{2,1},{3,2},{5,4},{6,5},{7,6},{9,8},{10,9},{11,10},{13,12},{... | collective-permute-start | bytes 442376 | tf_op jit(solution)/shard_map/ppermute | solution.py:19
  148.8 7.2 %collective-permute-start.22 = (f32[2,18816]{1,0:T(2,128)S(1)}, f32[2,18816]{1,0:T(2,128)S(1)}, u32[]{:S(2)}, u32[]{:S(2)}) collective-permute-start(f32[2,18816]{1,0:T(2,128)S(1)} %bitcast.118), channel_id=1, source_target_pairs={{0,1},{1,0},{2,3},{3,2},{4,5},{5,4},{6,7},{7,6},{8,9},{9,8},{10,11... | collective-permute-start | bytes 451592 | tf_op jit(solution)/shard_map/ppermute | solution.py:69
  154.2 76.3 %collective-permute-start.19 = (bf16[192,1536]{1,0:T(8,128)(2,1)}, bf16[192,1536]{1,0:T(8,128)(2,1)S(1)}, u32[]{:S(2)}, u32[]{:S(2)}) collective-permute-start(bf16[192,1536]{1,0:T(8,128)(2,1)} %fusion.13), channel_id=1, source_target_pairs={{0,8},{8,16},{16,24},{24,28},{28,20},{20,12},{12,4},{4,0},{1,9},{9... | collective-permute-start | bytes 1769480 | tf_op jit(solution)/shard_map/ppermute | solution.py:145
  156.1 4.4 %collective-permute-start.23 = (f32[1,18816]{1,0:T(1,128)S(1)}, f32[1,18816]{1,0:T(1,128)S(1)}, u32[]{:S(2)}, u32[]{:S(2)}) collective-permute-start(f32[1,18816]{1,0:T(1,128)S(1)} %constant_dynamic-slice_fusion), channel_id=1, source_target_pairs={{0,2},{1,3},{2,0},{3,1},{4,6},{5,7},{6,4},{7,5},{8,10},{9,11},{10,... | collective-permute-start | bytes 225800 | tf_op jit(solution)/shard_map/ppermute | solution.py:69
  230.4 3.7 %collective-permute-start.24 = (f32[1,18816]{1,0:T(1,128)}, f32[1,18816]{1,0:T(1,128)S(1)}, u32[]{:S(2)}, u32[]{:S(2)}) collective-permute-start(f32[1,18816]{1,0:T(1,128)} %all-reduce.5.cloned.1.call-done), channel_id=1, source_target_pairs={{0,1},{1,0},{2,3},{3,2},{4,5},{5,4},{6,7},{7,6},{8,9},{9,8},{10,11... | collective-permute-start | bytes 225800 | tf_op jit(solution)/shard_map/ppermute | solution.py:168
  232.0 15.8 %collective-permute-start.16 = (bf16[192,1536]{1,0:T(8,128)(2,1)S(1)}, bf16[192,1536]{1,0:T(8,128)(2,1)S(1)}, u32[]{:S(2)}, u32[]{:S(2)}) collective-permute-start(bf16[192,1536]{1,0:T(8,128)(2,1)S(1)} %get-tuple-element.129), channel_id=1, source_target_pairs={{0,4},{8,0},{16,8},{24,16},{28,24},{20,28},{12,20},{4,12},{1,5},{9... | collective-permute-start | bytes 1769480 | tf_op jit(solution)/shard_map/ppermute | solution.py:147
  233.5 15.4 %collective-permute-start.20 = (bf16[192,1536]{1,0:T(8,128)(2,1)S(1)}, bf16[192,1536]{1,0:T(8,128)(2,1)S(1)}, u32[]{:S(2)}, u32[]{:S(2)}) collective-permute-start(bf16[192,1536]{1,0:T(8,128)(2,1)S(1)} %get-tuple-element.130), channel_id=1, source_target_pairs={{0,8},{8,16},{16,24},{24,28},{28,20},{20,12},{12,4},{4,0},{1,9},{9... | collective-permute-start | bytes 1769480 | tf_op jit(solution)/shard_map/ppermute | solution.py:145
  234.4 18.1 %collective-permute-start.25 = (f32[2,18816]{1,0:T(2,128)S(1)}, f32[2,18816]{1,0:T(2,128)S(1)}, u32[]{:S(2)}, u32[]{:S(2)}) collective-permute-start(f32[2,18816]{1,0:T(2,128)S(1)} %maximum_select_fusion.3), channel_id=1, source_target_pairs={{0,2},{1,3},{2,0},{3,1},{4,6},{5,7},{6,4},{7,5},{8,10},{9,11},{10,... | collective-permute-start | bytes 451592 | tf_op jit(solution)/shard_map/ppermute | solution.py:168
  250.4 14.6 %collective-permute-start.17 = (bf16[192,1536]{1,0:T(8,128)(2,1)S(1)}, bf16[192,1536]{1,0:T(8,128)(2,1)S(1)}, u32[]{:S(2)}, u32[]{:S(2)}) collective-permute-start(bf16[192,1536]{1,0:T(8,128)(2,1)S(1)} %get-tuple-element.127), channel_id=1, source_target_pairs={{0,4},{8,0},{16,8},{24,16},{28,24},{20,28},{12,20},{4,12},{1,5},{9... | collective-permute-start | bytes 1769480 | tf_op jit(solution)/shard_map/ppermute | solution.py:147
  252.1 14.3 %collective-permute-start.21 = (bf16[192,1536]{1,0:T(8,128)(2,1)S(1)}, bf16[192,1536]{1,0:T(8,128)(2,1)S(1)}, u32[]{:S(2)}, u32[]{:S(2)}) collective-permute-start(bf16[192,1536]{1,0:T(8,128)(2,1)S(1)} %get-tuple-element.128), channel_id=1, source_target_pairs={{0,8},{8,16},{16,24},{24,28},{28,20},{20,12},{12,4},{4,0},{1,9},{9... | collective-permute-start | bytes 1769480 | tf_op jit(solution)/shard_map/ppermute | solution.py:145
  (24 other events, 131.8 us)
Sparse Core Ops, SparseCore 0:
  161.4 68.9 all-reduce.4

commit v10 on v7

--- a/solution.py
+++ b/solution.py
@@ -258,7 +258,8 @@
 ):
     slab = frames[0]
     chans = slab.shape[2]
-    columns, slab = ring_all_gather(up_weight, "fsdp", ring, slab)
+    staged = jnp.where(up_weight == up_weight, up_weight, jnp.zeros_like(up_weight))
+    columns, slab = ring_all_gather(staged, "fsdp", ring, slab)
     padded = extended(slab, (("rows", 0),), 3)
     activation_rows = conv_rows(padded, kernel, kernel_bias)
     normed_output, standardized_input, inverse_deviation = apply_layer_norm(

time: 216 us -> 212 us (0.981)
  local copies, waits for them, and re-layouts: 14.7 us -> 9.72 us
    slice x3, local copies, waits for them, and re-layouts: 4.66 us -> 1.41 us  [conv_rows(): kern[i, j]]
  transfers between devices with their start and end apart: 26 -> 26, of which waited for: 19 -> 19; matrix products, arithmetic and copies ran while one was open for 13% -> 11% of each run, Pallas kernels for 0% -> 0%
where the time goes in v10:
time: 212 us; the launch traced here: 211 us
  waiting for transfers between devices  91.9 us (43%)
  starting transfers between devices  36.3 us (17%)
  between operations  34.9 us (16%)
  other arithmetic  19.2 us (9%)
  matrix products  12.4 us (6%)
  local copies, waits for them, and re-layouts  9.72 us (5%)
  blocking collectives  6.61 us (3%)
    reduce_scatter x1, waiting for transfers between devices, body(): lax.psum_scatter(w_term.astype(jnp.bfloat16), 'fsdp', scatter_dimension=0...  27.9 us
    ppermute x4, waiting for transfers between devices, ring_all_gather(): cw = lax.ppermute(cw, axis, forward)  20.6 us
    ppermute x5, waiting for transfers between devices, tree_allreduce(): flat = keep + lax.ppermute(give, axis, perm)  15 us
    ppermute x5, waiting for transfers between devices, tree_allreduce(): other = lax.ppermute(flat, axis, perm)  10.7 us
    ppermute x4, starting transfers between devices, ring_all_gather(): cw = lax.ppermute(cw, axis, forward)  9.54 us
    ppermute x2, waiting for transfers between devices, tree_reduce_scatter(): lax.ppermute(give, axis, perm).astype(jnp.float32)  8.3 us
    ppermute x5, starting transfers between devices, tree_allreduce(): other = lax.ppermute(flat, axis, perm)  8.2 us
    ppermute x5, starting transfers between devices, tree_allreduce(): flat = keep + lax.ppermute(give, axis, perm)  7.15 us
  transfers between devices with their start and end apart: 26, of which 19 were waited for; matrix products, arithmetic and copies ran while one was open for 11% of the time, Pallas kernels for 0%

profile of v10, /device:TPU:0, one launch (start us, length us, event | category | flops | bytes accessed | tf_op | source)
XLA Modules:
  0.0 211.1 jit_solution(12607801490100066346)
XLA Ops:
  7.2 1.1 compare_select_fusion
  8.4 3.1 %collective-permute-start = (bf16[192,1536]{1,0:T(8,128)(2,1)S(1)}, bf16[192,1536]{1,0:T(8,128)(2,1)S(1)}, u32[]{:S(2)}, u32[]{:S(2)}) collective-permute-start(bf16[192,1536]{1,0:T(8,128)(2,1)S(1)} %compare_select_fusion), channel_id=1, source_target_pairs={{0,8},{8,16},{16,24},{24,28},{28,20},{20,12},{12,4},{4,0},{1,9},{9... | collective-permute-start | bytes 1769480 | tf_op jit(solution)/shard_map/ppermute | solution.py:112
  26.6 0.9 slice_reduce_fusion.47
  34.2 1.5 collective-permute-start.2
  35.7 1.3 collective-permute-start.3
  37.0 1.9 collective-permute-start.6
  39.3 1.7 collective-permute-done.3
  41.4 3.4 %fusion.152 = (f32[3,16]{1,0:T(4,128)S(1)}, f32[3,16,1536]{2,1,0:T(8,128)S(1)}) fusion(f32[1536]{0:T(1024)S(1)} %get-tuple-element.105, bf16[9,22,1536]{2,1,0:T(8,128)(2,1)S(1)} %select_maximum_fusion.2, f32[1536]{0:T(1024)S(1)} %get-tuple-element.106, f32[1536]{0:T(1024)S(1)} %get-tuple-element.59, f32[1536]{0:T(1024)S(1)} %get-tuple-element.60, ...), kind=kLoop, calls=%fused_computation.374 | loop fusion | flops 10911696 | bytes 7827648 | tf_op jit(solution)/shard_map/reduce_sum | solution.py:214
  45.2 4.1 %collective-permute-start.4 = (bf16[1,3,16,1536]{3,2,1,0:T(8,128)(2,1)S(1)}, bf16[1,3,16,1536]{3,2,1,0:T(8,128)(2,1)S(1)}, u32[]{:S(2)}, u32[]{:S(2)}) collective-permute-start(bf16[1,3,16,1536]{3,2,1,0:T(8,128)(2,1)S(1)} %fusion.143), channel_id=1, source_target_pairs={{0,1},{1,0},{2,3},{3,2},{4,5},{5,4},{6,7},{7,6},{8,9},{9,8},{10,11... | collective-permute-start | bytes 442376 | tf_op jit(solution)/shard_map/ppermute | solution.py:168
  49.3 1.0 collective-permute-done.4
  51.0 2.1 %collective-permute-start.8 = (bf16[192,1536]{1,0:T(8,128)(2,1)S(1)}, bf16[192,1536]{1,0:T(8,128)(2,1)S(1)}, u32[]{:S(2)}, u32[]{:S(2)}) collective-permute-start(bf16[192,1536]{1,0:T(8,128)(2,1)S(1)} %collective-permute-done.6), channel_id=1, source_target_pairs={{0,8},{8,16},{16,24},{24,28},{28,20},{20,12},{12,4},{4,0},{1,9},{9... | collective-permute-start | bytes 1769480 | tf_op jit(solution)/shard_map/ppermute | solution.py:112
  53.5 6.1 %collective-permute-done.5 = bf16[2,3,16,1536]{3,2,1,0:T(8,128)(2,1)S(1)} collective-permute-done((bf16[2,3,16,1536]{3,2,1,0:T(8,128)(2,1)S(1)}, bf16[2,3,16,1536]{3,2,1,0:T(8,128)(2,1)S(1)}, u32[]{:S(2)}, u32[]{:S(2)}) %collective-permute-start.5) | collective-permute-done | bytes 294944 | tf_op jit(solution)/shard_map/ppermute | solution.py:168
  59.7 6.2 %collective-permute-done.8 = bf16[192,1536]{1,0:T(8,128)(2,1)S(1)} collective-permute-done((bf16[192,1536]{1,0:T(8,128)(2,1)S(1)}, bf16[192,1536]{1,0:T(8,128)(2,1)S(1)}, u32[]{:S(2)}, u32[]{:S(2)}) %collective-permute-start.8) | collective-permute-done | bytes 589856 | tf_op jit(solution)/shard_map/ppermute | solution.py:112
  65.9 2.4 %collective-permute-start.10 = (bf16[192,1536]{1,0:T(8,128)(2,1)S(1)}, bf16[192,1536]{1,0:T(8,128)(2,1)S(1)}, u32[]{:S(2)}, u32[]{:S(2)}) collective-permute-start(bf16[192,1536]{1,0:T(8,128)(2,1)S(1)} %collective-permute-done.8), channel_id=1, source_target_pairs={{0,8},{8,16},{16,24},{24,28},{28,20},{20,12},{12,4},{4,0},{1,9},{9... | collective-permute-start | bytes 1769480 | tf_op jit(solution)/shard_map/ppermute | solution.py:112
  68.9 13.7 %collective-permute-done.10 = bf16[192,1536]{1,0:T(8,128)(2,1)S(1)} collective-permute-done((bf16[192,1536]{1,0:T(8,128)(2,1)S(1)}, bf16[192,1536]{1,0:T(8,128)(2,1)S(1)}, u32[]{:S(2)}, u32[]{:S(2)}) %collective-permute-start.10) | collective-permute-done | bytes 589856 | tf_op jit(solution)/shard_map/ppermute | solution.py:112
  82.7 4.8 %fusion.4 = (f32[1536]{0:T(1024)S(1)}, f32[1536]{0:T(1024)S(1)}, f32[192,1536]{1,0:T(8,128)}, f32[192,1536]{1,0:T(8,128)}) fusion(bf16[1,12,16,1536]{3,2,1,0:T(8,128)(2,1)S(1)} %copy-done.3, f32[1536]{0:T(1024)S(1)} %copy-done.54, bf16[192,1536]{1,0:T(8,128)(2,1)S(1)} %bitcast.64, bf16[1536,1536]{1,0:T(8,128)(2,1)S(1)} %bitcast.62), kind=kOutput, calls=%fused_computation.64 | convolution fusion | flops 926610432 | bytes 8275968 | tf_op jit(solution)/shard_map/dot_general | solution.py:272
  88.2 6.6 %all-reduce.2 = (f32[]{:T(128)}, f32[]{:T(128)}) all-reduce(f32[]{:T(128)} %get-tuple-element.127, f32[]{:T(128)} %get-tuple-element.126), channel_id=1, replica_groups=mesh['fsdp'=8,'rows'=4] {'rows'}, use_global_device_ids=true, to_apply=%region_4.5 | all-reduce | flops 2 | bytes 16 | tf_op jit(solution)/shard_map/psum | solution.py:277
  96.2 3.4 %fusion.3 = (bf16[192,1536]{1,0:T(8,128)(2,1)S(1)}, bf16[192,1536]{1,0:T(8,128)(2,1)}) fusion(f32[192,1536]{1,0:T(8,128)} %get-tuple-element.149, f32[192,1536]{1,0:T(8,128)} %get-tuple-element.134, bf16[1,12,16,1536]{3,2,1,0:T(8,128)(2,1)} %param.21, f32[1536]{0:T(1024)S(1)} %get-tuple-element.141, f32[1536]{0:T(1024)S(1)} %get-tuple-element.132, ...), kind=kLoop, calls=%fused_computation.63 | loop fusion | flops 5603328 | bytes 4159488 | tf_op jit(solution)/shard_map/convert_element_type | solution.py:284
  99.6 3.6 %convolution_convert_fusion = bf16[1536,1536]{1,0:T(8,128)(2,1)} fusion(bf16[192,1536]{1,0:T(8,128)(2,1)S(1)} %bitcast.65, bf16[192,1536]{1,0:T(8,128)(2,1)S(1)} %get-tuple-element.137), kind=kOutput, calls=%fused_computation | convolution fusion | flops 908328960 | bytes 5898240 | tf_op jit(solution)/shard_map/dot_general | solution.py:285
  103.2 4.0 %convolution_convert_fusion.1 = bf16[12,16,1536]{2,1,0:T(8,128)(2,1)S(1)} fusion(bf16[12,16,1536]{2,1,0:T(8,128)(2,1)S(1)} %bitcast.66, bf16[1536,1536,1]{1,0,2:T(8,128)(2,1)} %bitcast.63), kind=kOutput, calls=%fused_computation.52 | convolution fusion | flops 906264576 | bytes 5898240 | tf_op jit(solution)/shard_map/hwf,cf->hwc/dot_general | solution.py:292
  108.0 0.9 collective-permute-done.11
  108.9 1.0 convert_add_fusion
  110.0 1.7 collective-permute-start.12
  111.7 7.4 %collective-permute-done.12 = f32[1,3,16,1536]{3,2,1,0:T(8,128)S(1)} collective-permute-done((f32[1,3,16,1536]{3,2,1,0:T(8,128)S(1)}, f32[1,3,16,1536]{3,2,1,0:T(8,128)S(1)}, u32[]{:S(2)}, u32[]{:S(2)}) %collective-permute-start.12) | collective-permute-done | bytes 294944 | tf_op jit(solution)/shard_map/ppermute | solution.py:69
  119.3 1.6 fusion.140
  123.8 0.9 dynamic-slice_reduce_fusion
  124.7 1.4 collective-permute-done.15
  126.6 1.7 collective-permute-start.16
  128.3 2.8 %collective-permute-done.16 = f32[18816]{0:T(1024)S(1)} collective-permute-done((f32[18816]{0:T(1024)S(1)}, f32[18816]{0:T(1024)S(1)}, u32[]{:S(2)}, u32[]{:S(2)}) %collective-permute-start.16) | collective-permute-done | bytes 75296 | tf_op jit(solution)/shard_map/ppermute | solution.py:49
  131.7 1.9 collective-permute-start.17
  133.5 3.0 %collective-permute-done.17 = f32[9408]{0:T(1024)S(1)} collective-permute-done((f32[9408]{0:T(1024)S(1)}, f32[9408]{0:T(1024)S(1)}, u32[]{:S(2)}, u32[]{:S(2)}) %collective-permute-start.17) | collective-permute-done | bytes 37664 | tf_op jit(solution)/shard_map/ppermute | solution.py:49
  136.8 1.6 collective-permute-start.18
  138.4 3.7 %collective-permute-done.18 = f32[4704]{0:T(1024)S(1)} collective-permute-done((f32[4704]{0:T(1024)S(1)}, f32[4704]{0:T(1024)S(1)}, u32[]{:S(2)}, u32[]{:S(2)}) %collective-permute-start.18) | collective-permute-done | bytes 18848 | tf_op jit(solution)/shard_map/ppermute | solution.py:49
  142.3 1.9 collective-permute-start.19
  144.2 4.1 %collective-permute-done.19 = f32[2352]{0:T(1024)S(1)} collective-permute-done((f32[2352]{0:T(1024)S(1)}, f32[2352]{0:T(1024)S(1)}, u32[]{:S(2)}, u32[]{:S(2)}) %collective-permute-start.19) | collective-permute-done | bytes 9440 | tf_op jit(solution)/shard_map/ppermute | solution.py:49
  148.3 0.9 collective-permute-start.20
  149.2 4.1 %collective-permute-done.20 = f32[2352]{0:T(1024)S(1)} collective-permute-done((f32[2352]{0:T(1024)S(1)}, f32[2352]{0:T(1024)S(1)}, u32[]{:S(2)}, u32[]{:S(2)}) %collective-permute-start.20) | collective-permute-done | bytes 9440 | tf_op jit(solution)/shard_map/ppermute | solution.py:52
  153.4 1.2 collective-permute-start.21
  154.6 2.5 %collective-permute-done.21 = f32[4704]{0:T(1024)S(1)} collective-permute-done((f32[4704]{0:T(1024)S(1)}, f32[4704]{0:T(1024)S(1)}, u32[]{:S(2)}, u32[]{:S(2)}) %collective-permute-start.21) | collective-permute-done | bytes 18848 | tf_op jit(solution)/shard_map/ppermute | solution.py:52
  157.3 1.6 collective-permute-start.22
  158.9 1.3 collective-permute-start.13
  160.2 1.3 collective-permute-start.14
  161.6 4.4 %collective-permute-start.23 = (f32[18816]{0:T(1024)S(1)}, f32[18816]{0:T(1024)S(1)}, u32[]{:S(2)}, u32[]{:S(2)}) collective-permute-start(f32[18816]{0:T(1024)S(1)} %maximum_select_fusion.4), channel_id=1, source_target_pairs={{0,2},{1,3},{2,0},{3,1},{4,6},{5,7},{6,4},{7,5},{8,10},{9,11},{10,... | collective-permute-start | bytes 225800 | tf_op jit(solution)/shard_map/ppermute | solution.py:52
  166.2 4.0 %collective-permute-done.23 = f32[18816]{0:T(1024)S(1)} collective-permute-done((f32[18816]{0:T(1024)S(1)}, f32[18816]{0:T(1024)S(1)}, u32[]{:S(2)}, u32[]{:S(2)}) %collective-permute-start.23) | collective-permute-done | bytes 75296 | tf_op jit(solution)/shard_map/ppermute | solution.py:52
  170.5 2.8 %fusion.146 = bf16[1,3,16,1536]{3,2,1,0:T(8,128)(2,1)} fusion(f32[1536]{0:T(1024)S(1)} %copy-done.44, bf16[9,22,1536]{2,1,0:T(8,128)(2,1)S(1)} %select_maximum_fusion, f32[1536]{0:T(1024)S(1)} %copy-done.46, f32[1536]{0:T(1024)S(1)} %get-tuple-element.59, f32[1536]{0:T(1024)S(1)} %get-tuple-element.60, bf16[3,16,1536]{2,1,0:T(8,128)(2,1)S(1)} %collective-permute-done.13, ...), kind=kLoop, calls=%fused_computation.297 | loop fusion | flops 11132928 | bytes 7084032 | tf_op jit(solution)/shard_map/reshape | solution.py:307
  173.3 0.8 select_n.294
  174.1 27.9 %reduce-scatter.2.cloned.1.call-done = bf16[192,1536]{1,0:T(8,128)(2,1)} async-done(((bf16[1536,1536]{1,0:T(8,128)(2,1)}), bf16[192,1536]{1,0:T(8,128)(2,1)}) %reduce-scatter.2.cloned.1.call-update) | async-done | bytes 589840 | tf_op jit(solution)/shard_map/reduce_scatter | solution.py:288
  202.1 2.2 %convert_element_type.497 = f32[192,1536]{1,0:T(8,128)} convert(bf16[192,1536]{1,0:T(8,128)(2,1)} %reduce-scatter.2.cloned.1.call-done) | non-fusion elementwise | flops 294912 | bytes 1769472 | tf_op jit(solution)/shard_map/convert_element_type | solution.py:290
  (232 shorter events, 12.7 us)
Async XLA Ops:
  7.2 194.9 %reduce-scatter.2.cloned.1.call-start = ((), (), s32[]{:S(2)}) async-start(), calls=%async_computation.1 | async-start | bytes 5308416 | tf_op jit(solution)/shard_map/reduce_scatter | solution.py:288
  8.4 25.1 %collective-permute-start = (bf16[192,1536]{1,0:T(8,128)(2,1)S(1)}, bf16[192,1536]{1,0:T(8,128)(2,1)S(1)}, u32[]{:S(2)}, u32[]{:S(2)}) collective-permute-start(bf16[192,1536]{1,0:T(8,128)(2,1)S(1)} %compare_select_fusion), channel_id=1, source_target_pairs={{0,8},{8,16},{16,24},{24,28},{28,20},{20,12},{12,4},{4,0},{1,9},{9... | collective-permute-start | bytes 1769480 | tf_op jit(solution)/shard_map/ppermute | solution.py:112
  11.5 22.0 %collective-permute-start.1 = (bf16[192,1536]{1,0:T(8,128)(2,1)S(1)}, bf16[192,1536]{1,0:T(8,128)(2,1)S(1)}, u32[]{:S(2)}, u32[]{:S(2)}) collective-permute-start(bf16[192,1536]{1,0:T(8,128)(2,1)S(1)} %compare_select_fusion), channel_id=1, source_target_pairs={{0,4},{8,0},{16,8},{24,16},{28,24},{20,28},{12,20},{4,12},{1,5},{9... | collective-permute-start | bytes 1769480 | tf_op jit(solution)/shard_map/ppermute | solution.py:114
  34.2 5.0 %collective-permute-start.2 = (bf16[3,16,1536]{2,1,0:T(8,128)(2,1)S(1)}, bf16[3,16,1536]{2,1,0:T(8,128)(2,1)S(1)}, u32[]{:S(2)}, u32[]{:S(2)}) collective-permute-start(bf16[3,16,1536]{2,1,0:T(8,128)(2,1)S(1)} %bitcast.67), channel_id=1, source_target_pairs={{0,1},{1,2},{2,3},{4,5},{5,6},{6,7},{8,9},{9,10},{10,11},{12,13},{... | collective-permute-start | bytes 442376 | tf_op jit(solution)/shard_map/ppermute | solution.py:16
  35.7 5.3 %collective-permute-start.3 = (bf16[3,16,1536]{2,1,0:T(8,128)(2,1)S(1)}, bf16[3,16,1536]{2,1,0:T(8,128)(2,1)S(1)}, u32[]{:S(2)}, u32[]{:S(2)}) collective-permute-start(bf16[3,16,1536]{2,1,0:T(8,128)(2,1)S(1)} %bitcast.68), channel_id=1, source_target_pairs={{1,0},{2,1},{3,2},{5,4},{6,5},{7,6},{9,8},{10,9},{11,10},{13,12},{... | collective-permute-start | bytes 442376 | tf_op jit(solution)/shard_map/ppermute | solution.py:19
  37.0 14.0 %collective-permute-start.6 = (bf16[192,1536]{1,0:T(8,128)(2,1)S(1)}, bf16[192,1536]{1,0:T(8,128)(2,1)S(1)}, u32[]{:S(2)}, u32[]{:S(2)}) collective-permute-start(bf16[192,1536]{1,0:T(8,128)(2,1)S(1)} %collective-permute-done), channel_id=1, source_target_pairs={{0,8},{8,16},{16,24},{24,28},{28,20},{20,12},{12,4},{4,0},{1,9},{9... | collective-permute-start | bytes 1769480 | tf_op jit(solution)/shard_map/ppermute | solution.py:112
  38.9 14.5 %collective-permute-start.7 = (bf16[192,1536]{1,0:T(8,128)(2,1)S(1)}, bf16[192,1536]{1,0:T(8,128)(2,1)S(1)}, u32[]{:S(2)}, u32[]{:S(2)}) collective-permute-start(bf16[192,1536]{1,0:T(8,128)(2,1)S(1)} %collective-permute-done.1), channel_id=1, source_target_pairs={{0,4},{8,0},{16,8},{24,16},{28,24},{20,28},{12,20},{4,12},{1,5},{9... | collective-permute-start | bytes 1769480 | tf_op jit(solution)/shard_map/ppermute | solution.py:114
  44.9 74.3 %copy-start.47 = (f32[3,16]{1,0:T(4,128)}, f32[3,16]{1,0:T(4,128)S(1)}, u32[]{:S(2)}) copy-start(f32[3,16]{1,0:T(4,128)S(1)} %broadcast_multiply_fusion.2) | copy-start | bytes 580
  45.1 74.1 %copy-start.48 = (f32[3,16]{1,0:T(4,128)}, f32[3,16]{1,0:T(4,128)S(1)}, u32[]{:S(2)}) copy-start(f32[3,16]{1,0:T(4,128)S(1)} %add_rsqrt_fusion) | copy-start | bytes 580
  45.2 5.1 %collective-permute-start.4 = (bf16[1,3,16,1536]{3,2,1,0:T(8,128)(2,1)S(1)}, bf16[1,3,16,1536]{3,2,1,0:T(8,128)(2,1)S(1)}, u32[]{:S(2)}, u32[]{:S(2)}) collective-permute-start(bf16[1,3,16,1536]{3,2,1,0:T(8,128)(2,1)S(1)} %fusion.143), channel_id=1, source_target_pairs={{0,1},{1,0},{2,3},{3,2},{4,5},{5,4},{6,7},{7,6},{8,9},{9,8},{10,11... | collective-permute-start | bytes 442376 | tf_op jit(solution)/shard_map/ppermute | solution.py:168
  50.3 9.3 %collective-permute-start.5 = (bf16[2,3,16,1536]{3,2,1,0:T(8,128)(2,1)S(1)}, bf16[2,3,16,1536]{3,2,1,0:T(8,128)(2,1)S(1)}, u32[]{:S(2)}, u32[]{:S(2)}) collective-permute-start(bf16[2,3,16,1536]{3,2,1,0:T(8,128)(2,1)S(1)} %maximum_select_fusion.2), channel_id=1, source_target_pairs={{0,2},{1,3},{2,0},{3,1},{4,6},{5,7},{6,4},{7,5},{8,10},{9,11},{10,... | collective-permute-start | bytes 884744 | tf_op jit(solution)/shard_map/ppermute | solution.py:168
  51.0 14.9 %collective-permute-start.8 = (bf16[192,1536]{1,0:T(8,128)(2,1)S(1)}, bf16[192,1536]{1,0:T(8,128)(2,1)S(1)}, u32[]{:S(2)}, u32[]{:S(2)}) collective-permute-start(bf16[192,1536]{1,0:T(8,128)(2,1)S(1)} %collective-permute-done.6), channel_id=1, source_target_pairs={{0,8},{8,16},{16,24},{24,28},{28,20},{20,12},{12,4},{4,0},{1,9},{9... | collective-permute-start | bytes 1769480 | tf_op jit(solution)/shard_map/ppermute | solution.py:112
  53.4 15.4 %collective-permute-start.9 = (bf16[192,1536]{1,0:T(8,128)(2,1)S(1)}, bf16[192,1536]{1,0:T(8,128)(2,1)S(1)}, u32[]{:S(2)}, u32[]{:S(2)}) collective-permute-start(bf16[192,1536]{1,0:T(8,128)(2,1)S(1)} %collective-permute-done.7), channel_id=1, source_target_pairs={{0,4},{8,0},{16,8},{24,16},{28,24},{20,28},{12,20},{4,12},{1,5},{9... | collective-permute-start | bytes 1769480 | tf_op jit(solution)/shard_map/ppermute | solution.py:114
  65.9 16.7 %collective-permute-start.10 = (bf16[192,1536]{1,0:T(8,128)(2,1)S(1)}, bf16[192,1536]{1,0:T(8,128)(2,1)S(1)}, u32[]{:S(2)}, u32[]{:S(2)}) collective-permute-start(bf16[192,1536]{1,0:T(8,128)(2,1)S(1)} %collective-permute-done.8), channel_id=1, source_target_pairs={{0,8},{8,16},{16,24},{24,28},{28,20},{20,12},{12,4},{4,0},{1,9},{9... | collective-permute-start | bytes 1769480 | tf_op jit(solution)/shard_map/ppermute | solution.py:112
  107.3 1.6 collective-permute-start.11
  110.0 9.1 %collective-permute-start.12 = (f32[1,3,16,1536]{3,2,1,0:T(8,128)S(1)}, f32[1,3,16,1536]{3,2,1,0:T(8,128)S(1)}, u32[]{:S(2)}, u32[]{:S(2)}) collective-permute-start(f32[1,3,16,1536]{3,2,1,0:T(8,128)S(1)} %constant_dynamic-slice_fusion), channel_id=1, source_target_pairs={{0,2},{1,3},{2,0},{3,1},{4,6},{5,7},{6,4},{7,5},{8,10},{9,11},{10,... | collective-permute-start | bytes 884744 | tf_op jit(solution)/shard_map/ppermute | solution.py:69
  124.6 1.4 collective-permute-start.15
  126.6 4.5 %collective-permute-start.16 = (f32[18816]{0:T(1024)S(1)}, f32[18816]{0:T(1024)S(1)}, u32[]{:S(2)}, u32[]{:S(2)}) collective-permute-start(f32[18816]{0:T(1024)S(1)} %get-tuple-element.111), channel_id=1, source_target_pairs={{0,2},{1,3},{2,0},{3,1},{4,6},{5,7},{6,4},{7,5},{8,10},{9,11},{10,... | collective-permute-start | bytes 225800 | tf_op jit(solution)/shard_map/ppermute | solution.py:49
  131.5 38.8 %copy-start.8 = (f32[1536]{0:T(1024)S(1)}, f32[1536]{0:T(1024)}, u32[]{:S(2)}) copy-start(f32[1536]{0:T(1024)} %get-tuple-element.87) | copy-start | bytes 18436
  131.5 38.8 %copy-start.10 = (f32[1536]{0:T(1024)S(1)}, f32[1536]{0:T(1024)}, u32[]{:S(2)}) copy-start(f32[1536]{0:T(1024)} %get-tuple-element.88) | copy-start | bytes 18436
  131.5 38.8 %copy-start.12 = (f32[1536]{0:T(1024)S(1)}, f32[1536]{0:T(1024)}, u32[]{:S(2)}) copy-start(f32[1536]{0:T(1024)} %get-tuple-element.89) | copy-start | bytes 18436
  131.5 38.8 %copy-start.14 = (f32[1536]{0:T(1024)S(1)}, f32[1536]{0:T(1024)}, u32[]{:S(2)}) copy-start(f32[1536]{0:T(1024)} %get-tuple-element.90) | copy-start | bytes 18436
  131.5 38.8 %copy-start.16 = (f32[1536]{0:T(1024)S(1)}, f32[1536]{0:T(1024)}, u32[]{:S(2)}) copy-start(f32[1536]{0:T(1024)} %get-tuple-element.91) | copy-start | bytes 18436
  131.5 38.8 %copy-start.18 = (f32[1536]{0:T(1024)S(1)}, f32[1536]{0:T(1024)}, u32[]{:S(2)}) copy-start(f32[1536]{0:T(1024)} %get-tuple-element.92) | copy-start | bytes 18436
  131.5 38.8 %copy-start.20 = (f32[1536]{0:T(1024)S(1)}, f32[1536]{0:T(1024)}, u32[]{:S(2)}) copy-start(f32[1536]{0:T(1024)} %get-tuple-element.93) | copy-start | bytes 18436
  131.5 38.8 %copy-start.22 = (f32[1536]{0:T(1024)S(1)}, f32[1536]{0:T(1024)}, u32[]{:S(2)}) copy-start(f32[1536]{0:T(1024)} %get-tuple-element.94) | copy-start | bytes 18436
  131.5 38.8 %copy-start.24 = (f32[1536]{0:T(1024)S(1)}, f32[1536]{0:T(1024)}, u32[]{:S(2)}) copy-start(f32[1536]{0:T(1024)} %get-tuple-element.95) | copy-start | bytes 18436
  131.5 38.8 %copy-start.26 = (f32[1536]{0:T(1024)S(1)}, f32[1536]{0:T(1024)}, u32[]{:S(2)}) copy-start(f32[1536]{0:T(1024)} %copy-done.25) | copy-start | bytes 18436
  131.6 38.8 %copy-start.28 = (f32[1536]{0:T(1024)S(1)}, f32[1536]{0:T(1024)}, u32[]{:S(2)}) copy-start(f32[1536]{0:T(1024)} %copy-done.27) | copy-start | bytes 18436
  131.6 38.8 %copy-start.30 = (f32[1536]{0:T(1024)S(1)}, f32[1536]{0:T(1024)}, u32[]{:S(2)}) copy-start(f32[1536]{0:T(1024)} %copy-done.29) | copy-start | bytes 18436
  131.6 38.8 %copy-start.32 = (f32[1536]{0:T(1024)S(1)}, f32[1536]{0:T(1024)}, u32[]{:S(2)}) copy-start(f32[1536]{0:T(1024)} %copy-done.31) | copy-start | bytes 18436
  131.6 38.8 %copy-start.34 = (f32[1536]{0:T(1024)S(1)}, f32[1536]{0:T(1024)}, u32[]{:S(2)}) copy-start(f32[1536]{0:T(1024)} %copy-done.33) | copy-start | bytes 18436
  131.6 38.8 %copy-start.36 = (f32[1536]{0:T(1024)S(1)}, f32[1536]{0:T(1024)}, u32[]{:S(2)}) copy-start(f32[1536]{0:T(1024)} %copy-done.35) | copy-start | bytes 18436
  131.6 38.8 %copy-start.38 = (f32[1536]{0:T(1024)S(1)}, f32[1536]{0:T(1024)}, u32[]{:S(2)}) copy-start(f32[1536]{0:T(1024)} %copy-done.37) | copy-start | bytes 18436
  131.6 38.8 %copy-start.40 = (f32[1536]{0:T(1024)S(1)}, f32[1536]{0:T(1024)}, u32[]{:S(2)}) copy-start(f32[1536]{0:T(1024)} %copy-done.39) | copy-start | bytes 18436
  131.6 38.8 %copy-start.42 = (f32[1536]{0:T(1024)S(1)}, f32[1536]{0:T(1024)}, u32[]{:S(2)}) copy-start(f32[1536]{0:T(1024)} %copy-done.41) | copy-start | bytes 18436
  131.6 38.8 %copy-start.44 = (f32[1536]{0:T(1024)S(1)}, f32[1536]{0:T(1024)}, u32[]{:S(2)}) copy-start(f32[1536]{0:T(1024)} %copy-done.43) | copy-start | bytes 18436
  131.6 38.8 %copy-start.46 = (f32[1536]{0:T(1024)S(1)}, f32[1536]{0:T(1024)}, u32[]{:S(2)}) copy-start(f32[1536]{0:T(1024)} %copy-done.45) | copy-start | bytes 18436
  131.7 4.9 %collective-permute-start.17 = (f32[9408]{0:T(1024)S(1)}, f32[9408]{0:T(1024)S(1)}, u32[]{:S(2)}, u32[]{:S(2)}) collective-permute-start(f32[9408]{0:T(1024)S(1)} %get-tuple-element.120), channel_id=1, source_target_pairs={{0,4},{4,0},{8,12},{12,8},{16,20},{20,16},{24,28},{28,24},{1,5},{5... | collective-permute-start | bytes 112904 | tf_op jit(solution)/shard_map/ppermute | solution.py:49
  136.8 5.3 %collective-permute-start.18 = (f32[4704]{0:T(1024)S(1)}, f32[4704]{0:T(1024)S(1)}, u32[]{:S(2)}, u32[]{:S(2)}) collective-permute-start(f32[4704]{0:T(1024)S(1)} %get-tuple-element.122), channel_id=1, source_target_pairs={{0,8},{4,12},{8,0},{12,4},{16,24},{20,28},{24,16},{28,20},{1,9},{5... | collective-permute-start | bytes 56456 | tf_op jit(solution)/shard_map/ppermute | solution.py:49
  142.3 6.0 %collective-permute-start.19 = (f32[2352]{0:T(1024)S(1)}, f32[2352]{0:T(1024)S(1)}, u32[]{:S(2)}, u32[]{:S(2)}) collective-permute-start(f32[2352]{0:T(1024)S(1)} %get-tuple-element.124), channel_id=1, source_target_pairs={{0,16},{4,20},{8,24},{12,28},{16,0},{20,4},{24,8},{28,12},{1,17},{... | collective-permute-start | bytes 28232 | tf_op jit(solution)/shard_map/ppermute | solution.py:49
  148.3 5.0 %collective-permute-start.20 = (f32[2352]{0:T(1024)S(1)}, f32[2352]{0:T(1024)S(1)}, u32[]{:S(2)}, u32[]{:S(2)}) collective-permute-start(f32[2352]{0:T(1024)S(1)} %add.722), channel_id=1, source_target_pairs={{0,16},{4,20},{8,24},{12,28},{16,0},{20,4},{24,8},{28,12},{1,17},{... | collective-permute-start | bytes 28232 | tf_op jit(solution)/shard_map/ppermute | solution.py:52
  153.4 3.8 %collective-permute-start.21 = (f32[4704]{0:T(1024)S(1)}, f32[4704]{0:T(1024)S(1)}, u32[]{:S(2)}, u32[]{:S(2)}) collective-permute-start(f32[4704]{0:T(1024)S(1)} %maximum_select_fusion.6), channel_id=1, source_target_pairs={{0,8},{4,12},{8,0},{12,4},{16,24},{20,28},{24,16},{28,20},{1,9},{5... | collective-permute-start | bytes 56456 | tf_op jit(solution)/shard_map/ppermute | solution.py:52
  157.3 4.2 %collective-permute-start.22 = (f32[9408]{0:T(1024)S(1)}, f32[9408]{0:T(1024)S(1)}, u32[]{:S(2)}, u32[]{:S(2)}) collective-permute-start(f32[9408]{0:T(1024)S(1)} %maximum_select_fusion.5), channel_id=1, source_target_pairs={{0,4},{4,0},{8,12},{12,8},{16,20},{20,16},{24,28},{28,24},{1,5},{5... | collective-permute-start | bytes 112904 | tf_op jit(solution)/shard_map/ppermute | solution.py:52
  158.9 7.1 %collective-permute-start.13 = (bf16[3,16,1536]{2,1,0:T(8,128)(2,1)S(1)}, bf16[3,16,1536]{2,1,0:T(8,128)(2,1)S(1)}, u32[]{:S(2)}, u32[]{:S(2)}) collective-permute-start(bf16[3,16,1536]{2,1,0:T(8,128)(2,1)S(1)} %get-tuple-element.130), channel_id=1, source_target_pairs={{0,1},{1,2},{2,3},{4,5},{5,6},{6,7},{8,9},{9,10},{10,11},{12,13},{... | collective-permute-start | bytes 442376 | tf_op jit(solution)/shard_map/ppermute | solution.py:16
  160.2 5.8 %collective-permute-start.14 = (bf16[3,16,1536]{2,1,0:T(8,128)(2,1)S(1)}, bf16[3,16,1536]{2,1,0:T(8,128)(2,1)S(1)}, u32[]{:S(2)}, u32[]{:S(2)}) collective-permute-start(bf16[3,16,1536]{2,1,0:T(8,128)(2,1)S(1)} %get-tuple-element.130), channel_id=1, source_target_pairs={{1,0},{2,1},{3,2},{5,4},{6,5},{7,6},{9,8},{10,9},{11,10},{13,12},{... | collective-permute-start | bytes 442376 | tf_op jit(solution)/shard_map/ppermute | solution.py:19
  161.6 8.6 %collective-permute-start.23 = (f32[18816]{0:T(1024)S(1)}, f32[18816]{0:T(1024)S(1)}, u32[]{:S(2)}, u32[]{:S(2)}) collective-permute-start(f32[18816]{0:T(1024)S(1)} %maximum_select_fusion.4), channel_id=1, source_target_pairs={{0,2},{1,3},{2,0},{3,1},{4,6},{5,7},{6,4},{7,5},{8,10},{9,11},{10,... | collective-permute-start | bytes 225800 | tf_op jit(solution)/shard_map/ppermute | solution.py:52
  170.2 3.1 %collective-permute-start.24 = (f32[37632]{0:T(1024)S(1)}, f32[37632]{0:T(1024)S(1)}, u32[]{:S(2)}, u32[]{:S(2)}) collective-permute-start(f32[37632]{0:T(1024)S(1)} %maximum_select_fusion.3), channel_id=1, source_target_pairs={{0,1},{1,0},{2,3},{3,2},{4,5},{5,4},{6,7},{7,6},{8,9},{9,8},{10,11... | collective-permute-start | bytes 451592 | tf_op jit(solution)/shard_map/ppermute | solution.py:52
  (34 other events, 216.3 us)
Sparse Core Ops, SparseCore 0:
  103.3 98.6 reduce-scatter.1

commit v11 on v10

--- a/solution.py
+++ b/solution.py
@@ -274,14 +274,16 @@
     norms = jnp.sqrt(jnp.sum(post * post, axis=0) + 1e-06)
     cot_f = grad_out[0].reshape(flat.shape[0], -1).astype(jnp.float32)
     dnorm = grn_gamma * jnp.sum(cot_f * post, axis=0)
-    norm_total = lax.psum(jnp.sum(norms), "rows")
+    slope = gelu_grad(pre)
+    slope, norm_local = lax.optimization_barrier((slope, jnp.sum(norms)))
+    norm_total = lax.psum(norm_local, "rows")
     denom = norm_total / FF + 1e-06
     ratio = norms / denom
     output = (grn_gamma * (post * ratio) + grn_beta + post).astype(jnp.bfloat16)
     cross = lax.psum(jnp.sum(dnorm * norms), "rows")
     dnorms = dnorm / denom - cross / (denom * denom) / FF
     dpost = cot_f * (1.0 + grn_gamma * ratio) + post * (dnorms / norms)
-    dpre = (dpost * gelu_grad(pre)).astype(jnp.bfloat16)
+    dpre = (dpost * slope).astype(jnp.bfloat16)
     w_term = lax.dot_general(
         flat, dpre, (((0,), (0,)), ((), ())), preferred_element_type=jnp.float32
     )

time: 212 us -> 212 us (level)
  no operation moved by 1% of the time
where the time goes in v11:
time: 212 us; the launch traced here: 211 us
  waiting for transfers between devices  91.9 us (43%)
  starting transfers between devices  36.4 us (17%)
  between operations  34.9 us (16%)
  other arithmetic  18.8 us (9%)
  matrix products  13 us (6%)
  local copies, waits for them, and re-layouts  9.72 us (5%)
  blocking collectives  6.61 us (3%)
    reduce_scatter x1, waiting for transfers between devices, body(): lax.psum_scatter(w_term.astype(jnp.bfloat16), 'fsdp', scatter_dimension=0...  28 us
    ppermute x4, waiting for transfers between devices, ring_all_gather(): cw = lax.ppermute(cw, axis, forward)  20.6 us
    ppermute x5, waiting for transfers between devices, tree_allreduce(): flat = keep + lax.ppermute(give, axis, perm)  15 us
    ppermute x5, waiting for transfers between devices, tree_allreduce(): other = lax.ppermute(flat, axis, perm)  10.6 us
    ppermute x4, starting transfers between devices, ring_all_gather(): cw = lax.ppermute(cw, axis, forward)  9.54 us
    ppermute x2, waiting for transfers between devices, tree_reduce_scatter(): lax.ppermute(give, axis, perm).astype(jnp.float32)  8.28 us
    ppermute x5, starting transfers between devices, tree_allreduce(): other = lax.ppermute(flat, axis, perm)  8.21 us
    ppermute x5, starting transfers between devices, tree_allreduce(): flat = keep + lax.ppermute(give, axis, perm)  7.16 us
  transfers between devices with their start and end apart: 26, of which 19 were waited for; matrix products, arithmetic and copies ran while one was open for 11% of the time, Pallas kernels for 0%

profile of v11, /device:TPU:0, one launch (start us, length us, event | category | flops | bytes accessed | tf_op | source)
XLA Modules:
  0.0 211.3 jit_solution(16169528045675785373)
XLA Ops:
  7.2 1.1 compare_select_fusion
  8.4 3.1 %collective-permute-start = (bf16[192,1536]{1,0:T(8,128)(2,1)S(1)}, bf16[192,1536]{1,0:T(8,128)(2,1)S(1)}, u32[]{:S(2)}, u32[]{:S(2)}) collective-permute-start(bf16[192,1536]{1,0:T(8,128)(2,1)S(1)} %compare_select_fusion), channel_id=1, source_target_pairs={{0,8},{8,16},{16,24},{24,28},{28,20},{20,12},{12,4},{4,0},{1,9},{9... | collective-permute-start | bytes 1769480 | tf_op jit(solution)/shard_map/ppermute | solution.py:112
  26.6 0.9 slice_reduce_fusion.47
  34.2 1.5 collective-permute-start.2
  35.7 1.3 collective-permute-start.3
  37.0 1.9 collective-permute-start.6
  39.3 1.7 collective-permute-done.3
  41.4 3.4 %fusion.152 = (f32[3,16]{1,0:T(4,128)S(1)}, f32[3,16,1536]{2,1,0:T(8,128)S(1)}) fusion(f32[1536]{0:T(1024)S(1)} %get-tuple-element.109, bf16[9,22,1536]{2,1,0:T(8,128)(2,1)S(1)} %select_maximum_fusion.2, f32[1536]{0:T(1024)S(1)} %get-tuple-element.110, f32[1536]{0:T(1024)S(1)} %get-tuple-element.63, f32[1536]{0:T(1024)S(1)} %get-tuple-element.64, ...), kind=kLoop, calls=%fused_computation.374 | loop fusion | flops 10911696 | bytes 7827648 | tf_op jit(solution)/shard_map/reduce_sum | solution.py:214
  45.2 4.1 %collective-permute-start.4 = (bf16[1,3,16,1536]{3,2,1,0:T(8,128)(2,1)S(1)}, bf16[1,3,16,1536]{3,2,1,0:T(8,128)(2,1)S(1)}, u32[]{:S(2)}, u32[]{:S(2)}) collective-permute-start(bf16[1,3,16,1536]{3,2,1,0:T(8,128)(2,1)S(1)} %fusion.143), channel_id=1, source_target_pairs={{0,1},{1,0},{2,3},{3,2},{4,5},{5,4},{6,7},{7,6},{8,9},{9,8},{10,11... | collective-permute-start | bytes 442376 | tf_op jit(solution)/shard_map/ppermute | solution.py:168
  49.3 1.0 collective-permute-done.4
  51.0 2.1 %collective-permute-start.8 = (bf16[192,1536]{1,0:T(8,128)(2,1)S(1)}, bf16[192,1536]{1,0:T(8,128)(2,1)S(1)}, u32[]{:S(2)}, u32[]{:S(2)}) collective-permute-start(bf16[192,1536]{1,0:T(8,128)(2,1)S(1)} %collective-permute-done.6), channel_id=1, source_target_pairs={{0,8},{8,16},{16,24},{24,28},{28,20},{20,12},{12,4},{4,0},{1,9},{9... | collective-permute-start | bytes 1769480 | tf_op jit(solution)/shard_map/ppermute | solution.py:112
  53.5 6.1 %collective-permute-done.5 = bf16[2,3,16,1536]{3,2,1,0:T(8,128)(2,1)S(1)} collective-permute-done((bf16[2,3,16,1536]{3,2,1,0:T(8,128)(2,1)S(1)}, bf16[2,3,16,1536]{3,2,1,0:T(8,128)(2,1)S(1)}, u32[]{:S(2)}, u32[]{:S(2)}) %collective-permute-start.5) | collective-permute-done | bytes 294944 | tf_op jit(solution)/shard_map/ppermute | solution.py:168
  59.7 6.2 %collective-permute-done.8 = bf16[192,1536]{1,0:T(8,128)(2,1)S(1)} collective-permute-done((bf16[192,1536]{1,0:T(8,128)(2,1)S(1)}, bf16[192,1536]{1,0:T(8,128)(2,1)S(1)}, u32[]{:S(2)}, u32[]{:S(2)}) %collective-permute-start.8) | collective-permute-done | bytes 589856 | tf_op jit(solution)/shard_map/ppermute | solution.py:112
  65.9 2.4 %collective-permute-start.10 = (bf16[192,1536]{1,0:T(8,128)(2,1)S(1)}, bf16[192,1536]{1,0:T(8,128)(2,1)S(1)}, u32[]{:S(2)}, u32[]{:S(2)}) collective-permute-start(bf16[192,1536]{1,0:T(8,128)(2,1)S(1)} %collective-permute-done.8), channel_id=1, source_target_pairs={{0,8},{8,16},{16,24},{24,28},{28,20},{20,12},{12,4},{4,0},{1,9},{9... | collective-permute-start | bytes 1769480 | tf_op jit(solution)/shard_map/ppermute | solution.py:112
  68.9 13.7 %collective-permute-done.10 = bf16[192,1536]{1,0:T(8,128)(2,1)S(1)} collective-permute-done((bf16[192,1536]{1,0:T(8,128)(2,1)S(1)}, bf16[192,1536]{1,0:T(8,128)(2,1)S(1)}, u32[]{:S(2)}, u32[]{:S(2)}) %collective-permute-start.10) | collective-permute-done | bytes 589856 | tf_op jit(solution)/shard_map/ppermute | solution.py:112
  82.7 5.4 %fusion.4 = (f32[1536]{0:T(1024)S(1)}, f32[1536]{0:T(1024)S(1)}, f32[192,1536]{1,0:T(8,128)}, f32[192,1536]{1,0:T(8,128)}) fusion(bf16[1,12,16,1536]{3,2,1,0:T(8,128)(2,1)S(1)} %copy-done.3, f32[1536]{0:T(1024)S(1)} %copy-done.54, bf16[192,1536]{1,0:T(8,128)(2,1)S(1)} %bitcast.64, bf16[1536,1536]{1,0:T(8,128)(2,1)S(1)} %bitcast.62), kind=kOutput, calls=%fused_computation.64 | convolution fusion | flops 928969728 | bytes 8275968 | tf_op jit(solution)/shard_map/dot_general | solution.py:272
  88.8 6.6 %all-reduce.2 = (f32[]{:T(128)}, f32[]{:T(128)}) all-reduce(f32[]{:T(128)} %get-tuple-element.12, f32[]{:T(128)} %get-tuple-element.130), channel_id=1, replica_groups=mesh['fsdp'=8,'rows'=4] {'rows'}, use_global_device_ids=true, to_apply=%region_4.5 | all-reduce | flops 2 | bytes 16 | tf_op jit(solution)/shard_map/psum | solution.py:279
  96.8 3.0 %fusion.3 = (bf16[192,1536]{1,0:T(8,128)(2,1)S(1)}, bf16[192,1536]{1,0:T(8,128)(2,1)}) fusion(f32[192,1536]{1,0:T(8,128)} %get-tuple-element.13, f32[192,1536]{1,0:T(8,128)} %get-tuple-element.138, bf16[1,12,16,1536]{3,2,1,0:T(8,128)(2,1)} %param.21, f32[1536]{0:T(1024)S(1)} %get-tuple-element.146, f32[1536]{0:T(1024)S(1)} %get-tuple-element.136, ...), kind=kLoop, calls=%fused_computation.63 | loop fusion | flops 3244032 | bytes 4159488 | tf_op jit(solution)/shard_map/convert_element_type | solution.py:286
  99.8 3.5 %convolution_convert_fusion = bf16[1536,1536]{1,0:T(8,128)(2,1)} fusion(bf16[192,1536]{1,0:T(8,128)(2,1)S(1)} %bitcast.65, bf16[192,1536]{1,0:T(8,128)(2,1)S(1)} %get-tuple-element.141), kind=kOutput, calls=%fused_computation | convolution fusion | flops 908328960 | bytes 5898240 | tf_op jit(solution)/shard_map/dot_general | solution.py:287
  103.4 4.0 %convolution_convert_fusion.1 = bf16[12,16,1536]{2,1,0:T(8,128)(2,1)S(1)} fusion(bf16[12,16,1536]{2,1,0:T(8,128)(2,1)S(1)} %bitcast.66, bf16[1536,1536,1]{1,0,2:T(8,128)(2,1)} %bitcast.63), kind=kOutput, calls=%fused_computation.52 | convolution fusion | flops 906264576 | bytes 5898240 | tf_op jit(solution)/shard_map/hwf,cf->hwc/dot_general | solution.py:294
  108.2 0.9 collective-permute-done.11
  109.1 1.0 convert_add_fusion
  110.2 1.7 collective-permute-start.12
  111.9 7.4 %collective-permute-done.12 = f32[1,3,16,1536]{3,2,1,0:T(8,128)S(1)} collective-permute-done((f32[1,3,16,1536]{3,2,1,0:T(8,128)S(1)}, f32[1,3,16,1536]{3,2,1,0:T(8,128)S(1)}, u32[]{:S(2)}, u32[]{:S(2)}) %collective-permute-start.12) | collective-permute-done | bytes 294944 | tf_op jit(solution)/shard_map/ppermute | solution.py:69
  119.5 1.6 fusion.140
  124.0 0.9 dynamic-slice_reduce_fusion
  124.9 1.4 collective-permute-done.15
  126.8 1.7 collective-permute-start.16
  128.5 2.8 %collective-permute-done.16 = f32[18816]{0:T(1024)S(1)} collective-permute-done((f32[18816]{0:T(1024)S(1)}, f32[18816]{0:T(1024)S(1)}, u32[]{:S(2)}, u32[]{:S(2)}) %collective-permute-start.16) | collective-permute-done | bytes 75296 | tf_op jit(solution)/shard_map/ppermute | solution.py:49
  131.8 1.9 collective-permute-start.17
  133.7 3.0 %collective-permute-done.17 = f32[9408]{0:T(1024)S(1)} collective-permute-done((f32[9408]{0:T(1024)S(1)}, f32[9408]{0:T(1024)S(1)}, u32[]{:S(2)}, u32[]{:S(2)}) %collective-permute-start.17) | collective-permute-done | bytes 37664 | tf_op jit(solution)/shard_map/ppermute | solution.py:49
  137.0 1.6 collective-permute-start.18
  138.6 3.7 %collective-permute-done.18 = f32[4704]{0:T(1024)S(1)} collective-permute-done((f32[4704]{0:T(1024)S(1)}, f32[4704]{0:T(1024)S(1)}, u32[]{:S(2)}, u32[]{:S(2)}) %collective-permute-start.18) | collective-permute-done | bytes 18848 | tf_op jit(solution)/shard_map/ppermute | solution.py:49
  142.5 1.9 collective-permute-start.19
  144.4 4.1 %collective-permute-done.19 = f32[2352]{0:T(1024)S(1)} collective-permute-done((f32[2352]{0:T(1024)S(1)}, f32[2352]{0:T(1024)S(1)}, u32[]{:S(2)}, u32[]{:S(2)}) %collective-permute-start.19) | collective-permute-done | bytes 9440 | tf_op jit(solution)/shard_map/ppermute | solution.py:49
  148.5 0.9 collective-permute-start.20
  149.4 4.1 %collective-permute-done.20 = f32[2352]{0:T(1024)S(1)} collective-permute-done((f32[2352]{0:T(1024)S(1)}, f32[2352]{0:T(1024)S(1)}, u32[]{:S(2)}, u32[]{:S(2)}) %collective-permute-start.20) | collective-permute-done | bytes 9440 | tf_op jit(solution)/shard_map/ppermute | solution.py:52
  153.6 1.2 collective-permute-start.21
  154.8 2.5 %collective-permute-done.21 = f32[4704]{0:T(1024)S(1)} collective-permute-done((f32[4704]{0:T(1024)S(1)}, f32[4704]{0:T(1024)S(1)}, u32[]{:S(2)}, u32[]{:S(2)}) %collective-permute-start.21) | collective-permute-done | bytes 18848 | tf_op jit(solution)/shard_map/ppermute | solution.py:52
  157.5 1.6 collective-permute-start.22
  159.1 1.3 collective-permute-start.13
  160.3 1.3 collective-permute-start.14
  161.8 4.4 %collective-permute-start.23 = (f32[18816]{0:T(1024)S(1)}, f32[18816]{0:T(1024)S(1)}, u32[]{:S(2)}, u32[]{:S(2)}) collective-permute-start(f32[18816]{0:T(1024)S(1)} %maximum_select_fusion.4), channel_id=1, source_target_pairs={{0,2},{1,3},{2,0},{3,1},{4,6},{5,7},{6,4},{7,5},{8,10},{9,11},{10,... | collective-permute-start | bytes 225800 | tf_op jit(solution)/shard_map/ppermute | solution.py:52
  166.4 4.0 %collective-permute-done.23 = f32[18816]{0:T(1024)S(1)} collective-permute-done((f32[18816]{0:T(1024)S(1)}, f32[18816]{0:T(1024)S(1)}, u32[]{:S(2)}, u32[]{:S(2)}) %collective-permute-start.23) | collective-permute-done | bytes 75296 | tf_op jit(solution)/shard_map/ppermute | solution.py:52
  170.7 2.8 %fusion.146 = bf16[1,3,16,1536]{3,2,1,0:T(8,128)(2,1)} fusion(f32[1536]{0:T(1024)S(1)} %copy-done.44, bf16[9,22,1536]{2,1,0:T(8,128)(2,1)S(1)} %select_maximum_fusion, f32[1536]{0:T(1024)S(1)} %copy-done.46, f32[1536]{0:T(1024)S(1)} %get-tuple-element.63, f32[1536]{0:T(1024)S(1)} %get-tuple-element.64, bf16[3,16,1536]{2,1,0:T(8,128)(2,1)S(1)} %collective-permute-done.13, ...), kind=kLoop, calls=%fused_computation.297 | loop fusion | flops 11132928 | bytes 7084032 | tf_op jit(solution)/shard_map/reshape | solution.py:309
  173.5 0.8 select_n.294
  174.3 28.0 %reduce-scatter.2.cloned.1.call-done = bf16[192,1536]{1,0:T(8,128)(2,1)} async-done(((bf16[1536,1536]{1,0:T(8,128)(2,1)}), bf16[192,1536]{1,0:T(8,128)(2,1)}) %reduce-scatter.2.cloned.1.call-update) | async-done | bytes 589840 | tf_op jit(solution)/shard_map/reduce_scatter | solution.py:290
  202.3 2.2 %convert_element_type.497 = f32[192,1536]{1,0:T(8,128)} convert(bf16[192,1536]{1,0:T(8,128)(2,1)} %reduce-scatter.2.cloned.1.call-done) | non-fusion elementwise | flops 294912 | bytes 1769472 | tf_op jit(solution)/shard_map/convert_element_type | solution.py:292
  (232 shorter events, 12.7 us)
Async XLA Ops:
  7.2 195.1 %reduce-scatter.2.cloned.1.call-start = ((), (), s32[]{:S(2)}) async-start(), calls=%async_computation.1 | async-start | bytes 5308416 | tf_op jit(solution)/shard_map/reduce_scatter | solution.py:290
  8.4 25.1 %collective-permute-start = (bf16[192,1536]{1,0:T(8,128)(2,1)S(1)}, bf16[192,1536]{1,0:T(8,128)(2,1)S(1)}, u32[]{:S(2)}, u32[]{:S(2)}) collective-permute-start(bf16[192,1536]{1,0:T(8,128)(2,1)S(1)} %compare_select_fusion), channel_id=1, source_target_pairs={{0,8},{8,16},{16,24},{24,28},{28,20},{20,12},{12,4},{4,0},{1,9},{9... | collective-permute-start | bytes 1769480 | tf_op jit(solution)/shard_map/ppermute | solution.py:112
  11.5 22.0 %collective-permute-start.1 = (bf16[192,1536]{1,0:T(8,128)(2,1)S(1)}, bf16[192,1536]{1,0:T(8,128)(2,1)S(1)}, u32[]{:S(2)}, u32[]{:S(2)}) collective-permute-start(bf16[192,1536]{1,0:T(8,128)(2,1)S(1)} %compare_select_fusion), channel_id=1, source_target_pairs={{0,4},{8,0},{16,8},{24,16},{28,24},{20,28},{12,20},{4,12},{1,5},{9... | collective-permute-start | bytes 1769480 | tf_op jit(solution)/shard_map/ppermute | solution.py:114
  34.2 5.0 %collective-permute-start.2 = (bf16[3,16,1536]{2,1,0:T(8,128)(2,1)S(1)}, bf16[3,16,1536]{2,1,0:T(8,128)(2,1)S(1)}, u32[]{:S(2)}, u32[]{:S(2)}) collective-permute-start(bf16[3,16,1536]{2,1,0:T(8,128)(2,1)S(1)} %bitcast.67), channel_id=1, source_target_pairs={{0,1},{1,2},{2,3},{4,5},{5,6},{6,7},{8,9},{9,10},{10,11},{12,13},{... | collective-permute-start | bytes 442376 | tf_op jit(solution)/shard_map/ppermute | solution.py:16
  35.7 5.3 %collective-permute-start.3 = (bf16[3,16,1536]{2,1,0:T(8,128)(2,1)S(1)}, bf16[3,16,1536]{2,1,0:T(8,128)(2,1)S(1)}, u32[]{:S(2)}, u32[]{:S(2)}) collective-permute-start(bf16[3,16,1536]{2,1,0:T(8,128)(2,1)S(1)} %bitcast.68), channel_id=1, source_target_pairs={{1,0},{2,1},{3,2},{5,4},{6,5},{7,6},{9,8},{10,9},{11,10},{13,12},{... | collective-permute-start | bytes 442376 | tf_op jit(solution)/shard_map/ppermute | solution.py:19
  37.0 14.0 %collective-permute-start.6 = (bf16[192,1536]{1,0:T(8,128)(2,1)S(1)}, bf16[192,1536]{1,0:T(8,128)(2,1)S(1)}, u32[]{:S(2)}, u32[]{:S(2)}) collective-permute-start(bf16[192,1536]{1,0:T(8,128)(2,1)S(1)} %collective-permute-done), channel_id=1, source_target_pairs={{0,8},{8,16},{16,24},{24,28},{28,20},{20,12},{12,4},{4,0},{1,9},{9... | collective-permute-start | bytes 1769480 | tf_op jit(solution)/shard_map/ppermute | solution.py:112
  38.9 14.5 %collective-permute-start.7 = (bf16[192,1536]{1,0:T(8,128)(2,1)S(1)}, bf16[192,1536]{1,0:T(8,128)(2,1)S(1)}, u32[]{:S(2)}, u32[]{:S(2)}) collective-permute-start(bf16[192,1536]{1,0:T(8,128)(2,1)S(1)} %collective-permute-done.1), channel_id=1, source_target_pairs={{0,4},{8,0},{16,8},{24,16},{28,24},{20,28},{12,20},{4,12},{1,5},{9... | collective-permute-start | bytes 1769480 | tf_op jit(solution)/shard_map/ppermute | solution.py:114
  44.9 74.4 %copy-start.47 = (f32[3,16]{1,0:T(4,128)}, f32[3,16]{1,0:T(4,128)S(1)}, u32[]{:S(2)}) copy-start(f32[3,16]{1,0:T(4,128)S(1)} %broadcast_multiply_fusion.2) | copy-start | bytes 580
  45.1 74.2 %copy-start.48 = (f32[3,16]{1,0:T(4,128)}, f32[3,16]{1,0:T(4,128)S(1)}, u32[]{:S(2)}) copy-start(f32[3,16]{1,0:T(4,128)S(1)} %add_rsqrt_fusion) | copy-start | bytes 580
  45.2 5.1 %collective-permute-start.4 = (bf16[1,3,16,1536]{3,2,1,0:T(8,128)(2,1)S(1)}, bf16[1,3,16,1536]{3,2,1,0:T(8,128)(2,1)S(1)}, u32[]{:S(2)}, u32[]{:S(2)}) collective-permute-start(bf16[1,3,16,1536]{3,2,1,0:T(8,128)(2,1)S(1)} %fusion.143), channel_id=1, source_target_pairs={{0,1},{1,0},{2,3},{3,2},{4,5},{5,4},{6,7},{7,6},{8,9},{9,8},{10,11... | collective-permute-start | bytes 442376 | tf_op jit(solution)/shard_map/ppermute | solution.py:168
  50.3 9.3 %collective-permute-start.5 = (bf16[2,3,16,1536]{3,2,1,0:T(8,128)(2,1)S(1)}, bf16[2,3,16,1536]{3,2,1,0:T(8,128)(2,1)S(1)}, u32[]{:S(2)}, u32[]{:S(2)}) collective-permute-start(bf16[2,3,16,1536]{3,2,1,0:T(8,128)(2,1)S(1)} %maximum_select_fusion.2), channel_id=1, source_target_pairs={{0,2},{1,3},{2,0},{3,1},{4,6},{5,7},{6,4},{7,5},{8,10},{9,11},{10,... | collective-permute-start | bytes 884744 | tf_op jit(solution)/shard_map/ppermute | solution.py:168
  51.0 14.9 %collective-permute-start.8 = (bf16[192,1536]{1,0:T(8,128)(2,1)S(1)}, bf16[192,1536]{1,0:T(8,128)(2,1)S(1)}, u32[]{:S(2)}, u32[]{:S(2)}) collective-permute-start(bf16[192,1536]{1,0:T(8,128)(2,1)S(1)} %collective-permute-done.6), channel_id=1, source_target_pairs={{0,8},{8,16},{16,24},{24,28},{28,20},{20,12},{12,4},{4,0},{1,9},{9... | collective-permute-start | bytes 1769480 | tf_op jit(solution)/shard_map/ppermute | solution.py:112
  53.4 15.4 %collective-permute-start.9 = (bf16[192,1536]{1,0:T(8,128)(2,1)S(1)}, bf16[192,1536]{1,0:T(8,128)(2,1)S(1)}, u32[]{:S(2)}, u32[]{:S(2)}) collective-permute-start(bf16[192,1536]{1,0:T(8,128)(2,1)S(1)} %collective-permute-done.7), channel_id=1, source_target_pairs={{0,4},{8,0},{16,8},{24,16},{28,24},{20,28},{12,20},{4,12},{1,5},{9... | collective-permute-start | bytes 1769480 | tf_op jit(solution)/shard_map/ppermute | solution.py:114
  65.9 16.7 %collective-permute-start.10 = (bf16[192,1536]{1,0:T(8,128)(2,1)S(1)}, bf16[192,1536]{1,0:T(8,128)(2,1)S(1)}, u32[]{:S(2)}, u32[]{:S(2)}) collective-permute-start(bf16[192,1536]{1,0:T(8,128)(2,1)S(1)} %collective-permute-done.8), channel_id=1, source_target_pairs={{0,8},{8,16},{16,24},{24,28},{28,20},{20,12},{12,4},{4,0},{1,9},{9... | collective-permute-start | bytes 1769480 | tf_op jit(solution)/shard_map/ppermute | solution.py:112
  107.5 1.6 collective-permute-start.11
  110.2 9.1 %collective-permute-start.12 = (f32[1,3,16,1536]{3,2,1,0:T(8,128)S(1)}, f32[1,3,16,1536]{3,2,1,0:T(8,128)S(1)}, u32[]{:S(2)}, u32[]{:S(2)}) collective-permute-start(f32[1,3,16,1536]{3,2,1,0:T(8,128)S(1)} %constant_dynamic-slice_fusion), channel_id=1, source_target_pairs={{0,2},{1,3},{2,0},{3,1},{4,6},{5,7},{6,4},{7,5},{8,10},{9,11},{10,... | collective-permute-start | bytes 884744 | tf_op jit(solution)/shard_map/ppermute | solution.py:69
  124.8 1.4 collective-permute-start.15
  126.8 4.5 %collective-permute-start.16 = (f32[18816]{0:T(1024)S(1)}, f32[18816]{0:T(1024)S(1)}, u32[]{:S(2)}, u32[]{:S(2)}) collective-permute-start(f32[18816]{0:T(1024)S(1)} %get-tuple-element.115), channel_id=1, source_target_pairs={{0,2},{1,3},{2,0},{3,1},{4,6},{5,7},{6,4},{7,5},{8,10},{9,11},{10,... | collective-permute-start | bytes 225800 | tf_op jit(solution)/shard_map/ppermute | solution.py:49
  131.6 38.8 %copy-start.8 = (f32[1536]{0:T(1024)S(1)}, f32[1536]{0:T(1024)}, u32[]{:S(2)}) copy-start(f32[1536]{0:T(1024)} %get-tuple-element.91) | copy-start | bytes 18436
  131.7 38.8 %copy-start.10 = (f32[1536]{0:T(1024)S(1)}, f32[1536]{0:T(1024)}, u32[]{:S(2)}) copy-start(f32[1536]{0:T(1024)} %get-tuple-element.92) | copy-start | bytes 18436
  131.7 38.8 %copy-start.12 = (f32[1536]{0:T(1024)S(1)}, f32[1536]{0:T(1024)}, u32[]{:S(2)}) copy-start(f32[1536]{0:T(1024)} %get-tuple-element.93) | copy-start | bytes 18436
  131.7 38.8 %copy-start.14 = (f32[1536]{0:T(1024)S(1)}, f32[1536]{0:T(1024)}, u32[]{:S(2)}) copy-start(f32[1536]{0:T(1024)} %get-tuple-element.94) | copy-start | bytes 18436
  131.7 38.8 %copy-start.16 = (f32[1536]{0:T(1024)S(1)}, f32[1536]{0:T(1024)}, u32[]{:S(2)}) copy-start(f32[1536]{0:T(1024)} %get-tuple-element.95) | copy-start | bytes 18436
  131.7 38.8 %copy-start.18 = (f32[1536]{0:T(1024)S(1)}, f32[1536]{0:T(1024)}, u32[]{:S(2)}) copy-start(f32[1536]{0:T(1024)} %get-tuple-element.96) | copy-start | bytes 18436
  131.7 38.8 %copy-start.20 = (f32[1536]{0:T(1024)S(1)}, f32[1536]{0:T(1024)}, u32[]{:S(2)}) copy-start(f32[1536]{0:T(1024)} %get-tuple-element.97) | copy-start | bytes 18436
  131.7 38.8 %copy-start.22 = (f32[1536]{0:T(1024)S(1)}, f32[1536]{0:T(1024)}, u32[]{:S(2)}) copy-start(f32[1536]{0:T(1024)} %get-tuple-element.98) | copy-start | bytes 18436
  131.7 38.8 %copy-start.24 = (f32[1536]{0:T(1024)S(1)}, f32[1536]{0:T(1024)}, u32[]{:S(2)}) copy-start(f32[1536]{0:T(1024)} %get-tuple-element.99) | copy-start | bytes 18436
  131.7 38.8 %copy-start.26 = (f32[1536]{0:T(1024)S(1)}, f32[1536]{0:T(1024)}, u32[]{:S(2)}) copy-start(f32[1536]{0:T(1024)} %copy-done.25) | copy-start | bytes 18436
  131.7 38.8 %copy-start.28 = (f32[1536]{0:T(1024)S(1)}, f32[1536]{0:T(1024)}, u32[]{:S(2)}) copy-start(f32[1536]{0:T(1024)} %copy-done.27) | copy-start | bytes 18436
  131.8 38.8 %copy-start.30 = (f32[1536]{0:T(1024)S(1)}, f32[1536]{0:T(1024)}, u32[]{:S(2)}) copy-start(f32[1536]{0:T(1024)} %copy-done.29) | copy-start | bytes 18436
  131.8 38.8 %copy-start.32 = (f32[1536]{0:T(1024)S(1)}, f32[1536]{0:T(1024)}, u32[]{:S(2)}) copy-start(f32[1536]{0:T(1024)} %copy-done.31) | copy-start | bytes 18436
  131.8 38.8 %copy-start.34 = (f32[1536]{0:T(1024)S(1)}, f32[1536]{0:T(1024)}, u32[]{:S(2)}) copy-start(f32[1536]{0:T(1024)} %copy-done.33) | copy-start | bytes 18436
  131.8 38.8 %copy-start.36 = (f32[1536]{0:T(1024)S(1)}, f32[1536]{0:T(1024)}, u32[]{:S(2)}) copy-start(f32[1536]{0:T(1024)} %copy-done.35) | copy-start | bytes 18436
  131.8 38.8 %copy-start.38 = (f32[1536]{0:T(1024)S(1)}, f32[1536]{0:T(1024)}, u32[]{:S(2)}) copy-start(f32[1536]{0:T(1024)} %copy-done.37) | copy-start | bytes 18436
  131.8 38.8 %copy-start.40 = (f32[1536]{0:T(1024)S(1)}, f32[1536]{0:T(1024)}, u32[]{:S(2)}) copy-start(f32[1536]{0:T(1024)} %copy-done.39) | copy-start | bytes 18436
  131.8 38.8 %copy-start.42 = (f32[1536]{0:T(1024)S(1)}, f32[1536]{0:T(1024)}, u32[]{:S(2)}) copy-start(f32[1536]{0:T(1024)} %copy-done.41) | copy-start | bytes 18436
  131.8 38.8 %copy-start.44 = (f32[1536]{0:T(1024)S(1)}, f32[1536]{0:T(1024)}, u32[]{:S(2)}) copy-start(f32[1536]{0:T(1024)} %copy-done.43) | copy-start | bytes 18436
  131.8 38.8 %copy-start.46 = (f32[1536]{0:T(1024)S(1)}, f32[1536]{0:T(1024)}, u32[]{:S(2)}) copy-start(f32[1536]{0:T(1024)} %copy-done.45) | copy-start | bytes 18436
  131.8 4.9 %collective-permute-start.17 = (f32[9408]{0:T(1024)S(1)}, f32[9408]{0:T(1024)S(1)}, u32[]{:S(2)}, u32[]{:S(2)}) collective-permute-start(f32[9408]{0:T(1024)S(1)} %get-tuple-element.124), channel_id=1, source_target_pairs={{0,4},{4,0},{8,12},{12,8},{16,20},{20,16},{24,28},{28,24},{1,5},{5... | collective-permute-start | bytes 112904 | tf_op jit(solution)/shard_map/ppermute | solution.py:49
  137.0 5.3 %collective-permute-start.18 = (f32[4704]{0:T(1024)S(1)}, f32[4704]{0:T(1024)S(1)}, u32[]{:S(2)}, u32[]{:S(2)}) collective-permute-start(f32[4704]{0:T(1024)S(1)} %get-tuple-element.126), channel_id=1, source_target_pairs={{0,8},{4,12},{8,0},{12,4},{16,24},{20,28},{24,16},{28,20},{1,9},{5... | collective-permute-start | bytes 56456 | tf_op jit(solution)/shard_map/ppermute | solution.py:49
  142.5 6.0 %collective-permute-start.19 = (f32[2352]{0:T(1024)S(1)}, f32[2352]{0:T(1024)S(1)}, u32[]{:S(2)}, u32[]{:S(2)}) collective-permute-start(f32[2352]{0:T(1024)S(1)} %get-tuple-element.128), channel_id=1, source_target_pairs={{0,16},{4,20},{8,24},{12,28},{16,0},{20,4},{24,8},{28,12},{1,17},{... | collective-permute-start | bytes 28232 | tf_op jit(solution)/shard_map/ppermute | solution.py:49
  148.5 5.0 %collective-permute-start.20 = (f32[2352]{0:T(1024)S(1)}, f32[2352]{0:T(1024)S(1)}, u32[]{:S(2)}, u32[]{:S(2)}) collective-permute-start(f32[2352]{0:T(1024)S(1)} %add.722), channel_id=1, source_target_pairs={{0,16},{4,20},{8,24},{12,28},{16,0},{20,4},{24,8},{28,12},{1,17},{... | collective-permute-start | bytes 28232 | tf_op jit(solution)/shard_map/ppermute | solution.py:52
  153.6 3.8 %collective-permute-start.21 = (f32[4704]{0:T(1024)S(1)}, f32[4704]{0:T(1024)S(1)}, u32[]{:S(2)}, u32[]{:S(2)}) collective-permute-start(f32[4704]{0:T(1024)S(1)} %maximum_select_fusion.6), channel_id=1, source_target_pairs={{0,8},{4,12},{8,0},{12,4},{16,24},{20,28},{24,16},{28,20},{1,9},{5... | collective-permute-start | bytes 56456 | tf_op jit(solution)/shard_map/ppermute | solution.py:52
  157.5 4.2 %collective-permute-start.22 = (f32[9408]{0:T(1024)S(1)}, f32[9408]{0:T(1024)S(1)}, u32[]{:S(2)}, u32[]{:S(2)}) collective-permute-start(f32[9408]{0:T(1024)S(1)} %maximum_select_fusion.5), channel_id=1, source_target_pairs={{0,4},{4,0},{8,12},{12,8},{16,20},{20,16},{24,28},{28,24},{1,5},{5... | collective-permute-start | bytes 112904 | tf_op jit(solution)/shard_map/ppermute | solution.py:52
  159.1 7.1 %collective-permute-start.13 = (bf16[3,16,1536]{2,1,0:T(8,128)(2,1)S(1)}, bf16[3,16,1536]{2,1,0:T(8,128)(2,1)S(1)}, u32[]{:S(2)}, u32[]{:S(2)}) collective-permute-start(bf16[3,16,1536]{2,1,0:T(8,128)(2,1)S(1)} %get-tuple-element.134), channel_id=1, source_target_pairs={{0,1},{1,2},{2,3},{4,5},{5,6},{6,7},{8,9},{9,10},{10,11},{12,13},{... | collective-permute-start | bytes 442376 | tf_op jit(solution)/shard_map/ppermute | solution.py:16
  160.3 5.8 %collective-permute-start.14 = (bf16[3,16,1536]{2,1,0:T(8,128)(2,1)S(1)}, bf16[3,16,1536]{2,1,0:T(8,128)(2,1)S(1)}, u32[]{:S(2)}, u32[]{:S(2)}) collective-permute-start(bf16[3,16,1536]{2,1,0:T(8,128)(2,1)S(1)} %get-tuple-element.134), channel_id=1, source_target_pairs={{1,0},{2,1},{3,2},{5,4},{6,5},{7,6},{9,8},{10,9},{11,10},{13,12},{... | collective-permute-start | bytes 442376 | tf_op jit(solution)/shard_map/ppermute | solution.py:19
  161.8 8.6 %collective-permute-start.23 = (f32[18816]{0:T(1024)S(1)}, f32[18816]{0:T(1024)S(1)}, u32[]{:S(2)}, u32[]{:S(2)}) collective-permute-start(f32[18816]{0:T(1024)S(1)} %maximum_select_fusion.4), channel_id=1, source_target_pairs={{0,2},{1,3},{2,0},{3,1},{4,6},{5,7},{6,4},{7,5},{8,10},{9,11},{10,... | collective-permute-start | bytes 225800 | tf_op jit(solution)/shard_map/ppermute | solution.py:52
  170.4 3.1 %collective-permute-start.24 = (f32[37632]{0:T(1024)S(1)}, f32[37632]{0:T(1024)S(1)}, u32[]{:S(2)}, u32[]{:S(2)}) collective-permute-start(f32[37632]{0:T(1024)S(1)} %maximum_select_fusion.3), channel_id=1, source_target_pairs={{0,1},{1,0},{2,3},{3,2},{4,5},{5,4},{6,7},{7,6},{8,9},{9,8},{10,11... | collective-permute-start | bytes 451592 | tf_op jit(solution)/shard_map/ppermute | solution.py:52
  (34 other events, 218.1 us)
Sparse Core Ops, SparseCore 0:
  103.5 98.7 reduce-scatter.1

commit v12 on v10

--- a/solution.py
+++ b/solution.py
@@ -285,9 +285,10 @@
     w_term = lax.dot_general(
         flat, dpre, (((0,), (0,)), ((), ())), preferred_element_type=jnp.float32
     )
-    up_grad = lax.psum_scatter(
-        w_term.astype(jnp.bfloat16), "fsdp", scatter_dimension=0, tiled=True
-    ).astype(jnp.float32)
+    n_fsdp = lax.axis_size("fsdp")
+    up_grad = ring_reduce_scatter(
+        w_term.astype(jnp.bfloat16).reshape((n_fsdp, chans // n_fsdp, -1)), "fsdp", ring
+    )
     dpre_rows = dpre.reshape(height, cols, -1)
     group_terms = jnp.einsum(
         "hwf,cf->hwc", dpre_rows, columns, preferred_element_type=jnp.float32

time: 212 us -> 219 us (1.033)
  waiting for transfers between devices: 91.9 us -> 77.3 us
  starting transfers between devices: 36.3 us -> 47.3 us
  between operations: 34.9 us -> 43.1 us
  other arithmetic: 19.2 us -> 23.8 us
    reduce_scatter x1 -> x0, waiting for transfers between devices: 27.9 us -> none  [body(): lax.psum_scatter(w_term.astype(jnp.bfloat16), 'fsdp', scatter_dimension=0...]
    ppermute x0 -> x7, waiting for transfers between devices: none -> 20.6 us  [the longest x3 18.3 us: ring_reduce_scatter(): ccw = lax.ppermute(ccw, axis, backward)]
    ppermute x0 -> x7, starting transfers between devices: none -> 9.64 us  [the longest x4 6.13 us: ring_reduce_scatter(): cw = lax.ppermute(cw, axis, forward)]
    ppermute x5, waiting for transfers between devices: 15 us -> 10 us  [tree_allreduce(): flat = keep + lax.ppermute(give, axis, perm)]
    ppermute x2, waiting for transfers between devices: 8.3 us -> 4.24 us  [tree_reduce_scatter(): lax.ppermute(give, axis, perm).astype(jnp.float32)]
    add x0 -> x1, other arithmetic: none -> 2.32 us  [ring_reduce_scatter(): total = total + cw.astype(jnp.float32)]
    convert_element_type x1 -> x3, other arithmetic: 2.21 us -> 4.43 us  [the longest x2 3.05 us: ring_reduce_scatter(): (ccw.astype(jnp.float32) + term(s - behind).astype(jnp.float32)).astype(t...]
  transfers between devices with their start and end apart: 26 -> 32, of which waited for: 19 -> 20; matrix products, arithmetic and copies ran while one was open for 11% -> 11% of each run, Pallas kernels for 0% -> 0%
where the time goes in v12:
time: 219 us; the launch traced here: 218 us
  waiting for transfers between devices  77.3 us (35%)
  starting transfers between devices  47.3 us (22%)
  between operations  43.1 us (20%)
  other arithmetic  23.8 us (11%)
  matrix products  10.3 us (5%)
  local copies, waits for them, and re-layouts  10.1 us (5%)
  blocking collectives  6.37 us (3%)
    ppermute x4, waiting for transfers between devices, ring_all_gather(): cw = lax.ppermute(cw, axis, forward)  20.6 us
    ppermute x3, waiting for transfers between devices, ring_reduce_scatter(): ccw = lax.ppermute(ccw, axis, backward)  18.3 us
    ppermute x5, waiting for transfers between devices, tree_allreduce(): other = lax.ppermute(flat, axis, perm)  12.3 us
    ppermute x5, waiting for transfers between devices, tree_allreduce(): flat = keep + lax.ppermute(give, axis, perm)  10 us
    ppermute x4, starting transfers between devices, ring_all_gather(): cw = lax.ppermute(cw, axis, forward)  9.54 us
    ppermute x5, starting transfers between devices, tree_allreduce(): flat = keep + lax.ppermute(give, axis, perm)  8.47 us
    ppermute x5, starting transfers between devices, tree_allreduce(): other = lax.ppermute(flat, axis, perm)  8.31 us
    ppermute x2, waiting for transfers between devices, tree_all_gather(): other = lax.ppermute(data, axis, perm)  7.06 us
  transfers between devices with their start and end apart: 32, of which 20 were waited for; matrix products, arithmetic and copies ran while one was open for 11% of the time, Pallas kernels for 0%

profile of v12, /device:TPU:0, one launch (start us, length us, event | category | flops | bytes accessed | tf_op | source)
XLA Modules:
  0.0 218.3 jit_solution(6832949826803167545)
XLA Ops:
  1.8 3.1 %collective-permute-start = (bf16[192,1536]{1,0:T(8,128)(2,1)S(1)}, bf16[192,1536]{1,0:T(8,128)(2,1)S(1)}, u32[]{:S(2)}, u32[]{:S(2)}) collective-permute-start(bf16[192,1536]{1,0:T(8,128)(2,1)S(1)} %compare_select_fusion), channel_id=1, source_target_pairs={{0,8},{8,16},{16,24},{24,28},{28,20},{20,12},{12,4},{4,0},{1,9},{9... | collective-permute-start | bytes 1769480 | tf_op jit(solution)/shard_map/ppermute | solution.py:112
  34.1 1.5 collective-permute-start.2
  35.5 1.3 collective-permute-start.3
  36.8 1.9 collective-permute-start.6
  39.0 1.8 collective-permute-done.3
  41.3 3.4 %fusion.158 = (f32[3,16]{1,0:T(4,128)S(1)}, f32[3,16,1536]{2,1,0:T(8,128)S(1)}) fusion(f32[1536]{0:T(1024)S(1)} %get-tuple-element.105, bf16[9,22,1536]{2,1,0:T(8,128)(2,1)S(1)} %select_maximum_fusion.2, f32[1536]{0:T(1024)S(1)} %get-tuple-element.106, f32[1536]{0:T(1024)S(1)} %get-tuple-element.59, f32[1536]{0:T(1024)S(1)} %get-tuple-element.60, ...), kind=kLoop, calls=%fused_computation.388 | loop fusion | flops 10911696 | bytes 7827648 | tf_op jit(solution)/shard_map/reduce_sum | solution.py:214
  45.0 4.1 %collective-permute-start.4 = (bf16[1,3,16,1536]{3,2,1,0:T(8,128)(2,1)S(1)}, bf16[1,3,16,1536]{3,2,1,0:T(8,128)(2,1)S(1)}, u32[]{:S(2)}, u32[]{:S(2)}) collective-permute-start(bf16[1,3,16,1536]{3,2,1,0:T(8,128)(2,1)S(1)} %fusion.149), channel_id=1, source_target_pairs={{0,1},{1,0},{2,3},{3,2},{4,5},{5,4},{6,7},{7,6},{8,9},{9,8},{10,11... | collective-permute-start | bytes 442376 | tf_op jit(solution)/shard_map/ppermute | solution.py:168
  50.9 2.1 collective-permute-start.8
  53.4 6.1 %collective-permute-done.5 = bf16[2,3,16,1536]{3,2,1,0:T(8,128)(2,1)S(1)} collective-permute-done((bf16[2,3,16,1536]{3,2,1,0:T(8,128)(2,1)S(1)}, bf16[2,3,16,1536]{3,2,1,0:T(8,128)(2,1)S(1)}, u32[]{:S(2)}, u32[]{:S(2)}) %collective-permute-start.5) | collective-permute-done | bytes 294944 | tf_op jit(solution)/shard_map/ppermute | solution.py:168
  59.6 6.2 %collective-permute-done.8 = bf16[192,1536]{1,0:T(8,128)(2,1)S(1)} collective-permute-done((bf16[192,1536]{1,0:T(8,128)(2,1)S(1)}, bf16[192,1536]{1,0:T(8,128)(2,1)S(1)}, u32[]{:S(2)}, u32[]{:S(2)}) %collective-permute-start.8) | collective-permute-done | bytes 589856 | tf_op jit(solution)/shard_map/ppermute | solution.py:112
  65.7 2.4 %collective-permute-start.10 = (bf16[192,1536]{1,0:T(8,128)(2,1)S(1)}, bf16[192,1536]{1,0:T(8,128)(2,1)S(1)}, u32[]{:S(2)}, u32[]{:S(2)}) collective-permute-start(bf16[192,1536]{1,0:T(8,128)(2,1)S(1)} %collective-permute-done.8), channel_id=1, source_target_pairs={{0,8},{8,16},{16,24},{24,28},{28,20},{20,12},{12,4},{4,0},{1,9},{9... | collective-permute-start | bytes 1769480 | tf_op jit(solution)/shard_map/ppermute | solution.py:112
  68.7 13.7 %collective-permute-done.10 = bf16[192,1536]{1,0:T(8,128)(2,1)S(1)} collective-permute-done((bf16[192,1536]{1,0:T(8,128)(2,1)S(1)}, bf16[192,1536]{1,0:T(8,128)(2,1)S(1)}, u32[]{:S(2)}, u32[]{:S(2)}) %collective-permute-start.10) | collective-permute-done | bytes 589856 | tf_op jit(solution)/shard_map/ppermute | solution.py:112
  82.6 4.8 %fusion.4 = (f32[1536]{0:T(1024)S(1)}, f32[1536]{0:T(1024)S(1)}, f32[192,1536]{1,0:T(8,128)}, f32[192,1536]{1,0:T(8,128)}) fusion(bf16[1,12,16,1536]{3,2,1,0:T(8,128)(2,1)S(1)} %copy-done.4, f32[1536]{0:T(1024)S(1)} %copy-done.56, bf16[192,1536]{1,0:T(8,128)(2,1)S(1)} %bitcast.101, bf16[1536,1536]{1,0:T(8,128)(2,1)S(1)} %bitcast.99), kind=kOutput, calls=%fused_computation.64 | convolution fusion | flops 926610432 | bytes 8275968 | tf_op jit(solution)/shard_map/dot_general | solution.py:272
  88.0 6.4 %all-reduce.2 = (f32[]{:T(128)}, f32[]{:T(128)}) all-reduce(f32[]{:T(128)} %get-tuple-element.127, f32[]{:T(128)} %get-tuple-element.126), channel_id=1, replica_groups=mesh['fsdp'=8,'rows'=4] {'rows'}, use_global_device_ids=true, to_apply=%region_4.5 | all-reduce | flops 2 | bytes 16 | tf_op jit(solution)/shard_map/psum | solution.py:277
  95.7 3.4 %fusion.3 = (bf16[192,1536]{1,0:T(8,128)(2,1)S(1)}, bf16[192,1536]{1,0:T(8,128)(2,1)}) fusion(f32[192,1536]{1,0:T(8,128)} %get-tuple-element.163, f32[192,1536]{1,0:T(8,128)} %get-tuple-element.134, bf16[1,12,16,1536]{3,2,1,0:T(8,128)(2,1)} %param.23, f32[1536]{0:T(1024)S(1)} %get-tuple-element.147, f32[1536]{0:T(1024)S(1)} %get-tuple-element.132, ...), kind=kLoop, calls=%fused_computation.63 | loop fusion | flops 5603328 | bytes 4159488 | tf_op jit(solution)/shard_map/convert_element_type | solution.py:284
  99.1 4.0 %convolution_convert_fusion.1 = bf16[12,16,1536]{2,1,0:T(8,128)(2,1)S(1)} fusion(bf16[12,16,1536]{2,1,0:T(8,128)(2,1)S(1)} %bitcast.103, bf16[1536,1536,1]{1,0,2:T(8,128)(2,1)} %bitcast.100), kind=kOutput, calls=%fused_computation.52 | convolution fusion | flops 906264576 | bytes 5898240 | tf_op jit(solution)/shard_map/hwf,cf->hwc/dot_general | solution.py:293
  109.5 1.7 collective-permute-start.12
  111.2 1.4 convolution_convert_fusion
  112.8 2.0 collective-permute-start.18
  114.7 4.2 %collective-permute-done.12 = f32[1,3,16,1536]{3,2,1,0:T(8,128)S(1)} collective-permute-done((f32[1,3,16,1536]{3,2,1,0:T(8,128)S(1)}, f32[1,3,16,1536]{3,2,1,0:T(8,128)S(1)}, u32[]{:S(2)}, u32[]{:S(2)}) %collective-permute-start.12) | collective-permute-done | bytes 294944 | tf_op jit(solution)/shard_map/ppermute | solution.py:69
  119.2 1.6 fusion.146
  124.6 1.4 collective-permute-done.22
  126.5 1.7 collective-permute-start.23
  128.2 2.8 %collective-permute-done.23 = f32[18816]{0:T(1024)S(1)} collective-permute-done((f32[18816]{0:T(1024)S(1)}, f32[18816]{0:T(1024)S(1)}, u32[]{:S(2)}, u32[]{:S(2)}) %collective-permute-start.23) | collective-permute-done | bytes 75296 | tf_op jit(solution)/shard_map/ppermute | solution.py:49
  131.3 1.9 collective-permute-start.24
  133.2 2.2 %collective-permute-done.24 = f32[9408]{0:T(1024)S(1)} collective-permute-done((f32[9408]{0:T(1024)S(1)}, f32[9408]{0:T(1024)S(1)}, u32[]{:S(2)}, u32[]{:S(2)}) %collective-permute-start.24) | collective-permute-done | bytes 37664 | tf_op jit(solution)/shard_map/ppermute | solution.py:49
  135.6 1.8 collective-permute-start.25
  137.5 2.0 collective-permute-done.25
  139.6 3.0 %collective-permute-start.26 = (f32[2352]{0:T(1024)S(1)}, f32[2352]{0:T(1024)S(1)}, u32[]{:S(2)}, u32[]{:S(2)}) collective-permute-start(f32[2352]{0:T(1024)S(1)} %get-tuple-element.124), channel_id=1, source_target_pairs={{0,16},{4,20},{8,24},{12,28},{16,0},{20,4},{24,8},{28,12},{1,17},{... | collective-permute-start | bytes 28232 | tf_op jit(solution)/shard_map/ppermute | solution.py:49
  142.6 1.7 collective-permute-done.26
  144.3 2.9 %collective-permute-start.27 = (f32[2352]{0:T(1024)S(1)}, f32[2352]{0:T(1024)S(1)}, u32[]{:S(2)}, u32[]{:S(2)}) collective-permute-start(f32[2352]{0:T(1024)S(1)} %add.874), channel_id=1, source_target_pairs={{0,16},{4,20},{8,24},{12,28},{16,0},{20,4},{24,8},{28,12},{1,17},{... | collective-permute-start | bytes 28232 | tf_op jit(solution)/shard_map/ppermute | solution.py:52
  158.4 1.7 collective-permute-start.15
  160.2 1.3 collective-permute-start.13
  161.5 1.3 collective-permute-start.14
  163.2 1.4 fusion.13
  164.6 1.7 collective-permute-start.19
  166.3 3.3 %collective-permute-done.28 = f32[4704]{0:T(1024)S(1)} collective-permute-done((f32[4704]{0:T(1024)S(1)}, f32[4704]{0:T(1024)S(1)}, u32[]{:S(2)}, u32[]{:S(2)}) %collective-permute-start.28) | collective-permute-done | bytes 18848 | tf_op jit(solution)/shard_map/ppermute | solution.py:52
  170.8 9.0 %collective-permute-done.29 = f32[9408]{0:T(1024)S(1)} collective-permute-done((f32[9408]{0:T(1024)S(1)}, f32[9408]{0:T(1024)S(1)}, u32[]{:S(2)}, u32[]{:S(2)}) %collective-permute-start.29) | collective-permute-done | bytes 37664 | tf_op jit(solution)/shard_map/ppermute | solution.py:52
  180.2 4.1 %collective-permute-start.30 = (f32[18816]{0:T(1024)S(1)}, f32[18816]{0:T(1024)S(1)}, u32[]{:S(2)}, u32[]{:S(2)}) collective-permute-start(f32[18816]{0:T(1024)S(1)} %maximum_select_fusion.4), channel_id=1, source_target_pairs={{0,2},{1,3},{2,0},{3,1},{4,6},{5,7},{6,4},{7,5},{8,10},{9,11},{10,... | collective-permute-start | bytes 225800 | tf_op jit(solution)/shard_map/ppermute | solution.py:52
  184.2 1.5 fusion.15
  185.8 2.0 collective-permute-start.20
  188.0 2.8 %fusion.152 = bf16[1,3,16,1536]{3,2,1,0:T(8,128)(2,1)} fusion(f32[1536]{0:T(1024)S(1)} %copy-done.46, bf16[9,22,1536]{2,1,0:T(8,128)(2,1)S(1)} %select_maximum_fusion, f32[1536]{0:T(1024)S(1)} %copy-done.48, f32[1536]{0:T(1024)S(1)} %get-tuple-element.59, f32[1536]{0:T(1024)S(1)} %get-tuple-element.60, bf16[3,16,1536]{2,1,0:T(8,128)(2,1)S(1)} %collective-permute-done.13, ...), kind=kLoop, calls=%fused_computation.311 | loop fusion | flops 11132928 | bytes 7084032 | tf_op jit(solution)/shard_map/reshape | solution.py:308
  190.9 7.8 %collective-permute-done.16 = bf16[192,1536]{1,0:T(8,128)(2,1)S(1)} collective-permute-done((bf16[192,1536]{1,0:T(8,128)(2,1)S(1)}, bf16[192,1536]{1,0:T(8,128)(2,1)S(1)}, u32[]{:S(2)}, u32[]{:S(2)}) %collective-permute-start.16) | collective-permute-done | bytes 589856 | tf_op jit(solution)/shard_map/ppermute | solution.py:147
  198.8 1.5 fusion.14
  200.3 1.7 collective-permute-start.17
  203.3 10.5 %collective-permute-done.17 = bf16[192,1536]{1,0:T(8,128)(2,1)S(1)} collective-permute-done((bf16[192,1536]{1,0:T(8,128)(2,1)S(1)}, bf16[192,1536]{1,0:T(8,128)(2,1)S(1)}, u32[]{:S(2)}, u32[]{:S(2)}) %collective-permute-start.17) | collective-permute-done | bytes 589856 | tf_op jit(solution)/shard_map/ppermute | solution.py:147
  213.7 2.2 %collective-permute-done.21 = bf16[192,1536]{1,0:T(8,128)(2,1)S(1)} collective-permute-done((bf16[192,1536]{1,0:T(8,128)(2,1)S(1)}, bf16[192,1536]{1,0:T(8,128)(2,1)S(1)}, u32[]{:S(2)}, u32[]{:S(2)}) %collective-permute-start.21) | collective-permute-done | bytes 589856 | tf_op jit(solution)/shard_map/ppermute | solution.py:145
  215.9 2.3 %fusion.16 = f32[192,1536]{1,0:T(8,128)} fusion(bf16[192,1536]{1,0:T(8,128)(2,1)S(1)} %collective-permute-done.21, bf16[192,1536]{1,0:T(8,128)(2,1)S(1)} %collective-permute-done.17, bf16[8,192,1536]{2,1,0:T(8,128)(2,1)} %bitcast.98, s32[]{:T(128)S(6)} %select_n.357), kind=kLoop, calls=%fused_computation.82 | loop fusion | flops 1474560 | bytes 2949124 | tf_op jit(solution)/shard_map/add | solution.py:151
  (251 shorter events, 20.5 us)
Async XLA Ops:
  0.6 16.1 %copy-start.7 = (s32[8]{0:T(128)S(1)}, s32[8]{0:T(128)}, u32[]{:S(2)}) copy-start(s32[8]{0:T(128)} %constant.361.clone) | copy-start | bytes 100
  0.7 25.9 %copy-start.6 = (f32[7,7,1536]{2,1,0:T(8,128)S(1)}, f32[7,7,1536]{2,1,0:T(8,128)}, u32[]{:S(2)}) copy-start(f32[7,7,1536]{2,1,0:T(8,128)} %param.15) | copy-start | bytes 903172
  1.8 31.5 %collective-permute-start = (bf16[192,1536]{1,0:T(8,128)(2,1)S(1)}, bf16[192,1536]{1,0:T(8,128)(2,1)S(1)}, u32[]{:S(2)}, u32[]{:S(2)}) collective-permute-start(bf16[192,1536]{1,0:T(8,128)(2,1)S(1)} %compare_select_fusion), channel_id=1, source_target_pairs={{0,8},{8,16},{16,24},{24,28},{28,20},{20,12},{12,4},{4,0},{1,9},{9... | collective-permute-start | bytes 1769480 | tf_op jit(solution)/shard_map/ppermute | solution.py:112
  4.9 28.4 %collective-permute-start.1 = (bf16[192,1536]{1,0:T(8,128)(2,1)S(1)}, bf16[192,1536]{1,0:T(8,128)(2,1)S(1)}, u32[]{:S(2)}, u32[]{:S(2)}) collective-permute-start(bf16[192,1536]{1,0:T(8,128)(2,1)S(1)} %compare_select_fusion), channel_id=1, source_target_pairs={{0,4},{8,0},{16,8},{24,16},{28,24},{20,28},{12,20},{4,12},{1,5},{9... | collective-permute-start | bytes 1769480 | tf_op jit(solution)/shard_map/ppermute | solution.py:114
  27.2 13.9 %copy-start.9 = (f32[1536]{0:T(1024)}, f32[1536]{0:T(1024)S(1)}, u32[]{:S(2)}) copy-start(f32[1536]{0:T(1024)S(1)} %get-tuple-element.87) | copy-start | bytes 18436
  27.2 13.9 %copy-start.11 = (f32[1536]{0:T(1024)}, f32[1536]{0:T(1024)S(1)}, u32[]{:S(2)}) copy-start(f32[1536]{0:T(1024)S(1)} %get-tuple-element.88) | copy-start | bytes 18436
  27.2 13.9 %copy-start.13 = (f32[1536]{0:T(1024)}, f32[1536]{0:T(1024)S(1)}, u32[]{:S(2)}) copy-start(f32[1536]{0:T(1024)S(1)} %get-tuple-element.89) | copy-start | bytes 18436
  27.2 13.9 %copy-start.15 = (f32[1536]{0:T(1024)}, f32[1536]{0:T(1024)S(1)}, u32[]{:S(2)}) copy-start(f32[1536]{0:T(1024)S(1)} %get-tuple-element.90) | copy-start | bytes 18436
  27.2 13.9 %copy-start.17 = (f32[1536]{0:T(1024)}, f32[1536]{0:T(1024)S(1)}, u32[]{:S(2)}) copy-start(f32[1536]{0:T(1024)S(1)} %get-tuple-element.91) | copy-start | bytes 18436
  27.2 13.9 %copy-start.19 = (f32[1536]{0:T(1024)}, f32[1536]{0:T(1024)S(1)}, u32[]{:S(2)}) copy-start(f32[1536]{0:T(1024)S(1)} %get-tuple-element.92) | copy-start | bytes 18436
  27.2 13.9 %copy-start.21 = (f32[1536]{0:T(1024)}, f32[1536]{0:T(1024)S(1)}, u32[]{:S(2)}) copy-start(f32[1536]{0:T(1024)S(1)} %get-tuple-element.93) | copy-start | bytes 18436
  27.2 13.9 %copy-start.23 = (f32[1536]{0:T(1024)}, f32[1536]{0:T(1024)S(1)}, u32[]{:S(2)}) copy-start(f32[1536]{0:T(1024)S(1)} %get-tuple-element.94) | copy-start | bytes 18436
  27.3 13.9 %copy-start.25 = (f32[1536]{0:T(1024)}, f32[1536]{0:T(1024)S(1)}, u32[]{:S(2)}) copy-start(f32[1536]{0:T(1024)S(1)} %get-tuple-element.95) | copy-start | bytes 18436
  34.1 4.9 %collective-permute-start.2 = (bf16[3,16,1536]{2,1,0:T(8,128)(2,1)S(1)}, bf16[3,16,1536]{2,1,0:T(8,128)(2,1)S(1)}, u32[]{:S(2)}, u32[]{:S(2)}) collective-permute-start(bf16[3,16,1536]{2,1,0:T(8,128)(2,1)S(1)} %bitcast.104), channel_id=1, source_target_pairs={{0,1},{1,2},{2,3},{4,5},{5,6},{6,7},{8,9},{9,10},{10,11},{12,13},{... | collective-permute-start | bytes 442376 | tf_op jit(solution)/shard_map/ppermute | solution.py:16
  35.5 5.3 %collective-permute-start.3 = (bf16[3,16,1536]{2,1,0:T(8,128)(2,1)S(1)}, bf16[3,16,1536]{2,1,0:T(8,128)(2,1)S(1)}, u32[]{:S(2)}, u32[]{:S(2)}) collective-permute-start(bf16[3,16,1536]{2,1,0:T(8,128)(2,1)S(1)} %bitcast.105), channel_id=1, source_target_pairs={{1,0},{2,1},{3,2},{5,4},{6,5},{7,6},{9,8},{10,9},{11,10},{13,12},{... | collective-permute-start | bytes 442376 | tf_op jit(solution)/shard_map/ppermute | solution.py:19
  36.8 14.0 %collective-permute-start.6 = (bf16[192,1536]{1,0:T(8,128)(2,1)S(1)}, bf16[192,1536]{1,0:T(8,128)(2,1)S(1)}, u32[]{:S(2)}, u32[]{:S(2)}) collective-permute-start(bf16[192,1536]{1,0:T(8,128)(2,1)S(1)} %collective-permute-done), channel_id=1, source_target_pairs={{0,8},{8,16},{16,24},{24,28},{28,20},{20,12},{12,4},{4,0},{1,9},{9... | collective-permute-start | bytes 1769480 | tf_op jit(solution)/shard_map/ppermute | solution.py:112
  38.7 14.5 %collective-permute-start.7 = (bf16[192,1536]{1,0:T(8,128)(2,1)S(1)}, bf16[192,1536]{1,0:T(8,128)(2,1)S(1)}, u32[]{:S(2)}, u32[]{:S(2)}) collective-permute-start(bf16[192,1536]{1,0:T(8,128)(2,1)S(1)} %collective-permute-done.1), channel_id=1, source_target_pairs={{0,4},{8,0},{16,8},{24,16},{28,24},{20,28},{12,20},{4,12},{1,5},{9... | collective-permute-start | bytes 1769480 | tf_op jit(solution)/shard_map/ppermute | solution.py:114
  44.7 74.3 %copy-start.49 = (f32[3,16]{1,0:T(4,128)}, f32[3,16]{1,0:T(4,128)S(1)}, u32[]{:S(2)}) copy-start(f32[3,16]{1,0:T(4,128)S(1)} %broadcast_multiply_fusion.2) | copy-start | bytes 580
  44.9 74.1 %copy-start.50 = (f32[3,16]{1,0:T(4,128)}, f32[3,16]{1,0:T(4,128)S(1)}, u32[]{:S(2)}) copy-start(f32[3,16]{1,0:T(4,128)S(1)} %add_rsqrt_fusion) | copy-start | bytes 580
  45.0 5.1 %collective-permute-start.4 = (bf16[1,3,16,1536]{3,2,1,0:T(8,128)(2,1)S(1)}, bf16[1,3,16,1536]{3,2,1,0:T(8,128)(2,1)S(1)}, u32[]{:S(2)}, u32[]{:S(2)}) collective-permute-start(bf16[1,3,16,1536]{3,2,1,0:T(8,128)(2,1)S(1)} %fusion.149), channel_id=1, source_target_pairs={{0,1},{1,0},{2,3},{3,2},{4,5},{5,4},{6,7},{7,6},{8,9},{9,8},{10,11... | collective-permute-start | bytes 442376 | tf_op jit(solution)/shard_map/ppermute | solution.py:168
  50.1 9.3 %collective-permute-start.5 = (bf16[2,3,16,1536]{3,2,1,0:T(8,128)(2,1)S(1)}, bf16[2,3,16,1536]{3,2,1,0:T(8,128)(2,1)S(1)}, u32[]{:S(2)}, u32[]{:S(2)}) collective-permute-start(bf16[2,3,16,1536]{3,2,1,0:T(8,128)(2,1)S(1)} %maximum_select_fusion.2), channel_id=1, source_target_pairs={{0,2},{1,3},{2,0},{3,1},{4,6},{5,7},{6,4},{7,5},{8,10},{9,11},{10,... | collective-permute-start | bytes 884744 | tf_op jit(solution)/shard_map/ppermute | solution.py:168
  50.9 14.9 %collective-permute-start.8 = (bf16[192,1536]{1,0:T(8,128)(2,1)S(1)}, bf16[192,1536]{1,0:T(8,128)(2,1)S(1)}, u32[]{:S(2)}, u32[]{:S(2)}) collective-permute-start(bf16[192,1536]{1,0:T(8,128)(2,1)S(1)} %collective-permute-done.6), channel_id=1, source_target_pairs={{0,8},{8,16},{16,24},{24,28},{28,20},{20,12},{12,4},{4,0},{1,9},{9... | collective-permute-start | bytes 1769480 | tf_op jit(solution)/shard_map/ppermute | solution.py:112
  53.3 15.4 %collective-permute-start.9 = (bf16[192,1536]{1,0:T(8,128)(2,1)S(1)}, bf16[192,1536]{1,0:T(8,128)(2,1)S(1)}, u32[]{:S(2)}, u32[]{:S(2)}) collective-permute-start(bf16[192,1536]{1,0:T(8,128)(2,1)S(1)} %collective-permute-done.7), channel_id=1, source_target_pairs={{0,4},{8,0},{16,8},{24,16},{28,24},{20,28},{12,20},{4,12},{1,5},{9... | collective-permute-start | bytes 1769480 | tf_op jit(solution)/shard_map/ppermute | solution.py:114
  65.7 16.7 %collective-permute-start.10 = (bf16[192,1536]{1,0:T(8,128)(2,1)S(1)}, bf16[192,1536]{1,0:T(8,128)(2,1)S(1)}, u32[]{:S(2)}, u32[]{:S(2)}) collective-permute-start(bf16[192,1536]{1,0:T(8,128)(2,1)S(1)} %collective-permute-done.8), channel_id=1, source_target_pairs={{0,8},{8,16},{16,24},{24,28},{28,20},{20,12},{12,4},{4,0},{1,9},{9... | collective-permute-start | bytes 1769480 | tf_op jit(solution)/shard_map/ppermute | solution.py:112
  68.2 14.3 %copy-start.4 = (bf16[1,12,16,1536]{3,2,1,0:T(8,128)(2,1)S(1)}, bf16[1,12,16,1536]{3,2,1,0:T(8,128)(2,1)}, u32[]{:S(2)}) copy-start(bf16[1,12,16,1536]{3,2,1,0:T(8,128)(2,1)} %param.23) | copy-start | bytes 1769476
  68.2 14.3 %copy-start.56 = (f32[1536]{0:T(1024)S(1)}, f32[1536]{0:T(1024)}, u32[]{:S(2)}) copy-start(f32[1536]{0:T(1024)} %param.20) | copy-start | bytes 18436
  82.6 13.2 %copy-start.54 = (f32[1536]{0:T(1024)S(1)}, f32[1536]{0:T(1024)}, u32[]{:S(2)}) copy-start(f32[1536]{0:T(1024)} %param.22) | copy-start | bytes 18436
  104.7 3.6 %collective-permute-start.11 = (bf16[2,3,16,1536]{3,2,1,0:T(8,128)(2,1)}, bf16[2,3,16,1536]{3,2,1,0:T(8,128)(2,1)}, u32[]{:S(2)}, u32[]{:S(2)}) collective-permute-start(bf16[2,3,16,1536]{3,2,1,0:T(8,128)(2,1)} %dynamic-slice_bitcast_fusion.2), channel_id=1, source_target_pairs={{0,1},{1,0},{2,3},{3,2},{4,5},{5,4},{6,7},{7,6},{8,9},{9,8},{10,11... | collective-permute-start | bytes 884744 | tf_op jit(solution)/shard_map/ppermute | solution.py:69
  109.5 9.5 %collective-permute-start.12 = (f32[1,3,16,1536]{3,2,1,0:T(8,128)S(1)}, f32[1,3,16,1536]{3,2,1,0:T(8,128)S(1)}, u32[]{:S(2)}, u32[]{:S(2)}) collective-permute-start(f32[1,3,16,1536]{3,2,1,0:T(8,128)S(1)} %constant_dynamic-slice_fusion), channel_id=1, source_target_pairs={{0,2},{1,3},{2,0},{3,1},{4,6},{5,7},{6,4},{7,5},{8,10},{9,11},{10,... | collective-permute-start | bytes 884744 | tf_op jit(solution)/shard_map/ppermute | solution.py:69
  112.8 50.4 %collective-permute-start.18 = (bf16[192,1536]{1,0:T(8,128)(2,1)S(1)}, bf16[192,1536]{1,0:T(8,128)(2,1)}, u32[]{:S(2)}, u32[]{:S(2)}) collective-permute-start(bf16[192,1536]{1,0:T(8,128)(2,1)S(1)} %get-tuple-element.142), channel_id=1, source_target_pairs={{0,8},{8,16},{16,24},{24,28},{28,20},{20,12},{12,4},{4,0},{1,9},{9... | collective-permute-start | bytes 1769480 | tf_op jit(solution)/shard_map/ppermute | solution.py:145
  124.5 1.4 collective-permute-start.22
  126.5 4.5 %collective-permute-start.23 = (f32[18816]{0:T(1024)S(1)}, f32[18816]{0:T(1024)S(1)}, u32[]{:S(2)}, u32[]{:S(2)}) collective-permute-start(f32[18816]{0:T(1024)S(1)} %get-tuple-element.111), channel_id=1, source_target_pairs={{0,2},{1,3},{2,0},{3,1},{4,6},{5,7},{6,4},{7,5},{8,10},{9,11},{10,... | collective-permute-start | bytes 225800 | tf_op jit(solution)/shard_map/ppermute | solution.py:49
  131.3 4.1 %collective-permute-start.24 = (f32[9408]{0:T(1024)S(1)}, f32[9408]{0:T(1024)S(1)}, u32[]{:S(2)}, u32[]{:S(2)}) collective-permute-start(f32[9408]{0:T(1024)S(1)} %get-tuple-element.120), channel_id=1, source_target_pairs={{0,4},{4,0},{8,12},{12,8},{16,20},{20,16},{24,28},{28,24},{1,5},{5... | collective-permute-start | bytes 112904 | tf_op jit(solution)/shard_map/ppermute | solution.py:49
  135.6 3.8 %collective-permute-start.25 = (f32[4704]{0:T(1024)S(1)}, f32[4704]{0:T(1024)S(1)}, u32[]{:S(2)}, u32[]{:S(2)}) collective-permute-start(f32[4704]{0:T(1024)S(1)} %get-tuple-element.122), channel_id=1, source_target_pairs={{0,8},{4,12},{8,0},{12,4},{16,24},{20,28},{24,16},{28,20},{1,9},{5... | collective-permute-start | bytes 56456 | tf_op jit(solution)/shard_map/ppermute | solution.py:49
  139.6 4.7 %collective-permute-start.26 = (f32[2352]{0:T(1024)S(1)}, f32[2352]{0:T(1024)S(1)}, u32[]{:S(2)}, u32[]{:S(2)}) collective-permute-start(f32[2352]{0:T(1024)S(1)} %get-tuple-element.124), channel_id=1, source_target_pairs={{0,16},{4,20},{8,24},{12,28},{16,0},{20,4},{24,8},{28,12},{1,17},{... | collective-permute-start | bytes 28232 | tf_op jit(solution)/shard_map/ppermute | solution.py:49
  144.3 18.4 %collective-permute-start.27 = (f32[2352]{0:T(1024)S(1)}, f32[2352]{0:T(1024)S(1)}, u32[]{:S(2)}, u32[]{:S(2)}) collective-permute-start(f32[2352]{0:T(1024)S(1)} %add.874), channel_id=1, source_target_pairs={{0,16},{4,20},{8,24},{12,28},{16,0},{20,4},{24,8},{28,12},{1,17},{... | collective-permute-start | bytes 28232 | tf_op jit(solution)/shard_map/ppermute | solution.py:52
  158.4 25.8 %collective-permute-start.15 = (bf16[192,1536]{1,0:T(8,128)(2,1)S(1)}, bf16[192,1536]{1,0:T(8,128)(2,1)S(1)}, u32[]{:S(2)}, u32[]{:S(2)}) collective-permute-start(bf16[192,1536]{1,0:T(8,128)(2,1)S(1)} %get-tuple-element.141), channel_id=1, source_target_pairs={{0,4},{8,0},{16,8},{24,16},{28,24},{20,28},{12,20},{4,12},{1,5},{9... | collective-permute-start | bytes 1769480 | tf_op jit(solution)/shard_map/ppermute | solution.py:147
  160.2 10.5 %collective-permute-start.13 = (bf16[3,16,1536]{2,1,0:T(8,128)(2,1)S(1)}, bf16[3,16,1536]{2,1,0:T(8,128)(2,1)S(1)}, u32[]{:S(2)}, u32[]{:S(2)}) collective-permute-start(bf16[3,16,1536]{2,1,0:T(8,128)(2,1)S(1)} %get-tuple-element.130), channel_id=1, source_target_pairs={{0,1},{1,2},{2,3},{4,5},{5,6},{6,7},{8,9},{9,10},{10,11},{12,13},{... | collective-permute-start | bytes 442376 | tf_op jit(solution)/shard_map/ppermute | solution.py:16
  161.5 9.2 %collective-permute-start.14 = (bf16[3,16,1536]{2,1,0:T(8,128)(2,1)S(1)}, bf16[3,16,1536]{2,1,0:T(8,128)(2,1)S(1)}, u32[]{:S(2)}, u32[]{:S(2)}) collective-permute-start(bf16[3,16,1536]{2,1,0:T(8,128)(2,1)S(1)} %get-tuple-element.130), channel_id=1, source_target_pairs={{1,0},{2,1},{3,2},{5,4},{6,5},{7,6},{9,8},{10,9},{11,10},{13,12},{... | collective-permute-start | bytes 442376 | tf_op jit(solution)/shard_map/ppermute | solution.py:19
  162.8 6.8 %collective-permute-start.28 = (f32[4704]{0:T(1024)S(1)}, f32[4704]{0:T(1024)S(1)}, u32[]{:S(2)}, u32[]{:S(2)}) collective-permute-start(f32[4704]{0:T(1024)S(1)} %maximum_select_fusion.6), channel_id=1, source_target_pairs={{0,8},{4,12},{8,0},{12,4},{16,24},{20,28},{24,16},{28,20},{1,9},{5... | collective-permute-start | bytes 56456 | tf_op jit(solution)/shard_map/ppermute | solution.py:52
  164.6 19.7 %collective-permute-start.19 = (bf16[192,1536]{1,0:T(8,128)(2,1)S(1)}, bf16[192,1536]{1,0:T(8,128)(2,1)S(1)}, u32[]{:S(2)}, u32[]{:S(2)}) collective-permute-start(bf16[192,1536]{1,0:T(8,128)(2,1)S(1)} %fusion.13), channel_id=1, source_target_pairs={{0,8},{8,16},{16,24},{24,28},{28,20},{20,12},{12,4},{4,0},{1,9},{9... | collective-permute-start | bytes 1769480 | tf_op jit(solution)/shard_map/ppermute | solution.py:145
  169.7 10.2 %collective-permute-start.29 = (f32[9408]{0:T(1024)S(1)}, f32[9408]{0:T(1024)S(1)}, u32[]{:S(2)}, u32[]{:S(2)}) collective-permute-start(f32[9408]{0:T(1024)S(1)} %maximum_select_fusion.5), channel_id=1, source_target_pairs={{0,4},{4,0},{8,12},{12,8},{16,20},{20,16},{24,28},{28,24},{1,5},{5... | collective-permute-start | bytes 112904 | tf_op jit(solution)/shard_map/ppermute | solution.py:52
  180.2 10.6 %collective-permute-start.30 = (f32[18816]{0:T(1024)S(1)}, f32[18816]{0:T(1024)S(1)}, u32[]{:S(2)}, u32[]{:S(2)}) collective-permute-start(f32[18816]{0:T(1024)S(1)} %maximum_select_fusion.4), channel_id=1, source_target_pairs={{0,2},{1,3},{2,0},{3,1},{4,6},{5,7},{6,4},{7,5},{8,10},{9,11},{10,... | collective-permute-start | bytes 225800 | tf_op jit(solution)/shard_map/ppermute | solution.py:52
  185.8 13.0 %collective-permute-start.16 = (bf16[192,1536]{1,0:T(8,128)(2,1)S(1)}, bf16[192,1536]{1,0:T(8,128)(2,1)S(1)}, u32[]{:S(2)}, u32[]{:S(2)}) collective-permute-start(bf16[192,1536]{1,0:T(8,128)(2,1)S(1)} %get-tuple-element.139), channel_id=1, source_target_pairs={{0,4},{8,0},{16,8},{24,16},{28,24},{20,28},{12,20},{4,12},{1,5},{9... | collective-permute-start | bytes 1769480 | tf_op jit(solution)/shard_map/ppermute | solution.py:147
  185.8 13.0 %collective-permute-start.20 = (bf16[192,1536]{1,0:T(8,128)(2,1)S(1)}, bf16[192,1536]{1,0:T(8,128)(2,1)S(1)}, u32[]{:S(2)}, u32[]{:S(2)}) collective-permute-start(bf16[192,1536]{1,0:T(8,128)(2,1)S(1)} %get-tuple-element.140), channel_id=1, source_target_pairs={{0,8},{8,16},{16,24},{24,28},{28,20},{20,12},{12,4},{4,0},{1,9},{9... | collective-permute-start | bytes 1769480 | tf_op jit(solution)/shard_map/ppermute | solution.py:145
  190.8 11.6 %collective-permute-start.31 = (f32[37632]{0:T(1024)S(1)}, f32[37632]{0:T(1024)S(1)}, u32[]{:S(2)}, u32[]{:S(2)}) collective-permute-start(f32[37632]{0:T(1024)S(1)} %maximum_select_fusion.3), channel_id=1, source_target_pairs={{0,1},{1,0},{2,3},{3,2},{4,5},{5,4},{6,7},{7,6},{8,9},{9,8},{10,11... | collective-permute-start | bytes 451592 | tf_op jit(solution)/shard_map/ppermute | solution.py:52
  200.3 13.4 %collective-permute-start.17 = (bf16[192,1536]{1,0:T(8,128)(2,1)S(1)}, bf16[192,1536]{1,0:T(8,128)(2,1)S(1)}, u32[]{:S(2)}, u32[]{:S(2)}) collective-permute-start(bf16[192,1536]{1,0:T(8,128)(2,1)S(1)} %get-tuple-element.137), channel_id=1, source_target_pairs={{0,4},{8,0},{16,8},{24,16},{28,24},{20,28},{12,20},{4,12},{1,5},{9... | collective-permute-start | bytes 1769480 | tf_op jit(solution)/shard_map/ppermute | solution.py:147
  202.0 13.9 %collective-permute-start.21 = (bf16[192,1536]{1,0:T(8,128)(2,1)S(1)}, bf16[192,1536]{1,0:T(8,128)(2,1)S(1)}, u32[]{:S(2)}, u32[]{:S(2)}) collective-permute-start(bf16[192,1536]{1,0:T(8,128)(2,1)S(1)} %get-tuple-element.138), channel_id=1, source_target_pairs={{0,8},{8,16},{16,24},{24,28},{28,20},{20,12},{12,4},{4,0},{1,9},{9... | collective-permute-start | bytes 1769480 | tf_op jit(solution)/shard_map/ppermute | solution.py:145
  (42 other events, 298.6 us)

commit v13 on v12

--- a/solution.py
+++ b/solution.py
@@ -122,7 +122,7 @@
     return gathered.reshape((count * block.shape[0],) + block.shape[1:]), held
 
 
-def ring_reduce_scatter(terms, axis, ring):
+def ring_reduce_scatter(terms, axis, ring, held=None):
     count = len(ring)
     place = [0] * count
     for k, j in enumerate(ring):
@@ -145,6 +145,8 @@
         cw = lax.ppermute(cw, axis, forward)
         if s <= behind:
             ccw = lax.ppermute(ccw, axis, backward)
+        if s == ahead - 1 and held is not None:
+            cw, ccw, held = lax.optimization_barrier((cw, ccw, held))
         if s < ahead:
             cw = (cw.astype(jnp.float32) + term(ahead - s).astype(jnp.float32)).astype(terms.dtype)
         else:
@@ -153,7 +155,7 @@
             ccw = (ccw.astype(jnp.float32) + term(s - behind).astype(jnp.float32)).astype(terms.dtype)
         elif s == behind:
             total = total + ccw.astype(jnp.float32)
-    return total
+    return total, held
 
 
 def tree_all_gather(block, axis):
@@ -286,9 +288,7 @@
         flat, dpre, (((0,), (0,)), ((), ())), preferred_element_type=jnp.float32
     )
     n_fsdp = lax.axis_size("fsdp")
-    up_grad = ring_reduce_scatter(
-        w_term.astype(jnp.bfloat16).reshape((n_fsdp, chans // n_fsdp, -1)), "fsdp", ring
-    )
+    w_parts = w_term.astype(jnp.bfloat16).reshape((n_fsdp, chans // n_fsdp, -1))
     dpre_rows = dpre.reshape(height, cols, -1)
     group_terms = jnp.einsum(
         "hwf,cf->hwc", dpre_rows, columns, preferred_element_type=jnp.float32
@@ -303,6 +303,7 @@
     grad_pad = extended(activation_gradient, (("rows", 0),), 3)
     dframe = back_conv(grad_pad, kernel).astype(jnp.bfloat16)
     kernel_local = kern_grad(padded, activation_gradient)
+    up_grad, kernel_local = ring_reduce_scatter(w_parts, "fsdp", ring, kernel_local)
     kernel_total = tree_allreduce(kernel_local, ("rows", "fsdp"))
     activation = output.reshape(1, height, cols, -1)
     return (activation, dframe.reshape((1,) + dframe.shape), up_grad, kernel_total)

time: 219 us -> 232 us (1.059)
  waiting for transfers between devices: 77.3 us -> 95.2 us
  starting transfers between devices: 47.3 us -> 41.6 us
    ppermute x4, waiting for transfers between devices: 2.27 us -> 41.7 us  [ring_reduce_scatter(): cw = lax.ppermute(cw, axis, forward)]
    ppermute x3, waiting for transfers between devices: 18.3 us -> 3.97 us  [ring_reduce_scatter(): ccw = lax.ppermute(ccw, axis, backward)]
    ppermute x5, waiting for transfers between devices: 12.3 us -> 3.09 us  [tree_allreduce(): other = lax.ppermute(flat, axis, perm)]
    ppermute x2, waiting for transfers between devices: 4.24 us -> 0.01 us  [tree_reduce_scatter(): lax.ppermute(give, axis, perm).astype(jnp.float32)]
    ppermute x2, waiting for transfers between devices: 1.76 us -> 5.3 us  [extended(): lax.ppermute(lax.slice_in_dim(block, 0, width, axis=dim), axis, backward)]
    ppermute x5, starting transfers between devices: 8.47 us -> 5.73 us  [tree_allreduce(): flat = keep + lax.ppermute(give, axis, perm)]
    ppermute x5, waiting for transfers between devices: 10 us -> 12.8 us  [tree_allreduce(): flat = keep + lax.ppermute(give, axis, perm)]
    ppermute x3, starting transfers between devices: 3.51 us -> 1.02 us  [ring_reduce_scatter(): ccw = lax.ppermute(ccw, axis, backward)]
  transfers between devices with their start and end apart: 32 -> 32, of which waited for: 20 -> 24; matrix products, arithmetic and copies ran while one was open for 11% -> 9% of each run, Pallas kernels for 0% -> 0%
where the time goes in v13:
time: 232 us; the launch traced here: 230 us
  waiting for transfers between devices  95.2 us (41%)
  between operations  43.3 us (19%)
  starting transfers between devices  41.6 us (18%)
  other arithmetic  23.7 us (10%)
  matrix products  10.3 us (4%)
  local copies, waits for them, and re-layouts  9.96 us (4%)
  blocking collectives  6.37 us (3%)
    ppermute x4, waiting for transfers between devices, ring_reduce_scatter(): cw = lax.ppermute(cw, axis, forward)  41.7 us
    ppermute x4, waiting for transfers between devices, ring_all_gather(): cw = lax.ppermute(cw, axis, forward)  20.6 us
    ppermute x5, waiting for transfers between devices, tree_allreduce(): flat = keep + lax.ppermute(give, axis, perm)  12.8 us
    ppermute x4, starting transfers between devices, ring_all_gather(): cw = lax.ppermute(cw, axis, forward)  9.54 us
    ppermute x5, starting transfers between devices, tree_allreduce(): other = lax.ppermute(flat, axis, perm)  8.39 us
    ppermute x2, waiting for transfers between devices, tree_all_gather(): other = lax.ppermute(data, axis, perm)  7.06 us
    psum x1, blocking collectives, body(): norm_total = lax.psum(jnp.sum(norms), 'rows')  6.37 us
    ppermute x5, starting transfers between devices, tree_allreduce(): flat = keep + lax.ppermute(give, axis, perm)  5.73 us
  transfers between devices with their start and end apart: 32, of which 24 were waited for; matrix products, arithmetic and copies ran while one was open for 9% of the time, Pallas kernels for 0%

profile of v13, /device:TPU:0, one launch (start us, length us, event | category | flops | bytes accessed | tf_op | source)
XLA Modules:
  0.0 230.4 jit_solution(11850957690178069145)
XLA Ops:
  0.7 1.2 compare_select_fusion
  1.8 3.1 %collective-permute-start = (bf16[192,1536]{1,0:T(8,128)(2,1)S(1)}, bf16[192,1536]{1,0:T(8,128)(2,1)S(1)}, u32[]{:S(2)}, u32[]{:S(2)}) collective-permute-start(bf16[192,1536]{1,0:T(8,128)(2,1)S(1)} %compare_select_fusion), channel_id=1, source_target_pairs={{0,8},{8,16},{16,24},{24,28},{28,20},{20,12},{12,4},{4,0},{1,9},{9... | collective-permute-start | bytes 1769480 | tf_op jit(solution)/shard_map/ppermute | solution.py:112
  42.3 1.5 collective-permute-start.2
  43.8 1.3 collective-permute-start.3
  45.1 1.9 collective-permute-start.6
  47.4 1.7 collective-permute-done.3
  49.5 3.4 %fusion.158 = (f32[3,16]{1,0:T(4,128)S(1)}, f32[3,16,1536]{2,1,0:T(8,128)S(1)}) fusion(f32[1536]{0:T(1024)S(1)} %get-tuple-element.111, bf16[9,22,1536]{2,1,0:T(8,128)(2,1)S(1)} %select_maximum_fusion.2, f32[1536]{0:T(1024)S(1)} %get-tuple-element.112, f32[1536]{0:T(1024)S(1)} %get-tuple-element.65, f32[1536]{0:T(1024)S(1)} %get-tuple-element.66, ...), kind=kLoop, calls=%fused_computation.388 | loop fusion | flops 10911696 | bytes 7827648 | tf_op jit(solution)/shard_map/reduce_sum | solution.py:216
  53.3 4.1 %collective-permute-start.4 = (bf16[1,3,16,1536]{3,2,1,0:T(8,128)(2,1)S(1)}, bf16[1,3,16,1536]{3,2,1,0:T(8,128)(2,1)S(1)}, u32[]{:S(2)}, u32[]{:S(2)}) collective-permute-start(bf16[1,3,16,1536]{3,2,1,0:T(8,128)(2,1)S(1)} %fusion.149), channel_id=1, source_target_pairs={{0,1},{1,0},{2,3},{3,2},{4,5},{5,4},{6,7},{7,6},{8,9},{9,8},{10,11... | collective-permute-start | bytes 442376 | tf_op jit(solution)/shard_map/ppermute | solution.py:170
  59.1 2.1 collective-permute-start.8
  61.6 6.1 %collective-permute-done.5 = bf16[2,3,16,1536]{3,2,1,0:T(8,128)(2,1)S(1)} collective-permute-done((bf16[2,3,16,1536]{3,2,1,0:T(8,128)(2,1)S(1)}, bf16[2,3,16,1536]{3,2,1,0:T(8,128)(2,1)S(1)}, u32[]{:S(2)}, u32[]{:S(2)}) %collective-permute-start.5) | collective-permute-done | bytes 294944 | tf_op jit(solution)/shard_map/ppermute | solution.py:170
  67.8 6.2 %collective-permute-done.8 = bf16[192,1536]{1,0:T(8,128)(2,1)S(1)} collective-permute-done((bf16[192,1536]{1,0:T(8,128)(2,1)S(1)}, bf16[192,1536]{1,0:T(8,128)(2,1)S(1)}, u32[]{:S(2)}, u32[]{:S(2)}) %collective-permute-start.8) | collective-permute-done | bytes 589856 | tf_op jit(solution)/shard_map/ppermute | solution.py:112
  74.0 2.4 %collective-permute-start.10 = (bf16[192,1536]{1,0:T(8,128)(2,1)S(1)}, bf16[192,1536]{1,0:T(8,128)(2,1)S(1)}, u32[]{:S(2)}, u32[]{:S(2)}) collective-permute-start(bf16[192,1536]{1,0:T(8,128)(2,1)S(1)} %collective-permute-done.8), channel_id=1, source_target_pairs={{0,8},{8,16},{16,24},{24,28},{28,20},{20,12},{12,4},{4,0},{1,9},{9... | collective-permute-start | bytes 1769480 | tf_op jit(solution)/shard_map/ppermute | solution.py:112
  77.0 13.7 %collective-permute-done.10 = bf16[192,1536]{1,0:T(8,128)(2,1)S(1)} collective-permute-done((bf16[192,1536]{1,0:T(8,128)(2,1)S(1)}, bf16[192,1536]{1,0:T(8,128)(2,1)S(1)}, u32[]{:S(2)}, u32[]{:S(2)}) %collective-permute-start.10) | collective-permute-done | bytes 589856 | tf_op jit(solution)/shard_map/ppermute | solution.py:112
  90.8 4.8 %fusion.4 = (f32[1536]{0:T(1024)S(1)}, f32[1536]{0:T(1024)S(1)}, f32[192,1536]{1,0:T(8,128)}, f32[192,1536]{1,0:T(8,128)}) fusion(bf16[1,12,16,1536]{3,2,1,0:T(8,128)(2,1)S(1)} %copy-done.4, f32[1536]{0:T(1024)S(1)} %copy-done.56, bf16[192,1536]{1,0:T(8,128)(2,1)S(1)} %bitcast.101, bf16[1536,1536]{1,0:T(8,128)(2,1)S(1)} %bitcast.99), kind=kOutput, calls=%fused_computation.64 | convolution fusion | flops 926610432 | bytes 8275968 | tf_op jit(solution)/shard_map/dot_general | solution.py:274
  96.3 6.4 %all-reduce.2 = (f32[]{:T(128)}, f32[]{:T(128)}) all-reduce(f32[]{:T(128)} %get-tuple-element.133, f32[]{:T(128)} %get-tuple-element.132), channel_id=1, replica_groups=mesh['fsdp'=8,'rows'=4] {'rows'}, use_global_device_ids=true, to_apply=%region_4.5 | all-reduce | flops 2 | bytes 16 | tf_op jit(solution)/shard_map/psum | solution.py:279
  104.0 3.2 %fusion.3 = (bf16[192,1536]{1,0:T(8,128)(2,1)S(1)}, bf16[192,1536]{1,0:T(8,128)(2,1)}) fusion(f32[192,1536]{1,0:T(8,128)} %get-tuple-element.169, f32[192,1536]{1,0:T(8,128)} %get-tuple-element.140, bf16[1,12,16,1536]{3,2,1,0:T(8,128)(2,1)S(1)} %copy-done.4, f32[1536]{0:T(1024)S(1)} %get-tuple-element.153, f32[1536]{0:T(1024)S(1)} %get-tuple-element.138, ...), kind=kLoop, calls=%fused_computation.63 | loop fusion | flops 5603328 | bytes 4159488 | tf_op jit(solution)/shard_map/convert_element_type | solution.py:286
  107.2 4.0 %convolution_convert_fusion.1 = bf16[12,16,1536]{2,1,0:T(8,128)(2,1)S(1)} fusion(bf16[12,16,1536]{2,1,0:T(8,128)(2,1)S(1)} %bitcast.103, bf16[1536,1536,1]{1,0,2:T(8,128)(2,1)} %bitcast.100), kind=kOutput, calls=%fused_computation.52 | convolution fusion | flops 906264576 | bytes 5898240 | tf_op jit(solution)/shard_map/hwf,cf->hwc/dot_general | solution.py:293
  111.4 1.4 convolution_convert_fusion
  112.9 1.8 collective-permute-start.15
  115.8 1.6 collective-permute-start.12
  117.5 11.3 %collective-permute-done.15 = bf16[192,1536]{1,0:T(8,128)(2,1)S(1)} collective-permute-done((bf16[192,1536]{1,0:T(8,128)(2,1)S(1)}, bf16[192,1536]{1,0:T(8,128)(2,1)S(1)}, u32[]{:S(2)}, u32[]{:S(2)}) %collective-permute-start.15) | collective-permute-done | bytes 589856 | tf_op jit(solution)/shard_map/ppermute | solution.py:145
  128.8 1.4 collective-permute-done.18
  131.3 1.6 collective-permute-start.16
  137.1 1.2 fusion.155
  138.3 8.0 %collective-permute-done.16 = bf16[192,1536]{1,0:T(8,128)(2,1)} collective-permute-done((bf16[192,1536]{1,0:T(8,128)(2,1)}, bf16[192,1536]{1,0:T(8,128)(2,1)}, u32[]{:S(2)}, u32[]{:S(2)}) %collective-permute-start.16) | collective-permute-done | bytes 589856 | tf_op jit(solution)/shard_map/ppermute | solution.py:145
  147.4 2.9 %fusion.12 = (bf16[192,1536]{1,0:T(8,128)(2,1)}, bf16[192,1536]{1,0:T(8,128)(2,1)}) fusion(bf16[192,1536]{1,0:T(8,128)(2,1)} %collective-permute-done.19, bf16[8,192,1536]{2,1,0:T(8,128)(2,1)} %bitcast.96, s32[]{:T(128)S(6)} %select_n.375, s32[]{:T(128)S(6)} %select_n.366, bf16[192,1536]{1,0:T(8,128)(2,1)} %collective-permute-done.16), kind=kLoop, calls=%fused_computation.74 | loop fusion | flops 2359296 | bytes 3538952 | tf_op jit(solution)/shard_map/convert_element_type | solution.py:155
  150.2 1.7 collective-permute-start.17
  155.8 8.1 %collective-permute-done.17 = bf16[192,1536]{1,0:T(8,128)(2,1)S(1)} collective-permute-done((bf16[192,1536]{1,0:T(8,128)(2,1)}, bf16[192,1536]{1,0:T(8,128)(2,1)S(1)}, u32[]{:S(2)}, u32[]{:S(2)}) %collective-permute-start.17) | collective-permute-done | bytes 589856 | tf_op jit(solution)/shard_map/ppermute | solution.py:145
  163.9 1.4 collective-permute-done.20
  166.5 1.4 collective-permute-done.22
  168.4 1.7 collective-permute-start.23
  170.1 2.8 %collective-permute-done.23 = f32[18816]{0:T(1024)S(1)} collective-permute-done((f32[18816]{0:T(1024)S(1)}, f32[18816]{0:T(1024)S(1)}, u32[]{:S(2)}, u32[]{:S(2)}) %collective-permute-start.23) | collective-permute-done | bytes 75296 | tf_op jit(solution)/shard_map/ppermute | solution.py:49
  173.8 3.7 %collective-permute-done.24 = f32[9408]{0:T(1024)S(1)} collective-permute-done((f32[9408]{0:T(1024)S(1)}, f32[9408]{0:T(1024)S(1)}, u32[]{:S(2)}, u32[]{:S(2)}) %collective-permute-start.24) | collective-permute-done | bytes 37664 | tf_op jit(solution)/shard_map/ppermute | solution.py:49
  177.7 1.7 collective-permute-start.25
  179.4 2.2 collective-permute-done.25
  181.8 1.9 collective-permute-start.26
  183.7 2.8 %collective-permute-done.26 = f32[2352]{0:T(1024)S(1)} collective-permute-done((f32[2352]{0:T(1024)S(1)}, f32[2352]{0:T(1024)S(1)}, u32[]{:S(2)}, u32[]{:S(2)}) %collective-permute-start.26) | collective-permute-done | bytes 9440 | tf_op jit(solution)/shard_map/ppermute | solution.py:49
  186.4 1.8 collective-permute-start.27
  188.3 2.8 %collective-permute-done.27 = f32[2352]{0:T(1024)S(1)} collective-permute-done((f32[2352]{0:T(1024)S(1)}, f32[2352]{0:T(1024)S(1)}, u32[]{:S(2)}, u32[]{:S(2)}) %collective-permute-start.27) | collective-permute-done | bytes 9440 | tf_op jit(solution)/shard_map/ppermute | solution.py:52
  191.1 1.6 collective-permute-start.28
  196.3 1.3 collective-permute-start.13
  197.6 1.3 collective-permute-start.14
  199.1 3.6 %collective-permute-done.14 = bf16[3,16,1536]{2,1,0:T(8,128)(2,1)S(1)} collective-permute-done((bf16[3,16,1536]{2,1,0:T(8,128)(2,1)S(1)}, bf16[3,16,1536]{2,1,0:T(8,128)(2,1)S(1)}, u32[]{:S(2)}, u32[]{:S(2)}) %collective-permute-start.14) | collective-permute-done | bytes 147488 | tf_op jit(solution)/shard_map/ppermute | solution.py:19
  203.1 4.7 %collective-permute-start.30 = (f32[18816]{0:T(1024)S(1)}, f32[18816]{0:T(1024)S(1)}, u32[]{:S(2)}, u32[]{:S(2)}) collective-permute-start(f32[18816]{0:T(1024)S(1)} %maximum_select_fusion.4), channel_id=1, source_target_pairs={{0,2},{1,3},{2,0},{3,1},{4,6},{5,7},{6,4},{7,5},{8,10},{9,11},{10,... | collective-permute-start | bytes 225800 | tf_op jit(solution)/shard_map/ppermute | solution.py:52
  208.0 2.8 %fusion.152 = bf16[1,3,16,1536]{3,2,1,0:T(8,128)(2,1)} fusion(f32[1536]{0:T(1024)S(1)} %copy-done.45, bf16[9,22,1536]{2,1,0:T(8,128)(2,1)S(1)} %select_maximum_fusion, f32[1536]{0:T(1024)S(1)} %copy-done.47, f32[1536]{0:T(1024)S(1)} %get-tuple-element.65, f32[1536]{0:T(1024)S(1)} %get-tuple-element.66, bf16[3,16,1536]{2,1,0:T(8,128)(2,1)S(1)} %collective-permute-done.13, ...), kind=kLoop, calls=%fused_computation.311 | loop fusion | flops 11132928 | bytes 7084032 | tf_op jit(solution)/shard_map/reshape | solution.py:309
  211.2 1.3 fusion.11
  213.7 14.4 %collective-permute-done.21 = bf16[192,1536]{1,0:T(8,128)(2,1)S(1)} collective-permute-done((bf16[192,1536]{1,0:T(8,128)(2,1)S(1)}, bf16[192,1536]{1,0:T(8,128)(2,1)S(1)}, u32[]{:S(2)}, u32[]{:S(2)}) %collective-permute-start.21) | collective-permute-done | bytes 589856 | tf_op jit(solution)/shard_map/ppermute | solution.py:145
  228.1 2.3 %fusion.16 = f32[192,1536]{1,0:T(8,128)} fusion(bf16[192,1536]{1,0:T(8,128)(2,1)S(1)} %collective-permute-done.21, bf16[192,1536]{1,0:T(8,128)(2,1)S(1)} %collective-permute-done.20, bf16[8,192,1536]{2,1,0:T(8,128)(2,1)} %bitcast.98, s32[]{:T(128)S(6)} %select_n.357), kind=kLoop, calls=%fused_computation.82 | loop fusion | flops 1474560 | bytes 2949124 | tf_op jit(solution)/shard_map/add | solution.py:153
  (252 shorter events, 21.7 us)
Async XLA Ops:
  1.8 39.7 %collective-permute-start = (bf16[192,1536]{1,0:T(8,128)(2,1)S(1)}, bf16[192,1536]{1,0:T(8,128)(2,1)S(1)}, u32[]{:S(2)}, u32[]{:S(2)}) collective-permute-start(bf16[192,1536]{1,0:T(8,128)(2,1)S(1)} %compare_select_fusion), channel_id=1, source_target_pairs={{0,8},{8,16},{16,24},{24,28},{28,20},{20,12},{12,4},{4,0},{1,9},{9... | collective-permute-start | bytes 1769480 | tf_op jit(solution)/shard_map/ppermute | solution.py:112
  4.9 36.7 %collective-permute-start.1 = (bf16[192,1536]{1,0:T(8,128)(2,1)S(1)}, bf16[192,1536]{1,0:T(8,128)(2,1)S(1)}, u32[]{:S(2)}, u32[]{:S(2)}) collective-permute-start(bf16[192,1536]{1,0:T(8,128)(2,1)S(1)} %compare_select_fusion), channel_id=1, source_target_pairs={{0,4},{8,0},{16,8},{24,16},{28,24},{20,28},{12,20},{4,12},{1,5},{9... | collective-permute-start | bytes 1769480 | tf_op jit(solution)/shard_map/ppermute | solution.py:114
  42.3 5.0 %collective-permute-start.2 = (bf16[3,16,1536]{2,1,0:T(8,128)(2,1)S(1)}, bf16[3,16,1536]{2,1,0:T(8,128)(2,1)S(1)}, u32[]{:S(2)}, u32[]{:S(2)}) collective-permute-start(bf16[3,16,1536]{2,1,0:T(8,128)(2,1)S(1)} %bitcast.104), channel_id=1, source_target_pairs={{0,1},{1,2},{2,3},{4,5},{5,6},{6,7},{8,9},{9,10},{10,11},{12,13},{... | collective-permute-start | bytes 442376 | tf_op jit(solution)/shard_map/ppermute | solution.py:16
  43.8 5.3 %collective-permute-start.3 = (bf16[3,16,1536]{2,1,0:T(8,128)(2,1)S(1)}, bf16[3,16,1536]{2,1,0:T(8,128)(2,1)S(1)}, u32[]{:S(2)}, u32[]{:S(2)}) collective-permute-start(bf16[3,16,1536]{2,1,0:T(8,128)(2,1)S(1)} %bitcast.105), channel_id=1, source_target_pairs={{1,0},{2,1},{3,2},{5,4},{6,5},{7,6},{9,8},{10,9},{11,10},{13,12},{... | collective-permute-start | bytes 442376 | tf_op jit(solution)/shard_map/ppermute | solution.py:19
  45.1 14.0 %collective-permute-start.6 = (bf16[192,1536]{1,0:T(8,128)(2,1)S(1)}, bf16[192,1536]{1,0:T(8,128)(2,1)S(1)}, u32[]{:S(2)}, u32[]{:S(2)}) collective-permute-start(bf16[192,1536]{1,0:T(8,128)(2,1)S(1)} %collective-permute-done), channel_id=1, source_target_pairs={{0,8},{8,16},{16,24},{24,28},{28,20},{20,12},{12,4},{4,0},{1,9},{9... | collective-permute-start | bytes 1769480 | tf_op jit(solution)/shard_map/ppermute | solution.py:112
  47.0 14.5 %collective-permute-start.7 = (bf16[192,1536]{1,0:T(8,128)(2,1)S(1)}, bf16[192,1536]{1,0:T(8,128)(2,1)S(1)}, u32[]{:S(2)}, u32[]{:S(2)}) collective-permute-start(bf16[192,1536]{1,0:T(8,128)(2,1)S(1)} %collective-permute-done.1), channel_id=1, source_target_pairs={{0,4},{8,0},{16,8},{24,16},{28,24},{20,28},{12,20},{4,12},{1,5},{9... | collective-permute-start | bytes 1769480 | tf_op jit(solution)/shard_map/ppermute | solution.py:114
  53.0 84.1 %copy-start.48 = (f32[3,16]{1,0:T(4,128)}, f32[3,16]{1,0:T(4,128)S(1)}, u32[]{:S(2)}) copy-start(f32[3,16]{1,0:T(4,128)S(1)} %broadcast_multiply_fusion.2) | copy-start | bytes 580
  53.2 83.9 %copy-start.50 = (f32[3,16]{1,0:T(4,128)}, f32[3,16]{1,0:T(4,128)S(1)}, u32[]{:S(2)}) copy-start(f32[3,16]{1,0:T(4,128)S(1)} %add_rsqrt_fusion) | copy-start | bytes 580
  53.3 5.1 %collective-permute-start.4 = (bf16[1,3,16,1536]{3,2,1,0:T(8,128)(2,1)S(1)}, bf16[1,3,16,1536]{3,2,1,0:T(8,128)(2,1)S(1)}, u32[]{:S(2)}, u32[]{:S(2)}) collective-permute-start(bf16[1,3,16,1536]{3,2,1,0:T(8,128)(2,1)S(1)} %fusion.149), channel_id=1, source_target_pairs={{0,1},{1,0},{2,3},{3,2},{4,5},{5,4},{6,7},{7,6},{8,9},{9,8},{10,11... | collective-permute-start | bytes 442376 | tf_op jit(solution)/shard_map/ppermute | solution.py:170
  58.4 9.3 %collective-permute-start.5 = (bf16[2,3,16,1536]{3,2,1,0:T(8,128)(2,1)S(1)}, bf16[2,3,16,1536]{3,2,1,0:T(8,128)(2,1)S(1)}, u32[]{:S(2)}, u32[]{:S(2)}) collective-permute-start(bf16[2,3,16,1536]{3,2,1,0:T(8,128)(2,1)S(1)} %maximum_select_fusion.2), channel_id=1, source_target_pairs={{0,2},{1,3},{2,0},{3,1},{4,6},{5,7},{6,4},{7,5},{8,10},{9,11},{10,... | collective-permute-start | bytes 884744 | tf_op jit(solution)/shard_map/ppermute | solution.py:170
  59.1 14.9 %collective-permute-start.8 = (bf16[192,1536]{1,0:T(8,128)(2,1)S(1)}, bf16[192,1536]{1,0:T(8,128)(2,1)S(1)}, u32[]{:S(2)}, u32[]{:S(2)}) collective-permute-start(bf16[192,1536]{1,0:T(8,128)(2,1)S(1)} %collective-permute-done.6), channel_id=1, source_target_pairs={{0,8},{8,16},{16,24},{24,28},{28,20},{20,12},{12,4},{4,0},{1,9},{9... | collective-permute-start | bytes 1769480 | tf_op jit(solution)/shard_map/ppermute | solution.py:112
  61.5 15.4 %collective-permute-start.9 = (bf16[192,1536]{1,0:T(8,128)(2,1)S(1)}, bf16[192,1536]{1,0:T(8,128)(2,1)S(1)}, u32[]{:S(2)}, u32[]{:S(2)}) collective-permute-start(bf16[192,1536]{1,0:T(8,128)(2,1)S(1)} %collective-permute-done.7), channel_id=1, source_target_pairs={{0,4},{8,0},{16,8},{24,16},{28,24},{20,28},{12,20},{4,12},{1,5},{9... | collective-permute-start | bytes 1769480 | tf_op jit(solution)/shard_map/ppermute | solution.py:114
  74.0 16.7 %collective-permute-start.10 = (bf16[192,1536]{1,0:T(8,128)(2,1)S(1)}, bf16[192,1536]{1,0:T(8,128)(2,1)S(1)}, u32[]{:S(2)}, u32[]{:S(2)}) collective-permute-start(bf16[192,1536]{1,0:T(8,128)(2,1)S(1)} %collective-permute-done.8), channel_id=1, source_target_pairs={{0,8},{8,16},{16,24},{24,28},{28,20},{20,12},{12,4},{4,0},{1,9},{9... | collective-permute-start | bytes 1769480 | tf_op jit(solution)/shard_map/ppermute | solution.py:112
  111.3 3.7 %collective-permute-start.11 = (bf16[2,3,16,1536]{3,2,1,0:T(8,128)(2,1)S(1)}, bf16[2,3,16,1536]{3,2,1,0:T(8,128)(2,1)S(1)}, u32[]{:S(2)}, u32[]{:S(2)}) collective-permute-start(bf16[2,3,16,1536]{3,2,1,0:T(8,128)(2,1)S(1)} %dynamic-slice_bitcast_fusion.2), channel_id=1, source_target_pairs={{0,1},{1,0},{2,3},{3,2},{4,5},{5,4},{6,7},{7,6},{8,9},{9,8},{10,11... | collective-permute-start | bytes 884744 | tf_op jit(solution)/shard_map/ppermute | solution.py:69
  112.9 15.8 %collective-permute-start.15 = (bf16[192,1536]{1,0:T(8,128)(2,1)S(1)}, bf16[192,1536]{1,0:T(8,128)(2,1)S(1)}, u32[]{:S(2)}, u32[]{:S(2)}) collective-permute-start(bf16[192,1536]{1,0:T(8,128)(2,1)S(1)} %get-tuple-element.148), channel_id=1, source_target_pairs={{0,8},{8,16},{16,24},{24,28},{28,20},{20,12},{12,4},{4,0},{1,9},{9... | collective-permute-start | bytes 1769480 | tf_op jit(solution)/shard_map/ppermute | solution.py:145
  114.8 15.4 %collective-permute-start.18 = (bf16[192,1536]{1,0:T(8,128)(2,1)S(1)}, bf16[192,1536]{1,0:T(8,128)(2,1)S(1)}, u32[]{:S(2)}, u32[]{:S(2)}) collective-permute-start(bf16[192,1536]{1,0:T(8,128)(2,1)S(1)} %get-tuple-element.147), channel_id=1, source_target_pairs={{0,4},{8,0},{16,8},{24,16},{28,24},{20,28},{12,20},{4,12},{1,5},{9... | collective-permute-start | bytes 1769480 | tf_op jit(solution)/shard_map/ppermute | solution.py:147
  115.8 21.2 %collective-permute-start.12 = (f32[1,3,16,1536]{3,2,1,0:T(8,128)}, f32[1,3,16,1536]{3,2,1,0:T(8,128)}, u32[]{:S(2)}, u32[]{:S(2)}) collective-permute-start(f32[1,3,16,1536]{3,2,1,0:T(8,128)} %constant_dynamic-slice_fusion), channel_id=1, source_target_pairs={{0,2},{1,3},{2,0},{3,1},{4,6},{5,7},{6,4},{7,5},{8,10},{9,11},{10,... | collective-permute-start | bytes 884744 | tf_op jit(solution)/shard_map/ppermute | solution.py:69
  131.3 14.9 %collective-permute-start.16 = (bf16[192,1536]{1,0:T(8,128)(2,1)}, bf16[192,1536]{1,0:T(8,128)(2,1)}, u32[]{:S(2)}, u32[]{:S(2)}) collective-permute-start(bf16[192,1536]{1,0:T(8,128)(2,1)} %get-tuple-element.146), channel_id=1, source_target_pairs={{0,8},{8,16},{16,24},{24,28},{28,20},{20,12},{12,4},{4,0},{1,9},{9... | collective-permute-start | bytes 1769480 | tf_op jit(solution)/shard_map/ppermute | solution.py:145
  132.9 14.4 %collective-permute-start.19 = (bf16[192,1536]{1,0:T(8,128)(2,1)S(1)}, bf16[192,1536]{1,0:T(8,128)(2,1)}, u32[]{:S(2)}, u32[]{:S(2)}) collective-permute-start(bf16[192,1536]{1,0:T(8,128)(2,1)S(1)} %get-tuple-element.145), channel_id=1, source_target_pairs={{0,4},{8,0},{16,8},{24,16},{28,24},{20,28},{12,20},{4,12},{1,5},{9... | collective-permute-start | bytes 1769480 | tf_op jit(solution)/shard_map/ppermute | solution.py:147
  150.2 13.6 %collective-permute-start.17 = (bf16[192,1536]{1,0:T(8,128)(2,1)}, bf16[192,1536]{1,0:T(8,128)(2,1)S(1)}, u32[]{:S(2)}, u32[]{:S(2)}) collective-permute-start(bf16[192,1536]{1,0:T(8,128)(2,1)} %get-tuple-element.144), channel_id=1, source_target_pairs={{0,8},{8,16},{16,24},{24,28},{28,20},{20,12},{12,4},{4,0},{1,9},{9... | collective-permute-start | bytes 1769480 | tf_op jit(solution)/shard_map/ppermute | solution.py:145
  152.0 13.3 %collective-permute-start.20 = (bf16[192,1536]{1,0:T(8,128)(2,1)}, bf16[192,1536]{1,0:T(8,128)(2,1)S(1)}, u32[]{:S(2)}, u32[]{:S(2)}) collective-permute-start(bf16[192,1536]{1,0:T(8,128)(2,1)} %get-tuple-element.143), channel_id=1, source_target_pairs={{0,4},{8,0},{16,8},{24,16},{28,24},{20,28},{12,20},{4,12},{1,5},{9... | collective-permute-start | bytes 1769480 | tf_op jit(solution)/shard_map/ppermute | solution.py:147
  166.4 1.4 collective-permute-start.22
  168.4 4.5 %collective-permute-start.23 = (f32[18816]{0:T(1024)S(1)}, f32[18816]{0:T(1024)S(1)}, u32[]{:S(2)}, u32[]{:S(2)}) collective-permute-start(f32[18816]{0:T(1024)S(1)} %get-tuple-element.117), channel_id=1, source_target_pairs={{0,2},{1,3},{2,0},{3,1},{4,6},{5,7},{6,4},{7,5},{8,10},{9,11},{10,... | collective-permute-start | bytes 225800 | tf_op jit(solution)/shard_map/ppermute | solution.py:49
  172.9 34.9 %copy-start.9 = (f32[1536]{0:T(1024)S(1)}, f32[1536]{0:T(1024)}, u32[]{:S(2)}) copy-start(f32[1536]{0:T(1024)} %get-tuple-element.74) | copy-start | bytes 18436
  172.9 34.9 %copy-start.11 = (f32[1536]{0:T(1024)S(1)}, f32[1536]{0:T(1024)}, u32[]{:S(2)}) copy-start(f32[1536]{0:T(1024)} %get-tuple-element.75) | copy-start | bytes 18436
  172.9 34.9 %copy-start.13 = (f32[1536]{0:T(1024)S(1)}, f32[1536]{0:T(1024)}, u32[]{:S(2)}) copy-start(f32[1536]{0:T(1024)} %get-tuple-element.76) | copy-start | bytes 18436
  172.9 34.9 %copy-start.15 = (f32[1536]{0:T(1024)S(1)}, f32[1536]{0:T(1024)}, u32[]{:S(2)}) copy-start(f32[1536]{0:T(1024)} %get-tuple-element.77) | copy-start | bytes 18436
  172.9 34.9 %copy-start.17 = (f32[1536]{0:T(1024)S(1)}, f32[1536]{0:T(1024)}, u32[]{:S(2)}) copy-start(f32[1536]{0:T(1024)} %get-tuple-element.78) | copy-start | bytes 18436
  173.0 34.9 %copy-start.19 = (f32[1536]{0:T(1024)S(1)}, f32[1536]{0:T(1024)}, u32[]{:S(2)}) copy-start(f32[1536]{0:T(1024)} %get-tuple-element.79) | copy-start | bytes 18436
  173.0 34.9 %copy-start.21 = (f32[1536]{0:T(1024)S(1)}, f32[1536]{0:T(1024)}, u32[]{:S(2)}) copy-start(f32[1536]{0:T(1024)} %get-tuple-element.80) | copy-start | bytes 18436
  173.0 34.9 %copy-start.23 = (f32[1536]{0:T(1024)S(1)}, f32[1536]{0:T(1024)}, u32[]{:S(2)}) copy-start(f32[1536]{0:T(1024)} %get-tuple-element.81) | copy-start | bytes 18436
  173.0 34.9 %copy-start.25 = (f32[1536]{0:T(1024)S(1)}, f32[1536]{0:T(1024)}, u32[]{:S(2)}) copy-start(f32[1536]{0:T(1024)} %get-tuple-element.82) | copy-start | bytes 18436
  173.0 34.9 %copy-start.27 = (f32[1536]{0:T(1024)S(1)}, f32[1536]{0:T(1024)}, u32[]{:S(2)}) copy-start(f32[1536]{0:T(1024)} %copy-done.26) | copy-start | bytes 18436
  173.0 34.9 %copy-start.29 = (f32[1536]{0:T(1024)S(1)}, f32[1536]{0:T(1024)}, u32[]{:S(2)}) copy-start(f32[1536]{0:T(1024)} %copy-done.28) | copy-start | bytes 18436
  173.0 34.9 %copy-start.31 = (f32[1536]{0:T(1024)S(1)}, f32[1536]{0:T(1024)}, u32[]{:S(2)}) copy-start(f32[1536]{0:T(1024)} %copy-done.30) | copy-start | bytes 18436
  173.0 34.9 %copy-start.33 = (f32[1536]{0:T(1024)S(1)}, f32[1536]{0:T(1024)}, u32[]{:S(2)}) copy-start(f32[1536]{0:T(1024)} %copy-done.32) | copy-start | bytes 18436
  173.0 34.9 %copy-start.35 = (f32[1536]{0:T(1024)S(1)}, f32[1536]{0:T(1024)}, u32[]{:S(2)}) copy-start(f32[1536]{0:T(1024)} %copy-done.34) | copy-start | bytes 18436
  173.4 4.1 %collective-permute-start.24 = (f32[9408]{0:T(1024)S(1)}, f32[9408]{0:T(1024)S(1)}, u32[]{:S(2)}, u32[]{:S(2)}) collective-permute-start(f32[9408]{0:T(1024)S(1)} %get-tuple-element.126), channel_id=1, source_target_pairs={{0,4},{4,0},{8,12},{12,8},{16,20},{20,16},{24,28},{28,24},{1,5},{5... | collective-permute-start | bytes 112904 | tf_op jit(solution)/shard_map/ppermute | solution.py:49
  177.7 3.8 %collective-permute-start.25 = (f32[4704]{0:T(1024)S(1)}, f32[4704]{0:T(1024)S(1)}, u32[]{:S(2)}, u32[]{:S(2)}) collective-permute-start(f32[4704]{0:T(1024)S(1)} %get-tuple-element.128), channel_id=1, source_target_pairs={{0,8},{4,12},{8,0},{12,4},{16,24},{20,28},{24,16},{28,20},{1,9},{5... | collective-permute-start | bytes 56456 | tf_op jit(solution)/shard_map/ppermute | solution.py:49
  181.8 4.7 %collective-permute-start.26 = (f32[2352]{0:T(1024)S(1)}, f32[2352]{0:T(1024)S(1)}, u32[]{:S(2)}, u32[]{:S(2)}) collective-permute-start(f32[2352]{0:T(1024)S(1)} %get-tuple-element.130), channel_id=1, source_target_pairs={{0,16},{4,20},{8,24},{12,28},{16,0},{20,4},{24,8},{28,12},{1,17},{... | collective-permute-start | bytes 28232 | tf_op jit(solution)/shard_map/ppermute | solution.py:49
  186.4 4.6 %collective-permute-start.27 = (f32[2352]{0:T(1024)S(1)}, f32[2352]{0:T(1024)S(1)}, u32[]{:S(2)}, u32[]{:S(2)}) collective-permute-start(f32[2352]{0:T(1024)S(1)} %add.874), channel_id=1, source_target_pairs={{0,16},{4,20},{8,24},{12,28},{16,0},{20,4},{24,8},{28,12},{1,17},{... | collective-permute-start | bytes 28232 | tf_op jit(solution)/shard_map/ppermute | solution.py:52
  191.1 7.8 %collective-permute-start.28 = (f32[4704]{0:T(1024)S(1)}, f32[4704]{0:T(1024)S(1)}, u32[]{:S(2)}, u32[]{:S(2)}) collective-permute-start(f32[4704]{0:T(1024)S(1)} %maximum_select_fusion.6), channel_id=1, source_target_pairs={{0,8},{4,12},{8,0},{12,4},{16,24},{20,28},{24,16},{28,20},{1,9},{5... | collective-permute-start | bytes 56456 | tf_op jit(solution)/shard_map/ppermute | solution.py:52
  196.3 2.8 %collective-permute-start.13 = (bf16[3,16,1536]{2,1,0:T(8,128)(2,1)S(1)}, bf16[3,16,1536]{2,1,0:T(8,128)(2,1)S(1)}, u32[]{:S(2)}, u32[]{:S(2)}) collective-permute-start(bf16[3,16,1536]{2,1,0:T(8,128)(2,1)S(1)} %get-tuple-element.136), channel_id=1, source_target_pairs={{0,1},{1,2},{2,3},{4,5},{5,6},{6,7},{8,9},{9,10},{10,11},{12,13},{... | collective-permute-start | bytes 442376 | tf_op jit(solution)/shard_map/ppermute | solution.py:16
  197.6 5.1 %collective-permute-start.14 = (bf16[3,16,1536]{2,1,0:T(8,128)(2,1)S(1)}, bf16[3,16,1536]{2,1,0:T(8,128)(2,1)S(1)}, u32[]{:S(2)}, u32[]{:S(2)}) collective-permute-start(bf16[3,16,1536]{2,1,0:T(8,128)(2,1)S(1)} %get-tuple-element.136), channel_id=1, source_target_pairs={{1,0},{2,1},{3,2},{5,4},{6,5},{7,6},{9,8},{10,9},{11,10},{13,12},{... | collective-permute-start | bytes 442376 | tf_op jit(solution)/shard_map/ppermute | solution.py:19
  199.0 4.1 %collective-permute-start.29 = (f32[9408]{0:T(1024)S(1)}, f32[9408]{0:T(1024)S(1)}, u32[]{:S(2)}, u32[]{:S(2)}) collective-permute-start(f32[9408]{0:T(1024)S(1)} %maximum_select_fusion.5), channel_id=1, source_target_pairs={{0,4},{4,0},{8,12},{12,8},{16,20},{20,16},{24,28},{28,24},{1,5},{5... | collective-permute-start | bytes 112904 | tf_op jit(solution)/shard_map/ppermute | solution.py:52
  203.1 7.8 %collective-permute-start.30 = (f32[18816]{0:T(1024)S(1)}, f32[18816]{0:T(1024)S(1)}, u32[]{:S(2)}, u32[]{:S(2)}) collective-permute-start(f32[18816]{0:T(1024)S(1)} %maximum_select_fusion.4), channel_id=1, source_target_pairs={{0,2},{1,3},{2,0},{3,1},{4,6},{5,7},{6,4},{7,5},{8,10},{9,11},{10,... | collective-permute-start | bytes 225800 | tf_op jit(solution)/shard_map/ppermute | solution.py:52
  211.0 1.9 collective-permute-start.31
  212.4 15.7 %collective-permute-start.21 = (bf16[192,1536]{1,0:T(8,128)(2,1)S(1)}, bf16[192,1536]{1,0:T(8,128)(2,1)S(1)}, u32[]{:S(2)}, u32[]{:S(2)}) collective-permute-start(bf16[192,1536]{1,0:T(8,128)(2,1)S(1)} %fusion.11), channel_id=1, source_target_pairs={{0,8},{8,16},{16,24},{24,28},{28,20},{20,12},{12,4},{4,0},{1,9},{9... | collective-permute-start | bytes 1769480 | tf_op jit(solution)/shard_map/ppermute | solution.py:145
  (42 other events, 484.4 us)

commit v14 on v10

--- a/solution.py
+++ b/solution.py
@@ -108,7 +108,21 @@
     gathered = lax.dynamic_update_index_in_dim(gathered, block, me, 0)
     cw = block
     ccw = block
+    split = count % 2 == 0 and count > 2
     for s in range(1, ahead + 1):
+        if split and s == ahead:
+            half = block.shape[-1] // 2
+            cw = jnp.concatenate(
+                [
+                    lax.ppermute(cw[..., :half], axis, forward),
+                    lax.ppermute(ccw[..., half:], axis, backward),
+                ],
+                axis=-1,
+            )
+            gathered = lax.dynamic_update_index_in_dim(
+                gathered, cw, ring_arr[(spot - s) % count], 0
+            )
+            break
         cw = lax.ppermute(cw, axis, forward)
         if s <= behind:
             ccw = lax.ppermute(ccw, axis, backward)

time: 212 us -> 206 us (0.972)
  starting transfers between devices: 36.3 us -> 31.8 us
    ppermute x4 -> x3, waiting for transfers between devices: 20.6 us -> 6.79 us  [ring_all_gather(): cw = lax.ppermute(cw, axis, forward)]
    ppermute x0 -> x2, waiting for transfers between devices: none -> 9.37 us  [the longest x1 7.31 us: ring_all_gather(): lax.ppermute(cw[..., :half], axis, forward)]
    ppermute x5, starting transfers between devices: 8.2 us -> 5.46 us  [tree_allreduce(): other = lax.ppermute(flat, axis, perm)]
    ppermute x0 -> x2, starting transfers between devices: none -> 2.55 us  [the longest x1 2.49 us: ring_all_gather(): lax.ppermute(cw[..., :half], axis, forward)]
    ppermute x4 -> x3, starting transfers between devices: 9.54 us -> 7.1 us  [ring_all_gather(): cw = lax.ppermute(cw, axis, forward)]
  transfers between devices with their start and end apart: 26 -> 27, of which waited for: 19 -> 21; matrix products, arithmetic and copies ran while one was open for 11% -> 11% of each run, Pallas kernels for 0% -> 0%
where the time goes in v14:
time: 206 us; the launch traced here: 205 us
  waiting for transfers between devices  90.4 us (44%)
  between operations  34.9 us (17%)
  starting transfers between devices  31.8 us (15%)
  other arithmetic  19.3 us (9%)
  matrix products  12.4 us (6%)
  local copies, waits for them, and re-layouts  9.73 us (5%)
  blocking collectives  6.61 us (3%)
    reduce_scatter x1, waiting for transfers between devices, body(): lax.psum_scatter(w_term.astype(jnp.bfloat16), 'fsdp', scatter_dimension=0...  27.5 us
    ppermute x5, waiting for transfers between devices, tree_allreduce(): flat = keep + lax.ppermute(give, axis, perm)  17.1 us
    ppermute x5, waiting for transfers between devices, tree_allreduce(): other = lax.ppermute(flat, axis, perm)  11.9 us
    ppermute x2, waiting for transfers between devices, tree_reduce_scatter(): lax.ppermute(give, axis, perm).astype(jnp.float32)  8.25 us
    ppermute x1, waiting for transfers between devices, ring_all_gather(): lax.ppermute(cw[..., :half], axis, forward)  7.31 us
    ppermute x2, waiting for transfers between devices, tree_all_gather(): other = lax.ppermute(data, axis, perm)  7.11 us
    ppermute x3, starting transfers between devices, ring_all_gather(): cw = lax.ppermute(cw, axis, forward)  7.1 us
    ppermute x3, waiting for transfers between devices, ring_all_gather(): cw = lax.ppermute(cw, axis, forward)  6.79 us
  transfers between devices with their start and end apart: 27, of which 21 were waited for; matrix products, arithmetic and copies ran while one was open for 11% of the time, Pallas kernels for 0%

profile of v14, /device:TPU:0, one launch (start us, length us, event | category | flops | bytes accessed | tf_op | source)
XLA Modules:
  0.0 205.0 jit_solution(16736033880117981243)
XLA Ops:
  7.2 1.1 compare_select_fusion
  8.4 3.1 %collective-permute-start = (bf16[192,1536]{1,0:T(8,128)(2,1)S(1)}, bf16[192,1536]{1,0:T(8,128)(2,1)S(1)}, u32[]{:S(2)}, u32[]{:S(2)}) collective-permute-start(bf16[192,1536]{1,0:T(8,128)(2,1)S(1)} %compare_select_fusion), channel_id=1, source_target_pairs={{0,8},{8,16},{16,24},{24,28},{28,20},{20,12},{12,4},{4,0},{1,9},{9... | collective-permute-start | bytes 1769480 | tf_op jit(solution)/shard_map/ppermute | solution.py:126
  26.6 0.9 slice_reduce_fusion.47
  34.2 1.5 collective-permute-start.2
  35.7 1.3 collective-permute-start.3
  37.0 1.9 collective-permute-start.6
  39.3 1.7 collective-permute-done.3
  41.4 3.4 %fusion.153 = (f32[3,16]{1,0:T(4,128)S(1)}, f32[3,16,1536]{2,1,0:T(8,128)S(1)}) fusion(f32[1536]{0:T(1024)S(1)} %get-tuple-element.105, bf16[9,22,1536]{2,1,0:T(8,128)(2,1)S(1)} %select_maximum_fusion.2, f32[1536]{0:T(1024)S(1)} %get-tuple-element.106, f32[1536]{0:T(1024)S(1)} %get-tuple-element.59, f32[1536]{0:T(1024)S(1)} %get-tuple-element.60, ...), kind=kLoop, calls=%fused_computation.375 | loop fusion | flops 10911696 | bytes 7827648 | tf_op jit(solution)/shard_map/reduce_sum | solution.py:228
  45.2 4.1 %collective-permute-start.4 = (bf16[1,3,16,1536]{3,2,1,0:T(8,128)(2,1)S(1)}, bf16[1,3,16,1536]{3,2,1,0:T(8,128)(2,1)S(1)}, u32[]{:S(2)}, u32[]{:S(2)}) collective-permute-start(bf16[1,3,16,1536]{3,2,1,0:T(8,128)(2,1)S(1)} %fusion.144), channel_id=1, source_target_pairs={{0,1},{1,0},{2,3},{3,2},{4,5},{5,4},{6,7},{7,6},{8,9},{9,8},{10,11... | collective-permute-start | bytes 442376 | tf_op jit(solution)/shard_map/ppermute | solution.py:182
  49.3 1.0 collective-permute-done.4
  51.0 2.1 %collective-permute-start.8 = (bf16[192,1536]{1,0:T(8,128)(2,1)S(1)}, bf16[192,1536]{1,0:T(8,128)(2,1)S(1)}, u32[]{:S(2)}, u32[]{:S(2)}) collective-permute-start(bf16[192,1536]{1,0:T(8,128)(2,1)S(1)} %collective-permute-done.6), channel_id=1, source_target_pairs={{0,8},{8,16},{16,24},{24,28},{28,20},{20,12},{12,4},{4,0},{1,9},{9... | collective-permute-start | bytes 1769480 | tf_op jit(solution)/shard_map/ppermute | solution.py:126
  53.5 6.2 %collective-permute-done.5 = bf16[2,3,16,1536]{3,2,1,0:T(8,128)(2,1)S(1)} collective-permute-done((bf16[2,3,16,1536]{3,2,1,0:T(8,128)(2,1)S(1)}, bf16[2,3,16,1536]{3,2,1,0:T(8,128)(2,1)S(1)}, u32[]{:S(2)}, u32[]{:S(2)}) %collective-permute-start.5) | collective-permute-done | bytes 294944 | tf_op jit(solution)/shard_map/ppermute | solution.py:182
  59.8 6.1 %collective-permute-done.8 = bf16[192,1536]{1,0:T(8,128)(2,1)S(1)} collective-permute-done((bf16[192,1536]{1,0:T(8,128)(2,1)S(1)}, bf16[192,1536]{1,0:T(8,128)(2,1)S(1)}, u32[]{:S(2)}, u32[]{:S(2)}) %collective-permute-start.8) | collective-permute-done | bytes 589856 | tf_op jit(solution)/shard_map/ppermute | solution.py:126
  65.9 2.5 %collective-permute-start.10 = (bf16[192,768]{1,0:T(8,128)(2,1)S(1)}, bf16[192,768]{1,0:T(8,128)(2,1)S(1)}, u32[]{:S(2)}, u32[]{:S(2)}) collective-permute-start(bf16[192,768]{1,0:T(8,128)(2,1)S(1)} %slice.744), channel_id=1, source_target_pairs={{0,8},{8,16},{16,24},{24,28},{28,20},{20,12},{12,4},{4,0},{1,9},{9... | collective-permute-start | bytes 884744 | tf_op jit(solution)/shard_map/ppermute | solution.py:117
  69.1 7.3 %collective-permute-done.10 = bf16[192,768]{1,0:T(8,128)(2,1)S(1)} collective-permute-done((bf16[192,768]{1,0:T(8,128)(2,1)S(1)}, bf16[192,768]{1,0:T(8,128)(2,1)S(1)}, u32[]{:S(2)}, u32[]{:S(2)}) %collective-permute-start.10) | collective-permute-done | bytes 294944 | tf_op jit(solution)/shard_map/ppermute | solution.py:117
  76.4 2.1 %collective-permute-done.11 = bf16[192,768]{1,0:T(8,128)(2,1)S(1)} collective-permute-done((bf16[192,768]{1,0:T(8,128)(2,1)S(1)}, bf16[192,768]{1,0:T(8,128)(2,1)S(1)}, u32[]{:S(2)}, u32[]{:S(2)}) %collective-permute-start.11) | collective-permute-done | bytes 294944 | tf_op jit(solution)/shard_map/ppermute | solution.py:118
  78.5 4.8 %fusion.4 = (f32[1536]{0:T(1024)S(1)}, f32[1536]{0:T(1024)S(1)}, f32[192,1536]{1,0:T(8,128)}, f32[192,1536]{1,0:T(8,128)}) fusion(bf16[1,12,16,1536]{3,2,1,0:T(8,128)(2,1)S(1)} %copy-done.3, f32[1536]{0:T(1024)S(1)} %copy-done.54, bf16[192,1536]{1,0:T(8,128)(2,1)S(1)} %bitcast.66, bf16[1536,1536]{1,0:T(8,128)(2,1)S(1)} %bitcast.64), kind=kOutput, calls=%fused_computation.64 | convolution fusion | flops 926610432 | bytes 8275968 | tf_op jit(solution)/shard_map/dot_general | solution.py:286
  84.1 6.6 %all-reduce.2 = (f32[]{:T(128)}, f32[]{:T(128)}) all-reduce(f32[]{:T(128)} %get-tuple-element.127, f32[]{:T(128)} %get-tuple-element.126), channel_id=1, replica_groups=mesh['fsdp'=8,'rows'=4] {'rows'}, use_global_device_ids=true, to_apply=%region_4.5 | all-reduce | flops 2 | bytes 16 | tf_op jit(solution)/shard_map/psum | solution.py:291
  92.0 3.4 %fusion.3 = (bf16[192,1536]{1,0:T(8,128)(2,1)S(1)}, bf16[192,1536]{1,0:T(8,128)(2,1)}) fusion(f32[192,1536]{1,0:T(8,128)} %get-tuple-element.149, f32[192,1536]{1,0:T(8,128)} %get-tuple-element.134, bf16[1,12,16,1536]{3,2,1,0:T(8,128)(2,1)} %param.21, f32[1536]{0:T(1024)S(1)} %get-tuple-element.141, f32[1536]{0:T(1024)S(1)} %get-tuple-element.132, ...), kind=kLoop, calls=%fused_computation.63 | loop fusion | flops 5603328 | bytes 4159488 | tf_op jit(solution)/shard_map/convert_element_type | solution.py:298
  95.4 3.6 %convolution_convert_fusion = bf16[1536,1536]{1,0:T(8,128)(2,1)} fusion(bf16[192,1536]{1,0:T(8,128)(2,1)S(1)} %bitcast.67, bf16[192,1536]{1,0:T(8,128)(2,1)S(1)} %get-tuple-element.137), kind=kOutput, calls=%fused_computation | convolution fusion | flops 908328960 | bytes 5898240 | tf_op jit(solution)/shard_map/dot_general | solution.py:299
  99.0 4.0 %convolution_convert_fusion.1 = bf16[12,16,1536]{2,1,0:T(8,128)(2,1)S(1)} fusion(bf16[12,16,1536]{2,1,0:T(8,128)(2,1)S(1)} %bitcast.68, bf16[1536,1536,1]{1,0,2:T(8,128)(2,1)} %bitcast.65), kind=kOutput, calls=%fused_computation.52 | convolution fusion | flops 906264576 | bytes 5898240 | tf_op jit(solution)/shard_map/hwf,cf->hwc/dot_general | solution.py:306
  103.9 0.9 collective-permute-done.12
  104.7 1.0 convert_add_fusion
  105.8 1.7 collective-permute-start.13
  107.6 7.4 %collective-permute-done.13 = f32[1,3,16,1536]{3,2,1,0:T(8,128)S(1)} collective-permute-done((f32[1,3,16,1536]{3,2,1,0:T(8,128)S(1)}, f32[1,3,16,1536]{3,2,1,0:T(8,128)S(1)}, u32[]{:S(2)}, u32[]{:S(2)}) %collective-permute-start.13) | collective-permute-done | bytes 294944 | tf_op jit(solution)/shard_map/ppermute | solution.py:69
  115.1 1.6 fusion.141
  117.5 0.8 fusion.142
  119.6 0.9 dynamic-slice_reduce_fusion
  120.5 1.4 collective-permute-done.16
  122.4 1.7 collective-permute-start.17
  124.2 2.7 %collective-permute-done.17 = f32[18816]{0:T(1024)S(1)} collective-permute-done((f32[18816]{0:T(1024)S(1)}, f32[18816]{0:T(1024)S(1)}, u32[]{:S(2)}, u32[]{:S(2)}) %collective-permute-start.17) | collective-permute-done | bytes 75296 | tf_op jit(solution)/shard_map/ppermute | solution.py:49
  127.8 4.6 %collective-permute-done.18 = f32[9408]{0:T(1024)S(1)} collective-permute-done((f32[9408]{0:T(1024)S(1)}, f32[9408]{0:T(1024)S(1)}, u32[]{:S(2)}, u32[]{:S(2)}) %collective-permute-start.18) | collective-permute-done | bytes 37664 | tf_op jit(solution)/shard_map/ppermute | solution.py:49
  132.6 1.5 collective-permute-start.19
  134.1 3.8 %collective-permute-done.19 = f32[4704]{0:T(1024)S(1)} collective-permute-done((f32[4704]{0:T(1024)S(1)}, f32[4704]{0:T(1024)S(1)}, u32[]{:S(2)}, u32[]{:S(2)}) %collective-permute-start.19) | collective-permute-done | bytes 18848 | tf_op jit(solution)/shard_map/ppermute | solution.py:49
  138.1 1.5 collective-permute-start.20
  139.6 4.6 %collective-permute-done.20 = f32[2352]{0:T(1024)S(1)} collective-permute-done((f32[2352]{0:T(1024)S(1)}, f32[2352]{0:T(1024)S(1)}, u32[]{:S(2)}, u32[]{:S(2)}) %collective-permute-start.20) | collective-permute-done | bytes 9440 | tf_op jit(solution)/shard_map/ppermute | solution.py:49
  144.7 4.2 %collective-permute-done.21 = f32[2352]{0:T(1024)S(1)} collective-permute-done((f32[2352]{0:T(1024)S(1)}, f32[2352]{0:T(1024)S(1)}, u32[]{:S(2)}, u32[]{:S(2)}) %collective-permute-start.21) | collective-permute-done | bytes 9440 | tf_op jit(solution)/shard_map/ppermute | solution.py:52
  148.9 1.2 collective-permute-start.22
  150.1 2.6 %collective-permute-done.22 = f32[4704]{0:T(1024)S(1)} collective-permute-done((f32[4704]{0:T(1024)S(1)}, f32[4704]{0:T(1024)S(1)}, u32[]{:S(2)}, u32[]{:S(2)}) %collective-permute-start.22) | collective-permute-done | bytes 18848 | tf_op jit(solution)/shard_map/ppermute | solution.py:52
  153.2 1.3 collective-permute-start.14
  154.5 1.3 collective-permute-start.15
  155.8 1.0 collective-permute-done.23
  157.0 3.4 %collective-permute-start.24 = (f32[18816]{0:T(1024)S(1)}, f32[18816]{0:T(1024)S(1)}, u32[]{:S(2)}, u32[]{:S(2)}) collective-permute-start(f32[18816]{0:T(1024)S(1)} %maximum_select_fusion.4), channel_id=1, source_target_pairs={{0,2},{1,3},{2,0},{3,1},{4,6},{5,7},{6,4},{7,5},{8,10},{9,11},{10,... | collective-permute-start | bytes 225800 | tf_op jit(solution)/shard_map/ppermute | solution.py:52
  160.6 4.0 %collective-permute-done.24 = f32[18816]{0:T(1024)S(1)} collective-permute-done((f32[18816]{0:T(1024)S(1)}, f32[18816]{0:T(1024)S(1)}, u32[]{:S(2)}, u32[]{:S(2)}) %collective-permute-start.24) | collective-permute-done | bytes 75296 | tf_op jit(solution)/shard_map/ppermute | solution.py:52
  164.8 2.8 %fusion.147 = bf16[1,3,16,1536]{3,2,1,0:T(8,128)(2,1)} fusion(f32[1536]{0:T(1024)S(1)} %copy-done.44, bf16[9,22,1536]{2,1,0:T(8,128)(2,1)S(1)} %select_maximum_fusion, f32[1536]{0:T(1024)S(1)} %copy-done.46, f32[1536]{0:T(1024)S(1)} %get-tuple-element.59, f32[1536]{0:T(1024)S(1)} %get-tuple-element.60, bf16[3,16,1536]{2,1,0:T(8,128)(2,1)S(1)} %collective-permute-done.14, ...), kind=kLoop, calls=%fused_computation.298 | loop fusion | flops 11132928 | bytes 7084032 | tf_op jit(solution)/shard_map/reshape | solution.py:321
  167.7 0.8 select_n.294
  168.5 27.5 %reduce-scatter.2.cloned.1.call-done = bf16[192,1536]{1,0:T(8,128)(2,1)} async-done(((bf16[1536,1536]{1,0:T(8,128)(2,1)}), bf16[192,1536]{1,0:T(8,128)(2,1)}) %reduce-scatter.2.cloned.1.call-update) | async-done | bytes 589840 | tf_op jit(solution)/shard_map/reduce_scatter | solution.py:302
  196.0 2.2 %convert_element_type.497 = f32[192,1536]{1,0:T(8,128)} convert(bf16[192,1536]{1,0:T(8,128)(2,1)} %reduce-scatter.2.cloned.1.call-done) | non-fusion elementwise | flops 294912 | bytes 1769472 | tf_op jit(solution)/shard_map/convert_element_type | solution.py:304
  (236 shorter events, 13.2 us)
Async XLA Ops:
  7.2 188.8 %reduce-scatter.2.cloned.1.call-start = ((), (), s32[]{:S(2)}) async-start(), calls=%async_computation.1 | async-start | bytes 5308416 | tf_op jit(solution)/shard_map/reduce_scatter | solution.py:302
  8.4 25.1 %collective-permute-start = (bf16[192,1536]{1,0:T(8,128)(2,1)S(1)}, bf16[192,1536]{1,0:T(8,128)(2,1)S(1)}, u32[]{:S(2)}, u32[]{:S(2)}) collective-permute-start(bf16[192,1536]{1,0:T(8,128)(2,1)S(1)} %compare_select_fusion), channel_id=1, source_target_pairs={{0,8},{8,16},{16,24},{24,28},{28,20},{20,12},{12,4},{4,0},{1,9},{9... | collective-permute-start | bytes 1769480 | tf_op jit(solution)/shard_map/ppermute | solution.py:126
  11.5 22.0 %collective-permute-start.1 = (bf16[192,1536]{1,0:T(8,128)(2,1)S(1)}, bf16[192,1536]{1,0:T(8,128)(2,1)S(1)}, u32[]{:S(2)}, u32[]{:S(2)}) collective-permute-start(bf16[192,1536]{1,0:T(8,128)(2,1)S(1)} %compare_select_fusion), channel_id=1, source_target_pairs={{0,4},{8,0},{16,8},{24,16},{28,24},{20,28},{12,20},{4,12},{1,5},{9... | collective-permute-start | bytes 1769480 | tf_op jit(solution)/shard_map/ppermute | solution.py:128
  34.2 5.0 %collective-permute-start.2 = (bf16[3,16,1536]{2,1,0:T(8,128)(2,1)S(1)}, bf16[3,16,1536]{2,1,0:T(8,128)(2,1)S(1)}, u32[]{:S(2)}, u32[]{:S(2)}) collective-permute-start(bf16[3,16,1536]{2,1,0:T(8,128)(2,1)S(1)} %bitcast.69), channel_id=1, source_target_pairs={{0,1},{1,2},{2,3},{4,5},{5,6},{6,7},{8,9},{9,10},{10,11},{12,13},{... | collective-permute-start | bytes 442376 | tf_op jit(solution)/shard_map/ppermute | solution.py:16
  35.7 5.3 %collective-permute-start.3 = (bf16[3,16,1536]{2,1,0:T(8,128)(2,1)S(1)}, bf16[3,16,1536]{2,1,0:T(8,128)(2,1)S(1)}, u32[]{:S(2)}, u32[]{:S(2)}) collective-permute-start(bf16[3,16,1536]{2,1,0:T(8,128)(2,1)S(1)} %bitcast.70), channel_id=1, source_target_pairs={{1,0},{2,1},{3,2},{5,4},{6,5},{7,6},{9,8},{10,9},{11,10},{13,12},{... | collective-permute-start | bytes 442376 | tf_op jit(solution)/shard_map/ppermute | solution.py:19
  37.0 14.0 %collective-permute-start.6 = (bf16[192,1536]{1,0:T(8,128)(2,1)S(1)}, bf16[192,1536]{1,0:T(8,128)(2,1)S(1)}, u32[]{:S(2)}, u32[]{:S(2)}) collective-permute-start(bf16[192,1536]{1,0:T(8,128)(2,1)S(1)} %collective-permute-done), channel_id=1, source_target_pairs={{0,8},{8,16},{16,24},{24,28},{28,20},{20,12},{12,4},{4,0},{1,9},{9... | collective-permute-start | bytes 1769480 | tf_op jit(solution)/shard_map/ppermute | solution.py:126
  38.9 14.5 %collective-permute-start.7 = (bf16[192,1536]{1,0:T(8,128)(2,1)S(1)}, bf16[192,1536]{1,0:T(8,128)(2,1)S(1)}, u32[]{:S(2)}, u32[]{:S(2)}) collective-permute-start(bf16[192,1536]{1,0:T(8,128)(2,1)S(1)} %collective-permute-done.1), channel_id=1, source_target_pairs={{0,4},{8,0},{16,8},{24,16},{28,24},{20,28},{12,20},{4,12},{1,5},{9... | collective-permute-start | bytes 1769480 | tf_op jit(solution)/shard_map/ppermute | solution.py:128
  44.9 70.1 %copy-start.47 = (f32[3,16]{1,0:T(4,128)}, f32[3,16]{1,0:T(4,128)S(1)}, u32[]{:S(2)}) copy-start(f32[3,16]{1,0:T(4,128)S(1)} %broadcast_multiply_fusion.2) | copy-start | bytes 580
  45.1 69.9 %copy-start.48 = (f32[3,16]{1,0:T(4,128)}, f32[3,16]{1,0:T(4,128)S(1)}, u32[]{:S(2)}) copy-start(f32[3,16]{1,0:T(4,128)S(1)} %add_rsqrt_fusion) | copy-start | bytes 580
  45.2 5.1 %collective-permute-start.4 = (bf16[1,3,16,1536]{3,2,1,0:T(8,128)(2,1)S(1)}, bf16[1,3,16,1536]{3,2,1,0:T(8,128)(2,1)S(1)}, u32[]{:S(2)}, u32[]{:S(2)}) collective-permute-start(bf16[1,3,16,1536]{3,2,1,0:T(8,128)(2,1)S(1)} %fusion.144), channel_id=1, source_target_pairs={{0,1},{1,0},{2,3},{3,2},{4,5},{5,4},{6,7},{7,6},{8,9},{9,8},{10,11... | collective-permute-start | bytes 442376 | tf_op jit(solution)/shard_map/ppermute | solution.py:182
  50.3 9.3 %collective-permute-start.5 = (bf16[2,3,16,1536]{3,2,1,0:T(8,128)(2,1)S(1)}, bf16[2,3,16,1536]{3,2,1,0:T(8,128)(2,1)S(1)}, u32[]{:S(2)}, u32[]{:S(2)}) collective-permute-start(bf16[2,3,16,1536]{3,2,1,0:T(8,128)(2,1)S(1)} %maximum_select_fusion.2), channel_id=1, source_target_pairs={{0,2},{1,3},{2,0},{3,1},{4,6},{5,7},{6,4},{7,5},{8,10},{9,11},{10,... | collective-permute-start | bytes 884744 | tf_op jit(solution)/shard_map/ppermute | solution.py:182
  51.0 14.9 %collective-permute-start.8 = (bf16[192,1536]{1,0:T(8,128)(2,1)S(1)}, bf16[192,1536]{1,0:T(8,128)(2,1)S(1)}, u32[]{:S(2)}, u32[]{:S(2)}) collective-permute-start(bf16[192,1536]{1,0:T(8,128)(2,1)S(1)} %collective-permute-done.6), channel_id=1, source_target_pairs={{0,8},{8,16},{16,24},{24,28},{28,20},{20,12},{12,4},{4,0},{1,9},{9... | collective-permute-start | bytes 1769480 | tf_op jit(solution)/shard_map/ppermute | solution.py:126
  53.4 15.4 %collective-permute-start.9 = (bf16[192,1536]{1,0:T(8,128)(2,1)S(1)}, bf16[192,1536]{1,0:T(8,128)(2,1)S(1)}, u32[]{:S(2)}, u32[]{:S(2)}) collective-permute-start(bf16[192,1536]{1,0:T(8,128)(2,1)S(1)} %collective-permute-done.7), channel_id=1, source_target_pairs={{0,4},{8,0},{16,8},{24,16},{28,24},{20,28},{12,20},{4,12},{1,5},{9... | collective-permute-start | bytes 1769480 | tf_op jit(solution)/shard_map/ppermute | solution.py:128
  65.9 10.4 %collective-permute-start.10 = (bf16[192,768]{1,0:T(8,128)(2,1)S(1)}, bf16[192,768]{1,0:T(8,128)(2,1)S(1)}, u32[]{:S(2)}, u32[]{:S(2)}) collective-permute-start(bf16[192,768]{1,0:T(8,128)(2,1)S(1)} %slice.744), channel_id=1, source_target_pairs={{0,8},{8,16},{16,24},{24,28},{28,20},{20,12},{12,4},{4,0},{1,9},{9... | collective-permute-start | bytes 884744 | tf_op jit(solution)/shard_map/ppermute | solution.py:117
  68.9 9.6 %collective-permute-start.11 = (bf16[192,768]{1,0:T(8,128)(2,1)S(1)}, bf16[192,768]{1,0:T(8,128)(2,1)S(1)}, u32[]{:S(2)}, u32[]{:S(2)}) collective-permute-start(bf16[192,768]{1,0:T(8,128)(2,1)S(1)} %slice.745), channel_id=1, source_target_pairs={{0,4},{8,0},{16,8},{24,16},{28,24},{20,28},{12,20},{4,12},{1,5},{9... | collective-permute-start | bytes 884744 | tf_op jit(solution)/shard_map/ppermute | solution.py:118
  103.1 1.6 collective-permute-start.12
  105.8 9.1 %collective-permute-start.13 = (f32[1,3,16,1536]{3,2,1,0:T(8,128)S(1)}, f32[1,3,16,1536]{3,2,1,0:T(8,128)S(1)}, u32[]{:S(2)}, u32[]{:S(2)}) collective-permute-start(f32[1,3,16,1536]{3,2,1,0:T(8,128)S(1)} %constant_dynamic-slice_fusion), channel_id=1, source_target_pairs={{0,2},{1,3},{2,0},{3,1},{4,6},{5,7},{6,4},{7,5},{8,10},{9,11},{10,... | collective-permute-start | bytes 884744 | tf_op jit(solution)/shard_map/ppermute | solution.py:69
  120.5 1.4 collective-permute-start.16
  122.4 4.5 %collective-permute-start.17 = (f32[18816]{0:T(1024)S(1)}, f32[18816]{0:T(1024)S(1)}, u32[]{:S(2)}, u32[]{:S(2)}) collective-permute-start(f32[18816]{0:T(1024)S(1)} %get-tuple-element.111), channel_id=1, source_target_pairs={{0,2},{1,3},{2,0},{3,1},{4,6},{5,7},{6,4},{7,5},{8,10},{9,11},{10,... | collective-permute-start | bytes 225800 | tf_op jit(solution)/shard_map/ppermute | solution.py:49
  127.3 37.4 %copy-start.8 = (f32[1536]{0:T(1024)S(1)}, f32[1536]{0:T(1024)}, u32[]{:S(2)}) copy-start(f32[1536]{0:T(1024)} %get-tuple-element.87) | copy-start | bytes 18436
  127.3 37.4 %copy-start.10 = (f32[1536]{0:T(1024)S(1)}, f32[1536]{0:T(1024)}, u32[]{:S(2)}) copy-start(f32[1536]{0:T(1024)} %get-tuple-element.88) | copy-start | bytes 18436
  127.3 37.4 %copy-start.12 = (f32[1536]{0:T(1024)S(1)}, f32[1536]{0:T(1024)}, u32[]{:S(2)}) copy-start(f32[1536]{0:T(1024)} %get-tuple-element.89) | copy-start | bytes 18436
  127.3 37.4 %copy-start.14 = (f32[1536]{0:T(1024)S(1)}, f32[1536]{0:T(1024)}, u32[]{:S(2)}) copy-start(f32[1536]{0:T(1024)} %get-tuple-element.90) | copy-start | bytes 18436
  127.3 37.4 %copy-start.16 = (f32[1536]{0:T(1024)S(1)}, f32[1536]{0:T(1024)}, u32[]{:S(2)}) copy-start(f32[1536]{0:T(1024)} %get-tuple-element.91) | copy-start | bytes 18436
  127.3 37.4 %copy-start.18 = (f32[1536]{0:T(1024)S(1)}, f32[1536]{0:T(1024)}, u32[]{:S(2)}) copy-start(f32[1536]{0:T(1024)} %get-tuple-element.92) | copy-start | bytes 18436
  127.3 37.4 %copy-start.20 = (f32[1536]{0:T(1024)S(1)}, f32[1536]{0:T(1024)}, u32[]{:S(2)}) copy-start(f32[1536]{0:T(1024)} %get-tuple-element.93) | copy-start | bytes 18436
  127.4 37.4 %copy-start.22 = (f32[1536]{0:T(1024)S(1)}, f32[1536]{0:T(1024)}, u32[]{:S(2)}) copy-start(f32[1536]{0:T(1024)} %get-tuple-element.94) | copy-start | bytes 18436
  127.4 37.4 %copy-start.24 = (f32[1536]{0:T(1024)S(1)}, f32[1536]{0:T(1024)}, u32[]{:S(2)}) copy-start(f32[1536]{0:T(1024)} %get-tuple-element.95) | copy-start | bytes 18436
  127.4 37.4 %copy-start.26 = (f32[1536]{0:T(1024)S(1)}, f32[1536]{0:T(1024)}, u32[]{:S(2)}) copy-start(f32[1536]{0:T(1024)} %copy-done.25) | copy-start | bytes 18436
  127.4 37.4 %copy-start.28 = (f32[1536]{0:T(1024)S(1)}, f32[1536]{0:T(1024)}, u32[]{:S(2)}) copy-start(f32[1536]{0:T(1024)} %copy-done.27) | copy-start | bytes 18436
  127.4 37.4 %copy-start.30 = (f32[1536]{0:T(1024)S(1)}, f32[1536]{0:T(1024)}, u32[]{:S(2)}) copy-start(f32[1536]{0:T(1024)} %copy-done.29) | copy-start | bytes 18436
  127.4 37.4 %copy-start.32 = (f32[1536]{0:T(1024)S(1)}, f32[1536]{0:T(1024)}, u32[]{:S(2)}) copy-start(f32[1536]{0:T(1024)} %copy-done.31) | copy-start | bytes 18436
  127.4 37.4 %copy-start.34 = (f32[1536]{0:T(1024)S(1)}, f32[1536]{0:T(1024)}, u32[]{:S(2)}) copy-start(f32[1536]{0:T(1024)} %copy-done.33) | copy-start | bytes 18436
  127.4 37.4 %copy-start.36 = (f32[1536]{0:T(1024)S(1)}, f32[1536]{0:T(1024)}, u32[]{:S(2)}) copy-start(f32[1536]{0:T(1024)} %copy-done.35) | copy-start | bytes 18436
  127.4 37.4 %copy-start.38 = (f32[1536]{0:T(1024)S(1)}, f32[1536]{0:T(1024)}, u32[]{:S(2)}) copy-start(f32[1536]{0:T(1024)} %copy-done.37) | copy-start | bytes 18436
  127.4 37.4 %copy-start.40 = (f32[1536]{0:T(1024)S(1)}, f32[1536]{0:T(1024)}, u32[]{:S(2)}) copy-start(f32[1536]{0:T(1024)} %copy-done.39) | copy-start | bytes 18436
  127.5 37.4 %copy-start.42 = (f32[1536]{0:T(1024)S(1)}, f32[1536]{0:T(1024)}, u32[]{:S(2)}) copy-start(f32[1536]{0:T(1024)} %copy-done.41) | copy-start | bytes 18436
  127.5 37.4 %copy-start.44 = (f32[1536]{0:T(1024)S(1)}, f32[1536]{0:T(1024)}, u32[]{:S(2)}) copy-start(f32[1536]{0:T(1024)} %copy-done.43) | copy-start | bytes 18436
  127.5 4.9 %collective-permute-start.18 = (f32[9408]{0:T(1024)S(1)}, f32[9408]{0:T(1024)S(1)}, u32[]{:S(2)}, u32[]{:S(2)}) collective-permute-start(f32[9408]{0:T(1024)S(1)} %get-tuple-element.120), channel_id=1, source_target_pairs={{0,4},{4,0},{8,12},{12,8},{16,20},{20,16},{24,28},{28,24},{1,5},{5... | collective-permute-start | bytes 112904 | tf_op jit(solution)/shard_map/ppermute | solution.py:49
  132.6 5.3 %collective-permute-start.19 = (f32[4704]{0:T(1024)S(1)}, f32[4704]{0:T(1024)S(1)}, u32[]{:S(2)}, u32[]{:S(2)}) collective-permute-start(f32[4704]{0:T(1024)S(1)} %get-tuple-element.122), channel_id=1, source_target_pairs={{0,8},{4,12},{8,0},{12,4},{16,24},{20,28},{24,16},{28,20},{1,9},{5... | collective-permute-start | bytes 56456 | tf_op jit(solution)/shard_map/ppermute | solution.py:49
  138.1 6.1 %collective-permute-start.20 = (f32[2352]{0:T(1024)S(1)}, f32[2352]{0:T(1024)S(1)}, u32[]{:S(2)}, u32[]{:S(2)}) collective-permute-start(f32[2352]{0:T(1024)S(1)} %get-tuple-element.124), channel_id=1, source_target_pairs={{0,16},{4,20},{8,24},{12,28},{16,0},{20,4},{24,8},{28,12},{1,17},{... | collective-permute-start | bytes 28232 | tf_op jit(solution)/shard_map/ppermute | solution.py:49
  144.2 4.6 %collective-permute-start.21 = (f32[2352]{0:T(1024)S(1)}, f32[2352]{0:T(1024)S(1)}, u32[]{:S(2)}, u32[]{:S(2)}) collective-permute-start(f32[2352]{0:T(1024)S(1)} %add.722), channel_id=1, source_target_pairs={{0,16},{4,20},{8,24},{12,28},{16,0},{20,4},{24,8},{28,12},{1,17},{... | collective-permute-start | bytes 28232 | tf_op jit(solution)/shard_map/ppermute | solution.py:52
  148.9 3.8 %collective-permute-start.22 = (f32[4704]{0:T(1024)S(1)}, f32[4704]{0:T(1024)S(1)}, u32[]{:S(2)}, u32[]{:S(2)}) collective-permute-start(f32[4704]{0:T(1024)S(1)} %maximum_select_fusion.6), channel_id=1, source_target_pairs={{0,8},{4,12},{8,0},{12,4},{16,24},{20,28},{24,16},{28,20},{1,9},{5... | collective-permute-start | bytes 56456 | tf_op jit(solution)/shard_map/ppermute | solution.py:52
  152.8 4.1 %collective-permute-start.23 = (f32[9408]{0:T(1024)S(1)}, f32[9408]{0:T(1024)S(1)}, u32[]{:S(2)}, u32[]{:S(2)}) collective-permute-start(f32[9408]{0:T(1024)S(1)} %maximum_select_fusion.5), channel_id=1, source_target_pairs={{0,4},{4,0},{8,12},{12,8},{16,20},{20,16},{24,28},{28,24},{1,5},{5... | collective-permute-start | bytes 112904 | tf_op jit(solution)/shard_map/ppermute | solution.py:52
  153.2 7.1 %collective-permute-start.14 = (bf16[3,16,1536]{2,1,0:T(8,128)(2,1)S(1)}, bf16[3,16,1536]{2,1,0:T(8,128)(2,1)S(1)}, u32[]{:S(2)}, u32[]{:S(2)}) collective-permute-start(bf16[3,16,1536]{2,1,0:T(8,128)(2,1)S(1)} %get-tuple-element.130), channel_id=1, source_target_pairs={{0,1},{1,2},{2,3},{4,5},{5,6},{6,7},{8,9},{9,10},{10,11},{12,13},{... | collective-permute-start | bytes 442376 | tf_op jit(solution)/shard_map/ppermute | solution.py:16
  154.5 5.8 %collective-permute-start.15 = (bf16[3,16,1536]{2,1,0:T(8,128)(2,1)S(1)}, bf16[3,16,1536]{2,1,0:T(8,128)(2,1)S(1)}, u32[]{:S(2)}, u32[]{:S(2)}) collective-permute-start(bf16[3,16,1536]{2,1,0:T(8,128)(2,1)S(1)} %get-tuple-element.130), channel_id=1, source_target_pairs={{1,0},{2,1},{3,2},{5,4},{6,5},{7,6},{9,8},{10,9},{11,10},{13,12},{... | collective-permute-start | bytes 442376 | tf_op jit(solution)/shard_map/ppermute | solution.py:19
  157.0 7.6 %collective-permute-start.24 = (f32[18816]{0:T(1024)S(1)}, f32[18816]{0:T(1024)S(1)}, u32[]{:S(2)}, u32[]{:S(2)}) collective-permute-start(f32[18816]{0:T(1024)S(1)} %maximum_select_fusion.4), channel_id=1, source_target_pairs={{0,2},{1,3},{2,0},{3,1},{4,6},{5,7},{6,4},{7,5},{8,10},{9,11},{10,... | collective-permute-start | bytes 225800 | tf_op jit(solution)/shard_map/ppermute | solution.py:52
  164.6 3.1 %collective-permute-start.25 = (f32[37632]{0:T(1024)S(1)}, f32[37632]{0:T(1024)S(1)}, u32[]{:S(2)}, u32[]{:S(2)}) collective-permute-start(f32[37632]{0:T(1024)S(1)} %maximum_select_fusion.3), channel_id=1, source_target_pairs={{0,1},{1,0},{2,3},{3,2},{4,5},{5,4},{6,7},{7,6},{8,9},{9,8},{10,11... | collective-permute-start | bytes 451592 | tf_op jit(solution)/shard_map/ppermute | solution.py:52
  (35 other events, 244.1 us)
Sparse Core Ops, SparseCore 0:
  99.1 96.7 reduce-scatter.1

commit v15 on v14

--- a/solution.py
+++ b/solution.py
@@ -123,9 +123,20 @@
                 gathered, cw, ring_arr[(spot - s) % count], 0
             )
             break
-        cw = lax.ppermute(cw, axis, forward)
-        if s <= behind:
-            ccw = lax.ppermute(ccw, axis, backward)
+        if split and s == 1:
+            half = block.shape[-1] // 2
+            cw = jnp.concatenate(
+                [lax.ppermute(cw[..., :half], axis, forward), lax.ppermute(cw[..., half:], axis, forward)],
+                axis=-1,
+            )
+            ccw = jnp.concatenate(
+                [lax.ppermute(ccw[..., :half], axis, backward), lax.ppermute(ccw[..., half:], axis, backward)],
+                axis=-1,
+            )
+        else:
+            cw = lax.ppermute(cw, axis, forward)
+            if s <= behind:
+                ccw = lax.ppermute(ccw, axis, backward)
         if s == 1 and held is not None:
             cw, ccw, held = lax.optimization_barrier((cw, ccw, held))
         gathered = lax.dynamic_update_index_in_dim(gathered, cw, ring_arr[(spot - s) % count], 0)

time: 206 us -> 214 us (1.039)
  local copies, waits for them, and re-layouts: 9.73 us -> 15.7 us
  waiting for transfers between devices: 90.4 us -> 85.5 us
  matrix products: 12.4 us -> 14.9 us
    ppermute x0 -> x2, starting transfers between devices: none -> 3.14 us  [the longest x1 3.02 us: ring_all_gather(): lax.ppermute(ccw[..., :half], axis, backward)]
    ppermute x3 -> x2, starting transfers between devices: 7.1 us -> 4.34 us  [ring_all_gather(): cw = lax.ppermute(cw, axis, forward)]
    dot_general x1, matrix products: 4.85 us -> 7.33 us  [body(): pre = jnp.dot(flat, columns, preferred_element_type=jnp.float32) + up_bias]
    dynamic_update_slice x3, local copies, waits for them, and re-layouts: 0.13 us -> 2.62 us  [ring_all_gather(): lax.dynamic_update_index_in_dim(gathered, ccw, ring_arr[(spot + s) % coun...]
    dynamic_update_slice x3, local copies, waits for them, and re-layouts: 0.13 us -> 2.6 us  [ring_all_gather(): lax.dynamic_update_index_in_dim(gathered, cw, ring_arr[(spot - s) % count...]
    broadcast_in_dim x1, local copies, waits for them, and re-layouts: 0.4 us -> 2.57 us  [ring_all_gather(): gathered = jnp.zeros((count,) + block.shape, block.dtype)]
    ppermute x1 -> x2, waiting for transfers between devices: 7.31 us -> 5.67 us  [ring_all_gather(): lax.ppermute(cw[..., :half], axis, forward)]
    ppermute x3 -> x2, waiting for transfers between devices: 6.79 us -> 5.69 us  [ring_all_gather(): cw = lax.ppermute(cw, axis, forward)]
  transfers between devices with their start and end apart: 27 -> 29, of which waited for: 21 -> 21; matrix products, arithmetic and copies ran while one was open for 11% -> 14% of each run, Pallas kernels for 0% -> 0%
where the time goes in v15:
time: 214 us; the launch traced here: 213 us
  waiting for transfers between devices  85.5 us (40%)
  between operations  35.1 us (16%)
  starting transfers between devices  33.9 us (16%)
  other arithmetic  21 us (10%)
  local copies, waits for them, and re-layouts  15.7 us (7%)
  matrix products  14.9 us (7%)
  blocking collectives  6.61 us (3%)
    reduce_scatter x1, waiting for transfers between devices, body(): lax.psum_scatter(w_term.astype(jnp.bfloat16), 'fsdp', scatter_dimension=0...  27.4 us
    ppermute x5, waiting for transfers between devices, tree_allreduce(): flat = keep + lax.ppermute(give, axis, perm)  17.3 us
    ppermute x5, waiting for transfers between devices, tree_allreduce(): other = lax.ppermute(flat, axis, perm)  11.9 us
    ppermute x2, waiting for transfers between devices, tree_reduce_scatter(): lax.ppermute(give, axis, perm).astype(jnp.float32)  8.27 us
    dot_general x1, matrix products, body(): pre = jnp.dot(flat, columns, preferred_element_type=jnp.float32) + up_bias  7.33 us
    psum x1, blocking collectives, body(): norm_total = lax.psum(jnp.sum(norms), 'rows')  6.61 us
    ppermute x2, waiting for transfers between devices, ring_all_gather(): cw = lax.ppermute(cw, axis, forward)  5.69 us
    ppermute x2, waiting for transfers between devices, ring_all_gather(): lax.ppermute(cw[..., :half], axis, forward)  5.67 us
  transfers between devices with their start and end apart: 29, of which 21 were waited for; matrix products, arithmetic and copies ran while one was open for 14% of the time, Pallas kernels for 0%

profile of v15, /device:TPU:0, one launch (start us, length us, event | category | flops | bytes accessed | tf_op | source)
XLA Modules:
  0.0 212.7 jit_solution(5115628117740073428)
XLA Ops:
  7.2 1.1 compare_select_fusion
  8.4 3.0 %collective-permute-start.2 = (bf16[192,768]{1,0:T(8,128)(2,1)S(1)}, bf16[192,768]{1,0:T(8,128)(2,1)S(1)}, u32[]{:S(2)}, u32[]{:S(2)}) collective-permute-start(bf16[192,768]{1,0:T(8,128)(2,1)S(1)} %get-tuple-element.139), channel_id=1, source_target_pairs={{0,4},{8,0},{16,8},{24,16},{28,24},{20,28},{12,20},{4,12},{1,5},{9... | collective-permute-start | bytes 884744 | tf_op jit(solution)/shard_map/ppermute | solution.py:133
  11.5 1.9 collective-permute-start.3
  13.5 2.6 %broadcast_in_dim.50 = bf16[8,192,1536]{2,1,0:T(8,128)(2,1)} broadcast(bf16[]{:T(256)} %constant.257.clone.1), dimensions={} | broadcast | bytes 4718594 | tf_op jit(solution)/shard_map/broadcast_in_dim | solution.py:107
  16.1 1.0 bitcast_dynamic-update-slice_fusion.6
  38.6 1.3 collective-permute-start.4
  39.9 1.3 collective-permute-start.5
  41.2 2.0 collective-permute-start.8
  44.2 1.1 collective-permute-done.5
  45.8 3.4 %fusion.153 = (f32[3,16]{1,0:T(4,128)S(1)}, f32[3,16,1536]{2,1,0:T(8,128)S(1)}) fusion(f32[1536]{0:T(1024)S(1)} %get-tuple-element.105, bf16[9,22,1536]{2,1,0:T(8,128)(2,1)S(1)} %select_maximum_fusion.2, f32[1536]{0:T(1024)S(1)} %get-tuple-element.106, f32[1536]{0:T(1024)S(1)} %get-tuple-element.59, f32[1536]{0:T(1024)S(1)} %get-tuple-element.60, ...), kind=kLoop, calls=%fused_computation.377 | loop fusion | flops 10911696 | bytes 7827648 | tf_op jit(solution)/shard_map/reduce_sum | solution.py:239
  49.5 4.1 %collective-permute-start.6 = (bf16[1,3,16,1536]{3,2,1,0:T(8,128)(2,1)S(1)}, bf16[1,3,16,1536]{3,2,1,0:T(8,128)(2,1)S(1)}, u32[]{:S(2)}, u32[]{:S(2)}) collective-permute-start(bf16[1,3,16,1536]{3,2,1,0:T(8,128)(2,1)S(1)} %fusion.144), channel_id=1, source_target_pairs={{0,1},{1,0},{2,3},{3,2},{4,5},{5,4},{6,7},{7,6},{8,9},{9,8},{10,11... | collective-permute-start | bytes 442376 | tf_op jit(solution)/shard_map/ppermute | solution.py:193
  55.1 2.3 %collective-permute-start.10 = (bf16[192,1536]{1,0:T(8,128)(2,1)S(1)}, bf16[192,1536]{1,0:T(8,128)(2,1)S(1)}, u32[]{:S(2)}, u32[]{:S(2)}) collective-permute-start(bf16[192,1536]{1,0:T(8,128)(2,1)S(1)} %collective-permute-done.8), channel_id=1, source_target_pairs={{0,8},{8,16},{16,24},{24,28},{28,20},{20,12},{12,4},{4,0},{1,9},{9... | collective-permute-start | bytes 1769480 | tf_op jit(solution)/shard_map/ppermute | solution.py:137
  58.6 5.3 %collective-permute-done.7 = bf16[2,3,16,1536]{3,2,1,0:T(8,128)(2,1)S(1)} collective-permute-done((bf16[2,3,16,1536]{3,2,1,0:T(8,128)(2,1)S(1)}, bf16[2,3,16,1536]{3,2,1,0:T(8,128)(2,1)S(1)}, u32[]{:S(2)}, u32[]{:S(2)}) %collective-permute-start.7) | collective-permute-done | bytes 294944 | tf_op jit(solution)/shard_map/ppermute | solution.py:193
  64.9 5.4 %collective-permute-done.10 = bf16[192,1536]{1,0:T(8,128)(2,1)S(1)} collective-permute-done((bf16[192,1536]{1,0:T(8,128)(2,1)S(1)}, bf16[192,1536]{1,0:T(8,128)(2,1)S(1)}, u32[]{:S(2)}, u32[]{:S(2)}) %collective-permute-start.10) | collective-permute-done | bytes 589856 | tf_op jit(solution)/shard_map/ppermute | solution.py:137
  70.4 2.4 %collective-permute-start.12 = (bf16[192,768]{1,0:T(8,128)(2,1)S(1)}, bf16[192,768]{1,0:T(8,128)(2,1)S(1)}, u32[]{:S(2)}, u32[]{:S(2)}) collective-permute-start(bf16[192,768]{1,0:T(8,128)(2,1)S(1)} %slice.756), channel_id=1, source_target_pairs={{0,8},{8,16},{16,24},{24,28},{28,20},{20,12},{12,4},{4,0},{1,9},{9... | collective-permute-start | bytes 884744 | tf_op jit(solution)/shard_map/ppermute | solution.py:117
  74.1 0.9 bitcast_dynamic-update-slice_fusion
  75.1 5.7 %collective-permute-done.12 = bf16[192,768]{1,0:T(8,128)(2,1)S(1)} collective-permute-done((bf16[192,768]{1,0:T(8,128)(2,1)S(1)}, bf16[192,768]{1,0:T(8,128)(2,1)S(1)}, u32[]{:S(2)}, u32[]{:S(2)}) %collective-permute-start.12) | collective-permute-done | bytes 294944 | tf_op jit(solution)/shard_map/ppermute | solution.py:117
  80.7 2.1 collective-permute-done.13
  82.8 0.9 fusion.19
  83.7 7.3 %fusion.4 = (f32[1536]{0:T(1024)S(1)}, f32[1536]{0:T(1024)S(1)}, f32[192,1536]{1,0:T(8,128)}, f32[192,1536]{1,0:T(8,128)}) fusion(bf16[1,12,16,1536]{3,2,1,0:T(8,128)(2,1)S(1)} %copy-done.2, f32[1536]{0:T(1024)S(1)} %copy-done.53, bf16[192,1536]{1,0:T(8,128)(2,1)S(1)} %bitcast.64, bf16[1536,1536]{1,0:T(8,128)(2,1)} %bitcast.25), kind=kOutput, calls=%fused_computation.64 | convolution fusion | flops 926610432 | bytes 8275968 | tf_op jit(solution)/shard_map/dot_general | solution.py:297
  91.7 6.6 %all-reduce.2 = (f32[]{:T(128)}, f32[]{:T(128)}) all-reduce(f32[]{:T(128)} %get-tuple-element.127, f32[]{:T(128)} %get-tuple-element.126), channel_id=1, replica_groups=mesh['fsdp'=8,'rows'=4] {'rows'}, use_global_device_ids=true, to_apply=%region_4.5 | all-reduce | flops 2 | bytes 16 | tf_op jit(solution)/shard_map/psum | solution.py:302
  99.7 3.4 %fusion.3 = (bf16[192,1536]{1,0:T(8,128)(2,1)S(1)}, bf16[192,1536]{1,0:T(8,128)(2,1)}) fusion(f32[192,1536]{1,0:T(8,128)} %get-tuple-element.151, f32[192,1536]{1,0:T(8,128)} %get-tuple-element.134, bf16[1,12,16,1536]{3,2,1,0:T(8,128)(2,1)} %param.21, f32[1536]{0:T(1024)S(1)} %get-tuple-element.143, f32[1536]{0:T(1024)S(1)} %get-tuple-element.132, ...), kind=kLoop, calls=%fused_computation.63 | loop fusion | flops 5603328 | bytes 4159488 | tf_op jit(solution)/shard_map/convert_element_type | solution.py:309
  103.1 3.5 %convolution_convert_fusion = bf16[1536,1536]{1,0:T(8,128)(2,1)} fusion(bf16[192,1536]{1,0:T(8,128)(2,1)S(1)} %bitcast.65, bf16[192,1536]{1,0:T(8,128)(2,1)S(1)} %get-tuple-element.137), kind=kOutput, calls=%fused_computation | convolution fusion | flops 908328960 | bytes 5898240 | tf_op jit(solution)/shard_map/dot_general | solution.py:310
  106.7 4.0 %convolution_convert_fusion.1 = bf16[12,16,1536]{2,1,0:T(8,128)(2,1)S(1)} fusion(bf16[12,16,1536]{2,1,0:T(8,128)(2,1)S(1)} %bitcast.66, bf16[1536,1536,1]{1,0,2:T(8,128)(2,1)} %bitcast.30), kind=kOutput, calls=%fused_computation.52 | convolution fusion | flops 906264576 | bytes 5898240 | tf_op jit(solution)/shard_map/hwf,cf->hwc/dot_general | solution.py:317
  111.5 0.9 collective-permute-done.14
  112.4 1.0 convert_add_fusion
  113.5 1.7 collective-permute-start.15
  115.2 7.4 %collective-permute-done.15 = f32[1,3,16,1536]{3,2,1,0:T(8,128)S(1)} collective-permute-done((f32[1,3,16,1536]{3,2,1,0:T(8,128)S(1)}, f32[1,3,16,1536]{3,2,1,0:T(8,128)S(1)}, u32[]{:S(2)}, u32[]{:S(2)}) %collective-permute-start.15) | collective-permute-done | bytes 294944 | tf_op jit(solution)/shard_map/ppermute | solution.py:69
  122.8 1.6 fusion.141
  128.2 1.4 collective-permute-done.18
  130.1 1.7 collective-permute-start.19
  131.8 2.7 %collective-permute-done.19 = f32[18816]{0:T(1024)S(1)} collective-permute-done((f32[18816]{0:T(1024)S(1)}, f32[18816]{0:T(1024)S(1)}, u32[]{:S(2)}, u32[]{:S(2)}) %collective-permute-start.19) | collective-permute-done | bytes 75296 | tf_op jit(solution)/shard_map/ppermute | solution.py:49
  135.5 4.6 %collective-permute-done.20 = f32[9408]{0:T(1024)S(1)} collective-permute-done((f32[9408]{0:T(1024)S(1)}, f32[9408]{0:T(1024)S(1)}, u32[]{:S(2)}, u32[]{:S(2)}) %collective-permute-start.20) | collective-permute-done | bytes 37664 | tf_op jit(solution)/shard_map/ppermute | solution.py:49
  140.3 1.4 collective-permute-start.21
  141.7 4.0 %collective-permute-done.21 = f32[4704]{0:T(1024)S(1)} collective-permute-done((f32[4704]{0:T(1024)S(1)}, f32[4704]{0:T(1024)S(1)}, u32[]{:S(2)}, u32[]{:S(2)}) %collective-permute-start.21) | collective-permute-done | bytes 18848 | tf_op jit(solution)/shard_map/ppermute | solution.py:49
  145.8 1.5 collective-permute-start.22
  147.3 4.6 %collective-permute-done.22 = f32[2352]{0:T(1024)S(1)} collective-permute-done((f32[2352]{0:T(1024)S(1)}, f32[2352]{0:T(1024)S(1)}, u32[]{:S(2)}, u32[]{:S(2)}) %collective-permute-start.22) | collective-permute-done | bytes 9440 | tf_op jit(solution)/shard_map/ppermute | solution.py:49
  152.3 4.2 %collective-permute-done.23 = f32[2352]{0:T(1024)S(1)} collective-permute-done((f32[2352]{0:T(1024)S(1)}, f32[2352]{0:T(1024)S(1)}, u32[]{:S(2)}, u32[]{:S(2)}) %collective-permute-start.23) | collective-permute-done | bytes 9440 | tf_op jit(solution)/shard_map/ppermute | solution.py:52
  156.6 1.2 collective-permute-start.24
  157.8 2.6 %collective-permute-done.24 = f32[4704]{0:T(1024)S(1)} collective-permute-done((f32[4704]{0:T(1024)S(1)}, f32[4704]{0:T(1024)S(1)}, u32[]{:S(2)}, u32[]{:S(2)}) %collective-permute-start.24) | collective-permute-done | bytes 18848 | tf_op jit(solution)/shard_map/ppermute | solution.py:52
  160.9 1.3 collective-permute-start.16
  162.2 1.3 collective-permute-start.17
  163.5 1.1 collective-permute-done.25
  164.7 3.5 %collective-permute-start.26 = (f32[18816]{0:T(1024)S(1)}, f32[18816]{0:T(1024)S(1)}, u32[]{:S(2)}, u32[]{:S(2)}) collective-permute-start(f32[18816]{0:T(1024)S(1)} %maximum_select_fusion.4), channel_id=1, source_target_pairs={{0,2},{1,3},{2,0},{3,1},{4,6},{5,7},{6,4},{7,5},{8,10},{9,11},{10,... | collective-permute-start | bytes 225800 | tf_op jit(solution)/shard_map/ppermute | solution.py:52
  168.4 4.0 %collective-permute-done.26 = f32[18816]{0:T(1024)S(1)} collective-permute-done((f32[18816]{0:T(1024)S(1)}, f32[18816]{0:T(1024)S(1)}, u32[]{:S(2)}, u32[]{:S(2)}) %collective-permute-start.26) | collective-permute-done | bytes 75296 | tf_op jit(solution)/shard_map/ppermute | solution.py:52
  172.7 2.8 %fusion.147 = bf16[1,3,16,1536]{3,2,1,0:T(8,128)(2,1)} fusion(f32[1536]{0:T(1024)S(1)} %copy-done.43, bf16[9,22,1536]{2,1,0:T(8,128)(2,1)S(1)} %select_maximum_fusion, f32[1536]{0:T(1024)S(1)} %copy-done.45, f32[1536]{0:T(1024)S(1)} %get-tuple-element.59, f32[1536]{0:T(1024)S(1)} %get-tuple-element.60, bf16[3,16,1536]{2,1,0:T(8,128)(2,1)S(1)} %collective-permute-done.16, ...), kind=kLoop, calls=%fused_computation.300 | loop fusion | flops 11132928 | bytes 7084032 | tf_op jit(solution)/shard_map/reshape | solution.py:332
  176.3 27.4 %reduce-scatter.2.cloned.1.call-done = bf16[192,1536]{1,0:T(8,128)(2,1)} async-done(((bf16[1536,1536]{1,0:T(8,128)(2,1)}), bf16[192,1536]{1,0:T(8,128)(2,1)}) %reduce-scatter.2.cloned.1.call-update) | async-done | bytes 589840 | tf_op jit(solution)/shard_map/reduce_scatter | solution.py:313
  203.7 2.2 %convert_element_type.497 = f32[192,1536]{1,0:T(8,128)} convert(bf16[192,1536]{1,0:T(8,128)(2,1)} %reduce-scatter.2.cloned.1.call-done) | non-fusion elementwise | flops 294912 | bytes 1769472 | tf_op jit(solution)/shard_map/convert_element_type | solution.py:315
  (241 shorter events, 18.9 us)
Async XLA Ops:
  7.2 196.5 %reduce-scatter.2.cloned.1.call-start = ((), (), s32[]{:S(2)}) async-start(), calls=%async_computation.1 | async-start | bytes 5308416 | tf_op jit(solution)/shard_map/reduce_scatter | solution.py:313
  8.4 29.4 %collective-permute-start.2 = (bf16[192,768]{1,0:T(8,128)(2,1)S(1)}, bf16[192,768]{1,0:T(8,128)(2,1)S(1)}, u32[]{:S(2)}, u32[]{:S(2)}) collective-permute-start(bf16[192,768]{1,0:T(8,128)(2,1)S(1)} %get-tuple-element.139), channel_id=1, source_target_pairs={{0,4},{8,0},{16,8},{24,16},{28,24},{20,28},{12,20},{4,12},{1,5},{9... | collective-permute-start | bytes 884744 | tf_op jit(solution)/shard_map/ppermute | solution.py:133
  11.4 26.4 %collective-permute-start = (bf16[192,768]{1,0:T(8,128)(2,1)S(1)}, bf16[192,768]{1,0:T(8,128)(2,1)S(1)}, u32[]{:S(2)}, u32[]{:S(2)}) collective-permute-start(bf16[192,768]{1,0:T(8,128)(2,1)S(1)} %get-tuple-element.139), channel_id=1, source_target_pairs={{0,8},{8,16},{16,24},{24,28},{28,20},{20,12},{12,4},{4,0},{1,9},{9... | collective-permute-start | bytes 884744 | tf_op jit(solution)/shard_map/ppermute | solution.py:129
  11.5 26.2 %collective-permute-start.3 = (bf16[192,768]{1,0:T(8,128)(2,1)S(1)}, bf16[192,768]{1,0:T(8,128)(2,1)S(1)}, u32[]{:S(2)}, u32[]{:S(2)}) collective-permute-start(bf16[192,768]{1,0:T(8,128)(2,1)S(1)} %get-tuple-element.140), channel_id=1, source_target_pairs={{0,4},{8,0},{16,8},{24,16},{28,24},{20,28},{12,20},{4,12},{1,5},{9... | collective-permute-start | bytes 884744 | tf_op jit(solution)/shard_map/ppermute | solution.py:133
  13.4 24.4 %collective-permute-start.1 = (bf16[192,768]{1,0:T(8,128)(2,1)S(1)}, bf16[192,768]{1,0:T(8,128)(2,1)S(1)}, u32[]{:S(2)}, u32[]{:S(2)}) collective-permute-start(bf16[192,768]{1,0:T(8,128)(2,1)S(1)} %get-tuple-element.140), channel_id=1, source_target_pairs={{0,8},{8,16},{16,24},{24,28},{28,20},{20,12},{12,4},{4,0},{1,9},{9... | collective-permute-start | bytes 884744 | tf_op jit(solution)/shard_map/ppermute | solution.py:129
  38.6 5.5 %collective-permute-start.4 = (bf16[3,16,1536]{2,1,0:T(8,128)(2,1)S(1)}, bf16[3,16,1536]{2,1,0:T(8,128)(2,1)S(1)}, u32[]{:S(2)}, u32[]{:S(2)}) collective-permute-start(bf16[3,16,1536]{2,1,0:T(8,128)(2,1)S(1)} %bitcast.67), channel_id=1, source_target_pairs={{0,1},{1,2},{2,3},{4,5},{5,6},{6,7},{8,9},{9,10},{10,11},{12,13},{... | collective-permute-start | bytes 442376 | tf_op jit(solution)/shard_map/ppermute | solution.py:16
  39.9 5.4 %collective-permute-start.5 = (bf16[3,16,1536]{2,1,0:T(8,128)(2,1)S(1)}, bf16[3,16,1536]{2,1,0:T(8,128)(2,1)S(1)}, u32[]{:S(2)}, u32[]{:S(2)}) collective-permute-start(bf16[3,16,1536]{2,1,0:T(8,128)(2,1)S(1)} %bitcast.68), channel_id=1, source_target_pairs={{1,0},{2,1},{3,2},{5,4},{6,5},{7,6},{9,8},{10,9},{11,10},{13,12},{... | collective-permute-start | bytes 442376 | tf_op jit(solution)/shard_map/ppermute | solution.py:19
  41.2 13.9 %collective-permute-start.8 = (bf16[192,1536]{1,0:T(8,128)(2,1)S(1)}, bf16[192,1536]{1,0:T(8,128)(2,1)S(1)}, u32[]{:S(2)}, u32[]{:S(2)}) collective-permute-start(bf16[192,1536]{1,0:T(8,128)(2,1)S(1)} %pad_maximum_fusion), channel_id=1, source_target_pairs={{0,8},{8,16},{16,24},{24,28},{28,20},{20,12},{12,4},{4,0},{1,9},{9... | collective-permute-start | bytes 1769480 | tf_op jit(solution)/shard_map/ppermute | solution.py:137
  43.2 14.5 %collective-permute-start.9 = (bf16[192,1536]{1,0:T(8,128)(2,1)S(1)}, bf16[192,1536]{1,0:T(8,128)(2,1)S(1)}, u32[]{:S(2)}, u32[]{:S(2)}) collective-permute-start(bf16[192,1536]{1,0:T(8,128)(2,1)S(1)} %pad_maximum_fusion.1), channel_id=1, source_target_pairs={{0,4},{8,0},{16,8},{24,16},{28,24},{20,28},{12,20},{4,12},{1,5},{9... | collective-permute-start | bytes 1769480 | tf_op jit(solution)/shard_map/ppermute | solution.py:139
  49.2 73.4 %copy-start.46 = (f32[3,16]{1,0:T(4,128)}, f32[3,16]{1,0:T(4,128)S(1)}, u32[]{:S(2)}) copy-start(f32[3,16]{1,0:T(4,128)S(1)} %broadcast_multiply_fusion.2) | copy-start | bytes 580
  49.4 73.2 %copy-start.47 = (f32[3,16]{1,0:T(4,128)}, f32[3,16]{1,0:T(4,128)S(1)}, u32[]{:S(2)}) copy-start(f32[3,16]{1,0:T(4,128)S(1)} %add_rsqrt_fusion) | copy-start | bytes 580
  49.5 5.1 %collective-permute-start.6 = (bf16[1,3,16,1536]{3,2,1,0:T(8,128)(2,1)S(1)}, bf16[1,3,16,1536]{3,2,1,0:T(8,128)(2,1)S(1)}, u32[]{:S(2)}, u32[]{:S(2)}) collective-permute-start(bf16[1,3,16,1536]{3,2,1,0:T(8,128)(2,1)S(1)} %fusion.144), channel_id=1, source_target_pairs={{0,1},{1,0},{2,3},{3,2},{4,5},{5,4},{6,7},{7,6},{8,9},{9,8},{10,11... | collective-permute-start | bytes 442376 | tf_op jit(solution)/shard_map/ppermute | solution.py:193
  54.6 9.3 %collective-permute-start.7 = (bf16[2,3,16,1536]{3,2,1,0:T(8,128)(2,1)S(1)}, bf16[2,3,16,1536]{3,2,1,0:T(8,128)(2,1)S(1)}, u32[]{:S(2)}, u32[]{:S(2)}) collective-permute-start(bf16[2,3,16,1536]{3,2,1,0:T(8,128)(2,1)S(1)} %maximum_select_fusion.2), channel_id=1, source_target_pairs={{0,2},{1,3},{2,0},{3,1},{4,6},{5,7},{6,4},{7,5},{8,10},{9,11},{10,... | collective-permute-start | bytes 884744 | tf_op jit(solution)/shard_map/ppermute | solution.py:193
  55.1 15.2 %collective-permute-start.10 = (bf16[192,1536]{1,0:T(8,128)(2,1)S(1)}, bf16[192,1536]{1,0:T(8,128)(2,1)S(1)}, u32[]{:S(2)}, u32[]{:S(2)}) collective-permute-start(bf16[192,1536]{1,0:T(8,128)(2,1)S(1)} %collective-permute-done.8), channel_id=1, source_target_pairs={{0,8},{8,16},{16,24},{24,28},{28,20},{20,12},{12,4},{4,0},{1,9},{9... | collective-permute-start | bytes 1769480 | tf_op jit(solution)/shard_map/ppermute | solution.py:137
  57.8 15.4 %collective-permute-start.11 = (bf16[192,1536]{1,0:T(8,128)(2,1)S(1)}, bf16[192,1536]{1,0:T(8,128)(2,1)S(1)}, u32[]{:S(2)}, u32[]{:S(2)}) collective-permute-start(bf16[192,1536]{1,0:T(8,128)(2,1)S(1)} %collective-permute-done.9), channel_id=1, source_target_pairs={{0,4},{8,0},{16,8},{24,16},{28,24},{20,28},{12,20},{4,12},{1,5},{9... | collective-permute-start | bytes 1769480 | tf_op jit(solution)/shard_map/ppermute | solution.py:139
  70.4 10.3 %collective-permute-start.12 = (bf16[192,768]{1,0:T(8,128)(2,1)S(1)}, bf16[192,768]{1,0:T(8,128)(2,1)S(1)}, u32[]{:S(2)}, u32[]{:S(2)}) collective-permute-start(bf16[192,768]{1,0:T(8,128)(2,1)S(1)} %slice.756), channel_id=1, source_target_pairs={{0,8},{8,16},{16,24},{24,28},{28,20},{20,12},{12,4},{4,0},{1,9},{9... | collective-permute-start | bytes 884744 | tf_op jit(solution)/shard_map/ppermute | solution.py:117
  73.2 9.6 %collective-permute-start.13 = (bf16[192,768]{1,0:T(8,128)(2,1)S(1)}, bf16[192,768]{1,0:T(8,128)(2,1)S(1)}, u32[]{:S(2)}, u32[]{:S(2)}) collective-permute-start(bf16[192,768]{1,0:T(8,128)(2,1)S(1)} %slice.757), channel_id=1, source_target_pairs={{0,4},{8,0},{16,8},{24,16},{28,24},{20,28},{12,20},{4,12},{1,5},{9... | collective-permute-start | bytes 884744 | tf_op jit(solution)/shard_map/ppermute | solution.py:118
  110.8 1.6 collective-permute-start.14
  113.5 9.1 %collective-permute-start.15 = (f32[1,3,16,1536]{3,2,1,0:T(8,128)S(1)}, f32[1,3,16,1536]{3,2,1,0:T(8,128)S(1)}, u32[]{:S(2)}, u32[]{:S(2)}) collective-permute-start(f32[1,3,16,1536]{3,2,1,0:T(8,128)S(1)} %constant_dynamic-slice_fusion), channel_id=1, source_target_pairs={{0,2},{1,3},{2,0},{3,1},{4,6},{5,7},{6,4},{7,5},{8,10},{9,11},{10,... | collective-permute-start | bytes 884744 | tf_op jit(solution)/shard_map/ppermute | solution.py:69
  128.1 1.4 collective-permute-start.18
  130.1 4.5 %collective-permute-start.19 = (f32[18816]{0:T(1024)S(1)}, f32[18816]{0:T(1024)S(1)}, u32[]{:S(2)}, u32[]{:S(2)}) collective-permute-start(f32[18816]{0:T(1024)S(1)} %get-tuple-element.111), channel_id=1, source_target_pairs={{0,2},{1,3},{2,0},{3,1},{4,6},{5,7},{6,4},{7,5},{8,10},{9,11},{10,... | collective-permute-start | bytes 225800 | tf_op jit(solution)/shard_map/ppermute | solution.py:49
  135.0 37.5 %copy-start.7 = (f32[1536]{0:T(1024)S(1)}, f32[1536]{0:T(1024)}, u32[]{:S(2)}) copy-start(f32[1536]{0:T(1024)} %copy-done.6) | copy-start | bytes 18436
  135.0 37.5 %copy-start.9 = (f32[1536]{0:T(1024)S(1)}, f32[1536]{0:T(1024)}, u32[]{:S(2)}) copy-start(f32[1536]{0:T(1024)} %copy-done.8) | copy-start | bytes 18436
  135.0 37.5 %copy-start.11 = (f32[1536]{0:T(1024)S(1)}, f32[1536]{0:T(1024)}, u32[]{:S(2)}) copy-start(f32[1536]{0:T(1024)} %copy-done.10) | copy-start | bytes 18436
  135.0 37.5 %copy-start.13 = (f32[1536]{0:T(1024)S(1)}, f32[1536]{0:T(1024)}, u32[]{:S(2)}) copy-start(f32[1536]{0:T(1024)} %copy-done.12) | copy-start | bytes 18436
  135.0 37.5 %copy-start.15 = (f32[1536]{0:T(1024)S(1)}, f32[1536]{0:T(1024)}, u32[]{:S(2)}) copy-start(f32[1536]{0:T(1024)} %copy-done.14) | copy-start | bytes 18436
  135.0 37.5 %copy-start.17 = (f32[1536]{0:T(1024)S(1)}, f32[1536]{0:T(1024)}, u32[]{:S(2)}) copy-start(f32[1536]{0:T(1024)} %copy-done.16) | copy-start | bytes 18436
  135.0 37.5 %copy-start.19 = (f32[1536]{0:T(1024)S(1)}, f32[1536]{0:T(1024)}, u32[]{:S(2)}) copy-start(f32[1536]{0:T(1024)} %copy-done.18) | copy-start | bytes 18436
  135.0 37.5 %copy-start.21 = (f32[1536]{0:T(1024)S(1)}, f32[1536]{0:T(1024)}, u32[]{:S(2)}) copy-start(f32[1536]{0:T(1024)} %copy-done.20) | copy-start | bytes 18436
  135.0 37.5 %copy-start.23 = (f32[1536]{0:T(1024)S(1)}, f32[1536]{0:T(1024)}, u32[]{:S(2)}) copy-start(f32[1536]{0:T(1024)} %copy-done.22) | copy-start | bytes 18436
  135.0 37.5 %copy-start.25 = (f32[1536]{0:T(1024)S(1)}, f32[1536]{0:T(1024)}, u32[]{:S(2)}) copy-start(f32[1536]{0:T(1024)} %copy-done.24) | copy-start | bytes 18436
  135.1 37.5 %copy-start.27 = (f32[1536]{0:T(1024)S(1)}, f32[1536]{0:T(1024)}, u32[]{:S(2)}) copy-start(f32[1536]{0:T(1024)} %copy-done.26) | copy-start | bytes 18436
  135.1 37.5 %copy-start.29 = (f32[1536]{0:T(1024)S(1)}, f32[1536]{0:T(1024)}, u32[]{:S(2)}) copy-start(f32[1536]{0:T(1024)} %copy-done.28) | copy-start | bytes 18436
  135.1 37.5 %copy-start.31 = (f32[1536]{0:T(1024)S(1)}, f32[1536]{0:T(1024)}, u32[]{:S(2)}) copy-start(f32[1536]{0:T(1024)} %copy-done.30) | copy-start | bytes 18436
  135.1 37.5 %copy-start.33 = (f32[1536]{0:T(1024)S(1)}, f32[1536]{0:T(1024)}, u32[]{:S(2)}) copy-start(f32[1536]{0:T(1024)} %copy-done.32) | copy-start | bytes 18436
  135.1 37.5 %copy-start.35 = (f32[1536]{0:T(1024)S(1)}, f32[1536]{0:T(1024)}, u32[]{:S(2)}) copy-start(f32[1536]{0:T(1024)} %copy-done.34) | copy-start | bytes 18436
  135.1 37.5 %copy-start.37 = (f32[1536]{0:T(1024)S(1)}, f32[1536]{0:T(1024)}, u32[]{:S(2)}) copy-start(f32[1536]{0:T(1024)} %copy-done.36) | copy-start | bytes 18436
  135.1 37.5 %copy-start.39 = (f32[1536]{0:T(1024)S(1)}, f32[1536]{0:T(1024)}, u32[]{:S(2)}) copy-start(f32[1536]{0:T(1024)} %copy-done.38) | copy-start | bytes 18436
  135.2 4.9 %collective-permute-start.20 = (f32[9408]{0:T(1024)S(1)}, f32[9408]{0:T(1024)S(1)}, u32[]{:S(2)}, u32[]{:S(2)}) collective-permute-start(f32[9408]{0:T(1024)S(1)} %get-tuple-element.120), channel_id=1, source_target_pairs={{0,4},{4,0},{8,12},{12,8},{16,20},{20,16},{24,28},{28,24},{1,5},{5... | collective-permute-start | bytes 112904 | tf_op jit(solution)/shard_map/ppermute | solution.py:49
  140.3 5.3 %collective-permute-start.21 = (f32[4704]{0:T(1024)S(1)}, f32[4704]{0:T(1024)S(1)}, u32[]{:S(2)}, u32[]{:S(2)}) collective-permute-start(f32[4704]{0:T(1024)S(1)} %get-tuple-element.122), channel_id=1, source_target_pairs={{0,8},{4,12},{8,0},{12,4},{16,24},{20,28},{24,16},{28,20},{1,9},{5... | collective-permute-start | bytes 56456 | tf_op jit(solution)/shard_map/ppermute | solution.py:49
  145.8 6.1 %collective-permute-start.22 = (f32[2352]{0:T(1024)S(1)}, f32[2352]{0:T(1024)S(1)}, u32[]{:S(2)}, u32[]{:S(2)}) collective-permute-start(f32[2352]{0:T(1024)S(1)} %get-tuple-element.124), channel_id=1, source_target_pairs={{0,16},{4,20},{8,24},{12,28},{16,0},{20,4},{24,8},{28,12},{1,17},{... | collective-permute-start | bytes 28232 | tf_op jit(solution)/shard_map/ppermute | solution.py:49
  151.9 4.6 %collective-permute-start.23 = (f32[2352]{0:T(1024)S(1)}, f32[2352]{0:T(1024)S(1)}, u32[]{:S(2)}, u32[]{:S(2)}) collective-permute-start(f32[2352]{0:T(1024)S(1)} %add.722), channel_id=1, source_target_pairs={{0,16},{4,20},{8,24},{12,28},{16,0},{20,4},{24,8},{28,12},{1,17},{... | collective-permute-start | bytes 28232 | tf_op jit(solution)/shard_map/ppermute | solution.py:52
  156.6 3.8 %collective-permute-start.24 = (f32[4704]{0:T(1024)S(1)}, f32[4704]{0:T(1024)S(1)}, u32[]{:S(2)}, u32[]{:S(2)}) collective-permute-start(f32[4704]{0:T(1024)S(1)} %maximum_select_fusion.6), channel_id=1, source_target_pairs={{0,8},{4,12},{8,0},{12,4},{16,24},{20,28},{24,16},{28,20},{1,9},{5... | collective-permute-start | bytes 56456 | tf_op jit(solution)/shard_map/ppermute | solution.py:52
  160.5 4.1 %collective-permute-start.25 = (f32[9408]{0:T(1024)S(1)}, f32[9408]{0:T(1024)S(1)}, u32[]{:S(2)}, u32[]{:S(2)}) collective-permute-start(f32[9408]{0:T(1024)S(1)} %maximum_select_fusion.5), channel_id=1, source_target_pairs={{0,4},{4,0},{8,12},{12,8},{16,20},{20,16},{24,28},{28,24},{1,5},{5... | collective-permute-start | bytes 112904 | tf_op jit(solution)/shard_map/ppermute | solution.py:52
  160.9 7.2 %collective-permute-start.16 = (bf16[3,16,1536]{2,1,0:T(8,128)(2,1)S(1)}, bf16[3,16,1536]{2,1,0:T(8,128)(2,1)S(1)}, u32[]{:S(2)}, u32[]{:S(2)}) collective-permute-start(bf16[3,16,1536]{2,1,0:T(8,128)(2,1)S(1)} %get-tuple-element.130), channel_id=1, source_target_pairs={{0,1},{1,2},{2,3},{4,5},{5,6},{6,7},{8,9},{9,10},{10,11},{12,13},{... | collective-permute-start | bytes 442376 | tf_op jit(solution)/shard_map/ppermute | solution.py:16
  162.2 6.0 %collective-permute-start.17 = (bf16[3,16,1536]{2,1,0:T(8,128)(2,1)S(1)}, bf16[3,16,1536]{2,1,0:T(8,128)(2,1)S(1)}, u32[]{:S(2)}, u32[]{:S(2)}) collective-permute-start(bf16[3,16,1536]{2,1,0:T(8,128)(2,1)S(1)} %get-tuple-element.130), channel_id=1, source_target_pairs={{1,0},{2,1},{3,2},{5,4},{6,5},{7,6},{9,8},{10,9},{11,10},{13,12},{... | collective-permute-start | bytes 442376 | tf_op jit(solution)/shard_map/ppermute | solution.py:19
  164.7 7.7 %collective-permute-start.26 = (f32[18816]{0:T(1024)S(1)}, f32[18816]{0:T(1024)S(1)}, u32[]{:S(2)}, u32[]{:S(2)}) collective-permute-start(f32[18816]{0:T(1024)S(1)} %maximum_select_fusion.4), channel_id=1, source_target_pairs={{0,2},{1,3},{2,0},{3,1},{4,6},{5,7},{6,4},{7,5},{8,10},{9,11},{10,... | collective-permute-start | bytes 225800 | tf_op jit(solution)/shard_map/ppermute | solution.py:52
  172.4 3.1 %collective-permute-start.27 = (f32[37632]{0:T(1024)S(1)}, f32[37632]{0:T(1024)S(1)}, u32[]{:S(2)}, u32[]{:S(2)}) collective-permute-start(f32[37632]{0:T(1024)S(1)} %maximum_select_fusion.3), channel_id=1, source_target_pairs={{0,1},{1,0},{2,3},{3,2},{4,5},{5,4},{6,7},{7,6},{8,9},{9,8},{10,11... | collective-permute-start | bytes 451592 | tf_op jit(solution)/shard_map/ppermute | solution.py:52
  (36 other events, 732.0 us)
Sparse Core Ops, SparseCore 0:
  106.8 96.8 reduce-scatter.1

commit v16 on v14

--- a/solution.py
+++ b/solution.py
@@ -185,6 +185,16 @@
     return data.reshape((size * block.shape[0],) + block.shape[1:])
 
 
+def doubling_sum(value, axis):
+    size = lax.axis_size(axis)
+    assert size & (size - 1) == 0
+    mask = 1
+    while mask < size:
+        value = value + lax.ppermute(value, axis, [(j, j ^ mask) for j in range(size)])
+        mask *= 2
+    return value
+
+
 def conv_rows(framed, kern, kbias):
     rows = framed.shape[0] - 6
     cols = framed.shape[1]
@@ -288,11 +298,12 @@
     norms = jnp.sqrt(jnp.sum(post * post, axis=0) + 1e-06)
     cot_f = grad_out[0].reshape(flat.shape[0], -1).astype(jnp.float32)
     dnorm = grn_gamma * jnp.sum(cot_f * post, axis=0)
-    norm_total = lax.psum(jnp.sum(norms), "rows")
+    totals = doubling_sum(jnp.stack([jnp.sum(norms), jnp.sum(dnorm * norms)]), "rows")
+    norm_total = totals[0]
     denom = norm_total / FF + 1e-06
     ratio = norms / denom
     output = (grn_gamma * (post * ratio) + grn_beta + post).astype(jnp.bfloat16)
-    cross = lax.psum(jnp.sum(dnorm * norms), "rows")
+    cross = totals[1]
     dnorms = dnorm / denom - cross / (denom * denom) / FF
     dpost = cot_f * (1.0 + grn_gamma * ratio) + post * (dnorms / norms)
     dpre = (dpost * gelu_grad(pre)).astype(jnp.bfloat16)

time: 206 us -> 207 us (level)
  waiting for transfers between devices: 90.4 us -> 99.7 us
  blocking collectives: 6.61 us -> 0 us
  starting transfers between devices: 31.8 us -> 25.9 us
  other arithmetic: 19.3 us -> 23.4 us
    psum x1 -> x0, blocking collectives: 6.61 us -> none  [body(): norm_total = lax.psum(jnp.sum(norms), 'rows')]
    ppermute x0 -> x2, waiting for transfers between devices: none -> 4.63 us  [doubling_sum(): lax.ppermute(value, axis, [(j, j ^ mask) for j in range(size)])]
    add x0 -> x2, other arithmetic: none -> 2.7 us  [doubling_sum(): value + lax.ppermute(value, axis, [(j, j ^ mask) for j in range(size)])]
    ppermute x5, starting transfers between devices: 5.46 us -> 3.08 us  [tree_allreduce(): other = lax.ppermute(flat, axis, perm)]
  transfers between devices with their start and end apart: 27 -> 29, of which waited for: 21 -> 23; matrix products, arithmetic and copies ran while one was open for 11% -> 11% of each run, Pallas kernels for 0% -> 0%
where the time goes in v16:
time: 207 us
  waiting for transfers between devices  99.7 us (48%)
  between operations  34.9 us (17%)
  starting transfers between devices  25.9 us (13%)
  other arithmetic  23.4 us (11%)
  matrix products  12.6 us (6%)
  local copies, waits for them, and re-layouts  10.3 us (5%)
    reduce_scatter x1, waiting for transfers between devices, body(): lax.psum_scatter(w_term.astype(jnp.bfloat16), 'fsdp', scatter_dimension=0...  27.4 us
    ppermute x5, waiting for transfers between devices, tree_allreduce(): flat = keep + lax.ppermute(give, axis, perm)  18.8 us
    ppermute x5, waiting for transfers between devices, tree_allreduce(): other = lax.ppermute(flat, axis, perm)  13.3 us
    ppermute x2, waiting for transfers between devices, tree_reduce_scatter(): lax.ppermute(give, axis, perm).astype(jnp.float32)  9.86 us
    ppermute x1, waiting for transfers between devices, ring_all_gather(): lax.ppermute(cw[..., :half], axis, forward)  7.31 us
    ppermute x2, waiting for transfers between devices, tree_all_gather(): other = lax.ppermute(data, axis, perm)  7.11 us
    ppermute x3, starting transfers between devices, ring_all_gather(): cw = lax.ppermute(cw, axis, forward)  7.1 us
    ppermute x3, waiting for transfers between devices, ring_all_gather(): cw = lax.ppermute(cw, axis, forward)  6.79 us
  transfers between devices with their start and end apart: 29, of which 23 were waited for; matrix products, arithmetic and copies ran while one was open for 11% of the time, Pallas kernels for 0%

profile of v16, /device:TPU:0, one launch (start us, length us, event | category | flops | bytes accessed | tf_op | source)
XLA Modules:
  0.0 206.7 jit_solution(6219177651608787445)
XLA Ops:
  7.2 1.1 compare_select_fusion
  8.4 3.1 %collective-permute-start = (bf16[192,1536]{1,0:T(8,128)(2,1)S(1)}, bf16[192,1536]{1,0:T(8,128)(2,1)S(1)}, u32[]{:S(2)}, u32[]{:S(2)}) collective-permute-start(bf16[192,1536]{1,0:T(8,128)(2,1)S(1)} %compare_select_fusion), channel_id=1, source_target_pairs={{0,8},{8,16},{16,24},{24,28},{28,20},{20,12},{12,4},{4,0},{1,9},{9... | collective-permute-start | bytes 1769480 | tf_op jit(solution)/shard_map/ppermute | solution.py:126
  26.6 0.9 slice_reduce_fusion.47
  34.2 1.5 collective-permute-start.2
  35.7 1.3 collective-permute-start.3
  37.0 1.9 collective-permute-start.6
  39.3 1.7 collective-permute-done.3
  41.4 3.4 %fusion.153 = (f32[3,16]{1,0:T(4,128)S(1)}, f32[3,16,1536]{2,1,0:T(8,128)S(1)}) fusion(f32[1536]{0:T(1024)S(1)} %get-tuple-element.105, bf16[9,22,1536]{2,1,0:T(8,128)(2,1)S(1)} %select_maximum_fusion.2, f32[1536]{0:T(1024)S(1)} %get-tuple-element.106, f32[1536]{0:T(1024)S(1)} %get-tuple-element.59, f32[1536]{0:T(1024)S(1)} %get-tuple-element.60, ...), kind=kLoop, calls=%fused_computation.376 | loop fusion | flops 10911696 | bytes 7827648 | tf_op jit(solution)/shard_map/reduce_sum | solution.py:238
  45.2 4.1 %collective-permute-start.4 = (bf16[1,3,16,1536]{3,2,1,0:T(8,128)(2,1)S(1)}, bf16[1,3,16,1536]{3,2,1,0:T(8,128)(2,1)S(1)}, u32[]{:S(2)}, u32[]{:S(2)}) collective-permute-start(bf16[1,3,16,1536]{3,2,1,0:T(8,128)(2,1)S(1)} %fusion.144), channel_id=1, source_target_pairs={{0,1},{1,0},{2,3},{3,2},{4,5},{5,4},{6,7},{7,6},{8,9},{9,8},{10,11... | collective-permute-start | bytes 442376 | tf_op jit(solution)/shard_map/ppermute | solution.py:182
  49.3 1.0 collective-permute-done.4
  51.0 2.1 %collective-permute-start.8 = (bf16[192,1536]{1,0:T(8,128)(2,1)S(1)}, bf16[192,1536]{1,0:T(8,128)(2,1)S(1)}, u32[]{:S(2)}, u32[]{:S(2)}) collective-permute-start(bf16[192,1536]{1,0:T(8,128)(2,1)S(1)} %collective-permute-done.6), channel_id=1, source_target_pairs={{0,8},{8,16},{16,24},{24,28},{28,20},{20,12},{12,4},{4,0},{1,9},{9... | collective-permute-start | bytes 1769480 | tf_op jit(solution)/shard_map/ppermute | solution.py:126
  53.5 6.2 %collective-permute-done.5 = bf16[2,3,16,1536]{3,2,1,0:T(8,128)(2,1)S(1)} collective-permute-done((bf16[2,3,16,1536]{3,2,1,0:T(8,128)(2,1)S(1)}, bf16[2,3,16,1536]{3,2,1,0:T(8,128)(2,1)S(1)}, u32[]{:S(2)}, u32[]{:S(2)}) %collective-permute-start.5) | collective-permute-done | bytes 294944 | tf_op jit(solution)/shard_map/ppermute | solution.py:182
  59.8 6.1 %collective-permute-done.8 = bf16[192,1536]{1,0:T(8,128)(2,1)S(1)} collective-permute-done((bf16[192,1536]{1,0:T(8,128)(2,1)S(1)}, bf16[192,1536]{1,0:T(8,128)(2,1)S(1)}, u32[]{:S(2)}, u32[]{:S(2)}) %collective-permute-start.8) | collective-permute-done | bytes 589856 | tf_op jit(solution)/shard_map/ppermute | solution.py:126
  65.9 2.5 %collective-permute-start.10 = (bf16[192,768]{1,0:T(8,128)(2,1)S(1)}, bf16[192,768]{1,0:T(8,128)(2,1)S(1)}, u32[]{:S(2)}, u32[]{:S(2)}) collective-permute-start(bf16[192,768]{1,0:T(8,128)(2,1)S(1)} %slice.752), channel_id=1, source_target_pairs={{0,8},{8,16},{16,24},{24,28},{28,20},{20,12},{12,4},{4,0},{1,9},{9... | collective-permute-start | bytes 884744 | tf_op jit(solution)/shard_map/ppermute | solution.py:117
  69.1 7.3 %collective-permute-done.10 = bf16[192,768]{1,0:T(8,128)(2,1)S(1)} collective-permute-done((bf16[192,768]{1,0:T(8,128)(2,1)S(1)}, bf16[192,768]{1,0:T(8,128)(2,1)S(1)}, u32[]{:S(2)}, u32[]{:S(2)}) %collective-permute-start.10) | collective-permute-done | bytes 294944 | tf_op jit(solution)/shard_map/ppermute | solution.py:117
  76.4 2.1 collective-permute-done.11
  78.5 5.0 %fusion.1 = (f32[1536]{0:T(1024)S(1)}, f32[1536]{0:T(1024)S(1)}, f32[192,1536]{1,0:T(8,128)}, f32[192,1536]{1,0:T(8,128)}) fusion(bf16[1,12,16,1536]{3,2,1,0:T(8,128)(2,1)S(1)} %copy-done.3, f32[1536]{0:T(1024)S(1)} %copy-done.54, bf16[192,1536]{1,0:T(8,128)(2,1)S(1)} %bitcast.70, bf16[1536,1536]{1,0:T(8,128)(2,1)S(1)} %bitcast.68), kind=kOutput, calls=%fused_computation.61 | convolution fusion | flops 926610432 | bytes 8275968 | tf_op jit(solution)/shard_map/dot_general | solution.py:296
  84.2 1.3 pad_maximum_fusion.2
  85.6 1.1 collective-permute-done.12
  86.7 1.3 fusion.163
  88.1 3.5 %collective-permute-done.13 = f32[2]{0:T(128)S(1)} collective-permute-done((f32[2]{0:T(128)S(1)}, f32[2]{0:T(128)S(1)}, u32[]{:S(2)}, u32[]{:S(2)}) %collective-permute-start.13) | collective-permute-done | bytes 40 | tf_op jit(solution)/shard_map/ppermute | solution.py:193
  91.6 1.3 fusion.164
  94.9 3.4 %fusion.4 = (bf16[192,1536]{1,0:T(8,128)(2,1)S(1)}, bf16[192,1536]{1,0:T(8,128)(2,1)}) fusion(f32[192,1536]{1,0:T(8,128)} %get-tuple-element.150, f32[192,1536]{1,0:T(8,128)} %get-tuple-element.133, bf16[1,12,16,1536]{3,2,1,0:T(8,128)(2,1)} %param.21, f32[1536]{0:T(1024)S(1)} %get-tuple-element.140, f32[1536]{0:T(1024)S(1)} %get-tuple-element.130, ...), kind=kLoop, calls=%fused_computation.64 | loop fusion | flops 5603328 | bytes 4159488 | tf_op jit(solution)/shard_map/convert_element_type | solution.py:309
  98.2 3.6 %convolution_convert_fusion = bf16[1536,1536]{1,0:T(8,128)(2,1)} fusion(bf16[192,1536]{1,0:T(8,128)(2,1)S(1)} %bitcast.71, bf16[192,1536]{1,0:T(8,128)(2,1)S(1)} %get-tuple-element.136), kind=kOutput, calls=%fused_computation | convolution fusion | flops 908328960 | bytes 5898240 | tf_op jit(solution)/shard_map/dot_general | solution.py:310
  101.8 4.0 %convolution_convert_fusion.1 = bf16[12,16,1536]{2,1,0:T(8,128)(2,1)S(1)} fusion(bf16[12,16,1536]{2,1,0:T(8,128)(2,1)S(1)} %bitcast.72, bf16[1536,1536,1]{1,0,2:T(8,128)(2,1)} %bitcast.69), kind=kOutput, calls=%fused_computation.52 | convolution fusion | flops 906264576 | bytes 5898240 | tf_op jit(solution)/shard_map/hwf,cf->hwc/dot_general | solution.py:317
  106.7 0.9 collective-permute-done.14
  107.6 1.1 convert_add_fusion
  108.8 9.0 %collective-permute-done.15 = f32[1,3,16,1536]{3,2,1,0:T(8,128)S(1)} collective-permute-done((f32[1,3,16,1536]{3,2,1,0:T(8,128)S(1)}, f32[1,3,16,1536]{3,2,1,0:T(8,128)S(1)}, u32[]{:S(2)}, u32[]{:S(2)}) %collective-permute-start.15) | collective-permute-done | bytes 294944 | tf_op jit(solution)/shard_map/ppermute | solution.py:69
  118.0 1.6 fusion.141
  122.4 0.9 dynamic-slice_reduce_fusion
  123.4 1.4 collective-permute-done.18
  125.6 4.1 %collective-permute-done.19 = f32[18816]{0:T(1024)S(1)} collective-permute-done((f32[18816]{0:T(1024)S(1)}, f32[18816]{0:T(1024)S(1)}, u32[]{:S(2)}, u32[]{:S(2)}) %collective-permute-start.19) | collective-permute-done | bytes 75296 | tf_op jit(solution)/shard_map/ppermute | solution.py:49
  130.7 4.4 %collective-permute-done.20 = f32[9408]{0:T(1024)S(1)} collective-permute-done((f32[9408]{0:T(1024)S(1)}, f32[9408]{0:T(1024)S(1)}, u32[]{:S(2)}, u32[]{:S(2)}) %collective-permute-start.20) | collective-permute-done | bytes 37664 | tf_op jit(solution)/shard_map/ppermute | solution.py:49
  135.3 1.4 collective-permute-start.21
  136.7 4.2 %collective-permute-done.21 = f32[4704]{0:T(1024)S(1)} collective-permute-done((f32[4704]{0:T(1024)S(1)}, f32[4704]{0:T(1024)S(1)}, u32[]{:S(2)}, u32[]{:S(2)}) %collective-permute-start.21) | collective-permute-done | bytes 18848 | tf_op jit(solution)/shard_map/ppermute | solution.py:49
  141.1 1.2 collective-permute-start.22
  142.2 4.7 %collective-permute-done.22 = f32[2352]{0:T(1024)S(1)} collective-permute-done((f32[2352]{0:T(1024)S(1)}, f32[2352]{0:T(1024)S(1)}, u32[]{:S(2)}, u32[]{:S(2)}) %collective-permute-start.22) | collective-permute-done | bytes 9440 | tf_op jit(solution)/shard_map/ppermute | solution.py:49
  147.3 4.2 %collective-permute-done.23 = f32[2352]{0:T(1024)S(1)} collective-permute-done((f32[2352]{0:T(1024)S(1)}, f32[2352]{0:T(1024)S(1)}, u32[]{:S(2)}, u32[]{:S(2)}) %collective-permute-start.23) | collective-permute-done | bytes 9440 | tf_op jit(solution)/shard_map/ppermute | solution.py:52
  151.8 3.5 %collective-permute-done.24 = f32[4704]{0:T(1024)S(1)} collective-permute-done((f32[4704]{0:T(1024)S(1)}, f32[4704]{0:T(1024)S(1)}, u32[]{:S(2)}, u32[]{:S(2)}) %collective-permute-start.24) | collective-permute-done | bytes 18848 | tf_op jit(solution)/shard_map/ppermute | solution.py:52
  156.0 1.3 collective-permute-start.16
  157.3 1.3 collective-permute-start.17
  158.6 1.5 collective-permute-done.25
  160.2 1.8 collective-permute-start.26
  162.3 4.0 %collective-permute-done.26 = f32[18816]{0:T(1024)S(1)} collective-permute-done((f32[18816]{0:T(1024)S(1)}, f32[18816]{0:T(1024)S(1)}, u32[]{:S(2)}, u32[]{:S(2)}) %collective-permute-start.26) | collective-permute-done | bytes 75296 | tf_op jit(solution)/shard_map/ppermute | solution.py:52
  166.6 2.8 %fusion.147 = bf16[1,3,16,1536]{3,2,1,0:T(8,128)(2,1)} fusion(f32[1536]{0:T(1024)S(1)} %copy-done.44, bf16[9,22,1536]{2,1,0:T(8,128)(2,1)S(1)} %select_maximum_fusion, f32[1536]{0:T(1024)S(1)} %copy-done.46, f32[1536]{0:T(1024)S(1)} %get-tuple-element.59, f32[1536]{0:T(1024)S(1)} %get-tuple-element.60, bf16[3,16,1536]{2,1,0:T(8,128)(2,1)S(1)} %collective-permute-done.16, ...), kind=kLoop, calls=%fused_computation.298 | loop fusion | flops 11132928 | bytes 7084032 | tf_op jit(solution)/shard_map/reshape | solution.py:332
  169.5 0.8 select_n.294
  170.2 27.4 %reduce-scatter.2.cloned.1.call-done = bf16[192,1536]{1,0:T(8,128)(2,1)} async-done(((bf16[1536,1536]{1,0:T(8,128)(2,1)}), bf16[192,1536]{1,0:T(8,128)(2,1)}) %reduce-scatter.2.cloned.1.call-update) | async-done | bytes 589840 | tf_op jit(solution)/shard_map/reduce_scatter | solution.py:313
  197.7 2.2 %convert_element_type.497 = f32[192,1536]{1,0:T(8,128)} convert(bf16[192,1536]{1,0:T(8,128)(2,1)} %reduce-scatter.2.cloned.1.call-done) | non-fusion elementwise | flops 294912 | bytes 1769472 | tf_op jit(solution)/shard_map/convert_element_type | solution.py:315
  (243 shorter events, 15.3 us)
Async XLA Ops:
  7.2 190.5 %reduce-scatter.2.cloned.1.call-start = ((), (), s32[]{:S(2)}) async-start(), calls=%async_computation.1 | async-start | bytes 5308416 | tf_op jit(solution)/shard_map/reduce_scatter | solution.py:313
  8.4 25.1 %collective-permute-start = (bf16[192,1536]{1,0:T(8,128)(2,1)S(1)}, bf16[192,1536]{1,0:T(8,128)(2,1)S(1)}, u32[]{:S(2)}, u32[]{:S(2)}) collective-permute-start(bf16[192,1536]{1,0:T(8,128)(2,1)S(1)} %compare_select_fusion), channel_id=1, source_target_pairs={{0,8},{8,16},{16,24},{24,28},{28,20},{20,12},{12,4},{4,0},{1,9},{9... | collective-permute-start | bytes 1769480 | tf_op jit(solution)/shard_map/ppermute | solution.py:126
  11.5 22.0 %collective-permute-start.1 = (bf16[192,1536]{1,0:T(8,128)(2,1)S(1)}, bf16[192,1536]{1,0:T(8,128)(2,1)S(1)}, u32[]{:S(2)}, u32[]{:S(2)}) collective-permute-start(bf16[192,1536]{1,0:T(8,128)(2,1)S(1)} %compare_select_fusion), channel_id=1, source_target_pairs={{0,4},{8,0},{16,8},{24,16},{28,24},{20,28},{12,20},{4,12},{1,5},{9... | collective-permute-start | bytes 1769480 | tf_op jit(solution)/shard_map/ppermute | solution.py:128
  34.2 5.0 %collective-permute-start.2 = (bf16[3,16,1536]{2,1,0:T(8,128)(2,1)S(1)}, bf16[3,16,1536]{2,1,0:T(8,128)(2,1)S(1)}, u32[]{:S(2)}, u32[]{:S(2)}) collective-permute-start(bf16[3,16,1536]{2,1,0:T(8,128)(2,1)S(1)} %bitcast.73), channel_id=1, source_target_pairs={{0,1},{1,2},{2,3},{4,5},{5,6},{6,7},{8,9},{9,10},{10,11},{12,13},{... | collective-permute-start | bytes 442376 | tf_op jit(solution)/shard_map/ppermute | solution.py:16
  35.7 5.3 %collective-permute-start.3 = (bf16[3,16,1536]{2,1,0:T(8,128)(2,1)S(1)}, bf16[3,16,1536]{2,1,0:T(8,128)(2,1)S(1)}, u32[]{:S(2)}, u32[]{:S(2)}) collective-permute-start(bf16[3,16,1536]{2,1,0:T(8,128)(2,1)S(1)} %bitcast.74), channel_id=1, source_target_pairs={{1,0},{2,1},{3,2},{5,4},{6,5},{7,6},{9,8},{10,9},{11,10},{13,12},{... | collective-permute-start | bytes 442376 | tf_op jit(solution)/shard_map/ppermute | solution.py:19
  37.0 14.0 %collective-permute-start.6 = (bf16[192,1536]{1,0:T(8,128)(2,1)S(1)}, bf16[192,1536]{1,0:T(8,128)(2,1)S(1)}, u32[]{:S(2)}, u32[]{:S(2)}) collective-permute-start(bf16[192,1536]{1,0:T(8,128)(2,1)S(1)} %collective-permute-done), channel_id=1, source_target_pairs={{0,8},{8,16},{16,24},{24,28},{28,20},{20,12},{12,4},{4,0},{1,9},{9... | collective-permute-start | bytes 1769480 | tf_op jit(solution)/shard_map/ppermute | solution.py:126
  38.9 14.5 %collective-permute-start.7 = (bf16[192,1536]{1,0:T(8,128)(2,1)S(1)}, bf16[192,1536]{1,0:T(8,128)(2,1)S(1)}, u32[]{:S(2)}, u32[]{:S(2)}) collective-permute-start(bf16[192,1536]{1,0:T(8,128)(2,1)S(1)} %collective-permute-done.1), channel_id=1, source_target_pairs={{0,4},{8,0},{16,8},{24,16},{28,24},{20,28},{12,20},{4,12},{1,5},{9... | collective-permute-start | bytes 1769480 | tf_op jit(solution)/shard_map/ppermute | solution.py:128
  44.9 72.9 %copy-start.47 = (f32[3,16]{1,0:T(4,128)}, f32[3,16]{1,0:T(4,128)S(1)}, u32[]{:S(2)}) copy-start(f32[3,16]{1,0:T(4,128)S(1)} %broadcast_multiply_fusion.2) | copy-start | bytes 580
  45.1 72.7 %copy-start.48 = (f32[3,16]{1,0:T(4,128)}, f32[3,16]{1,0:T(4,128)S(1)}, u32[]{:S(2)}) copy-start(f32[3,16]{1,0:T(4,128)S(1)} %add_rsqrt_fusion) | copy-start | bytes 580
  45.2 5.1 %collective-permute-start.4 = (bf16[1,3,16,1536]{3,2,1,0:T(8,128)(2,1)S(1)}, bf16[1,3,16,1536]{3,2,1,0:T(8,128)(2,1)S(1)}, u32[]{:S(2)}, u32[]{:S(2)}) collective-permute-start(bf16[1,3,16,1536]{3,2,1,0:T(8,128)(2,1)S(1)} %fusion.144), channel_id=1, source_target_pairs={{0,1},{1,0},{2,3},{3,2},{4,5},{5,4},{6,7},{7,6},{8,9},{9,8},{10,11... | collective-permute-start | bytes 442376 | tf_op jit(solution)/shard_map/ppermute | solution.py:182
  50.3 9.3 %collective-permute-start.5 = (bf16[2,3,16,1536]{3,2,1,0:T(8,128)(2,1)S(1)}, bf16[2,3,16,1536]{3,2,1,0:T(8,128)(2,1)S(1)}, u32[]{:S(2)}, u32[]{:S(2)}) collective-permute-start(bf16[2,3,16,1536]{3,2,1,0:T(8,128)(2,1)S(1)} %maximum_select_fusion.2), channel_id=1, source_target_pairs={{0,2},{1,3},{2,0},{3,1},{4,6},{5,7},{6,4},{7,5},{8,10},{9,11},{10,... | collective-permute-start | bytes 884744 | tf_op jit(solution)/shard_map/ppermute | solution.py:182
  51.0 14.9 %collective-permute-start.8 = (bf16[192,1536]{1,0:T(8,128)(2,1)S(1)}, bf16[192,1536]{1,0:T(8,128)(2,1)S(1)}, u32[]{:S(2)}, u32[]{:S(2)}) collective-permute-start(bf16[192,1536]{1,0:T(8,128)(2,1)S(1)} %collective-permute-done.6), channel_id=1, source_target_pairs={{0,8},{8,16},{16,24},{24,28},{28,20},{20,12},{12,4},{4,0},{1,9},{9... | collective-permute-start | bytes 1769480 | tf_op jit(solution)/shard_map/ppermute | solution.py:126
  53.4 15.4 %collective-permute-start.9 = (bf16[192,1536]{1,0:T(8,128)(2,1)S(1)}, bf16[192,1536]{1,0:T(8,128)(2,1)S(1)}, u32[]{:S(2)}, u32[]{:S(2)}) collective-permute-start(bf16[192,1536]{1,0:T(8,128)(2,1)S(1)} %collective-permute-done.7), channel_id=1, source_target_pairs={{0,4},{8,0},{16,8},{24,16},{28,24},{20,28},{12,20},{4,12},{1,5},{9... | collective-permute-start | bytes 1769480 | tf_op jit(solution)/shard_map/ppermute | solution.py:128
  65.9 10.4 %collective-permute-start.10 = (bf16[192,768]{1,0:T(8,128)(2,1)S(1)}, bf16[192,768]{1,0:T(8,128)(2,1)S(1)}, u32[]{:S(2)}, u32[]{:S(2)}) collective-permute-start(bf16[192,768]{1,0:T(8,128)(2,1)S(1)} %slice.752), channel_id=1, source_target_pairs={{0,8},{8,16},{16,24},{24,28},{28,20},{20,12},{12,4},{4,0},{1,9},{9... | collective-permute-start | bytes 884744 | tf_op jit(solution)/shard_map/ppermute | solution.py:117
  68.9 9.6 %collective-permute-start.11 = (bf16[192,768]{1,0:T(8,128)(2,1)S(1)}, bf16[192,768]{1,0:T(8,128)(2,1)S(1)}, u32[]{:S(2)}, u32[]{:S(2)}) collective-permute-start(bf16[192,768]{1,0:T(8,128)(2,1)S(1)} %slice.753), channel_id=1, source_target_pairs={{0,4},{8,0},{16,8},{24,16},{28,24},{20,28},{12,20},{4,12},{1,5},{9... | collective-permute-start | bytes 884744 | tf_op jit(solution)/shard_map/ppermute | solution.py:118
  85.6 1.1 collective-permute-start.12
  88.0 3.5 %collective-permute-start.13 = (f32[2]{0:T(128)S(1)}, f32[2]{0:T(128)S(1)}, u32[]{:S(2)}, u32[]{:S(2)}) collective-permute-start(f32[2]{0:T(128)S(1)} %fusion.163), channel_id=1, source_target_pairs={{0,2},{1,3},{2,0},{3,1},{4,6},{5,7},{6,4},{7,5},{8,10},{9,11},{10,... | collective-permute-start | bytes 32 | tf_op jit(solution)/shard_map/ppermute | solution.py:193
  105.9 1.6 collective-permute-start.14
  108.7 9.1 %collective-permute-start.15 = (f32[1,3,16,1536]{3,2,1,0:T(8,128)S(1)}, f32[1,3,16,1536]{3,2,1,0:T(8,128)S(1)}, u32[]{:S(2)}, u32[]{:S(2)}) collective-permute-start(f32[1,3,16,1536]{3,2,1,0:T(8,128)S(1)} %constant_dynamic-slice_fusion), channel_id=1, source_target_pairs={{0,2},{1,3},{2,0},{3,1},{4,6},{5,7},{6,4},{7,5},{8,10},{9,11},{10,... | collective-permute-start | bytes 884744 | tf_op jit(solution)/shard_map/ppermute | solution.py:69
  123.3 1.4 collective-permute-start.18
  125.3 4.5 %collective-permute-start.19 = (f32[18816]{0:T(1024)S(1)}, f32[18816]{0:T(1024)S(1)}, u32[]{:S(2)}, u32[]{:S(2)}) collective-permute-start(f32[18816]{0:T(1024)S(1)} %get-tuple-element.111), channel_id=1, source_target_pairs={{0,2},{1,3},{2,0},{3,1},{4,6},{5,7},{6,4},{7,5},{8,10},{9,11},{10,... | collective-permute-start | bytes 225800 | tf_op jit(solution)/shard_map/ppermute | solution.py:49
  130.1 36.3 %copy-start.8 = (f32[1536]{0:T(1024)S(1)}, f32[1536]{0:T(1024)}, u32[]{:S(2)}) copy-start(f32[1536]{0:T(1024)} %get-tuple-element.87) | copy-start | bytes 18436
  130.1 36.3 %copy-start.10 = (f32[1536]{0:T(1024)S(1)}, f32[1536]{0:T(1024)}, u32[]{:S(2)}) copy-start(f32[1536]{0:T(1024)} %get-tuple-element.88) | copy-start | bytes 18436
  130.1 36.3 %copy-start.12 = (f32[1536]{0:T(1024)S(1)}, f32[1536]{0:T(1024)}, u32[]{:S(2)}) copy-start(f32[1536]{0:T(1024)} %get-tuple-element.89) | copy-start | bytes 18436
  130.1 36.3 %copy-start.14 = (f32[1536]{0:T(1024)S(1)}, f32[1536]{0:T(1024)}, u32[]{:S(2)}) copy-start(f32[1536]{0:T(1024)} %get-tuple-element.90) | copy-start | bytes 18436
  130.2 36.3 %copy-start.16 = (f32[1536]{0:T(1024)S(1)}, f32[1536]{0:T(1024)}, u32[]{:S(2)}) copy-start(f32[1536]{0:T(1024)} %get-tuple-element.91) | copy-start | bytes 18436
  130.2 36.3 %copy-start.18 = (f32[1536]{0:T(1024)S(1)}, f32[1536]{0:T(1024)}, u32[]{:S(2)}) copy-start(f32[1536]{0:T(1024)} %get-tuple-element.92) | copy-start | bytes 18436
  130.2 36.3 %copy-start.20 = (f32[1536]{0:T(1024)S(1)}, f32[1536]{0:T(1024)}, u32[]{:S(2)}) copy-start(f32[1536]{0:T(1024)} %get-tuple-element.93) | copy-start | bytes 18436
  130.2 36.3 %copy-start.22 = (f32[1536]{0:T(1024)S(1)}, f32[1536]{0:T(1024)}, u32[]{:S(2)}) copy-start(f32[1536]{0:T(1024)} %get-tuple-element.94) | copy-start | bytes 18436
  130.2 36.3 %copy-start.24 = (f32[1536]{0:T(1024)S(1)}, f32[1536]{0:T(1024)}, u32[]{:S(2)}) copy-start(f32[1536]{0:T(1024)} %get-tuple-element.95) | copy-start | bytes 18436
  130.2 36.3 %copy-start.26 = (f32[1536]{0:T(1024)S(1)}, f32[1536]{0:T(1024)}, u32[]{:S(2)}) copy-start(f32[1536]{0:T(1024)} %copy-done.25) | copy-start | bytes 18436
  130.2 36.3 %copy-start.28 = (f32[1536]{0:T(1024)S(1)}, f32[1536]{0:T(1024)}, u32[]{:S(2)}) copy-start(f32[1536]{0:T(1024)} %copy-done.27) | copy-start | bytes 18436
  130.2 36.3 %copy-start.30 = (f32[1536]{0:T(1024)S(1)}, f32[1536]{0:T(1024)}, u32[]{:S(2)}) copy-start(f32[1536]{0:T(1024)} %copy-done.29) | copy-start | bytes 18436
  130.2 36.3 %copy-start.32 = (f32[1536]{0:T(1024)S(1)}, f32[1536]{0:T(1024)}, u32[]{:S(2)}) copy-start(f32[1536]{0:T(1024)} %copy-done.31) | copy-start | bytes 18436
  130.2 36.3 %copy-start.34 = (f32[1536]{0:T(1024)S(1)}, f32[1536]{0:T(1024)}, u32[]{:S(2)}) copy-start(f32[1536]{0:T(1024)} %copy-done.33) | copy-start | bytes 18436
  130.3 36.3 %copy-start.36 = (f32[1536]{0:T(1024)S(1)}, f32[1536]{0:T(1024)}, u32[]{:S(2)}) copy-start(f32[1536]{0:T(1024)} %copy-done.35) | copy-start | bytes 18436
  130.3 36.3 %copy-start.38 = (f32[1536]{0:T(1024)S(1)}, f32[1536]{0:T(1024)}, u32[]{:S(2)}) copy-start(f32[1536]{0:T(1024)} %copy-done.37) | copy-start | bytes 18436
  130.3 36.3 %copy-start.40 = (f32[1536]{0:T(1024)S(1)}, f32[1536]{0:T(1024)}, u32[]{:S(2)}) copy-start(f32[1536]{0:T(1024)} %copy-done.39) | copy-start | bytes 18436
  130.3 4.7 %collective-permute-start.20 = (f32[9408]{0:T(1024)S(1)}, f32[9408]{0:T(1024)S(1)}, u32[]{:S(2)}, u32[]{:S(2)}) collective-permute-start(f32[9408]{0:T(1024)S(1)} %get-tuple-element.120), channel_id=1, source_target_pairs={{0,4},{4,0},{8,12},{12,8},{16,20},{20,16},{24,28},{28,24},{1,5},{5... | collective-permute-start | bytes 112904 | tf_op jit(solution)/shard_map/ppermute | solution.py:49
  135.3 5.6 %collective-permute-start.21 = (f32[4704]{0:T(1024)S(1)}, f32[4704]{0:T(1024)S(1)}, u32[]{:S(2)}, u32[]{:S(2)}) collective-permute-start(f32[4704]{0:T(1024)S(1)} %get-tuple-element.122), channel_id=1, source_target_pairs={{0,8},{4,12},{8,0},{12,4},{16,24},{20,28},{24,16},{28,20},{1,9},{5... | collective-permute-start | bytes 56456 | tf_op jit(solution)/shard_map/ppermute | solution.py:49
  141.1 5.8 %collective-permute-start.22 = (f32[2352]{0:T(1024)S(1)}, f32[2352]{0:T(1024)S(1)}, u32[]{:S(2)}, u32[]{:S(2)}) collective-permute-start(f32[2352]{0:T(1024)S(1)} %get-tuple-element.124), channel_id=1, source_target_pairs={{0,16},{4,20},{8,24},{12,28},{16,0},{20,4},{24,8},{28,12},{1,17},{... | collective-permute-start | bytes 28232 | tf_op jit(solution)/shard_map/ppermute | solution.py:49
  146.9 4.6 %collective-permute-start.23 = (f32[2352]{0:T(1024)S(1)}, f32[2352]{0:T(1024)S(1)}, u32[]{:S(2)}, u32[]{:S(2)}) collective-permute-start(f32[2352]{0:T(1024)S(1)} %add.730), channel_id=1, source_target_pairs={{0,16},{4,20},{8,24},{12,28},{16,0},{20,4},{24,8},{28,12},{1,17},{... | collective-permute-start | bytes 28232 | tf_op jit(solution)/shard_map/ppermute | solution.py:52
  151.6 3.8 %collective-permute-start.24 = (f32[4704]{0:T(1024)S(1)}, f32[4704]{0:T(1024)S(1)}, u32[]{:S(2)}, u32[]{:S(2)}) collective-permute-start(f32[4704]{0:T(1024)S(1)} %maximum_select_fusion.6), channel_id=1, source_target_pairs={{0,8},{4,12},{8,0},{12,4},{16,24},{20,28},{24,16},{28,20},{1,9},{5... | collective-permute-start | bytes 56456 | tf_op jit(solution)/shard_map/ppermute | solution.py:52
  155.5 4.7 %collective-permute-start.25 = (f32[9408]{0:T(1024)S(1)}, f32[9408]{0:T(1024)S(1)}, u32[]{:S(2)}, u32[]{:S(2)}) collective-permute-start(f32[9408]{0:T(1024)S(1)} %maximum_select_fusion.5), channel_id=1, source_target_pairs={{0,4},{4,0},{8,12},{12,8},{16,20},{20,16},{24,28},{28,24},{1,5},{5... | collective-permute-start | bytes 112904 | tf_op jit(solution)/shard_map/ppermute | solution.py:52
  156.0 6.0 %collective-permute-start.16 = (bf16[3,16,1536]{2,1,0:T(8,128)(2,1)S(1)}, bf16[3,16,1536]{2,1,0:T(8,128)(2,1)S(1)}, u32[]{:S(2)}, u32[]{:S(2)}) collective-permute-start(bf16[3,16,1536]{2,1,0:T(8,128)(2,1)S(1)} %get-tuple-element.128), channel_id=1, source_target_pairs={{0,1},{1,2},{2,3},{4,5},{5,6},{6,7},{8,9},{9,10},{10,11},{12,13},{... | collective-permute-start | bytes 442376 | tf_op jit(solution)/shard_map/ppermute | solution.py:16
  157.3 4.7 %collective-permute-start.17 = (bf16[3,16,1536]{2,1,0:T(8,128)(2,1)S(1)}, bf16[3,16,1536]{2,1,0:T(8,128)(2,1)S(1)}, u32[]{:S(2)}, u32[]{:S(2)}) collective-permute-start(bf16[3,16,1536]{2,1,0:T(8,128)(2,1)S(1)} %get-tuple-element.128), channel_id=1, source_target_pairs={{1,0},{2,1},{3,2},{5,4},{6,5},{7,6},{9,8},{10,9},{11,10},{13,12},{... | collective-permute-start | bytes 442376 | tf_op jit(solution)/shard_map/ppermute | solution.py:19
  160.2 6.1 %collective-permute-start.26 = (f32[18816]{0:T(1024)S(1)}, f32[18816]{0:T(1024)S(1)}, u32[]{:S(2)}, u32[]{:S(2)}) collective-permute-start(f32[18816]{0:T(1024)S(1)} %maximum_select_fusion.4), channel_id=1, source_target_pairs={{0,2},{1,3},{2,0},{3,1},{4,6},{5,7},{6,4},{7,5},{8,10},{9,11},{10,... | collective-permute-start | bytes 225800 | tf_op jit(solution)/shard_map/ppermute | solution.py:52
  166.3 3.1 %collective-permute-start.27 = (f32[37632]{0:T(1024)S(1)}, f32[37632]{0:T(1024)S(1)}, u32[]{:S(2)}, u32[]{:S(2)}) collective-permute-start(f32[37632]{0:T(1024)S(1)} %maximum_select_fusion.3), channel_id=1, source_target_pairs={{0,1},{1,0},{2,3},{3,2},{4,5},{5,4},{6,7},{7,6},{8,9},{9,8},{10,11... | collective-permute-start | bytes 451592 | tf_op jit(solution)/shard_map/ppermute | solution.py:52
  (37 other events, 318.8 us)
Sparse Core Ops, SparseCore 0:
  102.0 95.6 reduce-scatter.1

commit v17 on v14

--- a/solution.py
+++ b/solution.py
@@ -175,13 +175,17 @@
     assert size & (size - 1) == 0
     me = lax.axis_index(axis)
     data = block[None]
-    mask = 1
-    while mask < size:
+    mask = size // 2
+    bits = 0
+    while mask >= 1:
         bit = (me // mask) % 2
         perm = [(j, j ^ mask) for j in range(size)]
         other = lax.ppermute(data, axis, perm)
         data = jnp.where(bit == 0, jnp.concatenate([data, other]), jnp.concatenate([other, data]))
-        mask *= 2
+        mask //= 2
+        bits += 1
+    data = data.reshape((2,) * bits + block.shape)
+    data = jnp.transpose(data, tuple(reversed(range(bits))) + tuple(range(bits, data.ndim)))
     return data.reshape((size * block.shape[0],) + block.shape[1:])
 
 

time: 206 us -> 206 us (level)
    ppermute x3, waiting for transfers between devices: 6.79 us -> 13 us  [ring_all_gather(): cw = lax.ppermute(cw, axis, forward)]
    ppermute x2, waiting for transfers between devices: 7.11 us -> 4.07 us  [tree_all_gather(): other = lax.ppermute(data, axis, perm)]
  transfers between devices with their start and end apart: 27 -> 27, of which waited for: 21 -> 17; matrix products, arithmetic and copies ran while one was open for 11% -> 11% of each run, Pallas kernels for 0% -> 0%
where the time goes in v17:
time: 206 us
  waiting for transfers between devices  91.2 us (44%)
  between operations  34.9 us (17%)
  starting transfers between devices  31.9 us (15%)
  other arithmetic  19.3 us (9%)
  matrix products  12.4 us (6%)
  local copies, waits for them, and re-layouts  9.45 us (5%)
  blocking collectives  6.64 us (3%)
    reduce_scatter x1, waiting for transfers between devices, body(): lax.psum_scatter(w_term.astype(jnp.bfloat16), 'fsdp', scatter_dimension=0...  27.2 us
    ppermute x5, waiting for transfers between devices, tree_allreduce(): flat = keep + lax.ppermute(give, axis, perm)  16.7 us
    ppermute x3, waiting for transfers between devices, ring_all_gather(): cw = lax.ppermute(cw, axis, forward)  13 us
    ppermute x5, waiting for transfers between devices, tree_allreduce(): other = lax.ppermute(flat, axis, perm)  12.9 us
    ppermute x2, waiting for transfers between devices, tree_reduce_scatter(): lax.ppermute(give, axis, perm).astype(jnp.float32)  8.19 us
    psum x1, blocking collectives, body(): norm_total = lax.psum(jnp.sum(norms), 'rows')  6.64 us
    ppermute x3, starting transfers between devices, ring_all_gather(): cw = lax.ppermute(cw, axis, forward)  6.55 us
    ppermute x1, waiting for transfers between devices, ring_all_gather(): lax.ppermute(cw[..., :half], axis, forward)  5.92 us
  transfers between devices with their start and end apart: 27, of which 17 were waited for; matrix products, arithmetic and copies ran while one was open for 11% of the time, Pallas kernels for 0%

profile of v17, /device:TPU:0, one launch (start us, length us, event | category | flops | bytes accessed | tf_op | source)
XLA Modules:
  0.0 205.7 jit_solution(6186871061717634081)
XLA Ops:
  7.2 1.1 compare_select_fusion
  8.4 3.1 %collective-permute-start = (bf16[192,1536]{1,0:T(8,128)(2,1)S(1)}, bf16[192,1536]{1,0:T(8,128)(2,1)S(1)}, u32[]{:S(2)}, u32[]{:S(2)}) collective-permute-start(bf16[192,1536]{1,0:T(8,128)(2,1)S(1)} %compare_select_fusion), channel_id=1, source_target_pairs={{0,8},{8,16},{16,24},{24,28},{28,20},{20,12},{12,4},{4,0},{1,9},{9... | collective-permute-start | bytes 1769480 | tf_op jit(solution)/shard_map/ppermute | solution.py:126
  26.6 0.9 slice_reduce_fusion.47
  33.5 0.7 copy-done.2
  34.2 1.5 collective-permute-start.2
  35.7 1.3 collective-permute-start.3
  37.0 1.9 collective-permute-start.6
  39.3 1.7 collective-permute-done.3
  41.4 3.4 %fusion.153 = (f32[3,16]{1,0:T(4,128)S(1)}, f32[3,16,1536]{2,1,0:T(8,128)S(1)}) fusion(f32[1536]{0:T(1024)S(1)} %get-tuple-element.105, bf16[9,22,1536]{2,1,0:T(8,128)(2,1)S(1)} %select_maximum_fusion.2, f32[1536]{0:T(1024)S(1)} %get-tuple-element.106, f32[1536]{0:T(1024)S(1)} %get-tuple-element.59, f32[1536]{0:T(1024)S(1)} %get-tuple-element.60, ...), kind=kLoop, calls=%fused_computation.375 | loop fusion | flops 10911696 | bytes 7827648 | tf_op jit(solution)/shard_map/reduce_sum | solution.py:232
  45.2 3.5 %collective-permute-start.4 = (bf16[1,3,16,1536]{3,2,1,0:T(8,128)(2,1)S(1)}, bf16[1,3,16,1536]{3,2,1,0:T(8,128)(2,1)S(1)}, u32[]{:S(2)}, u32[]{:S(2)}) collective-permute-start(bf16[1,3,16,1536]{3,2,1,0:T(8,128)(2,1)S(1)} %fusion.144), channel_id=1, source_target_pairs={{0,2},{1,3},{2,0},{3,1},{4,6},{5,7},{6,4},{7,5},{8,10},{9,11},{10,... | collective-permute-start | bytes 442376 | tf_op jit(solution)/shard_map/ppermute | solution.py:183
  48.7 4.1 %collective-permute-done.4 = bf16[1,3,16,1536]{3,2,1,0:T(8,128)(2,1)S(1)} collective-permute-done((bf16[1,3,16,1536]{3,2,1,0:T(8,128)(2,1)S(1)}, bf16[1,3,16,1536]{3,2,1,0:T(8,128)(2,1)S(1)}, u32[]{:S(2)}, u32[]{:S(2)}) %collective-permute-start.4) | collective-permute-done | bytes 147488 | tf_op jit(solution)/shard_map/ppermute | solution.py:183
  52.8 0.8 collective-permute-start.5
  53.6 1.6 collective-permute-start.8
  55.9 13.0 %collective-permute-done.8 = bf16[192,1536]{1,0:T(8,128)(2,1)S(1)} collective-permute-done((bf16[192,1536]{1,0:T(8,128)(2,1)S(1)}, bf16[192,1536]{1,0:T(8,128)(2,1)S(1)}, u32[]{:S(2)}, u32[]{:S(2)}) %collective-permute-start.8) | collective-permute-done | bytes 589856 | tf_op jit(solution)/shard_map/ppermute | solution.py:126
  69.0 1.6 collective-permute-start.10
  71.2 5.9 %collective-permute-done.10 = bf16[192,768]{1,0:T(8,128)(2,1)S(1)} collective-permute-done((bf16[192,768]{1,0:T(8,128)(2,1)S(1)}, bf16[192,768]{1,0:T(8,128)(2,1)S(1)}, u32[]{:S(2)}, u32[]{:S(2)}) %collective-permute-start.10) | collective-permute-done | bytes 294944 | tf_op jit(solution)/shard_map/ppermute | solution.py:117
  77.2 1.4 collective-permute-done.11
  78.6 4.8 %fusion.4 = (f32[1536]{0:T(1024)S(1)}, f32[1536]{0:T(1024)S(1)}, f32[192,1536]{1,0:T(8,128)}, f32[192,1536]{1,0:T(8,128)}) fusion(bf16[1,12,16,1536]{3,2,1,0:T(8,128)(2,1)S(1)} %copy-done.3, f32[1536]{0:T(1024)S(1)} %copy-done.54, bf16[192,1536]{1,0:T(8,128)(2,1)S(1)} %bitcast.69, bf16[1536,1536]{1,0:T(8,128)(2,1)S(1)} %bitcast.67), kind=kOutput, calls=%fused_computation.64 | convolution fusion | flops 926610432 | bytes 8275968 | tf_op jit(solution)/shard_map/dot_general | solution.py:290
  84.2 6.6 %all-reduce.2 = (f32[]{:T(128)}, f32[]{:T(128)}) all-reduce(f32[]{:T(128)} %get-tuple-element.127, f32[]{:T(128)} %get-tuple-element.126), channel_id=1, replica_groups=mesh['fsdp'=8,'rows'=4] {'rows'}, use_global_device_ids=true, to_apply=%region_4.5 | all-reduce | flops 2 | bytes 16 | tf_op jit(solution)/shard_map/psum | solution.py:295
  92.2 3.4 %fusion.3 = (bf16[192,1536]{1,0:T(8,128)(2,1)S(1)}, bf16[192,1536]{1,0:T(8,128)(2,1)}) fusion(f32[192,1536]{1,0:T(8,128)} %get-tuple-element.149, f32[192,1536]{1,0:T(8,128)} %get-tuple-element.134, bf16[1,12,16,1536]{3,2,1,0:T(8,128)(2,1)} %param.21, f32[1536]{0:T(1024)S(1)} %get-tuple-element.141, f32[1536]{0:T(1024)S(1)} %get-tuple-element.132, ...), kind=kLoop, calls=%fused_computation.63 | loop fusion | flops 5603328 | bytes 4159488 | tf_op jit(solution)/shard_map/convert_element_type | solution.py:302
  95.6 3.5 %convolution_convert_fusion = bf16[1536,1536]{1,0:T(8,128)(2,1)} fusion(bf16[192,1536]{1,0:T(8,128)(2,1)S(1)} %bitcast.70, bf16[192,1536]{1,0:T(8,128)(2,1)S(1)} %get-tuple-element.137), kind=kOutput, calls=%fused_computation | convolution fusion | flops 908328960 | bytes 5898240 | tf_op jit(solution)/shard_map/dot_general | solution.py:303
  99.1 4.0 %convolution_convert_fusion.1 = bf16[12,16,1536]{2,1,0:T(8,128)(2,1)S(1)} fusion(bf16[12,16,1536]{2,1,0:T(8,128)(2,1)S(1)} %bitcast.71, bf16[1536,1536,1]{1,0,2:T(8,128)(2,1)} %bitcast.68), kind=kOutput, calls=%fused_computation.52 | convolution fusion | flops 906264576 | bytes 5898240 | tf_op jit(solution)/shard_map/hwf,cf->hwc/dot_general | solution.py:310
  104.0 0.9 collective-permute-done.12
  104.9 1.0 convert_add_fusion
  105.9 2.3 %collective-permute-start.13 = (f32[1,3,16,1536]{3,2,1,0:T(8,128)S(1)}, f32[1,3,16,1536]{3,2,1,0:T(8,128)S(1)}, u32[]{:S(2)}, u32[]{:S(2)}) collective-permute-start(f32[1,3,16,1536]{3,2,1,0:T(8,128)S(1)} %constant_dynamic-slice_fusion), channel_id=1, source_target_pairs={{0,2},{1,3},{2,0},{3,1},{4,6},{5,7},{6,4},{7,5},{8,10},{9,11},{10,... | collective-permute-start | bytes 884744 | tf_op jit(solution)/shard_map/ppermute | solution.py:69
  108.2 7.3 %collective-permute-done.13 = f32[1,3,16,1536]{3,2,1,0:T(8,128)S(1)} collective-permute-done((f32[1,3,16,1536]{3,2,1,0:T(8,128)S(1)}, f32[1,3,16,1536]{3,2,1,0:T(8,128)S(1)}, u32[]{:S(2)}, u32[]{:S(2)}) %collective-permute-start.13) | collective-permute-done | bytes 294944 | tf_op jit(solution)/shard_map/ppermute | solution.py:69
  115.7 1.6 fusion.141
  118.1 0.8 fusion.142
  120.2 0.9 dynamic-slice_reduce_fusion
  121.1 1.4 collective-permute-done.16
  123.0 1.8 collective-permute-start.17
  124.9 2.7 %collective-permute-done.17 = f32[18816]{0:T(1024)S(1)} collective-permute-done((f32[18816]{0:T(1024)S(1)}, f32[18816]{0:T(1024)S(1)}, u32[]{:S(2)}, u32[]{:S(2)}) %collective-permute-start.17) | collective-permute-done | bytes 75296 | tf_op jit(solution)/shard_map/ppermute | solution.py:49
  128.6 4.4 %collective-permute-done.18 = f32[9408]{0:T(1024)S(1)} collective-permute-done((f32[9408]{0:T(1024)S(1)}, f32[9408]{0:T(1024)S(1)}, u32[]{:S(2)}, u32[]{:S(2)}) %collective-permute-start.18) | collective-permute-done | bytes 37664 | tf_op jit(solution)/shard_map/ppermute | solution.py:49
  133.2 1.5 collective-permute-start.19
  134.7 3.8 %collective-permute-done.19 = f32[4704]{0:T(1024)S(1)} collective-permute-done((f32[4704]{0:T(1024)S(1)}, f32[4704]{0:T(1024)S(1)}, u32[]{:S(2)}, u32[]{:S(2)}) %collective-permute-start.19) | collective-permute-done | bytes 18848 | tf_op jit(solution)/shard_map/ppermute | solution.py:49
  138.7 1.7 collective-permute-start.20
  140.4 4.5 %collective-permute-done.20 = f32[2352]{0:T(1024)S(1)} collective-permute-done((f32[2352]{0:T(1024)S(1)}, f32[2352]{0:T(1024)S(1)}, u32[]{:S(2)}, u32[]{:S(2)}) %collective-permute-start.20) | collective-permute-done | bytes 9440 | tf_op jit(solution)/shard_map/ppermute | solution.py:49
  145.4 4.2 %collective-permute-done.21 = f32[2352]{0:T(1024)S(1)} collective-permute-done((f32[2352]{0:T(1024)S(1)}, f32[2352]{0:T(1024)S(1)}, u32[]{:S(2)}, u32[]{:S(2)}) %collective-permute-start.21) | collective-permute-done | bytes 9440 | tf_op jit(solution)/shard_map/ppermute | solution.py:52
  149.7 3.7 %collective-permute-done.22 = f32[4704]{0:T(1024)S(1)} collective-permute-done((f32[4704]{0:T(1024)S(1)}, f32[4704]{0:T(1024)S(1)}, u32[]{:S(2)}, u32[]{:S(2)}) %collective-permute-start.22) | collective-permute-done | bytes 18848 | tf_op jit(solution)/shard_map/ppermute | solution.py:52
  153.9 1.3 collective-permute-start.14
  155.2 1.3 collective-permute-start.15
  156.5 1.1 collective-permute-done.23
  157.7 3.6 %collective-permute-start.24 = (f32[18816]{0:T(1024)S(1)}, f32[18816]{0:T(1024)S(1)}, u32[]{:S(2)}, u32[]{:S(2)}) collective-permute-start(f32[18816]{0:T(1024)S(1)} %maximum_select_fusion.4), channel_id=1, source_target_pairs={{0,2},{1,3},{2,0},{3,1},{4,6},{5,7},{6,4},{7,5},{8,10},{9,11},{10,... | collective-permute-start | bytes 225800 | tf_op jit(solution)/shard_map/ppermute | solution.py:52
  161.5 4.0 %collective-permute-done.24 = f32[18816]{0:T(1024)S(1)} collective-permute-done((f32[18816]{0:T(1024)S(1)}, f32[18816]{0:T(1024)S(1)}, u32[]{:S(2)}, u32[]{:S(2)}) %collective-permute-start.24) | collective-permute-done | bytes 75296 | tf_op jit(solution)/shard_map/ppermute | solution.py:52
  165.8 2.8 %fusion.147 = bf16[1,3,16,1536]{3,2,1,0:T(8,128)(2,1)} fusion(f32[1536]{0:T(1024)S(1)} %copy-done.44, bf16[9,22,1536]{2,1,0:T(8,128)(2,1)S(1)} %select_maximum_fusion, f32[1536]{0:T(1024)S(1)} %copy-done.46, f32[1536]{0:T(1024)S(1)} %get-tuple-element.59, f32[1536]{0:T(1024)S(1)} %get-tuple-element.60, bf16[3,16,1536]{2,1,0:T(8,128)(2,1)S(1)} %collective-permute-done.14, ...), kind=kLoop, calls=%fused_computation.298 | loop fusion | flops 11132928 | bytes 7084032 | tf_op jit(solution)/shard_map/reshape | solution.py:325
  168.7 0.8 select_n.287
  169.4 27.2 %reduce-scatter.2.cloned.1.call-done = bf16[192,1536]{1,0:T(8,128)(2,1)} async-done(((bf16[1536,1536]{1,0:T(8,128)(2,1)}), bf16[192,1536]{1,0:T(8,128)(2,1)}) %reduce-scatter.2.cloned.1.call-update) | async-done | bytes 589840 | tf_op jit(solution)/shard_map/reduce_scatter | solution.py:306
  196.7 2.2 %convert_element_type.497 = f32[192,1536]{1,0:T(8,128)} convert(bf16[192,1536]{1,0:T(8,128)(2,1)} %reduce-scatter.2.cloned.1.call-done) | non-fusion elementwise | flops 294912 | bytes 1769472 | tf_op jit(solution)/shard_map/convert_element_type | solution.py:308
  (237 shorter events, 12.4 us)
Async XLA Ops:
  7.2 189.5 %reduce-scatter.2.cloned.1.call-start = ((), (), s32[]{:S(2)}) async-start(), calls=%async_computation.1 | async-start | bytes 5308416 | tf_op jit(solution)/shard_map/reduce_scatter | solution.py:306
  8.4 25.1 %collective-permute-start = (bf16[192,1536]{1,0:T(8,128)(2,1)S(1)}, bf16[192,1536]{1,0:T(8,128)(2,1)S(1)}, u32[]{:S(2)}, u32[]{:S(2)}) collective-permute-start(bf16[192,1536]{1,0:T(8,128)(2,1)S(1)} %compare_select_fusion), channel_id=1, source_target_pairs={{0,8},{8,16},{16,24},{24,28},{28,20},{20,12},{12,4},{4,0},{1,9},{9... | collective-permute-start | bytes 1769480 | tf_op jit(solution)/shard_map/ppermute | solution.py:126
  11.5 22.0 %collective-permute-start.1 = (bf16[192,1536]{1,0:T(8,128)(2,1)S(1)}, bf16[192,1536]{1,0:T(8,128)(2,1)S(1)}, u32[]{:S(2)}, u32[]{:S(2)}) collective-permute-start(bf16[192,1536]{1,0:T(8,128)(2,1)S(1)} %compare_select_fusion), channel_id=1, source_target_pairs={{0,4},{8,0},{16,8},{24,16},{28,24},{20,28},{12,20},{4,12},{1,5},{9... | collective-permute-start | bytes 1769480 | tf_op jit(solution)/shard_map/ppermute | solution.py:128
  34.2 5.0 %collective-permute-start.2 = (bf16[3,16,1536]{2,1,0:T(8,128)(2,1)S(1)}, bf16[3,16,1536]{2,1,0:T(8,128)(2,1)S(1)}, u32[]{:S(2)}, u32[]{:S(2)}) collective-permute-start(bf16[3,16,1536]{2,1,0:T(8,128)(2,1)S(1)} %bitcast.73), channel_id=1, source_target_pairs={{0,1},{1,2},{2,3},{4,5},{5,6},{6,7},{8,9},{9,10},{10,11},{12,13},{... | collective-permute-start | bytes 442376 | tf_op jit(solution)/shard_map/ppermute | solution.py:16
  35.7 5.3 %collective-permute-start.3 = (bf16[3,16,1536]{2,1,0:T(8,128)(2,1)S(1)}, bf16[3,16,1536]{2,1,0:T(8,128)(2,1)S(1)}, u32[]{:S(2)}, u32[]{:S(2)}) collective-permute-start(bf16[3,16,1536]{2,1,0:T(8,128)(2,1)S(1)} %bitcast.74), channel_id=1, source_target_pairs={{1,0},{2,1},{3,2},{5,4},{6,5},{7,6},{9,8},{10,9},{11,10},{13,12},{... | collective-permute-start | bytes 442376 | tf_op jit(solution)/shard_map/ppermute | solution.py:19
  37.0 16.6 %collective-permute-start.6 = (bf16[192,1536]{1,0:T(8,128)(2,1)S(1)}, bf16[192,1536]{1,0:T(8,128)(2,1)S(1)}, u32[]{:S(2)}, u32[]{:S(2)}) collective-permute-start(bf16[192,1536]{1,0:T(8,128)(2,1)S(1)} %collective-permute-done), channel_id=1, source_target_pairs={{0,8},{8,16},{16,24},{24,28},{28,20},{20,12},{12,4},{4,0},{1,9},{9... | collective-permute-start | bytes 1769480 | tf_op jit(solution)/shard_map/ppermute | solution.py:126
  38.9 16.3 %collective-permute-start.7 = (bf16[192,1536]{1,0:T(8,128)(2,1)S(1)}, bf16[192,1536]{1,0:T(8,128)(2,1)S(1)}, u32[]{:S(2)}, u32[]{:S(2)}) collective-permute-start(bf16[192,1536]{1,0:T(8,128)(2,1)S(1)} %collective-permute-done.1), channel_id=1, source_target_pairs={{0,4},{8,0},{16,8},{24,16},{28,24},{20,28},{12,20},{4,12},{1,5},{9... | collective-permute-start | bytes 1769480 | tf_op jit(solution)/shard_map/ppermute | solution.py:128
  44.9 70.7 %copy-start.47 = (f32[3,16]{1,0:T(4,128)}, f32[3,16]{1,0:T(4,128)S(1)}, u32[]{:S(2)}) copy-start(f32[3,16]{1,0:T(4,128)S(1)} %broadcast_multiply_fusion.2) | copy-start | bytes 580
  45.1 70.5 %copy-start.48 = (f32[3,16]{1,0:T(4,128)}, f32[3,16]{1,0:T(4,128)S(1)}, u32[]{:S(2)}) copy-start(f32[3,16]{1,0:T(4,128)S(1)} %add_rsqrt_fusion) | copy-start | bytes 580
  45.2 7.6 %collective-permute-start.4 = (bf16[1,3,16,1536]{3,2,1,0:T(8,128)(2,1)S(1)}, bf16[1,3,16,1536]{3,2,1,0:T(8,128)(2,1)S(1)}, u32[]{:S(2)}, u32[]{:S(2)}) collective-permute-start(bf16[1,3,16,1536]{3,2,1,0:T(8,128)(2,1)S(1)} %fusion.144), channel_id=1, source_target_pairs={{0,2},{1,3},{2,0},{3,1},{4,6},{5,7},{6,4},{7,5},{8,10},{9,11},{10,... | collective-permute-start | bytes 442376 | tf_op jit(solution)/shard_map/ppermute | solution.py:183
  52.8 2.9 %collective-permute-start.5 = (bf16[2,3,16,1536]{3,2,1,0:T(8,128)(2,1)S(1)}, bf16[2,3,16,1536]{3,2,1,0:T(8,128)(2,1)S(1)}, u32[]{:S(2)}, u32[]{:S(2)}) collective-permute-start(bf16[2,3,16,1536]{3,2,1,0:T(8,128)(2,1)S(1)} %maximum_select_fusion.2), channel_id=1, source_target_pairs={{0,1},{1,0},{2,3},{3,2},{4,5},{5,4},{6,7},{7,6},{8,9},{9,8},{10,11... | collective-permute-start | bytes 884744 | tf_op jit(solution)/shard_map/ppermute | solution.py:183
  53.6 15.3 %collective-permute-start.8 = (bf16[192,1536]{1,0:T(8,128)(2,1)S(1)}, bf16[192,1536]{1,0:T(8,128)(2,1)S(1)}, u32[]{:S(2)}, u32[]{:S(2)}) collective-permute-start(bf16[192,1536]{1,0:T(8,128)(2,1)S(1)} %collective-permute-done.6), channel_id=1, source_target_pairs={{0,8},{8,16},{16,24},{24,28},{28,20},{20,12},{12,4},{4,0},{1,9},{9... | collective-permute-start | bytes 1769480 | tf_op jit(solution)/shard_map/ppermute | solution.py:126
  55.2 15.4 %collective-permute-start.9 = (bf16[192,1536]{1,0:T(8,128)(2,1)S(1)}, bf16[192,1536]{1,0:T(8,128)(2,1)S(1)}, u32[]{:S(2)}, u32[]{:S(2)}) collective-permute-start(bf16[192,1536]{1,0:T(8,128)(2,1)S(1)} %collective-permute-done.7), channel_id=1, source_target_pairs={{0,4},{8,0},{16,8},{24,16},{28,24},{20,28},{12,20},{4,12},{1,5},{9... | collective-permute-start | bytes 1769480 | tf_op jit(solution)/shard_map/ppermute | solution.py:128
  69.0 8.2 %collective-permute-start.10 = (bf16[192,768]{1,0:T(8,128)(2,1)S(1)}, bf16[192,768]{1,0:T(8,128)(2,1)S(1)}, u32[]{:S(2)}, u32[]{:S(2)}) collective-permute-start(bf16[192,768]{1,0:T(8,128)(2,1)S(1)} %slice.744), channel_id=1, source_target_pairs={{0,8},{8,16},{16,24},{24,28},{28,20},{20,12},{12,4},{4,0},{1,9},{9... | collective-permute-start | bytes 884744 | tf_op jit(solution)/shard_map/ppermute | solution.py:117
  70.6 7.9 %collective-permute-start.11 = (bf16[192,768]{1,0:T(8,128)(2,1)S(1)}, bf16[192,768]{1,0:T(8,128)(2,1)S(1)}, u32[]{:S(2)}, u32[]{:S(2)}) collective-permute-start(bf16[192,768]{1,0:T(8,128)(2,1)S(1)} %slice.745), channel_id=1, source_target_pairs={{0,4},{8,0},{16,8},{24,16},{28,24},{20,28},{12,20},{4,12},{1,5},{9... | collective-permute-start | bytes 884744 | tf_op jit(solution)/shard_map/ppermute | solution.py:118
  103.2 1.6 collective-permute-start.12
  105.9 9.6 %collective-permute-start.13 = (f32[1,3,16,1536]{3,2,1,0:T(8,128)S(1)}, f32[1,3,16,1536]{3,2,1,0:T(8,128)S(1)}, u32[]{:S(2)}, u32[]{:S(2)}) collective-permute-start(f32[1,3,16,1536]{3,2,1,0:T(8,128)S(1)} %constant_dynamic-slice_fusion), channel_id=1, source_target_pairs={{0,2},{1,3},{2,0},{3,1},{4,6},{5,7},{6,4},{7,5},{8,10},{9,11},{10,... | collective-permute-start | bytes 884744 | tf_op jit(solution)/shard_map/ppermute | solution.py:69
  121.1 1.4 collective-permute-start.16
  123.0 4.5 %collective-permute-start.17 = (f32[18816]{0:T(1024)S(1)}, f32[18816]{0:T(1024)S(1)}, u32[]{:S(2)}, u32[]{:S(2)}) collective-permute-start(f32[18816]{0:T(1024)S(1)} %get-tuple-element.111), channel_id=1, source_target_pairs={{0,2},{1,3},{2,0},{3,1},{4,6},{5,7},{6,4},{7,5},{8,10},{9,11},{10,... | collective-permute-start | bytes 225800 | tf_op jit(solution)/shard_map/ppermute | solution.py:49
  127.9 37.7 %copy-start.8 = (f32[1536]{0:T(1024)S(1)}, f32[1536]{0:T(1024)}, u32[]{:S(2)}) copy-start(f32[1536]{0:T(1024)} %get-tuple-element.87) | copy-start | bytes 18436
  127.9 37.7 %copy-start.10 = (f32[1536]{0:T(1024)S(1)}, f32[1536]{0:T(1024)}, u32[]{:S(2)}) copy-start(f32[1536]{0:T(1024)} %get-tuple-element.88) | copy-start | bytes 18436
  127.9 37.7 %copy-start.12 = (f32[1536]{0:T(1024)S(1)}, f32[1536]{0:T(1024)}, u32[]{:S(2)}) copy-start(f32[1536]{0:T(1024)} %get-tuple-element.89) | copy-start | bytes 18436
  127.9 37.7 %copy-start.14 = (f32[1536]{0:T(1024)S(1)}, f32[1536]{0:T(1024)}, u32[]{:S(2)}) copy-start(f32[1536]{0:T(1024)} %get-tuple-element.90) | copy-start | bytes 18436
  127.9 37.7 %copy-start.16 = (f32[1536]{0:T(1024)S(1)}, f32[1536]{0:T(1024)}, u32[]{:S(2)}) copy-start(f32[1536]{0:T(1024)} %get-tuple-element.91) | copy-start | bytes 18436
  127.9 37.7 %copy-start.18 = (f32[1536]{0:T(1024)S(1)}, f32[1536]{0:T(1024)}, u32[]{:S(2)}) copy-start(f32[1536]{0:T(1024)} %get-tuple-element.92) | copy-start | bytes 18436
  127.9 37.7 %copy-start.20 = (f32[1536]{0:T(1024)S(1)}, f32[1536]{0:T(1024)}, u32[]{:S(2)}) copy-start(f32[1536]{0:T(1024)} %get-tuple-element.93) | copy-start | bytes 18436
  128.0 37.7 %copy-start.22 = (f32[1536]{0:T(1024)S(1)}, f32[1536]{0:T(1024)}, u32[]{:S(2)}) copy-start(f32[1536]{0:T(1024)} %get-tuple-element.94) | copy-start | bytes 18436
  128.0 37.7 %copy-start.24 = (f32[1536]{0:T(1024)S(1)}, f32[1536]{0:T(1024)}, u32[]{:S(2)}) copy-start(f32[1536]{0:T(1024)} %get-tuple-element.95) | copy-start | bytes 18436
  128.0 37.7 %copy-start.26 = (f32[1536]{0:T(1024)S(1)}, f32[1536]{0:T(1024)}, u32[]{:S(2)}) copy-start(f32[1536]{0:T(1024)} %copy-done.25) | copy-start | bytes 18436
  128.0 37.7 %copy-start.28 = (f32[1536]{0:T(1024)S(1)}, f32[1536]{0:T(1024)}, u32[]{:S(2)}) copy-start(f32[1536]{0:T(1024)} %copy-done.27) | copy-start | bytes 18436
  128.0 37.7 %copy-start.30 = (f32[1536]{0:T(1024)S(1)}, f32[1536]{0:T(1024)}, u32[]{:S(2)}) copy-start(f32[1536]{0:T(1024)} %copy-done.29) | copy-start | bytes 18436
  128.0 37.7 %copy-start.32 = (f32[1536]{0:T(1024)S(1)}, f32[1536]{0:T(1024)}, u32[]{:S(2)}) copy-start(f32[1536]{0:T(1024)} %copy-done.31) | copy-start | bytes 18436
  128.0 37.7 %copy-start.34 = (f32[1536]{0:T(1024)S(1)}, f32[1536]{0:T(1024)}, u32[]{:S(2)}) copy-start(f32[1536]{0:T(1024)} %copy-done.33) | copy-start | bytes 18436
  128.0 37.7 %copy-start.36 = (f32[1536]{0:T(1024)S(1)}, f32[1536]{0:T(1024)}, u32[]{:S(2)}) copy-start(f32[1536]{0:T(1024)} %copy-done.35) | copy-start | bytes 18436
  128.0 37.7 %copy-start.38 = (f32[1536]{0:T(1024)S(1)}, f32[1536]{0:T(1024)}, u32[]{:S(2)}) copy-start(f32[1536]{0:T(1024)} %copy-done.37) | copy-start | bytes 18436
  128.0 37.7 %copy-start.40 = (f32[1536]{0:T(1024)S(1)}, f32[1536]{0:T(1024)}, u32[]{:S(2)}) copy-start(f32[1536]{0:T(1024)} %copy-done.39) | copy-start | bytes 18436
  128.1 37.7 %copy-start.42 = (f32[1536]{0:T(1024)S(1)}, f32[1536]{0:T(1024)}, u32[]{:S(2)}) copy-start(f32[1536]{0:T(1024)} %copy-done.41) | copy-start | bytes 18436
  128.1 37.7 %copy-start.44 = (f32[1536]{0:T(1024)S(1)}, f32[1536]{0:T(1024)}, u32[]{:S(2)}) copy-start(f32[1536]{0:T(1024)} %copy-done.43) | copy-start | bytes 18436
  128.1 4.9 %collective-permute-start.18 = (f32[9408]{0:T(1024)S(1)}, f32[9408]{0:T(1024)S(1)}, u32[]{:S(2)}, u32[]{:S(2)}) collective-permute-start(f32[9408]{0:T(1024)S(1)} %get-tuple-element.120), channel_id=1, source_target_pairs={{0,4},{4,0},{8,12},{12,8},{16,20},{20,16},{24,28},{28,24},{1,5},{5... | collective-permute-start | bytes 112904 | tf_op jit(solution)/shard_map/ppermute | solution.py:49
  133.2 5.3 %collective-permute-start.19 = (f32[4704]{0:T(1024)S(1)}, f32[4704]{0:T(1024)S(1)}, u32[]{:S(2)}, u32[]{:S(2)}) collective-permute-start(f32[4704]{0:T(1024)S(1)} %get-tuple-element.122), channel_id=1, source_target_pairs={{0,8},{4,12},{8,0},{12,4},{16,24},{20,28},{24,16},{28,20},{1,9},{5... | collective-permute-start | bytes 56456 | tf_op jit(solution)/shard_map/ppermute | solution.py:49
  138.7 6.1 %collective-permute-start.20 = (f32[2352]{0:T(1024)S(1)}, f32[2352]{0:T(1024)S(1)}, u32[]{:S(2)}, u32[]{:S(2)}) collective-permute-start(f32[2352]{0:T(1024)S(1)} %get-tuple-element.124), channel_id=1, source_target_pairs={{0,16},{4,20},{8,24},{12,28},{16,0},{20,4},{24,8},{28,12},{1,17},{... | collective-permute-start | bytes 28232 | tf_op jit(solution)/shard_map/ppermute | solution.py:49
  144.8 4.7 %collective-permute-start.21 = (f32[2352]{0:T(1024)S(1)}, f32[2352]{0:T(1024)S(1)}, u32[]{:S(2)}, u32[]{:S(2)}) collective-permute-start(f32[2352]{0:T(1024)S(1)} %add.722), channel_id=1, source_target_pairs={{0,16},{4,20},{8,24},{12,28},{16,0},{20,4},{24,8},{28,12},{1,17},{... | collective-permute-start | bytes 28232 | tf_op jit(solution)/shard_map/ppermute | solution.py:52
  149.6 3.8 %collective-permute-start.22 = (f32[4704]{0:T(1024)S(1)}, f32[4704]{0:T(1024)S(1)}, u32[]{:S(2)}, u32[]{:S(2)}) collective-permute-start(f32[4704]{0:T(1024)S(1)} %maximum_select_fusion.6), channel_id=1, source_target_pairs={{0,8},{4,12},{8,0},{12,4},{16,24},{20,28},{24,16},{28,20},{1,9},{5... | collective-permute-start | bytes 56456 | tf_op jit(solution)/shard_map/ppermute | solution.py:52
  153.5 4.1 %collective-permute-start.23 = (f32[9408]{0:T(1024)S(1)}, f32[9408]{0:T(1024)S(1)}, u32[]{:S(2)}, u32[]{:S(2)}) collective-permute-start(f32[9408]{0:T(1024)S(1)} %maximum_select_fusion.5), channel_id=1, source_target_pairs={{0,4},{4,0},{8,12},{12,8},{16,20},{20,16},{24,28},{28,24},{1,5},{5... | collective-permute-start | bytes 112904 | tf_op jit(solution)/shard_map/ppermute | solution.py:52
  153.9 7.3 %collective-permute-start.14 = (bf16[3,16,1536]{2,1,0:T(8,128)(2,1)S(1)}, bf16[3,16,1536]{2,1,0:T(8,128)(2,1)S(1)}, u32[]{:S(2)}, u32[]{:S(2)}) collective-permute-start(bf16[3,16,1536]{2,1,0:T(8,128)(2,1)S(1)} %get-tuple-element.130), channel_id=1, source_target_pairs={{0,1},{1,2},{2,3},{4,5},{5,6},{6,7},{8,9},{9,10},{10,11},{12,13},{... | collective-permute-start | bytes 442376 | tf_op jit(solution)/shard_map/ppermute | solution.py:16
  155.2 6.1 %collective-permute-start.15 = (bf16[3,16,1536]{2,1,0:T(8,128)(2,1)S(1)}, bf16[3,16,1536]{2,1,0:T(8,128)(2,1)S(1)}, u32[]{:S(2)}, u32[]{:S(2)}) collective-permute-start(bf16[3,16,1536]{2,1,0:T(8,128)(2,1)S(1)} %get-tuple-element.130), channel_id=1, source_target_pairs={{1,0},{2,1},{3,2},{5,4},{6,5},{7,6},{9,8},{10,9},{11,10},{13,12},{... | collective-permute-start | bytes 442376 | tf_op jit(solution)/shard_map/ppermute | solution.py:19
  157.7 7.8 %collective-permute-start.24 = (f32[18816]{0:T(1024)S(1)}, f32[18816]{0:T(1024)S(1)}, u32[]{:S(2)}, u32[]{:S(2)}) collective-permute-start(f32[18816]{0:T(1024)S(1)} %maximum_select_fusion.4), channel_id=1, source_target_pairs={{0,2},{1,3},{2,0},{3,1},{4,6},{5,7},{6,4},{7,5},{8,10},{9,11},{10,... | collective-permute-start | bytes 225800 | tf_op jit(solution)/shard_map/ppermute | solution.py:52
  165.5 3.1 %collective-permute-start.25 = (f32[37632]{0:T(1024)S(1)}, f32[37632]{0:T(1024)S(1)}, u32[]{:S(2)}, u32[]{:S(2)}) collective-permute-start(f32[37632]{0:T(1024)S(1)} %maximum_select_fusion.3), channel_id=1, source_target_pairs={{0,1},{1,0},{2,3},{3,2},{4,5},{5,4},{6,7},{7,6},{8,9},{9,8},{10,11... | collective-permute-start | bytes 451592 | tf_op jit(solution)/shard_map/ppermute | solution.py:52
  (35 other events, 240.4 us)
Sparse Core Ops, SparseCore 0:
  99.3 97.3 reduce-scatter.1

commit v18 on v14

--- a/solution.py
+++ b/solution.py
@@ -273,7 +273,7 @@
     slab = frames[0]
     chans = slab.shape[2]
     staged = jnp.where(up_weight == up_weight, up_weight, jnp.zeros_like(up_weight))
-    columns, slab = ring_all_gather(staged, "fsdp", ring, slab)
+    columns, _ = ring_all_gather(staged, "fsdp", ring)
     padded = extended(slab, (("rows", 0),), 3)
     activation_rows = conv_rows(padded, kernel, kernel_bias)
     normed_output, standardized_input, inverse_deviation = apply_layer_norm(

time: 206 us -> 221 us (1.073)
  local copies, waits for them, and re-layouts: 9.73 us -> 16.1 us
  waiting for transfers between devices: 90.4 us -> 96.2 us
  matrix products: 12.4 us -> 14.9 us
    ppermute x3, waiting for transfers between devices: 6.79 us -> 16.1 us  [ring_all_gather(): cw = lax.ppermute(cw, axis, forward)]
    ppermute x1, waiting for transfers between devices: 7.31 us -> 3.28 us  [ring_all_gather(): lax.ppermute(cw[..., :half], axis, forward)]
    dot_general x1, matrix products: 4.85 us -> 7.34 us  [body(): pre = jnp.dot(flat, columns, preferred_element_type=jnp.float32) + up_bias]
    dynamic_update_slice x3, local copies, waits for them, and re-layouts: 0.13 us -> 2.62 us  [ring_all_gather(): lax.dynamic_update_index_in_dim(gathered, ccw, ring_arr[(spot + s) % coun...]
    dynamic_update_slice x3, local copies, waits for them, and re-layouts: 0.13 us -> 2.59 us  [ring_all_gather(): lax.dynamic_update_index_in_dim(gathered, cw, ring_arr[(spot - s) % count...]
  transfers between devices with their start and end apart: 27 -> 27, of which waited for: 21 -> 18; matrix products, arithmetic and copies ran while one was open for 11% -> 14% of each run, Pallas kernels for 0% -> 0%
where the time goes in v18:
time: 221 us
  waiting for transfers between devices  96.2 us (44%)
  between operations  35.7 us (16%)
  starting transfers between devices  31.2 us (14%)
  other arithmetic  19.9 us (9%)
  local copies, waits for them, and re-layouts  16.1 us (7%)
  matrix products  14.9 us (7%)
  blocking collectives  6.52 us (3%)
    reduce_scatter x1, waiting for transfers between devices, body(): lax.psum_scatter(w_term.astype(jnp.bfloat16), 'fsdp', scatter_dimension=0...  29.2 us
    ppermute x5, waiting for transfers between devices, tree_allreduce(): flat = keep + lax.ppermute(give, axis, perm)  16.7 us
    ppermute x3, waiting for transfers between devices, ring_all_gather(): cw = lax.ppermute(cw, axis, forward)  16.1 us
    ppermute x5, waiting for transfers between devices, tree_allreduce(): other = lax.ppermute(flat, axis, perm)  11.6 us
    ppermute x2, waiting for transfers between devices, tree_reduce_scatter(): lax.ppermute(give, axis, perm).astype(jnp.float32)  9.4 us
    dot_general x1, matrix products, body(): pre = jnp.dot(flat, columns, preferred_element_type=jnp.float32) + up_bias  7.34 us
    psum x1, blocking collectives, body(): norm_total = lax.psum(jnp.sum(norms), 'rows')  6.52 us
    ppermute x3, starting transfers between devices, ring_all_gather(): cw = lax.ppermute(cw, axis, forward)  6.22 us
  transfers between devices with their start and end apart: 27, of which 18 were waited for; matrix products, arithmetic and copies ran while one was open for 14% of the time, Pallas kernels for 0%

profile of v18, /device:TPU:0, one launch (start us, length us, event | category | flops | bytes accessed | tf_op | source)
XLA Modules:
  0.0 220.5 jit_solution(8525283628260805872)
XLA Ops:
  7.2 1.2 compare_select_fusion
  8.4 3.1 %collective-permute-start.4 = (bf16[192,1536]{1,0:T(8,128)(2,1)S(1)}, bf16[192,1536]{1,0:T(8,128)(2,1)S(1)}, u32[]{:S(2)}, u32[]{:S(2)}) collective-permute-start(bf16[192,1536]{1,0:T(8,128)(2,1)S(1)} %compare_select_fusion), channel_id=1, source_target_pairs={{0,8},{8,16},{16,24},{24,28},{28,20},{20,12},{12,4},{4,0},{1,9},{9... | collective-permute-start | bytes 1769480 | tf_op jit(solution)/shard_map/ppermute | solution.py:126
  11.5 1.5 collective-permute-start
  12.9 1.3 collective-permute-start.1
  15.5 2.7 %collective-permute-done.1 = bf16[3,16,1536]{2,1,0:T(8,128)(2,1)S(1)} collective-permute-done((bf16[3,16,1536]{2,1,0:T(8,128)(2,1)S(1)}, bf16[3,16,1536]{2,1,0:T(8,128)(2,1)S(1)}, u32[]{:S(2)}, u32[]{:S(2)}) %collective-permute-start.1) | collective-permute-done | bytes 147488 | tf_op jit(solution)/shard_map/ppermute | solution.py:19
  18.5 4.1 %fusion.155 = (f32[3,16]{1,0:T(4,128)S(1)}, f32[3,16,1536]{2,1,0:T(8,128)S(1)}) fusion(f32[1536]{0:T(1024)S(1)} %get-tuple-element.99, bf16[9,22,1536]{2,1,0:T(8,128)(2,1)S(1)} %select_maximum_fusion.2, f32[1536]{0:T(1024)S(1)} %get-tuple-element.100, f32[1536]{0:T(1024)S(1)} %get-tuple-element.53, f32[1536]{0:T(1024)S(1)} %get-tuple-element.54, ...), kind=kLoop, calls=%fused_computation.379 | loop fusion | flops 11206608 | bytes 7237824 | tf_op jit(solution)/shard_map/reduce_sum | solution.py:228
  24.2 4.1 %collective-permute-start.2 = (bf16[1,3,16,1536]{3,2,1,0:T(8,128)(2,1)S(1)}, bf16[1,3,16,1536]{3,2,1,0:T(8,128)(2,1)S(1)}, u32[]{:S(2)}, u32[]{:S(2)}) collective-permute-start(bf16[1,3,16,1536]{3,2,1,0:T(8,128)(2,1)S(1)} %fusion.144), channel_id=1, source_target_pairs={{0,1},{1,0},{2,3},{3,2},{4,5},{5,4},{6,7},{7,6},{8,9},{9,8},{10,11... | collective-permute-start | bytes 442376 | tf_op jit(solution)/shard_map/ppermute | solution.py:182
  28.3 2.6 %broadcast_in_dim.49 = bf16[8,192,1536]{2,1,0:T(8,128)(2,1)} broadcast(bf16[]{:T(256)} %constant.257.clone.1), dimensions={} | broadcast | bytes 4718594 | tf_op jit(solution)/shard_map/broadcast_in_dim | solution.py:107
  30.8 1.0 bitcast_dynamic-update-slice_fusion.6
  37.1 1.6 fusion.157
  52.4 1.6 collective-permute-start.6
  55.4 5.9 %collective-permute-done.3 = bf16[2,3,16,1536]{3,2,1,0:T(8,128)(2,1)S(1)} collective-permute-done((bf16[2,3,16,1536]{3,2,1,0:T(8,128)(2,1)S(1)}, bf16[2,3,16,1536]{3,2,1,0:T(8,128)(2,1)S(1)}, u32[]{:S(2)}, u32[]{:S(2)}) %collective-permute-start.3) | collective-permute-done | bytes 294944 | tf_op jit(solution)/shard_map/ppermute | solution.py:182
  62.3 5.4 %collective-permute-done.6 = bf16[192,1536]{1,0:T(8,128)(2,1)S(1)} collective-permute-done((bf16[192,1536]{1,0:T(8,128)(2,1)S(1)}, bf16[192,1536]{1,0:T(8,128)(2,1)S(1)}, u32[]{:S(2)}, u32[]{:S(2)}) %collective-permute-start.6) | collective-permute-done | bytes 589856 | tf_op jit(solution)/shard_map/ppermute | solution.py:126
  67.7 1.5 collective-permute-start.8
  71.5 10.6 %collective-permute-done.8 = bf16[192,1536]{1,0:T(8,128)(2,1)S(1)} collective-permute-done((bf16[192,1536]{1,0:T(8,128)(2,1)S(1)}, bf16[192,1536]{1,0:T(8,128)(2,1)S(1)}, u32[]{:S(2)}, u32[]{:S(2)}) %collective-permute-start.8) | collective-permute-done | bytes 589856 | tf_op jit(solution)/shard_map/ppermute | solution.py:126
  82.1 1.6 collective-permute-start.10
  86.1 3.3 %collective-permute-done.10 = bf16[192,768]{1,0:T(8,128)(2,1)S(1)} collective-permute-done((bf16[192,768]{1,0:T(8,128)(2,1)S(1)}, bf16[192,768]{1,0:T(8,128)(2,1)S(1)}, u32[]{:S(2)}, u32[]{:S(2)}) %collective-permute-start.10) | collective-permute-done | bytes 294944 | tf_op jit(solution)/shard_map/ppermute | solution.py:117
  89.3 1.3 collective-permute-done.11
  90.7 0.9 fusion.19
  91.7 7.3 %fusion.4 = (f32[1536]{0:T(1024)S(1)}, f32[1536]{0:T(1024)S(1)}, f32[192,1536]{1,0:T(8,128)}, f32[192,1536]{1,0:T(8,128)}) fusion(bf16[1,12,16,1536]{3,2,1,0:T(8,128)(2,1)S(1)} %copy-done.2, f32[1536]{0:T(1024)S(1)} %copy-done.89, bf16[192,1536]{1,0:T(8,128)(2,1)S(1)} %bitcast.65, bf16[1536,1536]{1,0:T(8,128)(2,1)} %bitcast.25), kind=kOutput, calls=%fused_computation.64 | convolution fusion | flops 926610432 | bytes 8275968 | tf_op jit(solution)/shard_map/dot_general | solution.py:286
  99.7 6.5 %all-reduce.2 = (f32[]{:T(128)}, f32[]{:T(128)}) all-reduce(f32[]{:T(128)} %get-tuple-element.125, f32[]{:T(128)} %get-tuple-element.124), channel_id=1, replica_groups=mesh['fsdp'=8,'rows'=4] {'rows'}, use_global_device_ids=true, to_apply=%region_4.5 | all-reduce | flops 2 | bytes 16 | tf_op jit(solution)/shard_map/psum | solution.py:291
  107.6 3.2 %fusion.3 = (bf16[192,1536]{1,0:T(8,128)(2,1)S(1)}, bf16[192,1536]{1,0:T(8,128)(2,1)}) fusion(f32[192,1536]{1,0:T(8,128)} %get-tuple-element.145, f32[192,1536]{1,0:T(8,128)} %get-tuple-element.132, bf16[1,12,16,1536]{3,2,1,0:T(8,128)(2,1)S(1)} %copy-done.2, f32[1536]{0:T(1024)S(1)} %get-tuple-element.137, f32[1536]{0:T(1024)S(1)} %get-tuple-element.130, ...), kind=kLoop, calls=%fused_computation.63 | loop fusion | flops 5603328 | bytes 4159488 | tf_op jit(solution)/shard_map/convert_element_type | solution.py:298
  110.8 3.5 %convolution_convert_fusion = bf16[1536,1536]{1,0:T(8,128)(2,1)} fusion(bf16[192,1536]{1,0:T(8,128)(2,1)S(1)} %bitcast.66, bf16[192,1536]{1,0:T(8,128)(2,1)S(1)} %get-tuple-element.135), kind=kOutput, calls=%fused_computation | convolution fusion | flops 908328960 | bytes 5898240 | tf_op jit(solution)/shard_map/dot_general | solution.py:299
  114.4 4.0 %convolution_convert_fusion.1 = bf16[12,16,1536]{2,1,0:T(8,128)(2,1)S(1)} fusion(bf16[12,16,1536]{2,1,0:T(8,128)(2,1)S(1)} %bitcast.67, bf16[1536,1536,1]{1,0,2:T(8,128)(2,1)} %bitcast.30), kind=kOutput, calls=%fused_computation.52 | convolution fusion | flops 906264576 | bytes 5898240 | tf_op jit(solution)/shard_map/hwf,cf->hwc/dot_general | solution.py:306
  118.6 1.6 collective-permute-done.12
  120.2 1.3 collective-permute-start.13
  121.5 7.8 %collective-permute-done.13 = f32[1,3,16,1536]{3,2,1,0:T(8,128)S(1)} collective-permute-done((f32[1,3,16,1536]{3,2,1,0:T(8,128)S(1)}, f32[1,3,16,1536]{3,2,1,0:T(8,128)S(1)}, u32[]{:S(2)}, u32[]{:S(2)}) %collective-permute-start.13) | collective-permute-done | bytes 294944 | tf_op jit(solution)/shard_map/ppermute | solution.py:69
  129.6 0.9 fusion.141
  134.3 1.4 collective-permute-done.16
  136.2 1.3 collective-permute-start.17
  137.4 3.2 %collective-permute-done.17 = f32[18816]{0:T(1024)S(1)} collective-permute-done((f32[18816]{0:T(1024)S(1)}, f32[18816]{0:T(1024)S(1)}, u32[]{:S(2)}, u32[]{:S(2)}) %collective-permute-start.17) | collective-permute-done | bytes 75296 | tf_op jit(solution)/shard_map/ppermute | solution.py:49
  141.9 4.4 %collective-permute-done.18 = f32[9408]{0:T(1024)S(1)} collective-permute-done((f32[9408]{0:T(1024)S(1)}, f32[9408]{0:T(1024)S(1)}, u32[]{:S(2)}, u32[]{:S(2)}) %collective-permute-start.18) | collective-permute-done | bytes 37664 | tf_op jit(solution)/shard_map/ppermute | solution.py:49
  146.5 1.4 collective-permute-start.19
  147.9 3.9 %collective-permute-done.19 = f32[4704]{0:T(1024)S(1)} collective-permute-done((f32[4704]{0:T(1024)S(1)}, f32[4704]{0:T(1024)S(1)}, u32[]{:S(2)}, u32[]{:S(2)}) %collective-permute-start.19) | collective-permute-done | bytes 18848 | tf_op jit(solution)/shard_map/ppermute | solution.py:49
  152.0 1.7 collective-permute-start.20
  153.7 3.8 %collective-permute-done.20 = f32[2352]{0:T(1024)S(1)} collective-permute-done((f32[2352]{0:T(1024)S(1)}, f32[2352]{0:T(1024)S(1)}, u32[]{:S(2)}, u32[]{:S(2)}) %collective-permute-start.20) | collective-permute-done | bytes 9440 | tf_op jit(solution)/shard_map/ppermute | solution.py:49
  157.5 1.3 collective-permute-start.21
  158.8 3.8 %collective-permute-done.21 = f32[2352]{0:T(1024)S(1)} collective-permute-done((f32[2352]{0:T(1024)S(1)}, f32[2352]{0:T(1024)S(1)}, u32[]{:S(2)}, u32[]{:S(2)}) %collective-permute-start.21) | collective-permute-done | bytes 9440 | tf_op jit(solution)/shard_map/ppermute | solution.py:52
  162.6 1.3 collective-permute-start.22
  163.9 2.5 %collective-permute-done.22 = f32[4704]{0:T(1024)S(1)} collective-permute-done((f32[4704]{0:T(1024)S(1)}, f32[4704]{0:T(1024)S(1)}, u32[]{:S(2)}, u32[]{:S(2)}) %collective-permute-start.22) | collective-permute-done | bytes 18848 | tf_op jit(solution)/shard_map/ppermute | solution.py:52
  166.7 1.3 collective-permute-start.14
  167.9 1.3 collective-permute-start.15
  169.2 1.3 collective-permute-done.23
  170.7 3.3 %collective-permute-start.24 = (f32[18816]{0:T(1024)S(1)}, f32[18816]{0:T(1024)S(1)}, u32[]{:S(2)}, u32[]{:S(2)}) collective-permute-start(f32[18816]{0:T(1024)S(1)} %maximum_select_fusion.4), channel_id=1, source_target_pairs={{0,2},{1,3},{2,0},{3,1},{4,6},{5,7},{6,4},{7,5},{8,10},{9,11},{10,... | collective-permute-start | bytes 225800 | tf_op jit(solution)/shard_map/ppermute | solution.py:52
  174.2 4.0 %collective-permute-done.24 = f32[18816]{0:T(1024)S(1)} collective-permute-done((f32[18816]{0:T(1024)S(1)}, f32[18816]{0:T(1024)S(1)}, u32[]{:S(2)}, u32[]{:S(2)}) %collective-permute-start.24) | collective-permute-done | bytes 75296 | tf_op jit(solution)/shard_map/ppermute | solution.py:52
  178.7 2.8 %fusion.149 = bf16[1,3,16,1536]{3,2,1,0:T(8,128)(2,1)} fusion(f32[1536]{0:T(1024)S(1)} %copy-done.40, bf16[9,22,1536]{2,1,0:T(8,128)(2,1)S(1)} %select_maximum_fusion, f32[1536]{0:T(1024)S(1)} %copy-done.42, f32[1536]{0:T(1024)S(1)} %get-tuple-element.53, f32[1536]{0:T(1024)S(1)} %get-tuple-element.54, bf16[3,16,1536]{2,1,0:T(8,128)(2,1)S(1)} %collective-permute-done.14, ...), kind=kLoop, calls=%fused_computation.306 | loop fusion | flops 11132928 | bytes 7084032 | tf_op jit(solution)/shard_map/reshape | solution.py:321
  182.3 29.2 %reduce-scatter.2.cloned.1.call-done = bf16[192,1536]{1,0:T(8,128)(2,1)} async-done(((bf16[1536,1536]{1,0:T(8,128)(2,1)}), bf16[192,1536]{1,0:T(8,128)(2,1)}) %reduce-scatter.2.cloned.1.call-update) | async-done | bytes 589840 | tf_op jit(solution)/shard_map/reduce_scatter | solution.py:302
  211.5 2.2 %convert_element_type.497 = f32[192,1536]{1,0:T(8,128)} convert(bf16[192,1536]{1,0:T(8,128)(2,1)} %reduce-scatter.2.cloned.1.call-done) | non-fusion elementwise | flops 294912 | bytes 1769472 | tf_op jit(solution)/shard_map/convert_element_type | solution.py:304
  (303 shorter events, 18.0 us)
Async XLA Ops:
  7.2 204.3 %reduce-scatter.2.cloned.1.call-start = ((), (), s32[]{:S(2)}) async-start(), calls=%async_computation.1 | async-start | bytes 5308416 | tf_op jit(solution)/shard_map/reduce_scatter | solution.py:302
  8.4 44.0 %collective-permute-start.4 = (bf16[192,1536]{1,0:T(8,128)(2,1)S(1)}, bf16[192,1536]{1,0:T(8,128)(2,1)S(1)}, u32[]{:S(2)}, u32[]{:S(2)}) collective-permute-start(bf16[192,1536]{1,0:T(8,128)(2,1)S(1)} %compare_select_fusion), channel_id=1, source_target_pairs={{0,8},{8,16},{16,24},{24,28},{28,20},{20,12},{12,4},{4,0},{1,9},{9... | collective-permute-start | bytes 1769480 | tf_op jit(solution)/shard_map/ppermute | solution.py:126
  11.5 42.5 %collective-permute-start.5 = (bf16[192,1536]{1,0:T(8,128)(2,1)S(1)}, bf16[192,1536]{1,0:T(8,128)(2,1)S(1)}, u32[]{:S(2)}, u32[]{:S(2)}) collective-permute-start(bf16[192,1536]{1,0:T(8,128)(2,1)S(1)} %compare_select_fusion), channel_id=1, source_target_pairs={{0,4},{8,0},{16,8},{24,16},{28,24},{20,28},{12,20},{4,12},{1,5},{9... | collective-permute-start | bytes 1769480 | tf_op jit(solution)/shard_map/ppermute | solution.py:128
  11.5 4.0 %collective-permute-start = (bf16[3,16,1536]{2,1,0:T(8,128)(2,1)S(1)}, bf16[3,16,1536]{2,1,0:T(8,128)(2,1)S(1)}, u32[]{:S(2)}, u32[]{:S(2)}) collective-permute-start(bf16[3,16,1536]{2,1,0:T(8,128)(2,1)S(1)} %bitcast.68), channel_id=1, source_target_pairs={{0,1},{1,2},{2,3},{4,5},{5,6},{6,7},{8,9},{9,10},{10,11},{12,13},{... | collective-permute-start | bytes 442376 | tf_op jit(solution)/shard_map/ppermute | solution.py:16
  12.9 5.3 %collective-permute-start.1 = (bf16[3,16,1536]{2,1,0:T(8,128)(2,1)S(1)}, bf16[3,16,1536]{2,1,0:T(8,128)(2,1)S(1)}, u32[]{:S(2)}, u32[]{:S(2)}) collective-permute-start(bf16[3,16,1536]{2,1,0:T(8,128)(2,1)S(1)} %bitcast.69), channel_id=1, source_target_pairs={{1,0},{2,1},{3,2},{5,4},{6,5},{7,6},{9,8},{10,9},{11,10},{13,12},{... | collective-permute-start | bytes 442376 | tf_op jit(solution)/shard_map/ppermute | solution.py:19
  24.2 28.1 %collective-permute-start.2 = (bf16[1,3,16,1536]{3,2,1,0:T(8,128)(2,1)S(1)}, bf16[1,3,16,1536]{3,2,1,0:T(8,128)(2,1)S(1)}, u32[]{:S(2)}, u32[]{:S(2)}) collective-permute-start(bf16[1,3,16,1536]{3,2,1,0:T(8,128)(2,1)S(1)} %fusion.144), channel_id=1, source_target_pairs={{0,1},{1,0},{2,3},{3,2},{4,5},{5,4},{6,7},{7,6},{8,9},{9,8},{10,11... | collective-permute-start | bytes 442376 | tf_op jit(solution)/shard_map/ppermute | solution.py:182
  52.3 9.0 %collective-permute-start.3 = (bf16[2,3,16,1536]{3,2,1,0:T(8,128)(2,1)S(1)}, bf16[2,3,16,1536]{3,2,1,0:T(8,128)(2,1)S(1)}, u32[]{:S(2)}, u32[]{:S(2)}) collective-permute-start(bf16[2,3,16,1536]{3,2,1,0:T(8,128)(2,1)S(1)} %maximum_select_fusion.2), channel_id=1, source_target_pairs={{0,2},{1,3},{2,0},{3,1},{4,6},{5,7},{6,4},{7,5},{8,10},{9,11},{10,... | collective-permute-start | bytes 884744 | tf_op jit(solution)/shard_map/ppermute | solution.py:182
  52.4 15.3 %collective-permute-start.6 = (bf16[192,1536]{1,0:T(8,128)(2,1)S(1)}, bf16[192,1536]{1,0:T(8,128)(2,1)S(1)}, u32[]{:S(2)}, u32[]{:S(2)}) collective-permute-start(bf16[192,1536]{1,0:T(8,128)(2,1)S(1)} %collective-permute-done.4), channel_id=1, source_target_pairs={{0,8},{8,16},{16,24},{24,28},{28,20},{20,12},{12,4},{4,0},{1,9},{9... | collective-permute-start | bytes 1769480 | tf_op jit(solution)/shard_map/ppermute | solution.py:126
  54.0 15.2 %collective-permute-start.7 = (bf16[192,1536]{1,0:T(8,128)(2,1)S(1)}, bf16[192,1536]{1,0:T(8,128)(2,1)S(1)}, u32[]{:S(2)}, u32[]{:S(2)}) collective-permute-start(bf16[192,1536]{1,0:T(8,128)(2,1)S(1)} %collective-permute-done.5), channel_id=1, source_target_pairs={{0,4},{8,0},{16,8},{24,16},{28,24},{20,28},{12,20},{4,12},{1,5},{9... | collective-permute-start | bytes 1769480 | tf_op jit(solution)/shard_map/ppermute | solution.py:128
  67.7 14.4 %collective-permute-start.8 = (bf16[192,1536]{1,0:T(8,128)(2,1)S(1)}, bf16[192,1536]{1,0:T(8,128)(2,1)S(1)}, u32[]{:S(2)}, u32[]{:S(2)}) collective-permute-start(bf16[192,1536]{1,0:T(8,128)(2,1)S(1)} %collective-permute-done.6), channel_id=1, source_target_pairs={{0,8},{8,16},{16,24},{24,28},{28,20},{20,12},{12,4},{4,0},{1,9},{9... | collective-permute-start | bytes 1769480 | tf_op jit(solution)/shard_map/ppermute | solution.py:126
  69.3 14.5 %collective-permute-start.9 = (bf16[192,1536]{1,0:T(8,128)(2,1)S(1)}, bf16[192,1536]{1,0:T(8,128)(2,1)S(1)}, u32[]{:S(2)}, u32[]{:S(2)}) collective-permute-start(bf16[192,1536]{1,0:T(8,128)(2,1)S(1)} %collective-permute-done.7), channel_id=1, source_target_pairs={{0,4},{8,0},{16,8},{24,16},{28,24},{20,28},{12,20},{4,12},{1,5},{9... | collective-permute-start | bytes 1769480 | tf_op jit(solution)/shard_map/ppermute | solution.py:128
  82.1 7.2 %collective-permute-start.10 = (bf16[192,768]{1,0:T(8,128)(2,1)S(1)}, bf16[192,768]{1,0:T(8,128)(2,1)S(1)}, u32[]{:S(2)}, u32[]{:S(2)}) collective-permute-start(bf16[192,768]{1,0:T(8,128)(2,1)S(1)} %slice.744), channel_id=1, source_target_pairs={{0,8},{8,16},{16,24},{24,28},{28,20},{20,12},{12,4},{4,0},{1,9},{9... | collective-permute-start | bytes 884744 | tf_op jit(solution)/shard_map/ppermute | solution.py:117
  83.8 6.9 %collective-permute-start.11 = (bf16[192,768]{1,0:T(8,128)(2,1)S(1)}, bf16[192,768]{1,0:T(8,128)(2,1)S(1)}, u32[]{:S(2)}, u32[]{:S(2)}) collective-permute-start(bf16[192,768]{1,0:T(8,128)(2,1)S(1)} %slice.745), channel_id=1, source_target_pairs={{0,4},{8,0},{16,8},{24,16},{28,24},{20,28},{12,20},{4,12},{1,5},{9... | collective-permute-start | bytes 884744 | tf_op jit(solution)/shard_map/ppermute | solution.py:118
  118.5 1.6 collective-permute-start.12
  120.2 9.1 %collective-permute-start.13 = (f32[1,3,16,1536]{3,2,1,0:T(8,128)S(1)}, f32[1,3,16,1536]{3,2,1,0:T(8,128)S(1)}, u32[]{:S(2)}, u32[]{:S(2)}) collective-permute-start(f32[1,3,16,1536]{3,2,1,0:T(8,128)S(1)} %constant_dynamic-slice_fusion), channel_id=1, source_target_pairs={{0,2},{1,3},{2,0},{3,1},{4,6},{5,7},{6,4},{7,5},{8,10},{9,11},{10,... | collective-permute-start | bytes 884744 | tf_op jit(solution)/shard_map/ppermute | solution.py:69
  134.2 1.4 collective-permute-start.16
  136.2 4.5 %collective-permute-start.17 = (f32[18816]{0:T(1024)S(1)}, f32[18816]{0:T(1024)S(1)}, u32[]{:S(2)}, u32[]{:S(2)}) collective-permute-start(f32[18816]{0:T(1024)S(1)} %get-tuple-element.109), channel_id=1, source_target_pairs={{0,2},{1,3},{2,0},{3,1},{4,6},{5,7},{6,4},{7,5},{8,10},{9,11},{10,... | collective-permute-start | bytes 225800 | tf_op jit(solution)/shard_map/ppermute | solution.py:49
  141.0 37.3 %copy-start.6 = (f32[1536]{0:T(1024)S(1)}, f32[1536]{0:T(1024)}, u32[]{:S(2)}) copy-start(f32[1536]{0:T(1024)} %copy-done.5) | copy-start | bytes 18436
  141.0 37.3 %copy-start.8 = (f32[1536]{0:T(1024)S(1)}, f32[1536]{0:T(1024)}, u32[]{:S(2)}) copy-start(f32[1536]{0:T(1024)} %copy-done.7) | copy-start | bytes 18436
  141.0 37.3 %copy-start.10 = (f32[1536]{0:T(1024)S(1)}, f32[1536]{0:T(1024)}, u32[]{:S(2)}) copy-start(f32[1536]{0:T(1024)} %copy-done.9) | copy-start | bytes 18436
  141.0 37.3 %copy-start.12 = (f32[1536]{0:T(1024)S(1)}, f32[1536]{0:T(1024)}, u32[]{:S(2)}) copy-start(f32[1536]{0:T(1024)} %copy-done.11) | copy-start | bytes 18436
  141.0 37.3 %copy-start.14 = (f32[1536]{0:T(1024)S(1)}, f32[1536]{0:T(1024)}, u32[]{:S(2)}) copy-start(f32[1536]{0:T(1024)} %copy-done.13) | copy-start | bytes 18436
  141.0 37.3 %copy-start.16 = (f32[1536]{0:T(1024)S(1)}, f32[1536]{0:T(1024)}, u32[]{:S(2)}) copy-start(f32[1536]{0:T(1024)} %copy-done.15) | copy-start | bytes 18436
  141.1 37.3 %copy-start.18 = (f32[1536]{0:T(1024)S(1)}, f32[1536]{0:T(1024)}, u32[]{:S(2)}) copy-start(f32[1536]{0:T(1024)} %copy-done.17) | copy-start | bytes 18436
  141.1 37.3 %copy-start.20 = (f32[1536]{0:T(1024)S(1)}, f32[1536]{0:T(1024)}, u32[]{:S(2)}) copy-start(f32[1536]{0:T(1024)} %copy-done.19) | copy-start | bytes 18436
  141.1 37.3 %copy-start.22 = (f32[1536]{0:T(1024)S(1)}, f32[1536]{0:T(1024)}, u32[]{:S(2)}) copy-start(f32[1536]{0:T(1024)} %copy-done.21) | copy-start | bytes 18436
  141.1 37.3 %copy-start.24 = (f32[1536]{0:T(1024)S(1)}, f32[1536]{0:T(1024)}, u32[]{:S(2)}) copy-start(f32[1536]{0:T(1024)} %copy-done.23) | copy-start | bytes 18436
  141.1 37.3 %copy-start.26 = (f32[1536]{0:T(1024)S(1)}, f32[1536]{0:T(1024)}, u32[]{:S(2)}) copy-start(f32[1536]{0:T(1024)} %copy-done.25) | copy-start | bytes 18436
  141.1 37.3 %copy-start.28 = (f32[1536]{0:T(1024)S(1)}, f32[1536]{0:T(1024)}, u32[]{:S(2)}) copy-start(f32[1536]{0:T(1024)} %copy-done.27) | copy-start | bytes 18436
  141.1 37.3 %copy-start.30 = (f32[1536]{0:T(1024)S(1)}, f32[1536]{0:T(1024)}, u32[]{:S(2)}) copy-start(f32[1536]{0:T(1024)} %copy-done.29) | copy-start | bytes 18436
  141.1 37.3 %copy-start.32 = (f32[1536]{0:T(1024)S(1)}, f32[1536]{0:T(1024)}, u32[]{:S(2)}) copy-start(f32[1536]{0:T(1024)} %copy-done.31) | copy-start | bytes 18436
  141.1 37.3 %copy-start.34 = (f32[1536]{0:T(1024)S(1)}, f32[1536]{0:T(1024)}, u32[]{:S(2)}) copy-start(f32[1536]{0:T(1024)} %copy-done.33) | copy-start | bytes 18436
  141.1 37.3 %copy-start.36 = (f32[1536]{0:T(1024)S(1)}, f32[1536]{0:T(1024)}, u32[]{:S(2)}) copy-start(f32[1536]{0:T(1024)} %copy-done.35) | copy-start | bytes 18436
  141.2 37.3 %copy-start.38 = (f32[1536]{0:T(1024)S(1)}, f32[1536]{0:T(1024)}, u32[]{:S(2)}) copy-start(f32[1536]{0:T(1024)} %copy-done.37) | copy-start | bytes 18436
  141.2 37.3 %copy-start.40 = (f32[1536]{0:T(1024)S(1)}, f32[1536]{0:T(1024)}, u32[]{:S(2)}) copy-start(f32[1536]{0:T(1024)} %copy-done.39) | copy-start | bytes 18436
  141.2 37.3 %copy-start.42 = (f32[1536]{0:T(1024)S(1)}, f32[1536]{0:T(1024)}, u32[]{:S(2)}) copy-start(f32[1536]{0:T(1024)} %copy-done.41) | copy-start | bytes 18436
  141.2 37.3 %copy-start.44 = (f32[1536]{0:T(1024)S(1)}, f32[1536]{0:T(1024)}, u32[]{:S(2)}) copy-start(f32[1536]{0:T(1024)} %copy-done.43) | copy-start | bytes 18436
  141.2 37.3 %copy-start.46 = (f32[1536]{0:T(1024)S(1)}, f32[1536]{0:T(1024)}, u32[]{:S(2)}) copy-start(f32[1536]{0:T(1024)} %copy-done.45) | copy-start | bytes 18436
  141.4 4.9 %collective-permute-start.18 = (f32[9408]{0:T(1024)S(1)}, f32[9408]{0:T(1024)S(1)}, u32[]{:S(2)}, u32[]{:S(2)}) collective-permute-start(f32[9408]{0:T(1024)S(1)} %get-tuple-element.118), channel_id=1, source_target_pairs={{0,4},{4,0},{8,12},{12,8},{16,20},{20,16},{24,28},{28,24},{1,5},{5... | collective-permute-start | bytes 112904 | tf_op jit(solution)/shard_map/ppermute | solution.py:49
  146.5 5.3 %collective-permute-start.19 = (f32[4704]{0:T(1024)S(1)}, f32[4704]{0:T(1024)S(1)}, u32[]{:S(2)}, u32[]{:S(2)}) collective-permute-start(f32[4704]{0:T(1024)S(1)} %get-tuple-element.120), channel_id=1, source_target_pairs={{0,8},{4,12},{8,0},{12,4},{16,24},{20,28},{24,16},{28,20},{1,9},{5... | collective-permute-start | bytes 56456 | tf_op jit(solution)/shard_map/ppermute | solution.py:49
  152.0 5.5 %collective-permute-start.20 = (f32[2352]{0:T(1024)S(1)}, f32[2352]{0:T(1024)S(1)}, u32[]{:S(2)}, u32[]{:S(2)}) collective-permute-start(f32[2352]{0:T(1024)S(1)} %get-tuple-element.122), channel_id=1, source_target_pairs={{0,16},{4,20},{8,24},{12,28},{16,0},{20,4},{24,8},{28,12},{1,17},{... | collective-permute-start | bytes 28232 | tf_op jit(solution)/shard_map/ppermute | solution.py:49
  157.5 5.1 %collective-permute-start.21 = (f32[2352]{0:T(1024)S(1)}, f32[2352]{0:T(1024)S(1)}, u32[]{:S(2)}, u32[]{:S(2)}) collective-permute-start(f32[2352]{0:T(1024)S(1)} %add.722), channel_id=1, source_target_pairs={{0,16},{4,20},{8,24},{12,28},{16,0},{20,4},{24,8},{28,12},{1,17},{... | collective-permute-start | bytes 28232 | tf_op jit(solution)/shard_map/ppermute | solution.py:52
  162.6 3.8 %collective-permute-start.22 = (f32[4704]{0:T(1024)S(1)}, f32[4704]{0:T(1024)S(1)}, u32[]{:S(2)}, u32[]{:S(2)}) collective-permute-start(f32[4704]{0:T(1024)S(1)} %maximum_select_fusion.6), channel_id=1, source_target_pairs={{0,8},{4,12},{8,0},{12,4},{16,24},{20,28},{24,16},{28,20},{1,9},{5... | collective-permute-start | bytes 56456 | tf_op jit(solution)/shard_map/ppermute | solution.py:52
  166.5 4.1 %collective-permute-start.23 = (f32[9408]{0:T(1024)S(1)}, f32[9408]{0:T(1024)S(1)}, u32[]{:S(2)}, u32[]{:S(2)}) collective-permute-start(f32[9408]{0:T(1024)S(1)} %maximum_select_fusion.5), channel_id=1, source_target_pairs={{0,4},{4,0},{8,12},{12,8},{16,20},{20,16},{24,28},{28,24},{1,5},{5... | collective-permute-start | bytes 112904 | tf_op jit(solution)/shard_map/ppermute | solution.py:52
  166.7 7.3 %collective-permute-start.14 = (bf16[3,16,1536]{2,1,0:T(8,128)(2,1)S(1)}, bf16[3,16,1536]{2,1,0:T(8,128)(2,1)S(1)}, u32[]{:S(2)}, u32[]{:S(2)}) collective-permute-start(bf16[3,16,1536]{2,1,0:T(8,128)(2,1)S(1)} %get-tuple-element.128), channel_id=1, source_target_pairs={{0,1},{1,2},{2,3},{4,5},{5,6},{6,7},{8,9},{9,10},{10,11},{12,13},{... | collective-permute-start | bytes 442376 | tf_op jit(solution)/shard_map/ppermute | solution.py:16
  167.9 6.0 %collective-permute-start.15 = (bf16[3,16,1536]{2,1,0:T(8,128)(2,1)S(1)}, bf16[3,16,1536]{2,1,0:T(8,128)(2,1)S(1)}, u32[]{:S(2)}, u32[]{:S(2)}) collective-permute-start(bf16[3,16,1536]{2,1,0:T(8,128)(2,1)S(1)} %get-tuple-element.128), channel_id=1, source_target_pairs={{1,0},{2,1},{3,2},{5,4},{6,5},{7,6},{9,8},{10,9},{11,10},{13,12},{... | collective-permute-start | bytes 442376 | tf_op jit(solution)/shard_map/ppermute | solution.py:19
  170.7 7.5 %collective-permute-start.24 = (f32[18816]{0:T(1024)S(1)}, f32[18816]{0:T(1024)S(1)}, u32[]{:S(2)}, u32[]{:S(2)}) collective-permute-start(f32[18816]{0:T(1024)S(1)} %maximum_select_fusion.4), channel_id=1, source_target_pairs={{0,2},{1,3},{2,0},{3,1},{4,6},{5,7},{6,4},{7,5},{8,10},{9,11},{10,... | collective-permute-start | bytes 225800 | tf_op jit(solution)/shard_map/ppermute | solution.py:52
  178.2 3.3 %collective-permute-start.25 = (f32[37632]{0:T(1024)S(1)}, f32[37632]{0:T(1024)S(1)}, u32[]{:S(2)}, u32[]{:S(2)}) collective-permute-start(f32[37632]{0:T(1024)S(1)} %maximum_select_fusion.3), channel_id=1, source_target_pairs={{0,1},{1,0},{2,3},{3,2},{4,5},{5,4},{6,7},{7,6},{8,9},{9,8},{10,11... | collective-permute-start | bytes 451592 | tf_op jit(solution)/shard_map/ppermute | solution.py:52
  (70 other events, 1025.7 us)
Sparse Core Ops, SparseCore 0:
  114.5 96.9 reduce-scatter.1

commit v19 on v14

--- a/solution.py
+++ b/solution.py
@@ -127,7 +127,7 @@
         if s <= behind:
             ccw = lax.ppermute(ccw, axis, backward)
         if s == 1 and held is not None:
-            cw, ccw, held = lax.optimization_barrier((cw, ccw, held))
+            cw, held = lax.optimization_barrier((cw, held))
         gathered = lax.dynamic_update_index_in_dim(gathered, cw, ring_arr[(spot - s) % count], 0)
         if s <= behind:
             gathered = lax.dynamic_update_index_in_dim(

time: 206 us -> 206 us (level)
  no operation moved by 1% of the time
where the time goes in v19:
time: 206 us; the launch traced here: 205 us
  waiting for transfers between devices  91.8 us (45%)
  between operations  34.9 us (17%)
  starting transfers between devices  30.5 us (15%)
  other arithmetic  19.3 us (9%)
  matrix products  12.4 us (6%)
  local copies, waits for them, and re-layouts  9.43 us (5%)
  blocking collectives  6.61 us (3%)
    reduce_scatter x1, waiting for transfers between devices, body(): lax.psum_scatter(w_term.astype(jnp.bfloat16), 'fsdp', scatter_dimension=0...  27.5 us
    ppermute x5, waiting for transfers between devices, tree_allreduce(): flat = keep + lax.ppermute(give, axis, perm)  17.1 us
    ppermute x5, waiting for transfers between devices, tree_allreduce(): other = lax.ppermute(flat, axis, perm)  13 us
    ppermute x2, waiting for transfers between devices, tree_reduce_scatter(): lax.ppermute(give, axis, perm).astype(jnp.float32)  8.28 us
    ppermute x3, starting transfers between devices, ring_all_gather(): cw = lax.ppermute(cw, axis, forward)  7.1 us
    ppermute x1, waiting for transfers between devices, ring_all_gather(): lax.ppermute(cw[..., :half], axis, forward)  7.09 us
    ppermute x2, waiting for transfers between devices, tree_all_gather(): other = lax.ppermute(data, axis, perm)  6.9 us
    ppermute x3, waiting for transfers between devices, ring_all_gather(): cw = lax.ppermute(cw, axis, forward)  6.79 us
  transfers between devices with their start and end apart: 27, of which 21 were waited for; matrix products, arithmetic and copies ran while one was open for 11% of the time, Pallas kernels for 0%

profile of v19, /device:TPU:0, one launch (start us, length us, event | category | flops | bytes accessed | tf_op | source)
XLA Modules:
  0.0 205.0 jit_solution(2173826256059492440)
XLA Ops:
  7.2 1.1 compare_select_fusion
  8.4 3.1 %collective-permute-start = (bf16[192,1536]{1,0:T(8,128)(2,1)S(1)}, bf16[192,1536]{1,0:T(8,128)(2,1)S(1)}, u32[]{:S(2)}, u32[]{:S(2)}) collective-permute-start(bf16[192,1536]{1,0:T(8,128)(2,1)S(1)} %compare_select_fusion), channel_id=1, source_target_pairs={{0,8},{8,16},{16,24},{24,28},{28,20},{20,12},{12,4},{4,0},{1,9},{9... | collective-permute-start | bytes 1769480 | tf_op jit(solution)/shard_map/ppermute | solution.py:126
  26.6 0.9 slice_reduce_fusion.47
  33.9 1.5 collective-permute-start.1
  35.4 1.3 collective-permute-start.2
  36.7 1.9 collective-permute-start.6
  39.0 1.6 collective-permute-done.2
  41.1 3.4 %fusion.153 = (f32[3,16]{1,0:T(4,128)S(1)}, f32[3,16,1536]{2,1,0:T(8,128)S(1)}) fusion(f32[1536]{0:T(1024)S(1)} %get-tuple-element.103, bf16[9,22,1536]{2,1,0:T(8,128)(2,1)S(1)} %select_maximum_fusion.2, f32[1536]{0:T(1024)S(1)} %get-tuple-element.104, f32[1536]{0:T(1024)S(1)} %get-tuple-element.57, f32[1536]{0:T(1024)S(1)} %get-tuple-element.58, ...), kind=kLoop, calls=%fused_computation.375 | loop fusion | flops 10911696 | bytes 7827648 | tf_op jit(solution)/shard_map/reduce_sum | solution.py:228
  44.9 4.1 %collective-permute-start.3 = (bf16[1,3,16,1536]{3,2,1,0:T(8,128)(2,1)S(1)}, bf16[1,3,16,1536]{3,2,1,0:T(8,128)(2,1)S(1)}, u32[]{:S(2)}, u32[]{:S(2)}) collective-permute-start(bf16[1,3,16,1536]{3,2,1,0:T(8,128)(2,1)S(1)} %fusion.144), channel_id=1, source_target_pairs={{0,1},{1,0},{2,3},{3,2},{4,5},{5,4},{6,7},{7,6},{8,9},{9,8},{10,11... | collective-permute-start | bytes 442376 | tf_op jit(solution)/shard_map/ppermute | solution.py:182
  49.0 1.0 collective-permute-done.3
  50.7 2.1 %collective-permute-start.8 = (bf16[192,1536]{1,0:T(8,128)(2,1)S(1)}, bf16[192,1536]{1,0:T(8,128)(2,1)S(1)}, u32[]{:S(2)}, u32[]{:S(2)}) collective-permute-start(bf16[192,1536]{1,0:T(8,128)(2,1)S(1)} %collective-permute-done.6), channel_id=1, source_target_pairs={{0,8},{8,16},{16,24},{24,28},{28,20},{20,12},{12,4},{4,0},{1,9},{9... | collective-permute-start | bytes 1769480 | tf_op jit(solution)/shard_map/ppermute | solution.py:126
  53.4 5.9 %collective-permute-done.4 = bf16[2,3,16,1536]{3,2,1,0:T(8,128)(2,1)S(1)} collective-permute-done((bf16[2,3,16,1536]{3,2,1,0:T(8,128)(2,1)S(1)}, bf16[2,3,16,1536]{3,2,1,0:T(8,128)(2,1)S(1)}, u32[]{:S(2)}, u32[]{:S(2)}) %collective-permute-start.4) | collective-permute-done | bytes 294944 | tf_op jit(solution)/shard_map/ppermute | solution.py:182
  59.5 6.1 %collective-permute-done.8 = bf16[192,1536]{1,0:T(8,128)(2,1)S(1)} collective-permute-done((bf16[192,1536]{1,0:T(8,128)(2,1)S(1)}, bf16[192,1536]{1,0:T(8,128)(2,1)S(1)}, u32[]{:S(2)}, u32[]{:S(2)}) %collective-permute-start.8) | collective-permute-done | bytes 589856 | tf_op jit(solution)/shard_map/ppermute | solution.py:126
  65.6 2.4 %collective-permute-start.10 = (bf16[192,768]{1,0:T(8,128)(2,1)S(1)}, bf16[192,768]{1,0:T(8,128)(2,1)S(1)}, u32[]{:S(2)}, u32[]{:S(2)}) collective-permute-start(bf16[192,768]{1,0:T(8,128)(2,1)S(1)} %slice.744), channel_id=1, source_target_pairs={{0,8},{8,16},{16,24},{24,28},{28,20},{20,12},{12,4},{4,0},{1,9},{9... | collective-permute-start | bytes 884744 | tf_op jit(solution)/shard_map/ppermute | solution.py:117
  68.0 0.7 collective-permute-done.9
  69.0 7.1 %collective-permute-done.10 = bf16[192,768]{1,0:T(8,128)(2,1)S(1)} collective-permute-done((bf16[192,768]{1,0:T(8,128)(2,1)S(1)}, bf16[192,768]{1,0:T(8,128)(2,1)S(1)}, u32[]{:S(2)}, u32[]{:S(2)}) %collective-permute-start.10) | collective-permute-done | bytes 294944 | tf_op jit(solution)/shard_map/ppermute | solution.py:117
  76.1 2.3 %collective-permute-done.11 = bf16[192,768]{1,0:T(8,128)(2,1)S(1)} collective-permute-done((bf16[192,768]{1,0:T(8,128)(2,1)S(1)}, bf16[192,768]{1,0:T(8,128)(2,1)S(1)}, u32[]{:S(2)}, u32[]{:S(2)}) %collective-permute-start.11) | collective-permute-done | bytes 294944 | tf_op jit(solution)/shard_map/ppermute | solution.py:118
  78.5 4.8 %fusion.4 = (f32[1536]{0:T(1024)S(1)}, f32[1536]{0:T(1024)S(1)}, f32[192,1536]{1,0:T(8,128)}, f32[192,1536]{1,0:T(8,128)}) fusion(bf16[1,12,16,1536]{3,2,1,0:T(8,128)(2,1)S(1)} %copy-done.3, f32[1536]{0:T(1024)S(1)} %copy-done.54, bf16[192,1536]{1,0:T(8,128)(2,1)S(1)} %bitcast.66, bf16[1536,1536]{1,0:T(8,128)(2,1)S(1)} %bitcast.64), kind=kOutput, calls=%fused_computation.64 | convolution fusion | flops 926610432 | bytes 8275968 | tf_op jit(solution)/shard_map/dot_general | solution.py:286
  84.0 6.6 %all-reduce.2 = (f32[]{:T(128)}, f32[]{:T(128)}) all-reduce(f32[]{:T(128)} %get-tuple-element.125, f32[]{:T(128)} %get-tuple-element.124), channel_id=1, replica_groups=mesh['fsdp'=8,'rows'=4] {'rows'}, use_global_device_ids=true, to_apply=%region_4.5 | all-reduce | flops 2 | bytes 16 | tf_op jit(solution)/shard_map/psum | solution.py:291
  92.0 3.4 %fusion.3 = (bf16[192,1536]{1,0:T(8,128)(2,1)S(1)}, bf16[192,1536]{1,0:T(8,128)(2,1)}) fusion(f32[192,1536]{1,0:T(8,128)} %get-tuple-element.147, f32[192,1536]{1,0:T(8,128)} %get-tuple-element.132, bf16[1,12,16,1536]{3,2,1,0:T(8,128)(2,1)} %param.21, f32[1536]{0:T(1024)S(1)} %get-tuple-element.139, f32[1536]{0:T(1024)S(1)} %get-tuple-element.130, ...), kind=kLoop, calls=%fused_computation.63 | loop fusion | flops 5603328 | bytes 4159488 | tf_op jit(solution)/shard_map/convert_element_type | solution.py:298
  95.4 3.6 %convolution_convert_fusion = bf16[1536,1536]{1,0:T(8,128)(2,1)} fusion(bf16[192,1536]{1,0:T(8,128)(2,1)S(1)} %bitcast.67, bf16[192,1536]{1,0:T(8,128)(2,1)S(1)} %get-tuple-element.135), kind=kOutput, calls=%fused_computation | convolution fusion | flops 908328960 | bytes 5898240 | tf_op jit(solution)/shard_map/dot_general | solution.py:299
  98.9 4.0 %convolution_convert_fusion.1 = bf16[12,16,1536]{2,1,0:T(8,128)(2,1)S(1)} fusion(bf16[12,16,1536]{2,1,0:T(8,128)(2,1)S(1)} %bitcast.68, bf16[1536,1536,1]{1,0,2:T(8,128)(2,1)} %bitcast.65), kind=kOutput, calls=%fused_computation.52 | convolution fusion | flops 906264576 | bytes 5898240 | tf_op jit(solution)/shard_map/hwf,cf->hwc/dot_general | solution.py:306
  103.8 0.9 collective-permute-done.12
  104.7 1.0 convert_add_fusion
  105.7 1.7 collective-permute-start.13
  107.5 7.4 %collective-permute-done.13 = f32[1,3,16,1536]{3,2,1,0:T(8,128)S(1)} collective-permute-done((f32[1,3,16,1536]{3,2,1,0:T(8,128)S(1)}, f32[1,3,16,1536]{3,2,1,0:T(8,128)S(1)}, u32[]{:S(2)}, u32[]{:S(2)}) %collective-permute-start.13) | collective-permute-done | bytes 294944 | tf_op jit(solution)/shard_map/ppermute | solution.py:69
  115.1 1.6 fusion.141
  117.5 0.8 fusion.142
  119.5 0.9 dynamic-slice_reduce_fusion
  120.5 1.4 collective-permute-done.16
  122.4 1.7 collective-permute-start.17
  124.1 2.8 %collective-permute-done.17 = f32[18816]{0:T(1024)S(1)} collective-permute-done((f32[18816]{0:T(1024)S(1)}, f32[18816]{0:T(1024)S(1)}, u32[]{:S(2)}, u32[]{:S(2)}) %collective-permute-start.17) | collective-permute-done | bytes 75296 | tf_op jit(solution)/shard_map/ppermute | solution.py:49
  127.7 4.6 %collective-permute-done.18 = f32[9408]{0:T(1024)S(1)} collective-permute-done((f32[9408]{0:T(1024)S(1)}, f32[9408]{0:T(1024)S(1)}, u32[]{:S(2)}, u32[]{:S(2)}) %collective-permute-start.18) | collective-permute-done | bytes 37664 | tf_op jit(solution)/shard_map/ppermute | solution.py:49
  132.5 1.5 collective-permute-start.19
  134.0 3.9 %collective-permute-done.19 = f32[4704]{0:T(1024)S(1)} collective-permute-done((f32[4704]{0:T(1024)S(1)}, f32[4704]{0:T(1024)S(1)}, u32[]{:S(2)}, u32[]{:S(2)}) %collective-permute-start.19) | collective-permute-done | bytes 18848 | tf_op jit(solution)/shard_map/ppermute | solution.py:49
  138.0 1.5 collective-permute-start.20
  139.5 4.5 %collective-permute-done.20 = f32[2352]{0:T(1024)S(1)} collective-permute-done((f32[2352]{0:T(1024)S(1)}, f32[2352]{0:T(1024)S(1)}, u32[]{:S(2)}, u32[]{:S(2)}) %collective-permute-start.20) | collective-permute-done | bytes 9440 | tf_op jit(solution)/shard_map/ppermute | solution.py:49
  144.6 4.2 %collective-permute-done.21 = f32[2352]{0:T(1024)S(1)} collective-permute-done((f32[2352]{0:T(1024)S(1)}, f32[2352]{0:T(1024)S(1)}, u32[]{:S(2)}, u32[]{:S(2)}) %collective-permute-start.21) | collective-permute-done | bytes 9440 | tf_op jit(solution)/shard_map/ppermute | solution.py:52
  149.0 3.7 %collective-permute-done.22 = f32[4704]{0:T(1024)S(1)} collective-permute-done((f32[4704]{0:T(1024)S(1)}, f32[4704]{0:T(1024)S(1)}, u32[]{:S(2)}, u32[]{:S(2)}) %collective-permute-start.22) | collective-permute-done | bytes 18848 | tf_op jit(solution)/shard_map/ppermute | solution.py:52
  153.2 1.3 collective-permute-start.14
  154.5 1.3 collective-permute-start.15
  155.8 1.1 collective-permute-done.23
  156.9 3.3 %collective-permute-start.24 = (f32[18816]{0:T(1024)S(1)}, f32[18816]{0:T(1024)S(1)}, u32[]{:S(2)}, u32[]{:S(2)}) collective-permute-start(f32[18816]{0:T(1024)S(1)} %maximum_select_fusion.4), channel_id=1, source_target_pairs={{0,2},{1,3},{2,0},{3,1},{4,6},{5,7},{6,4},{7,5},{8,10},{9,11},{10,... | collective-permute-start | bytes 225800 | tf_op jit(solution)/shard_map/ppermute | solution.py:52
  160.5 4.0 %collective-permute-done.24 = f32[18816]{0:T(1024)S(1)} collective-permute-done((f32[18816]{0:T(1024)S(1)}, f32[18816]{0:T(1024)S(1)}, u32[]{:S(2)}, u32[]{:S(2)}) %collective-permute-start.24) | collective-permute-done | bytes 75296 | tf_op jit(solution)/shard_map/ppermute | solution.py:52
  164.8 2.8 %fusion.147 = bf16[1,3,16,1536]{3,2,1,0:T(8,128)(2,1)} fusion(f32[1536]{0:T(1024)S(1)} %copy-done.44, bf16[9,22,1536]{2,1,0:T(8,128)(2,1)S(1)} %select_maximum_fusion, f32[1536]{0:T(1024)S(1)} %copy-done.46, f32[1536]{0:T(1024)S(1)} %get-tuple-element.57, f32[1536]{0:T(1024)S(1)} %get-tuple-element.58, bf16[3,16,1536]{2,1,0:T(8,128)(2,1)S(1)} %collective-permute-done.14, ...), kind=kLoop, calls=%fused_computation.298 | loop fusion | flops 11132928 | bytes 7084032 | tf_op jit(solution)/shard_map/reshape | solution.py:321
  167.6 0.8 select_n.294
  168.4 27.5 %reduce-scatter.2.cloned.1.call-done = bf16[192,1536]{1,0:T(8,128)(2,1)} async-done(((bf16[1536,1536]{1,0:T(8,128)(2,1)}), bf16[192,1536]{1,0:T(8,128)(2,1)}) %reduce-scatter.2.cloned.1.call-update) | async-done | bytes 589840 | tf_op jit(solution)/shard_map/reduce_scatter | solution.py:302
  195.9 2.2 %convert_element_type.497 = f32[192,1536]{1,0:T(8,128)} convert(bf16[192,1536]{1,0:T(8,128)(2,1)} %reduce-scatter.2.cloned.1.call-done) | non-fusion elementwise | flops 294912 | bytes 1769472 | tf_op jit(solution)/shard_map/convert_element_type | solution.py:304
  (236 shorter events, 12.9 us)
Async XLA Ops:
  7.2 188.7 %reduce-scatter.2.cloned.1.call-start = ((), (), s32[]{:S(2)}) async-start(), calls=%async_computation.1 | async-start | bytes 5308416 | tf_op jit(solution)/shard_map/reduce_scatter | solution.py:302
  8.4 25.1 %collective-permute-start = (bf16[192,1536]{1,0:T(8,128)(2,1)S(1)}, bf16[192,1536]{1,0:T(8,128)(2,1)S(1)}, u32[]{:S(2)}, u32[]{:S(2)}) collective-permute-start(bf16[192,1536]{1,0:T(8,128)(2,1)S(1)} %compare_select_fusion), channel_id=1, source_target_pairs={{0,8},{8,16},{16,24},{24,28},{28,20},{20,12},{12,4},{4,0},{1,9},{9... | collective-permute-start | bytes 1769480 | tf_op jit(solution)/shard_map/ppermute | solution.py:126
  11.5 27.3 %collective-permute-start.5 = (bf16[192,1536]{1,0:T(8,128)(2,1)S(1)}, bf16[192,1536]{1,0:T(8,128)(2,1)S(1)}, u32[]{:S(2)}, u32[]{:S(2)}) collective-permute-start(bf16[192,1536]{1,0:T(8,128)(2,1)S(1)} %compare_select_fusion), channel_id=1, source_target_pairs={{0,4},{8,0},{16,8},{24,16},{28,24},{20,28},{12,20},{4,12},{1,5},{9... | collective-permute-start | bytes 1769480 | tf_op jit(solution)/shard_map/ppermute | solution.py:128
  33.9 5.1 %collective-permute-start.1 = (bf16[3,16,1536]{2,1,0:T(8,128)(2,1)S(1)}, bf16[3,16,1536]{2,1,0:T(8,128)(2,1)S(1)}, u32[]{:S(2)}, u32[]{:S(2)}) collective-permute-start(bf16[3,16,1536]{2,1,0:T(8,128)(2,1)S(1)} %bitcast.69), channel_id=1, source_target_pairs={{0,1},{1,2},{2,3},{4,5},{5,6},{6,7},{8,9},{9,10},{10,11},{12,13},{... | collective-permute-start | bytes 442376 | tf_op jit(solution)/shard_map/ppermute | solution.py:16
  35.4 5.3 %collective-permute-start.2 = (bf16[3,16,1536]{2,1,0:T(8,128)(2,1)S(1)}, bf16[3,16,1536]{2,1,0:T(8,128)(2,1)S(1)}, u32[]{:S(2)}, u32[]{:S(2)}) collective-permute-start(bf16[3,16,1536]{2,1,0:T(8,128)(2,1)S(1)} %bitcast.70), channel_id=1, source_target_pairs={{1,0},{2,1},{3,2},{5,4},{6,5},{7,6},{9,8},{10,9},{11,10},{13,12},{... | collective-permute-start | bytes 442376 | tf_op jit(solution)/shard_map/ppermute | solution.py:19
  36.7 14.0 %collective-permute-start.6 = (bf16[192,1536]{1,0:T(8,128)(2,1)S(1)}, bf16[192,1536]{1,0:T(8,128)(2,1)S(1)}, u32[]{:S(2)}, u32[]{:S(2)}) collective-permute-start(bf16[192,1536]{1,0:T(8,128)(2,1)S(1)} %collective-permute-done), channel_id=1, source_target_pairs={{0,8},{8,16},{16,24},{24,28},{28,20},{20,12},{12,4},{4,0},{1,9},{9... | collective-permute-start | bytes 1769480 | tf_op jit(solution)/shard_map/ppermute | solution.py:126
  38.7 14.6 %collective-permute-start.7 = (bf16[192,1536]{1,0:T(8,128)(2,1)S(1)}, bf16[192,1536]{1,0:T(8,128)(2,1)S(1)}, u32[]{:S(2)}, u32[]{:S(2)}) collective-permute-start(bf16[192,1536]{1,0:T(8,128)(2,1)S(1)} %collective-permute-done.5), channel_id=1, source_target_pairs={{0,4},{8,0},{16,8},{24,16},{28,24},{20,28},{12,20},{4,12},{1,5},{9... | collective-permute-start | bytes 1769480 | tf_op jit(solution)/shard_map/ppermute | solution.py:128
  44.6 70.3 %copy-start.47 = (f32[3,16]{1,0:T(4,128)}, f32[3,16]{1,0:T(4,128)S(1)}, u32[]{:S(2)}) copy-start(f32[3,16]{1,0:T(4,128)S(1)} %broadcast_multiply_fusion.2) | copy-start | bytes 580
  44.8 70.1 %copy-start.48 = (f32[3,16]{1,0:T(4,128)}, f32[3,16]{1,0:T(4,128)S(1)}, u32[]{:S(2)}) copy-start(f32[3,16]{1,0:T(4,128)S(1)} %add_rsqrt_fusion) | copy-start | bytes 580
  44.9 5.1 %collective-permute-start.3 = (bf16[1,3,16,1536]{3,2,1,0:T(8,128)(2,1)S(1)}, bf16[1,3,16,1536]{3,2,1,0:T(8,128)(2,1)S(1)}, u32[]{:S(2)}, u32[]{:S(2)}) collective-permute-start(bf16[1,3,16,1536]{3,2,1,0:T(8,128)(2,1)S(1)} %fusion.144), channel_id=1, source_target_pairs={{0,1},{1,0},{2,3},{3,2},{4,5},{5,4},{6,7},{7,6},{8,9},{9,8},{10,11... | collective-permute-start | bytes 442376 | tf_op jit(solution)/shard_map/ppermute | solution.py:182
  50.0 9.3 %collective-permute-start.4 = (bf16[2,3,16,1536]{3,2,1,0:T(8,128)(2,1)S(1)}, bf16[2,3,16,1536]{3,2,1,0:T(8,128)(2,1)S(1)}, u32[]{:S(2)}, u32[]{:S(2)}) collective-permute-start(bf16[2,3,16,1536]{3,2,1,0:T(8,128)(2,1)S(1)} %maximum_select_fusion.2), channel_id=1, source_target_pairs={{0,2},{1,3},{2,0},{3,1},{4,6},{5,7},{6,4},{7,5},{8,10},{9,11},{10,... | collective-permute-start | bytes 884744 | tf_op jit(solution)/shard_map/ppermute | solution.py:182
  50.7 14.9 %collective-permute-start.8 = (bf16[192,1536]{1,0:T(8,128)(2,1)S(1)}, bf16[192,1536]{1,0:T(8,128)(2,1)S(1)}, u32[]{:S(2)}, u32[]{:S(2)}) collective-permute-start(bf16[192,1536]{1,0:T(8,128)(2,1)S(1)} %collective-permute-done.6), channel_id=1, source_target_pairs={{0,8},{8,16},{16,24},{24,28},{28,20},{20,12},{12,4},{4,0},{1,9},{9... | collective-permute-start | bytes 1769480 | tf_op jit(solution)/shard_map/ppermute | solution.py:126
  53.3 15.4 %collective-permute-start.9 = (bf16[192,1536]{1,0:T(8,128)(2,1)S(1)}, bf16[192,1536]{1,0:T(8,128)(2,1)S(1)}, u32[]{:S(2)}, u32[]{:S(2)}) collective-permute-start(bf16[192,1536]{1,0:T(8,128)(2,1)S(1)} %collective-permute-done.7), channel_id=1, source_target_pairs={{0,4},{8,0},{16,8},{24,16},{28,24},{20,28},{12,20},{4,12},{1,5},{9... | collective-permute-start | bytes 1769480 | tf_op jit(solution)/shard_map/ppermute | solution.py:128
  65.6 10.4 %collective-permute-start.10 = (bf16[192,768]{1,0:T(8,128)(2,1)S(1)}, bf16[192,768]{1,0:T(8,128)(2,1)S(1)}, u32[]{:S(2)}, u32[]{:S(2)}) collective-permute-start(bf16[192,768]{1,0:T(8,128)(2,1)S(1)} %slice.744), channel_id=1, source_target_pairs={{0,8},{8,16},{16,24},{24,28},{28,20},{20,12},{12,4},{4,0},{1,9},{9... | collective-permute-start | bytes 884744 | tf_op jit(solution)/shard_map/ppermute | solution.py:117
  68.8 9.6 %collective-permute-start.11 = (bf16[192,768]{1,0:T(8,128)(2,1)S(1)}, bf16[192,768]{1,0:T(8,128)(2,1)S(1)}, u32[]{:S(2)}, u32[]{:S(2)}) collective-permute-start(bf16[192,768]{1,0:T(8,128)(2,1)S(1)} %slice.745), channel_id=1, source_target_pairs={{0,4},{8,0},{16,8},{24,16},{28,24},{20,28},{12,20},{4,12},{1,5},{9... | collective-permute-start | bytes 884744 | tf_op jit(solution)/shard_map/ppermute | solution.py:118
  103.0 1.6 collective-permute-start.12
  105.7 9.1 %collective-permute-start.13 = (f32[1,3,16,1536]{3,2,1,0:T(8,128)S(1)}, f32[1,3,16,1536]{3,2,1,0:T(8,128)S(1)}, u32[]{:S(2)}, u32[]{:S(2)}) collective-permute-start(f32[1,3,16,1536]{3,2,1,0:T(8,128)S(1)} %constant_dynamic-slice_fusion), channel_id=1, source_target_pairs={{0,2},{1,3},{2,0},{3,1},{4,6},{5,7},{6,4},{7,5},{8,10},{9,11},{10,... | collective-permute-start | bytes 884744 | tf_op jit(solution)/shard_map/ppermute | solution.py:69
  120.4 1.4 collective-permute-start.16
  122.4 4.5 %collective-permute-start.17 = (f32[18816]{0:T(1024)S(1)}, f32[18816]{0:T(1024)S(1)}, u32[]{:S(2)}, u32[]{:S(2)}) collective-permute-start(f32[18816]{0:T(1024)S(1)} %get-tuple-element.109), channel_id=1, source_target_pairs={{0,2},{1,3},{2,0},{3,1},{4,6},{5,7},{6,4},{7,5},{8,10},{9,11},{10,... | collective-permute-start | bytes 225800 | tf_op jit(solution)/shard_map/ppermute | solution.py:49
  127.2 37.4 %copy-start.8 = (f32[1536]{0:T(1024)S(1)}, f32[1536]{0:T(1024)}, u32[]{:S(2)}) copy-start(f32[1536]{0:T(1024)} %get-tuple-element.85) | copy-start | bytes 18436
  127.2 37.4 %copy-start.10 = (f32[1536]{0:T(1024)S(1)}, f32[1536]{0:T(1024)}, u32[]{:S(2)}) copy-start(f32[1536]{0:T(1024)} %get-tuple-element.86) | copy-start | bytes 18436
  127.2 37.4 %copy-start.12 = (f32[1536]{0:T(1024)S(1)}, f32[1536]{0:T(1024)}, u32[]{:S(2)}) copy-start(f32[1536]{0:T(1024)} %get-tuple-element.87) | copy-start | bytes 18436
  127.2 37.4 %copy-start.14 = (f32[1536]{0:T(1024)S(1)}, f32[1536]{0:T(1024)}, u32[]{:S(2)}) copy-start(f32[1536]{0:T(1024)} %get-tuple-element.88) | copy-start | bytes 18436
  127.2 37.4 %copy-start.16 = (f32[1536]{0:T(1024)S(1)}, f32[1536]{0:T(1024)}, u32[]{:S(2)}) copy-start(f32[1536]{0:T(1024)} %get-tuple-element.89) | copy-start | bytes 18436
  127.3 37.4 %copy-start.18 = (f32[1536]{0:T(1024)S(1)}, f32[1536]{0:T(1024)}, u32[]{:S(2)}) copy-start(f32[1536]{0:T(1024)} %get-tuple-element.90) | copy-start | bytes 18436
  127.3 37.4 %copy-start.20 = (f32[1536]{0:T(1024)S(1)}, f32[1536]{0:T(1024)}, u32[]{:S(2)}) copy-start(f32[1536]{0:T(1024)} %get-tuple-element.91) | copy-start | bytes 18436
  127.3 37.4 %copy-start.22 = (f32[1536]{0:T(1024)S(1)}, f32[1536]{0:T(1024)}, u32[]{:S(2)}) copy-start(f32[1536]{0:T(1024)} %get-tuple-element.92) | copy-start | bytes 18436
  127.3 37.4 %copy-start.24 = (f32[1536]{0:T(1024)S(1)}, f32[1536]{0:T(1024)}, u32[]{:S(2)}) copy-start(f32[1536]{0:T(1024)} %get-tuple-element.93) | copy-start | bytes 18436
  127.3 37.4 %copy-start.26 = (f32[1536]{0:T(1024)S(1)}, f32[1536]{0:T(1024)}, u32[]{:S(2)}) copy-start(f32[1536]{0:T(1024)} %copy-done.25) | copy-start | bytes 18436
  127.3 37.4 %copy-start.28 = (f32[1536]{0:T(1024)S(1)}, f32[1536]{0:T(1024)}, u32[]{:S(2)}) copy-start(f32[1536]{0:T(1024)} %copy-done.27) | copy-start | bytes 18436
  127.3 37.4 %copy-start.30 = (f32[1536]{0:T(1024)S(1)}, f32[1536]{0:T(1024)}, u32[]{:S(2)}) copy-start(f32[1536]{0:T(1024)} %copy-done.29) | copy-start | bytes 18436
  127.3 37.4 %copy-start.32 = (f32[1536]{0:T(1024)S(1)}, f32[1536]{0:T(1024)}, u32[]{:S(2)}) copy-start(f32[1536]{0:T(1024)} %copy-done.31) | copy-start | bytes 18436
  127.3 37.4 %copy-start.34 = (f32[1536]{0:T(1024)S(1)}, f32[1536]{0:T(1024)}, u32[]{:S(2)}) copy-start(f32[1536]{0:T(1024)} %copy-done.33) | copy-start | bytes 18436
  127.3 37.4 %copy-start.36 = (f32[1536]{0:T(1024)S(1)}, f32[1536]{0:T(1024)}, u32[]{:S(2)}) copy-start(f32[1536]{0:T(1024)} %copy-done.35) | copy-start | bytes 18436
  127.4 37.4 %copy-start.38 = (f32[1536]{0:T(1024)S(1)}, f32[1536]{0:T(1024)}, u32[]{:S(2)}) copy-start(f32[1536]{0:T(1024)} %copy-done.37) | copy-start | bytes 18436
  127.4 37.4 %copy-start.40 = (f32[1536]{0:T(1024)S(1)}, f32[1536]{0:T(1024)}, u32[]{:S(2)}) copy-start(f32[1536]{0:T(1024)} %copy-done.39) | copy-start | bytes 18436
  127.4 37.4 %copy-start.42 = (f32[1536]{0:T(1024)S(1)}, f32[1536]{0:T(1024)}, u32[]{:S(2)}) copy-start(f32[1536]{0:T(1024)} %copy-done.41) | copy-start | bytes 18436
  127.4 37.4 %copy-start.44 = (f32[1536]{0:T(1024)S(1)}, f32[1536]{0:T(1024)}, u32[]{:S(2)}) copy-start(f32[1536]{0:T(1024)} %copy-done.43) | copy-start | bytes 18436
  127.4 4.9 %collective-permute-start.18 = (f32[9408]{0:T(1024)S(1)}, f32[9408]{0:T(1024)S(1)}, u32[]{:S(2)}, u32[]{:S(2)}) collective-permute-start(f32[9408]{0:T(1024)S(1)} %get-tuple-element.118), channel_id=1, source_target_pairs={{0,4},{4,0},{8,12},{12,8},{16,20},{20,16},{24,28},{28,24},{1,5},{5... | collective-permute-start | bytes 112904 | tf_op jit(solution)/shard_map/ppermute | solution.py:49
  132.5 5.3 %collective-permute-start.19 = (f32[4704]{0:T(1024)S(1)}, f32[4704]{0:T(1024)S(1)}, u32[]{:S(2)}, u32[]{:S(2)}) collective-permute-start(f32[4704]{0:T(1024)S(1)} %get-tuple-element.120), channel_id=1, source_target_pairs={{0,8},{4,12},{8,0},{12,4},{16,24},{20,28},{24,16},{28,20},{1,9},{5... | collective-permute-start | bytes 56456 | tf_op jit(solution)/shard_map/ppermute | solution.py:49
  138.0 6.0 %collective-permute-start.20 = (f32[2352]{0:T(1024)S(1)}, f32[2352]{0:T(1024)S(1)}, u32[]{:S(2)}, u32[]{:S(2)}) collective-permute-start(f32[2352]{0:T(1024)S(1)} %get-tuple-element.122), channel_id=1, source_target_pairs={{0,16},{4,20},{8,24},{12,28},{16,0},{20,4},{24,8},{28,12},{1,17},{... | collective-permute-start | bytes 28232 | tf_op jit(solution)/shard_map/ppermute | solution.py:49
  144.1 4.7 %collective-permute-start.21 = (f32[2352]{0:T(1024)S(1)}, f32[2352]{0:T(1024)S(1)}, u32[]{:S(2)}, u32[]{:S(2)}) collective-permute-start(f32[2352]{0:T(1024)S(1)} %add.722), channel_id=1, source_target_pairs={{0,16},{4,20},{8,24},{12,28},{16,0},{20,4},{24,8},{28,12},{1,17},{... | collective-permute-start | bytes 28232 | tf_op jit(solution)/shard_map/ppermute | solution.py:52
  148.9 3.8 %collective-permute-start.22 = (f32[4704]{0:T(1024)S(1)}, f32[4704]{0:T(1024)S(1)}, u32[]{:S(2)}, u32[]{:S(2)}) collective-permute-start(f32[4704]{0:T(1024)S(1)} %maximum_select_fusion.6), channel_id=1, source_target_pairs={{0,8},{4,12},{8,0},{12,4},{16,24},{20,28},{24,16},{28,20},{1,9},{5... | collective-permute-start | bytes 56456 | tf_op jit(solution)/shard_map/ppermute | solution.py:52
  152.8 4.1 %collective-permute-start.23 = (f32[9408]{0:T(1024)S(1)}, f32[9408]{0:T(1024)S(1)}, u32[]{:S(2)}, u32[]{:S(2)}) collective-permute-start(f32[9408]{0:T(1024)S(1)} %maximum_select_fusion.5), channel_id=1, source_target_pairs={{0,4},{4,0},{8,12},{12,8},{16,20},{20,16},{24,28},{28,24},{1,5},{5... | collective-permute-start | bytes 112904 | tf_op jit(solution)/shard_map/ppermute | solution.py:52
  153.2 7.1 %collective-permute-start.14 = (bf16[3,16,1536]{2,1,0:T(8,128)(2,1)S(1)}, bf16[3,16,1536]{2,1,0:T(8,128)(2,1)S(1)}, u32[]{:S(2)}, u32[]{:S(2)}) collective-permute-start(bf16[3,16,1536]{2,1,0:T(8,128)(2,1)S(1)} %get-tuple-element.128), channel_id=1, source_target_pairs={{0,1},{1,2},{2,3},{4,5},{5,6},{6,7},{8,9},{9,10},{10,11},{12,13},{... | collective-permute-start | bytes 442376 | tf_op jit(solution)/shard_map/ppermute | solution.py:16
  154.5 5.8 %collective-permute-start.15 = (bf16[3,16,1536]{2,1,0:T(8,128)(2,1)S(1)}, bf16[3,16,1536]{2,1,0:T(8,128)(2,1)S(1)}, u32[]{:S(2)}, u32[]{:S(2)}) collective-permute-start(bf16[3,16,1536]{2,1,0:T(8,128)(2,1)S(1)} %get-tuple-element.128), channel_id=1, source_target_pairs={{1,0},{2,1},{3,2},{5,4},{6,5},{7,6},{9,8},{10,9},{11,10},{13,12},{... | collective-permute-start | bytes 442376 | tf_op jit(solution)/shard_map/ppermute | solution.py:19
  156.9 7.6 %collective-permute-start.24 = (f32[18816]{0:T(1024)S(1)}, f32[18816]{0:T(1024)S(1)}, u32[]{:S(2)}, u32[]{:S(2)}) collective-permute-start(f32[18816]{0:T(1024)S(1)} %maximum_select_fusion.4), channel_id=1, source_target_pairs={{0,2},{1,3},{2,0},{3,1},{4,6},{5,7},{6,4},{7,5},{8,10},{9,11},{10,... | collective-permute-start | bytes 225800 | tf_op jit(solution)/shard_map/ppermute | solution.py:52
  164.5 3.1 %collective-permute-start.25 = (f32[37632]{0:T(1024)S(1)}, f32[37632]{0:T(1024)S(1)}, u32[]{:S(2)}, u32[]{:S(2)}) collective-permute-start(f32[37632]{0:T(1024)S(1)} %maximum_select_fusion.3), channel_id=1, source_target_pairs={{0,1},{1,0},{2,3},{3,2},{4,5},{5,4},{6,7},{7,6},{8,9},{9,8},{10,11... | collective-permute-start | bytes 451592 | tf_op jit(solution)/shard_map/ppermute | solution.py:52
  (35 other events, 229.2 us)
Sparse Core Ops, SparseCore 0:
  99.1 96.8 reduce-scatter.1
